TPU v7x, 32 devices: a whole 2x2x4 slice. The times are simulated.
32 devices in a mesh: groups: 1, gx: 32 (over z, y, x, core).
Axes of the slice: x: 2, y: 2, z: 4, core: 2. Of those that a mesh axis runs over, the one named last changes fastest.
Arguments:
- solid_state: float32 [9, 2, 1, 256, 4, 128], P(None, None, 'groups', 'gx'), may hold values from -6 to 6
- water_state: float32 [4, 2, 1, 128, 12, 256], P(None, None, 'groups', 'gx'), may hold values from -6 to 6
- lame_lambda: float32 [256, 4, 128], P('gx'), may hold values from 0.4 to 1.2
- shear_mu: float32 [256, 4, 128], P('gx'), may hold values from 0.1 to 0.5
- solid_buoy: float32 [256, 4, 128], P('gx'), may hold values from 0.4 to 1
- water_kappa: float32 [128, 12, 256], P('gx'), may hold values from 0.5 to 1
- water_buoy: float32 [128, 12, 256], P('gx'), may hold values from 0.6 to 1.2
- seafloor: int32 [128, 256], P('gx'), may hold values from 6 to 12
- source_cell: int32 [1], P('groups'), may hold values from 0 to 196607
- wavelet: float32 [4, 1], P(None, 'groups'), may hold values from -48 to 48
- receiver_column: int32 [128], replicated, may hold values from 0 to 32767
- observed: float32 [4, 1, 128], P(None, 'groups'), may hold values from -6 to 6
Outputs:
- grad_lambda: float32 [256, 4, 128], P('gx', 'groups')
- grad_mu: float32 [256, 4, 128], P('gx', 'groups')
- grad_kappa: float32 [128, 12, 256], P('gx', 'groups')
- residuals: float32 [4, 1, 128], P(None, 'groups')
Inputs may be any that keep to these rules, and one draw needn't show every extreme that they name: Every column holds water from z = 0 to z = seafloor - 1 and rock below it. source_cell is (z * 128 + y) * 256 + x of a water cell with z below 6. receiver_column is y * 256 + x; two nodes may share a column.
All inputs are finite; a program needn't handle non-finite values.
Results may differ from a plain program's by a relative error of at most 0.00014.
Values sent between devices are 32-bit elements; how exact they have to be, the bound alone decides.
No kernel may reach another device: no remote copies, remote signals or barrier semaphores. Data moves between devices by JAX's collectives and lax.ppermute only.
A program may use at most 64 MiB of HBM per device.

v0:
```python
import jax
import jax.numpy as jnp
from jax import lax
from jax.sharding import PartitionSpec as P

COEFF = (1225.0 / 1024.0, -245.0 / 3072.0, 49.0 / 5120.0, -5.0 / 7168.0)
TIME_STEP = 0.2


def with_halo(array, sides, width):
    for axis, dim in sides:
        devices, length = (lax.axis_size(axis), array.shape[dim])
        up = [(i, (i + 1) % devices) for i in range(devices - 1)]
        down = [(j, i) for i, j in up]
        last = lax.slice_in_dim(array, length - width, length, axis=dim)
        first = lax.slice_in_dim(array, 0, width, axis=dim)
        before = lax.ppermute(last, axis, up)
        after = lax.ppermute(first, axis, down)
        array = jnp.concatenate([before, array, after], axis=dim)
    return array


def stencil(padded, axis, forward):
    length = padded.shape[axis] - 8
    summed = None
    for offset in range(1, 5):
        if forward:
            front_at, back_at = (4 + offset, 5 - offset)
        else:
            front_at, back_at = (3 + offset, 4 - offset)
        front = lax.slice_in_dim(padded, front_at, front_at + length, axis=axis)
        back = lax.slice_in_dim(padded, back_at, back_at + length, axis=axis)
        addend = COEFF[offset - 1] * (front - back)
        summed = addend if summed is None else summed + addend
    return summed


def padded_zero(field, axis):
    widths = [(0, 0)] * field.ndim
    widths[axis] = (4, 4)
    return jnp.pad(field, widths)


def derive(field, axis, forward):
    return stencil(padded_zero(field, axis), axis, forward)


def on_device(
    solid_state,
    water_state,
    lame_lambda,
    shear_mu,
    solid_buoy,
    water_kappa,
    water_buoy,
    seafloor,
    source_cell,
    wavelet,
    receiver_column,
    observed,
):
    parts = lax.axis_size("gx")
    place = lax.axis_index("gx")
    width_x = solid_state.shape[3]
    total_y = solid_state.shape[5]
    total_x = width_x * parts
    shots = solid_state.shape[2]
    shard_axis = 2
    anchor_y = place * water_state.shape[3]
    anchor_x = 0

    def water_halo(field):
        return with_halo(field, (("gx", 2),), 4)

    def water_derive(field, axis, forward):
        if axis == shard_axis:
            return stencil(water_halo(field), axis, forward)
        return derive(field, axis, forward)

    def solid_halo(stacked):
        return with_halo(stacked, (("gx", 3),), 4)

    vel_x, vel_y, vel_z = (solid_state[0], solid_state[1], solid_state[2])
    sig_xx, sig_yy, sig_zz = (solid_state[3], solid_state[4], solid_state[5])
    sig_xy, sig_xz, sig_yz = (solid_state[6], solid_state[7], solid_state[8])
    pressure, flow_x, flow_y, flow_z = (
        water_state[0],
        water_state[1],
        water_state[2],
        water_state[3],
    )
    local_y = pressure.shape[2]
    depth_rows = pressure.shape[3]
    local_x = pressure.shape[4]
    depth_idx = lax.broadcasted_iota(jnp.int32, (1, depth_rows, 1), 1)
    floor_rows = seafloor[:, None, :]
    live = (depth_idx < floor_rows).astype(jnp.float32)
    bottom = (depth_idx == floor_rows - 1).astype(jnp.float32)
    above = (depth_idx < floor_rows - 1).astype(jnp.float32)
    rows_y = lax.broadcasted_iota(jnp.int32, (local_y, 1, 1), 0) + anchor_y
    cols_x = lax.broadcasted_iota(jnp.int32, (1, 1, local_x), 2) + anchor_x
    flat_cell = (depth_idx * total_y + rows_y) * total_x + cols_x
    source_hot = (flat_cell[None] == source_cell[:, None, None, None]).astype(jnp.float32)
    node_y = receiver_column // total_x
    node_x = receiver_column % total_x
    inside = (
        (node_y >= anchor_y)
        & (node_y < anchor_y + local_y)
        & (node_x >= anchor_x)
        & (node_x < anchor_x + local_x)
    )
    local_col = (node_y - anchor_y) * local_x + (node_x - anchor_x)
    column_iota = lax.broadcasted_iota(jnp.int32, (1, local_y * local_x), 1)
    node_hot = ((column_iota == local_col[:, None]) & inside[:, None]).astype(jnp.float32)
    grad_lambda = jnp.zeros(lame_lambda.shape, jnp.float32)
    grad_mu = jnp.zeros(lame_lambda.shape, jnp.float32)
    grad_kappa = jnp.zeros(water_kappa.shape, jnp.float32)
    misfits = []
    for step in range(wavelet.shape[0]):
        floor_pressure = jnp.sum(pressure * bottom, axis=3)
        stress_pad = solid_halo(jnp.stack([sig_xx, sig_xy, sig_xz]))
        vel_x = vel_x + TIME_STEP * solid_buoy * (
            stencil(stress_pad[0], 2, True) + derive(sig_xy, 4, False) + derive(sig_xz, 3, False)
        )
        vel_y = vel_y + TIME_STEP * solid_buoy * (
            stencil(stress_pad[1], 2, False) + derive(sig_yy, 4, True) + derive(sig_yz, 3, False)
        )
        vel_z = vel_z + TIME_STEP * solid_buoy * (
            stencil(stress_pad[2], 2, False) + derive(sig_yz, 4, False) + derive(sig_zz, 3, True)
        )
        floor_velocity = lax.all_to_all(
            jnp.transpose(vel_z[:, :, :, 0, :], (0, 1, 3, 2)),
            "gx",
            split_axis=2,
            concat_axis=3,
            tiled=True,
        )
        flow_x = (flow_x - TIME_STEP * water_buoy * water_derive(pressure, 4, True)) * live
        flow_y = (flow_y - TIME_STEP * water_buoy * water_derive(pressure, 2, True)) * live
        flow_z = (
            flow_z - TIME_STEP * water_buoy * derive(pressure, 3, True)
        ) * above + floor_velocity[:, :, :, None, :] * bottom
        velocity_pad = solid_halo(jnp.stack([vel_x, vel_y, vel_z]))
        strain_x = stencil(velocity_pad[0], 2, False)
        strain_y = derive(vel_y, 4, False)
        strain_z = derive(vel_z, 3, False)
        dilation = strain_x + strain_y + strain_z
        shear_xy = derive(vel_x, 4, True) + stencil(velocity_pad[1], 2, True)
        shear_xz = derive(vel_x, 3, True) + stencil(velocity_pad[2], 2, True)
        shear_yz = derive(vel_y, 3, True) + derive(vel_z, 4, True)
        lam_part = lame_lambda * dilation
        sig_xx = sig_xx + TIME_STEP * (lam_part + 2.0 * shear_mu * strain_x)
        sig_yy = sig_yy + TIME_STEP * (lam_part + 2.0 * shear_mu * strain_y)
        sig_zz = sig_zz + TIME_STEP * (lam_part + 2.0 * shear_mu * strain_z)
        sig_xy = sig_xy + TIME_STEP * shear_mu * shear_xy
        sig_xz = sig_xz + TIME_STEP * shear_mu * shear_xz
        sig_yz = sig_yz + TIME_STEP * shear_mu * shear_yz
        rock_pressure = jnp.transpose(
            lax.all_to_all(floor_pressure, "gx", split_axis=3, concat_axis=2, tiled=True),
            (0, 1, 3, 2),
        )
        sig_zz = sig_zz.at[:, :, :, 0, :].set(-rock_pressure)
        grad_lambda = grad_lambda + jnp.sum(dilation[0] * dilation[1], axis=0)
        normal_part = (
            strain_x[0] * strain_x[1] + strain_y[0] * strain_y[1] + strain_z[0] * strain_z[1]
        )
        shear_part = (
            shear_xy[0] * shear_xy[1] + shear_xz[0] * shear_xz[1] + shear_yz[0] * shear_yz[1]
        )
        grad_mu = grad_mu + jnp.sum(2.0 * normal_part + shear_part, axis=0)
        pressure = (
            pressure
            - TIME_STEP
            * water_kappa
            * (
                water_derive(flow_x, 4, False)
                + water_derive(flow_y, 2, False)
                + derive(flow_z, 3, False)
            )
        ) * live
        pressure = pressure.at[0].add(wavelet[step][:, None, None, None] * source_hot)
        surface = jnp.sum(pressure * bottom, axis=3)
        partial_record = jnp.einsum(
            "sc,rc->sr",
            surface[0].reshape(shots, local_y * local_x),
            node_hot,
            precision=lax.Precision.HIGHEST,
        )
        recorded = lax.psum(partial_record, "gx")
        misfit = recorded - observed[step]
        scaled = misfit * lax.rsqrt(jnp.mean(misfit * misfit, axis=1, keepdims=True) + 1e-06)
        inject = jnp.dot(
            scaled, node_hot, precision=lax.Precision.HIGHEST, preferred_element_type=jnp.float32
        ).reshape(shots, local_y, local_x)
        pressure = pressure.at[1].add(inject[:, :, None, :] * bottom)
        grad_kappa = grad_kappa + jnp.sum(pressure[0] * pressure[1], axis=0)
        misfits.append(misfit)
    return (grad_lambda, grad_mu, grad_kappa, jnp.stack(misfits))


def solution(mesh):
    placed = (
        P(None, None, "groups", "gx", None, None),
        P(None, None, "groups", "gx", None, None),
        P("gx", None, None),
        P("gx", None, None),
        P("gx", None, None),
        P("gx", None, None),
        P("gx", None, None),
        P("gx", None),
        P("groups"),
        P(None, "groups"),
        P(),
        P(None, "groups", None),
    )
    return jax.shard_map(
        on_device,
        mesh=mesh,
        in_specs=placed,
        out_specs=(
            P("gx", "groups", None),
            P("gx", "groups", None),
            P("gx", "groups", None),
            P(None, "groups", None),
        ),
        check_vma=False,
    )
```

profile of v0, /device:TPU:0, one launch (start us, length us, event | category | flops | bytes accessed | tf_op | source)
XLA Modules:
  0.0 367.0 jit_solution(11349562170741559003)
XLA Ops:
  2.9 3.0 collective-permute-start.11
  8.1 5.1 %collective-permute-start = (f32[3,2,1,4,4,128]{5,4,3,2,1,0:T(4,128)S(1)}, f32[3,2,1,4,4,128]{5,4,3,2,1,0:T(4,128)S(1)}, u32[]{:S(2)}, u32[]{:S(2)}) collective-permute-start(f32[3,2,1,4,4,128]{5,4,3,2,1,0:T(4,128)S(1)} %get-tuple-element.248), channel_id=1, source_target_pairs={{0,1},{1,2},{2,3},{3,4},{4,5},{5,6},{6,7},{7,8},{8,9},{9,10},{10,1... | collective-permute-start | bytes 147464 | tf_op jit(solution)/shard_map/ppermute | solution.py:17
  19.5 9.7 %all-to-all-start.1 = ((f32[2,1,128,8]{3,0,1,2:T(2,128)}), f32[2,1,128,8]{3,0,1,2:T(2,128)S(1)}, u32[]{:S(2)}, u32[]{:S(2)}) async-start(f32[2,1,128,8]{3,0,1,2:T(2,128)} %copy.963), calls=%async_computation.1 | async-start | bytes 262144 | tf_op jit(solution)/shard_map/all_to_all | solution.py:131
  34.2 3.3 all-to-all-done.1
  40.4 3.0 collective-permute-start.4
  43.9 3.4 collective-permute-start.12
  52.6 12.4 %all-to-all-start = ((f32[2,1,4,256]{2,0,1,3:T(2,128)}), f32[2,1,4,256]{2,0,1,3:T(2,128)S(1)}, u32[]{:S(2)}, u32[]{:S(2)}) async-start(f32[2,1,4,256]{2,0,1,3:T(2,128)} %copy.948), calls=%async_computation | async-start | bytes 524288 | tf_op jit(solution)/shard_map/all_to_all | solution.py:159
  65.5 40.5 %psum.28 = f32[1,128]{1,0:T(1,128)S(1)} all-reduce(f32[1,128]{1,0:T(1,128)S(1)} %fusion.7), channel_id=1, replica_groups=mesh['groups'=1,'gx'=32] {'gx'}, use_global_device_ids=true, to_apply=%region_2.3 | all-reduce | flops 128 | bytes 1024 | tf_op jit(solution)/shard_map/psum | solution.py:189
  109.1 3.0 collective-permute-start.19
  113.6 6.2 %all-to-all-start.3 = ((f32[2,1,128,8]{3,0,1,2:T(2,128)}), f32[2,1,128,8]{3,0,1,2:T(2,128)S(1)}, u32[]{:S(2)}, u32[]{:S(2)}) async-start(f32[2,1,128,8]{3,0,1,2:T(2,128)} %copy.978), calls=%async_computation.3 | async-start | bytes 262144 | tf_op jit(solution)/shard_map/all_to_all | solution.py:131
  124.2 3.8 %all-to-all-done.3 = f32[2,1,128,8]{3,0,1,2:T(2,128)S(1)} async-done(((f32[2,1,128,8]{3,0,1,2:T(2,128)}), f32[2,1,128,8]{3,0,1,2:T(2,128)S(1)}, u32[]{:S(2)}, u32[]{:S(2)}) %all-to-all-start.3) | async-done | bytes 8224 | tf_op jit(solution)/shard_map/all_to_all | solution.py:131
  133.9 3.4 collective-permute-start.20
  142.7 11.9 %all-to-all-start.2 = ((f32[2,1,4,256]{2,0,1,3:T(2,128)}), f32[2,1,4,256]{2,0,1,3:T(2,128)S(1)}, u32[]{:S(2)}, u32[]{:S(2)}) async-start(f32[2,1,4,256]{2,0,1,3:T(2,128)} %copy.966), calls=%async_computation.2 | async-start | bytes 524288 | tf_op jit(solution)/shard_map/all_to_all | solution.py:159
  155.0 40.5 %psum.29 = f32[1,128]{1,0:T(1,128)S(1)} all-reduce(f32[1,128]{1,0:T(1,128)S(1)} %fusion.5), channel_id=1, replica_groups=mesh['groups'=1,'gx'=32] {'gx'}, use_global_device_ids=true, to_apply=%region_6.7 | all-reduce | flops 128 | bytes 1024 | tf_op jit(solution)/shard_map/psum | solution.py:189
  198.6 3.0 collective-permute-start.25
  203.1 6.2 %all-to-all-start.5 = ((f32[2,1,128,8]{3,0,1,2:T(2,128)}), f32[2,1,128,8]{3,0,1,2:T(2,128)S(1)}, u32[]{:S(2)}, u32[]{:S(2)}) async-start(f32[2,1,128,8]{3,0,1,2:T(2,128)} %copy.989), calls=%async_computation.5 | async-start | bytes 262144 | tf_op jit(solution)/shard_map/all_to_all | solution.py:131
  213.7 3.8 %all-to-all-done.5 = f32[2,1,128,8]{3,0,1,2:T(2,128)S(1)} async-done(((f32[2,1,128,8]{3,0,1,2:T(2,128)}), f32[2,1,128,8]{3,0,1,2:T(2,128)S(1)}, u32[]{:S(2)}, u32[]{:S(2)}) %all-to-all-start.5) | async-done | bytes 8224 | tf_op jit(solution)/shard_map/all_to_all | solution.py:131
  223.4 3.4 collective-permute-start.26
  232.2 11.9 %all-to-all-start.4 = ((f32[2,1,4,256]{2,0,1,3:T(2,128)}), f32[2,1,4,256]{2,0,1,3:T(2,128)S(1)}, u32[]{:S(2)}, u32[]{:S(2)}) async-start(f32[2,1,4,256]{2,0,1,3:T(2,128)} %copy.981), calls=%async_computation.4 | async-start | bytes 524288 | tf_op jit(solution)/shard_map/all_to_all | solution.py:159
  244.5 40.5 %psum.30 = f32[1,128]{1,0:T(1,128)S(1)} all-reduce(f32[1,128]{1,0:T(1,128)S(1)} %fusion.3), channel_id=1, replica_groups=mesh['groups'=1,'gx'=32] {'gx'}, use_global_device_ids=true, to_apply=%region_10.11 | all-reduce | flops 128 | bytes 1024 | tf_op jit(solution)/shard_map/psum | solution.py:189
  288.1 3.0 collective-permute-start.29
  292.6 6.2 %all-to-all-start.6 = ((f32[2,1,128,8]{3,0,1,2:T(2,128)}), f32[2,1,128,8]{3,0,1,2:T(2,128)S(1)}, u32[]{:S(2)}, u32[]{:S(2)}) async-start(f32[2,1,128,8]{3,0,1,2:T(2,128)} %copy.992), calls=%async_computation.6 | async-start | bytes 262144 | tf_op jit(solution)/shard_map/all_to_all | solution.py:131
  303.2 3.8 %all-to-all-done.6 = f32[2,1,128,8]{3,0,1,2:T(2,128)S(1)} async-done(((f32[2,1,128,8]{3,0,1,2:T(2,128)}), f32[2,1,128,8]{3,0,1,2:T(2,128)S(1)}, u32[]{:S(2)}, u32[]{:S(2)}) %all-to-all-start.6) | async-done | bytes 8224 | tf_op jit(solution)/shard_map/all_to_all | solution.py:131
  316.8 46.5 %psum.31 = f32[1,128]{1,0:T(1,128)S(1)} all-reduce(f32[1,128]{1,0:T(1,128)S(1)} %fusion.1), channel_id=1, replica_groups=mesh['groups'=1,'gx'=32] {'gx'}, use_global_device_ids=true, to_apply=%region_13.14 | all-reduce | flops 128 | bytes 1024 | tf_op jit(solution)/shard_map/psum | solution.py:189
  (250 shorter events, 84.0 us)
Async XLA Ops:
  1.6 41.8 %collective-permute-start.10 = (f32[2,1,4,12,256]{4,2,3,1,0:T(4,128)S(1)}, f32[2,1,4,12,256]{4,2,3,1,0:T(4,128)S(1)}, u32[]{:S(2)}, u32[]{:S(2)}) collective-permute-start(f32[2,1,4,12,256]{4,2,3,1,0:T(4,128)S(1)} %slice_bitcast_fusion.3), channel_id=1, source_target_pairs={{1,0},{2,1},{3,2},{4,3},{5,4},{6,5},{7,6},{8,7},{9,8},{10,9},{11,1... | collective-permute-start | bytes 294920 | tf_op jit(solution)/shard_map/ppermute | solution.py:18
  2.9 40.5 %collective-permute-start.11 = (f32[2,1,4,12,256]{4,2,3,1,0:T(4,128)S(1)}, f32[2,1,4,12,256]{4,2,3,1,0:T(4,128)S(1)}, u32[]{:S(2)}, u32[]{:S(2)}) collective-permute-start(f32[2,1,4,12,256]{4,2,3,1,0:T(4,128)S(1)} %slice_bitcast_fusion.3), channel_id=1, source_target_pairs={{0,1},{1,2},{2,3},{3,4},{4,5},{5,6},{6,7},{7,8},{8,9},{9,10},{10,1... | collective-permute-start | bytes 294920 | tf_op jit(solution)/shard_map/ppermute | solution.py:17
  6.8 11.5 %collective-permute-start.1 = (f32[3,2,1,4,4,128]{5,4,3,2,1,0:T(4,128)S(1)}, f32[3,2,1,4,4,128]{5,4,3,2,1,0:T(4,128)S(1)}, u32[]{:S(2)}, u32[]{:S(2)}) collective-permute-start(f32[3,2,1,4,4,128]{5,4,3,2,1,0:T(4,128)S(1)} %get-tuple-element.249), channel_id=1, source_target_pairs={{1,0},{2,1},{3,2},{4,3},{5,4},{6,5},{7,6},{8,7},{9,8},{10,9},{11,1... | collective-permute-start | bytes 147464 | tf_op jit(solution)/shard_map/ppermute | solution.py:18
  8.1 10.3 %collective-permute-start = (f32[3,2,1,4,4,128]{5,4,3,2,1,0:T(4,128)S(1)}, f32[3,2,1,4,4,128]{5,4,3,2,1,0:T(4,128)S(1)}, u32[]{:S(2)}, u32[]{:S(2)}) collective-permute-start(f32[3,2,1,4,4,128]{5,4,3,2,1,0:T(4,128)S(1)} %get-tuple-element.248), channel_id=1, source_target_pairs={{0,1},{1,2},{2,3},{3,4},{4,5},{5,6},{6,7},{7,8},{8,9},{9,10},{10,1... | collective-permute-start | bytes 147464 | tf_op jit(solution)/shard_map/ppermute | solution.py:17
  19.5 18.0 %all-to-all-start.1 = ((f32[2,1,128,8]{3,0,1,2:T(2,128)}), f32[2,1,128,8]{3,0,1,2:T(2,128)S(1)}, u32[]{:S(2)}, u32[]{:S(2)}) async-start(f32[2,1,128,8]{3,0,1,2:T(2,128)} %copy.963), calls=%async_computation.1 | async-start | bytes 262144 | tf_op jit(solution)/shard_map/all_to_all | solution.py:131
  39.1 9.5 %collective-permute-start.5 = (f32[3,2,1,4,4,128]{5,4,3,2,1,0:T(4,128)S(1)}, f32[3,2,1,4,4,128]{5,4,3,2,1,0:T(4,128)S(1)}, u32[]{:S(2)}, u32[]{:S(2)}) collective-permute-start(f32[3,2,1,4,4,128]{5,4,3,2,1,0:T(4,128)S(1)} %get-tuple-element.245), channel_id=1, source_target_pairs={{1,0},{2,1},{3,2},{4,3},{5,4},{6,5},{7,6},{8,7},{9,8},{10,9},{11,1... | collective-permute-start | bytes 147464 | tf_op jit(solution)/shard_map/ppermute | solution.py:18
  52.6 59.5 %all-to-all-start = ((f32[2,1,4,256]{2,0,1,3:T(2,128)}), f32[2,1,4,256]{2,0,1,3:T(2,128)S(1)}, u32[]{:S(2)}, u32[]{:S(2)}) async-start(f32[2,1,4,256]{2,0,1,3:T(2,128)} %copy.948), calls=%async_computation | async-start | bytes 524288 | tf_op jit(solution)/shard_map/all_to_all | solution.py:159
  107.8 25.7 %collective-permute-start.18 = (f32[2,1,4,12,256]{4,2,3,1,0:T(4,128)S(1)}, f32[2,1,4,12,256]{4,2,3,1,0:T(4,128)S(1)}, u32[]{:S(2)}, u32[]{:S(2)}) collective-permute-start(f32[2,1,4,12,256]{4,2,3,1,0:T(4,128)S(1)} %fusion.1104), channel_id=1, source_target_pairs={{1,0},{2,1},{3,2},{4,3},{5,4},{6,5},{7,6},{8,7},{9,8},{10,9},{11,1... | collective-permute-start | bytes 294920 | tf_op jit(solution)/shard_map/ppermute | solution.py:18
  109.1 24.4 %collective-permute-start.19 = (f32[2,1,4,12,256]{4,2,3,1,0:T(4,128)S(1)}, f32[2,1,4,12,256]{4,2,3,1,0:T(4,128)S(1)}, u32[]{:S(2)}, u32[]{:S(2)}) collective-permute-start(f32[2,1,4,12,256]{4,2,3,1,0:T(4,128)S(1)} %fusion.1104), channel_id=1, source_target_pairs={{0,1},{1,2},{2,3},{3,4},{4,5},{5,6},{6,7},{7,8},{8,9},{9,10},{10,1... | collective-permute-start | bytes 294920 | tf_op jit(solution)/shard_map/ppermute | solution.py:17
  113.6 14.4 %all-to-all-start.3 = ((f32[2,1,128,8]{3,0,1,2:T(2,128)}), f32[2,1,128,8]{3,0,1,2:T(2,128)S(1)}, u32[]{:S(2)}, u32[]{:S(2)}) async-start(f32[2,1,128,8]{3,0,1,2:T(2,128)} %copy.978), calls=%async_computation.3 | async-start | bytes 262144 | tf_op jit(solution)/shard_map/all_to_all | solution.py:131
  119.9 8.4 %collective-permute-start.7 = (f32[3,2,1,4,4,128]{5,4,3,2,1,0:T(4,128)S(1)}, f32[3,2,1,4,4,128]{5,4,3,2,1,0:T(4,128)S(1)}, u32[]{:S(2)}, u32[]{:S(2)}) collective-permute-start(f32[3,2,1,4,4,128]{5,4,3,2,1,0:T(4,128)S(1)} %get-tuple-element.243), channel_id=1, source_target_pairs={{1,0},{2,1},{3,2},{4,3},{5,4},{6,5},{7,6},{8,7},{9,8},{10,9},{11,1... | collective-permute-start | bytes 147464 | tf_op jit(solution)/shard_map/ppermute | solution.py:18
  129.1 9.5 %collective-permute-start.9 = (f32[3,2,1,4,4,128]{5,4,3,2,1,0:T(4,128)S(1)}, f32[3,2,1,4,4,128]{5,4,3,2,1,0:T(4,128)S(1)}, u32[]{:S(2)}, u32[]{:S(2)}) collective-permute-start(f32[3,2,1,4,4,128]{5,4,3,2,1,0:T(4,128)S(1)} %get-tuple-element.241), channel_id=1, source_target_pairs={{1,0},{2,1},{3,2},{4,3},{5,4},{6,5},{7,6},{8,7},{9,8},{10,9},{11,1... | collective-permute-start | bytes 147464 | tf_op jit(solution)/shard_map/ppermute | solution.py:18
  142.7 59.0 %all-to-all-start.2 = ((f32[2,1,4,256]{2,0,1,3:T(2,128)}), f32[2,1,4,256]{2,0,1,3:T(2,128)S(1)}, u32[]{:S(2)}, u32[]{:S(2)}) async-start(f32[2,1,4,256]{2,0,1,3:T(2,128)} %copy.966), calls=%async_computation.2 | async-start | bytes 524288 | tf_op jit(solution)/shard_map/all_to_all | solution.py:159
  197.3 25.7 %collective-permute-start.24 = (f32[2,1,4,12,256]{4,2,3,1,0:T(4,128)S(1)}, f32[2,1,4,12,256]{4,2,3,1,0:T(4,128)S(1)}, u32[]{:S(2)}, u32[]{:S(2)}) collective-permute-start(f32[2,1,4,12,256]{4,2,3,1,0:T(4,128)S(1)} %fusion.1105), channel_id=1, source_target_pairs={{1,0},{2,1},{3,2},{4,3},{5,4},{6,5},{7,6},{8,7},{9,8},{10,9},{11,1... | collective-permute-start | bytes 294920 | tf_op jit(solution)/shard_map/ppermute | solution.py:18
  198.6 24.4 %collective-permute-start.25 = (f32[2,1,4,12,256]{4,2,3,1,0:T(4,128)S(1)}, f32[2,1,4,12,256]{4,2,3,1,0:T(4,128)S(1)}, u32[]{:S(2)}, u32[]{:S(2)}) collective-permute-start(f32[2,1,4,12,256]{4,2,3,1,0:T(4,128)S(1)} %fusion.1105), channel_id=1, source_target_pairs={{0,1},{1,2},{2,3},{3,4},{4,5},{5,6},{6,7},{7,8},{8,9},{9,10},{10,1... | collective-permute-start | bytes 294920 | tf_op jit(solution)/shard_map/ppermute | solution.py:17
  203.1 14.4 %all-to-all-start.5 = ((f32[2,1,128,8]{3,0,1,2:T(2,128)}), f32[2,1,128,8]{3,0,1,2:T(2,128)S(1)}, u32[]{:S(2)}, u32[]{:S(2)}) async-start(f32[2,1,128,8]{3,0,1,2:T(2,128)} %copy.989), calls=%async_computation.5 | async-start | bytes 262144 | tf_op jit(solution)/shard_map/all_to_all | solution.py:131
  209.4 8.4 %collective-permute-start.15 = (f32[3,2,1,4,4,128]{5,4,3,2,1,0:T(4,128)S(1)}, f32[3,2,1,4,4,128]{5,4,3,2,1,0:T(4,128)S(1)}, u32[]{:S(2)}, u32[]{:S(2)}) collective-permute-start(f32[3,2,1,4,4,128]{5,4,3,2,1,0:T(4,128)S(1)} %get-tuple-element.239), channel_id=1, source_target_pairs={{1,0},{2,1},{3,2},{4,3},{5,4},{6,5},{7,6},{8,7},{9,8},{10,9},{11,1... | collective-permute-start | bytes 147464 | tf_op jit(solution)/shard_map/ppermute | solution.py:18
  218.6 9.5 %collective-permute-start.17 = (f32[3,2,1,4,4,128]{5,4,3,2,1,0:T(4,128)S(1)}, f32[3,2,1,4,4,128]{5,4,3,2,1,0:T(4,128)S(1)}, u32[]{:S(2)}, u32[]{:S(2)}) collective-permute-start(f32[3,2,1,4,4,128]{5,4,3,2,1,0:T(4,128)S(1)} %get-tuple-element.237), channel_id=1, source_target_pairs={{1,0},{2,1},{3,2},{4,3},{5,4},{6,5},{7,6},{8,7},{9,8},{10,9},{11,1... | collective-permute-start | bytes 147464 | tf_op jit(solution)/shard_map/ppermute | solution.py:18
  219.9 8.2 %collective-permute-start.16 = (f32[3,2,1,4,4,128]{5,4,3,2,1,0:T(4,128)S(1)}, f32[3,2,1,4,4,128]{5,4,3,2,1,0:T(4,128)S(1)}, u32[]{:S(2)}, u32[]{:S(2)}) collective-permute-start(f32[3,2,1,4,4,128]{5,4,3,2,1,0:T(4,128)S(1)} %get-tuple-element.236), channel_id=1, source_target_pairs={{0,1},{1,2},{2,3},{3,4},{4,5},{5,6},{6,7},{7,8},{8,9},{9,10},{10,1... | collective-permute-start | bytes 147464 | tf_op jit(solution)/shard_map/ppermute | solution.py:17
  232.2 59.0 %all-to-all-start.4 = ((f32[2,1,4,256]{2,0,1,3:T(2,128)}), f32[2,1,4,256]{2,0,1,3:T(2,128)S(1)}, u32[]{:S(2)}, u32[]{:S(2)}) async-start(f32[2,1,4,256]{2,0,1,3:T(2,128)} %copy.981), calls=%async_computation.4 | async-start | bytes 524288 | tf_op jit(solution)/shard_map/all_to_all | solution.py:159
  286.8 21.9 %collective-permute-start.28 = (f32[2,1,4,12,256]{4,2,3,1,0:T(4,128)S(1)}, f32[2,1,4,12,256]{4,2,3,1,0:T(4,128)S(1)}, u32[]{:S(2)}, u32[]{:S(2)}) collective-permute-start(f32[2,1,4,12,256]{4,2,3,1,0:T(4,128)S(1)} %fusion.1106), channel_id=1, source_target_pairs={{1,0},{2,1},{3,2},{4,3},{5,4},{6,5},{7,6},{8,7},{9,8},{10,9},{11,1... | collective-permute-start | bytes 294920 | tf_op jit(solution)/shard_map/ppermute | solution.py:18
  288.1 20.6 %collective-permute-start.29 = (f32[2,1,4,12,256]{4,2,3,1,0:T(4,128)S(1)}, f32[2,1,4,12,256]{4,2,3,1,0:T(4,128)S(1)}, u32[]{:S(2)}, u32[]{:S(2)}) collective-permute-start(f32[2,1,4,12,256]{4,2,3,1,0:T(4,128)S(1)} %fusion.1106), channel_id=1, source_target_pairs={{0,1},{1,2},{2,3},{3,4},{4,5},{5,6},{6,7},{7,8},{8,9},{9,10},{10,1... | collective-permute-start | bytes 294920 | tf_op jit(solution)/shard_map/ppermute | solution.py:17
  292.6 14.4 %all-to-all-start.6 = ((f32[2,1,128,8]{3,0,1,2:T(2,128)}), f32[2,1,128,8]{3,0,1,2:T(2,128)S(1)}, u32[]{:S(2)}, u32[]{:S(2)}) async-start(f32[2,1,128,8]{3,0,1,2:T(2,128)} %copy.992), calls=%async_computation.6 | async-start | bytes 262144 | tf_op jit(solution)/shard_map/all_to_all | solution.py:131
  298.9 8.4 %collective-permute-start.23 = (f32[3,2,1,4,4,128]{5,4,3,2,1,0:T(4,128)S(1)}, f32[3,2,1,4,4,128]{5,4,3,2,1,0:T(4,128)S(1)}, u32[]{:S(2)}, u32[]{:S(2)}) collective-permute-start(f32[3,2,1,4,4,128]{5,4,3,2,1,0:T(4,128)S(1)} %get-tuple-element.235), channel_id=1, source_target_pairs={{1,0},{2,1},{3,2},{4,3},{5,4},{6,5},{7,6},{8,7},{9,8},{10,9},{11,1... | collective-permute-start | bytes 147464 | tf_op jit(solution)/shard_map/ppermute | solution.py:18
  (26 other events, 152.1 us)
where the time goes:
time: 369 us; the launch traced here: 367 us
  blocking collectives  168 us (46%)
  starting transfers between devices  136 us (37%)
  waiting for transfers between devices  21 us (6%)
  other arithmetic  18.8 us (5%)
  local copies, waits for them, and re-layouts  14.5 us (4%)
  between operations  5.44 us (1%)
    psum x4, blocking collectives, on_device(): recorded = lax.psum(partial_record, 'gx')  168 us
    ppermute x16, starting transfers between devices, with_halo(): before = lax.ppermute(last, axis, up)  50.7 us
    all_to_all x3, starting transfers between devices, on_device(): lax.all_to_all(floor_pressure, 'gx', split_axis=3, concat_axis=2, tiled=T...  36.3 us
    all_to_all x4, starting transfers between devices, on_device(): lax.all_to_all(jnp.transpose(vel_z[:, :, :, 0, :], (0, 1, 3, 2)), 'gx', s...  28.3 us
    ppermute x16, starting transfers between devices, with_halo(): after = lax.ppermute(first, axis, down)  20.8 us
    all_to_all x4, waiting for transfers between devices, on_device(): lax.all_to_all(jnp.transpose(vel_z[:, :, :, 0, :], (0, 1, 3, 2)), 'gx', s...  14.8 us
  transfers between devices with their start and end apart: 39, of which 8 were waited for; matrix products, arithmetic and copies ran while one was open for 5% of the time, Pallas kernels for 0%

commit v1 on v0

--- a/solution.py
+++ b/solution.py
@@ -18,6 +18,11 @@
         after = lax.ppermute(first, axis, down)
         array = jnp.concatenate([before, array, after], axis=dim)
     return array
+
+
+def gather_sum(partial, parts):
+    copies = jnp.broadcast_to(partial[None], (parts,) + partial.shape)
+    return jnp.sum(lax.all_to_all(copies, "gx", 0, 0, tiled=True), axis=0)
 
 
 def stencil(padded, axis, forward):
@@ -186,7 +191,7 @@
             node_hot,
             precision=lax.Precision.HIGHEST,
         )
-        recorded = lax.psum(partial_record, "gx")
+        recorded = gather_sum(partial_record, parts)
         misfit = recorded - observed[step]
         scaled = misfit * lax.rsqrt(jnp.mean(misfit * misfit, axis=1, keepdims=True) + 1e-06)
         inject = jnp.dot(

time: 369 us -> 279 us (0.76)
  blocking collectives: 168 us -> 0 us
  waiting for transfers between devices: 21 us -> 70 us
  starting transfers between devices: 136 us -> 162 us
    psum x4 -> x0, blocking collectives: 168 us -> none  [on_device(): recorded = lax.psum(partial_record, 'gx')]
    all_to_all x3, waiting for transfers between devices: 0.01 us -> 30.4 us  [on_device(): lax.all_to_all(floor_pressure, 'gx', split_axis=3, concat_axis=2, tiled=T...]
    all_to_all x0 -> x4, starting transfers between devices: none -> 19.6 us  [gather_sum(): return jnp.sum(lax.all_to_all(copies, 'gx', 0, 0, tiled=True), axis=0)]
    all_to_all x0 -> x4, waiting for transfers between devices: none -> 11.5 us  [gather_sum(): return jnp.sum(lax.all_to_all(copies, 'gx', 0, 0, tiled=True), axis=0)]
    all_to_all x3, starting transfers between devices: 36.3 us -> 42.8 us  [on_device(): lax.all_to_all(floor_pressure, 'gx', split_axis=3, concat_axis=2, tiled=T...]
    ppermute x16, waiting for transfers between devices: 6.14 us -> 11.6 us  [with_halo(): after = lax.ppermute(first, axis, down)]
  transfers between devices with their start and end apart: 39 -> 43, of which waited for: 8 -> 17; matrix products, arithmetic and copies ran while one was open for 5% -> 6% of each run, Pallas kernels for 0% -> 0%
where the time goes in v1:
time: 279 us; the launch traced here: 277 us
  starting transfers between devices  162 us (58%)
  waiting for transfers between devices  70 us (25%)
  other arithmetic  18.9 us (7%)
  local copies, waits for them, and re-layouts  17.7 us (6%)
  between operations  5.46 us (2%)
  matrix products  3.42 us (1%)
    ppermute x16, starting transfers between devices, with_halo(): before = lax.ppermute(last, axis, up)  53.2 us
    all_to_all x3, starting transfers between devices, on_device(): lax.all_to_all(floor_pressure, 'gx', split_axis=3, concat_axis=2, tiled=T...  42.8 us
    all_to_all x3, waiting for transfers between devices, on_device(): lax.all_to_all(floor_pressure, 'gx', split_axis=3, concat_axis=2, tiled=T...  30.4 us
    all_to_all x4, starting transfers between devices, on_device(): lax.all_to_all(jnp.transpose(vel_z[:, :, :, 0, :], (0, 1, 3, 2)), 'gx', s...  25.2 us
    ppermute x16, starting transfers between devices, with_halo(): after = lax.ppermute(first, axis, down)  20.8 us
    all_to_all x4, starting transfers between devices, gather_sum(): return jnp.sum(lax.all_to_all(copies, 'gx', 0, 0, tiled=True), axis=0)  19.6 us
    all_to_all x4, waiting for transfers between devices, on_device(): lax.all_to_all(jnp.transpose(vel_z[:, :, :, 0, :], (0, 1, 3, 2)), 'gx', s...  15 us
    ppermute x16, waiting for transfers between devices, with_halo(): after = lax.ppermute(first, axis, down)  11.6 us
  transfers between devices with their start and end apart: 43, of which 17 were waited for; matrix products, arithmetic and copies ran while one was open for 6% of the time, Pallas kernels for 0%

profile of v1, /device:TPU:0, one launch (start us, length us, event | category | flops | bytes accessed | tf_op | source)
XLA Modules:
  0.0 277.0 jit_solution(11786345631001558201)
XLA Ops:
  2.9 3.0 %collective-permute-start.11 = (f32[2,1,4,12,256]{4,2,3,1,0:T(4,128)S(1)}, f32[2,1,4,12,256]{4,2,3,1,0:T(4,128)S(1)}, u32[]{:S(2)}, u32[]{:S(2)}) collective-permute-start(f32[2,1,4,12,256]{4,2,3,1,0:T(4,128)S(1)} %slice_bitcast_fusion.3), channel_id=1, source_target_pairs={{0,1},{1,2},{2,3},{3,4},{4,5},{5,6},{6,7},{7,8},{8,9},{9,10},{10,1... | collective-permute-start | bytes 294920 | tf_op jit(solution)/shard_map/ppermute | solution.py:17
  8.1 5.1 %collective-permute-start = (f32[3,2,1,4,4,128]{5,4,3,2,1,0:T(4,128)S(1)}, f32[3,2,1,4,4,128]{5,4,3,2,1,0:T(4,128)S(1)}, u32[]{:S(2)}, u32[]{:S(2)}) collective-permute-start(f32[3,2,1,4,4,128]{5,4,3,2,1,0:T(4,128)S(1)} %get-tuple-element.248), channel_id=1, source_target_pairs={{0,1},{1,2},{2,3},{3,4},{4,5},{5,6},{6,7},{7,8},{8,9},{9,10},{10,1... | collective-permute-start | bytes 147464 | tf_op jit(solution)/shard_map/ppermute | solution.py:17
  19.5 9.7 %all-to-all-start.1 = ((f32[2,1,128,8]{3,0,1,2:T(2,128)}), f32[2,1,128,8]{3,0,1,2:T(2,128)S(1)}, u32[]{:S(2)}, u32[]{:S(2)}) async-start(f32[2,1,128,8]{3,0,1,2:T(2,128)} %copy.1035), calls=%async_computation.1 | async-start | bytes 262144 | tf_op jit(solution)/shard_map/all_to_all | solution.py:136
  34.2 3.3 %all-to-all-done.1 = f32[2,1,128,8]{3,0,1,2:T(2,128)S(1)} async-done(((f32[2,1,128,8]{3,0,1,2:T(2,128)}), f32[2,1,128,8]{3,0,1,2:T(2,128)S(1)}, u32[]{:S(2)}, u32[]{:S(2)}) %all-to-all-start.1) | async-done | bytes 8224 | tf_op jit(solution)/shard_map/all_to_all | solution.py:136
  43.9 3.4 %collective-permute-start.12 = (f32[2,1,4,12,256]{4,2,3,1,0:T(4,128)S(1)}, f32[2,1,4,12,256]{4,2,3,1,0:T(4,128)S(1)}, u32[]{:S(2)}, u32[]{:S(2)}) collective-permute-start(f32[2,1,4,12,256]{4,2,3,1,0:T(4,128)S(1)} %get-tuple-element.190), channel_id=1, source_target_pairs={{0,1},{1,2},{2,3},{3,4},{4,5},{5,6},{6,7},{7,8},{8,9},{9,10},{10,1... | collective-permute-start | bytes 294920 | tf_op jit(solution)/shard_map/ppermute | solution.py:17
  52.7 12.4 %all-to-all-start = ((f32[2,1,4,256]{2,0,1,3:T(2,128)}), f32[2,1,4,256]{2,0,1,3:T(2,128)S(1)}, u32[]{:S(2)}, u32[]{:S(2)}) async-start(f32[2,1,4,256]{2,0,1,3:T(2,128)} %copy.1020), calls=%async_computation | async-start | bytes 524288 | tf_op jit(solution)/shard_map/all_to_all | solution.py:164
  65.6 10.1 %all-to-all-done = f32[2,1,4,256]{2,0,1,3:T(2,128)S(1)} async-done(((f32[2,1,4,256]{2,0,1,3:T(2,128)}), f32[2,1,4,256]{2,0,1,3:T(2,128)S(1)}, u32[]{:S(2)}, u32[]{:S(2)}) %all-to-all-start) | async-done | bytes 8224 | tf_op jit(solution)/shard_map/all_to_all | solution.py:164
  85.9 6.4 %all-to-all-start.4 = ((f32[2,1,128,8]{3,0,1,2:T(2,128)}), f32[2,1,128,8]{3,0,1,2:T(2,128)S(1)}, u32[]{:S(2)}, u32[]{:S(2)}) async-start(f32[2,1,128,8]{3,0,1,2:T(2,128)} %copy.1051), calls=%async_computation.4 | async-start | bytes 262144 | tf_op jit(solution)/shard_map/all_to_all | solution.py:136
  96.2 3.0 %collective-permute-start.19 = (f32[2,1,4,12,256]{4,2,3,1,0:T(4,128)S(1)}, f32[2,1,4,12,256]{4,2,3,1,0:T(4,128)S(1)}, u32[]{:S(2)}, u32[]{:S(2)}) collective-permute-start(f32[2,1,4,12,256]{4,2,3,1,0:T(4,128)S(1)} %fusion.1100), channel_id=1, source_target_pairs={{0,1},{1,2},{2,3},{3,4},{4,5},{5,6},{6,7},{7,8},{8,9},{9,10},{10,1... | collective-permute-start | bytes 294920 | tf_op jit(solution)/shard_map/ppermute | solution.py:17
  107.5 3.7 %collective-permute-start.20 = (f32[2,1,4,12,256]{4,2,3,1,0:T(4,128)S(1)}, f32[2,1,4,12,256]{4,2,3,1,0:T(4,128)S(1)}, u32[]{:S(2)}, u32[]{:S(2)}) collective-permute-start(f32[2,1,4,12,256]{4,2,3,1,0:T(4,128)S(1)} %get-tuple-element.220), channel_id=1, source_target_pairs={{0,1},{1,2},{2,3},{3,4},{4,5},{5,6},{6,7},{7,8},{8,9},{9,10},{10,1... | collective-permute-start | bytes 294920 | tf_op jit(solution)/shard_map/ppermute | solution.py:17
  112.7 3.5 %collective-permute-done.21 = f32[2,1,4,12,256]{4,2,3,1,0:T(4,128)S(1)} collective-permute-done((f32[2,1,4,12,256]{4,2,3,1,0:T(4,128)S(1)}, f32[2,1,4,12,256]{4,2,3,1,0:T(4,128)S(1)}, u32[]{:S(2)}, u32[]{:S(2)}) %collective-permute-start.21) | collective-permute-done | bytes 98336 | tf_op jit(solution)/shard_map/ppermute | solution.py:18
  118.4 14.7 %all-to-all-start.3 = ((f32[2,1,4,256]{2,0,1,3:T(2,128)}), f32[2,1,4,256]{2,0,1,3:T(2,128)S(1)}, u32[]{:S(2)}, u32[]{:S(2)}) async-start(f32[2,1,4,256]{2,0,1,3:T(2,128)} %copy.1039), calls=%async_computation.3 | async-start | bytes 524288 | tf_op jit(solution)/shard_map/all_to_all | solution.py:164
  133.6 10.1 %all-to-all-done.3 = f32[2,1,4,256]{2,0,1,3:T(2,128)S(1)} async-done(((f32[2,1,4,256]{2,0,1,3:T(2,128)}), f32[2,1,4,256]{2,0,1,3:T(2,128)S(1)}, u32[]{:S(2)}, u32[]{:S(2)}) %all-to-all-start.3) | async-done | bytes 8224 | tf_op jit(solution)/shard_map/all_to_all | solution.py:164
  147.8 8.2 %all-to-all-done.7 = f32[2,1,128,8]{3,0,1,2:T(2,128)S(1)} async-done(((f32[2,1,128,8]{3,0,1,2:T(2,128)}), f32[2,1,128,8]{3,0,1,2:T(2,128)S(1)}, u32[]{:S(2)}, u32[]{:S(2)}) %all-to-all-start.7) | async-done | bytes 8224 | tf_op jit(solution)/shard_map/all_to_all | solution.py:136
  169.3 3.2 %collective-permute-start.25 = (f32[2,1,4,12,256]{4,2,3,1,0:T(4,128)S(1)}, f32[2,1,4,12,256]{4,2,3,1,0:T(4,128)S(1)}, u32[]{:S(2)}, u32[]{:S(2)}) collective-permute-start(f32[2,1,4,12,256]{4,2,3,1,0:T(4,128)S(1)} %fusion.1101), channel_id=1, source_target_pairs={{0,1},{1,2},{2,3},{3,4},{4,5},{5,6},{6,7},{7,8},{8,9},{9,10},{10,1... | collective-permute-start | bytes 294920 | tf_op jit(solution)/shard_map/ppermute | solution.py:17
  174.6 3.6 %collective-permute-start.16 = (f32[3,2,1,4,4,128]{5,4,3,2,1,0:T(4,128)S(1)}, f32[3,2,1,4,4,128]{5,4,3,2,1,0:T(4,128)S(1)}, u32[]{:S(2)}, u32[]{:S(2)}) collective-permute-start(f32[3,2,1,4,4,128]{5,4,3,2,1,0:T(4,128)S(1)} %get-tuple-element.236), channel_id=1, source_target_pairs={{0,1},{1,2},{2,3},{3,4},{4,5},{5,6},{6,7},{7,8},{8,9},{9,10},{10,1... | collective-permute-start | bytes 147464 | tf_op jit(solution)/shard_map/ppermute | solution.py:17
  179.9 3.9 %collective-permute-start.26 = (f32[2,1,4,12,256]{4,2,3,1,0:T(4,128)S(1)}, f32[2,1,4,12,256]{4,2,3,1,0:T(4,128)S(1)}, u32[]{:S(2)}, u32[]{:S(2)}) collective-permute-start(f32[2,1,4,12,256]{4,2,3,1,0:T(4,128)S(1)} %get-tuple-element.212), channel_id=1, source_target_pairs={{0,1},{1,2},{2,3},{3,4},{4,5},{5,6},{6,7},{7,8},{8,9},{9,10},{10,1... | collective-permute-start | bytes 294920 | tf_op jit(solution)/shard_map/ppermute | solution.py:17
  185.4 3.5 %collective-permute-done.27 = f32[2,1,4,12,256]{4,2,3,1,0:T(4,128)S(1)} collective-permute-done((f32[2,1,4,12,256]{4,2,3,1,0:T(4,128)S(1)}, f32[2,1,4,12,256]{4,2,3,1,0:T(4,128)S(1)}, u32[]{:S(2)}, u32[]{:S(2)}) %collective-permute-start.27) | collective-permute-done | bytes 98336 | tf_op jit(solution)/shard_map/ppermute | solution.py:18
  191.1 15.7 %all-to-all-start.6 = ((f32[2,1,4,256]{2,0,1,3:T(2,128)}), f32[2,1,4,256]{2,0,1,3:T(2,128)S(1)}, u32[]{:S(2)}, u32[]{:S(2)}) async-start(f32[2,1,4,256]{2,0,1,3:T(2,128)} %copy.1055), calls=%async_computation.6 | async-start | bytes 524288 | tf_op jit(solution)/shard_map/all_to_all | solution.py:164
  207.2 10.1 %all-to-all-done.6 = f32[2,1,4,256]{2,0,1,3:T(2,128)S(1)} async-done(((f32[2,1,4,256]{2,0,1,3:T(2,128)}), f32[2,1,4,256]{2,0,1,3:T(2,128)S(1)}, u32[]{:S(2)}, u32[]{:S(2)}) %all-to-all-start.6) | async-done | bytes 8224 | tf_op jit(solution)/shard_map/all_to_all | solution.py:164
  227.6 6.4 %all-to-all-start.9 = ((f32[2,1,128,8]{3,0,1,2:T(2,128)}), f32[2,1,128,8]{3,0,1,2:T(2,128)S(1)}, u32[]{:S(2)}, u32[]{:S(2)}) async-start(f32[2,1,128,8]{3,0,1,2:T(2,128)} %copy.1067), calls=%async_computation.9 | async-start | bytes 262144 | tf_op jit(solution)/shard_map/all_to_all | solution.py:136
  248.7 3.1 %collective-permute-done.31 = f32[2,1,4,12,256]{4,2,3,1,0:T(4,128)S(1)} collective-permute-done((f32[2,1,4,12,256]{4,2,3,1,0:T(4,128)S(1)}, f32[2,1,4,12,256]{4,2,3,1,0:T(4,128)S(1)}, u32[]{:S(2)}, u32[]{:S(2)}) %collective-permute-start.31) | collective-permute-done | bytes 98336 | tf_op jit(solution)/shard_map/ppermute | solution.py:18
  254.2 11.9 %all-to-all-start.10 = ((f32[32,1,128]{2,1,0:T(1,128)}), f32[32,1,128]{2,1,0:T(1,128)S(1)}, u32[]{:S(2)}, u32[]{:S(2)}) async-start(f32[32,1,128]{2,1,0:T(1,128)} %broadcast_in_dim.11), calls=%async_computation.10 | async-start | bytes 32768 | tf_op jit(solution)/shard_map/all_to_all | solution.py:25
  266.8 6.5 %all-to-all-done.10 = f32[32,1,128]{2,1,0:T(1,128)S(1)} async-done(((f32[32,1,128]{2,1,0:T(1,128)}), f32[32,1,128]{2,1,0:T(1,128)S(1)}, u32[]{:S(2)}, u32[]{:S(2)}) %all-to-all-start.10) | async-done | bytes 16416 | tf_op jit(solution)/shard_map/all_to_all | solution.py:25
  (266 shorter events, 106.8 us)
Async XLA Ops:
  1.6 41.8 %collective-permute-start.10 = (f32[2,1,4,12,256]{4,2,3,1,0:T(4,128)S(1)}, f32[2,1,4,12,256]{4,2,3,1,0:T(4,128)S(1)}, u32[]{:S(2)}, u32[]{:S(2)}) collective-permute-start(f32[2,1,4,12,256]{4,2,3,1,0:T(4,128)S(1)} %slice_bitcast_fusion.3), channel_id=1, source_target_pairs={{1,0},{2,1},{3,2},{4,3},{5,4},{6,5},{7,6},{8,7},{9,8},{10,9},{11,1... | collective-permute-start | bytes 294920 | tf_op jit(solution)/shard_map/ppermute | solution.py:18
  2.9 40.6 %collective-permute-start.11 = (f32[2,1,4,12,256]{4,2,3,1,0:T(4,128)S(1)}, f32[2,1,4,12,256]{4,2,3,1,0:T(4,128)S(1)}, u32[]{:S(2)}, u32[]{:S(2)}) collective-permute-start(f32[2,1,4,12,256]{4,2,3,1,0:T(4,128)S(1)} %slice_bitcast_fusion.3), channel_id=1, source_target_pairs={{0,1},{1,2},{2,3},{3,4},{4,5},{5,6},{6,7},{7,8},{8,9},{9,10},{10,1... | collective-permute-start | bytes 294920 | tf_op jit(solution)/shard_map/ppermute | solution.py:17
  6.8 11.6 %collective-permute-start.1 = (f32[3,2,1,4,4,128]{5,4,3,2,1,0:T(4,128)S(1)}, f32[3,2,1,4,4,128]{5,4,3,2,1,0:T(4,128)S(1)}, u32[]{:S(2)}, u32[]{:S(2)}) collective-permute-start(f32[3,2,1,4,4,128]{5,4,3,2,1,0:T(4,128)S(1)} %get-tuple-element.249), channel_id=1, source_target_pairs={{1,0},{2,1},{3,2},{4,3},{5,4},{6,5},{7,6},{8,7},{9,8},{10,9},{11,1... | collective-permute-start | bytes 147464 | tf_op jit(solution)/shard_map/ppermute | solution.py:18
  8.1 10.3 %collective-permute-start = (f32[3,2,1,4,4,128]{5,4,3,2,1,0:T(4,128)S(1)}, f32[3,2,1,4,4,128]{5,4,3,2,1,0:T(4,128)S(1)}, u32[]{:S(2)}, u32[]{:S(2)}) collective-permute-start(f32[3,2,1,4,4,128]{5,4,3,2,1,0:T(4,128)S(1)} %get-tuple-element.248), channel_id=1, source_target_pairs={{0,1},{1,2},{2,3},{3,4},{4,5},{5,6},{6,7},{7,8},{8,9},{9,10},{10,1... | collective-permute-start | bytes 147464 | tf_op jit(solution)/shard_map/ppermute | solution.py:17
  19.5 18.0 %all-to-all-start.1 = ((f32[2,1,128,8]{3,0,1,2:T(2,128)}), f32[2,1,128,8]{3,0,1,2:T(2,128)S(1)}, u32[]{:S(2)}, u32[]{:S(2)}) async-start(f32[2,1,128,8]{3,0,1,2:T(2,128)} %copy.1035), calls=%async_computation.1 | async-start | bytes 262144 | tf_op jit(solution)/shard_map/all_to_all | solution.py:136
  52.7 23.0 %all-to-all-start = ((f32[2,1,4,256]{2,0,1,3:T(2,128)}), f32[2,1,4,256]{2,0,1,3:T(2,128)S(1)}, u32[]{:S(2)}, u32[]{:S(2)}) async-start(f32[2,1,4,256]{2,0,1,3:T(2,128)} %copy.1020), calls=%async_computation | async-start | bytes 524288 | tf_op jit(solution)/shard_map/all_to_all | solution.py:164
  76.3 9.6 %all-to-all-start.2 = ((f32[32,1,128]{2,1,0:T(1,128)}), f32[32,1,128]{2,1,0:T(1,128)S(1)}, u32[]{:S(2)}, u32[]{:S(2)}) async-start(f32[32,1,128]{2,1,0:T(1,128)} %broadcast_in_dim.8), calls=%async_computation.2 | async-start | bytes 32768 | tf_op jit(solution)/shard_map/all_to_all | solution.py:25
  79.6 21.2 %collective-permute-start.7 = (f32[3,2,1,4,4,128]{5,4,3,2,1,0:T(4,128)S(1)}, f32[3,2,1,4,4,128]{5,4,3,2,1,0:T(4,128)S(1)}, u32[]{:S(2)}, u32[]{:S(2)}) collective-permute-start(f32[3,2,1,4,4,128]{5,4,3,2,1,0:T(4,128)S(1)} %get-tuple-element.243), channel_id=1, source_target_pairs={{1,0},{2,1},{3,2},{4,3},{5,4},{6,5},{7,6},{8,7},{9,8},{10,9},{11,1... | collective-permute-start | bytes 147464 | tf_op jit(solution)/shard_map/ppermute | solution.py:18
  80.9 19.9 %collective-permute-start.6 = (f32[3,2,1,4,4,128]{5,4,3,2,1,0:T(4,128)S(1)}, f32[3,2,1,4,4,128]{5,4,3,2,1,0:T(4,128)S(1)}, u32[]{:S(2)}, u32[]{:S(2)}) collective-permute-start(f32[3,2,1,4,4,128]{5,4,3,2,1,0:T(4,128)S(1)} %get-tuple-element.242), channel_id=1, source_target_pairs={{0,1},{1,2},{2,3},{3,4},{4,5},{5,6},{6,7},{7,8},{8,9},{9,10},{10,1... | collective-permute-start | bytes 147464 | tf_op jit(solution)/shard_map/ppermute | solution.py:17
  85.9 14.7 %all-to-all-start.4 = ((f32[2,1,128,8]{3,0,1,2:T(2,128)}), f32[2,1,128,8]{3,0,1,2:T(2,128)S(1)}, u32[]{:S(2)}, u32[]{:S(2)}) async-start(f32[2,1,128,8]{3,0,1,2:T(2,128)} %copy.1051), calls=%async_computation.4 | async-start | bytes 262144 | tf_op jit(solution)/shard_map/all_to_all | solution.py:136
  94.9 12.2 %collective-permute-start.18 = (f32[2,1,4,12,256]{4,2,3,1,0:T(4,128)S(1)}, f32[2,1,4,12,256]{4,2,3,1,0:T(4,128)S(1)}, u32[]{:S(2)}, u32[]{:S(2)}) collective-permute-start(f32[2,1,4,12,256]{4,2,3,1,0:T(4,128)S(1)} %fusion.1100), channel_id=1, source_target_pairs={{1,0},{2,1},{3,2},{4,3},{5,4},{6,5},{7,6},{8,7},{9,8},{10,9},{11,1... | collective-permute-start | bytes 294920 | tf_op jit(solution)/shard_map/ppermute | solution.py:18
  96.2 10.9 %collective-permute-start.19 = (f32[2,1,4,12,256]{4,2,3,1,0:T(4,128)S(1)}, f32[2,1,4,12,256]{4,2,3,1,0:T(4,128)S(1)}, u32[]{:S(2)}, u32[]{:S(2)}) collective-permute-start(f32[2,1,4,12,256]{4,2,3,1,0:T(4,128)S(1)} %fusion.1100), channel_id=1, source_target_pairs={{0,1},{1,2},{2,3},{3,4},{4,5},{5,6},{6,7},{7,8},{8,9},{9,10},{10,1... | collective-permute-start | bytes 294920 | tf_op jit(solution)/shard_map/ppermute | solution.py:17
  118.4 25.3 %all-to-all-start.3 = ((f32[2,1,4,256]{2,0,1,3:T(2,128)}), f32[2,1,4,256]{2,0,1,3:T(2,128)S(1)}, u32[]{:S(2)}, u32[]{:S(2)}) async-start(f32[2,1,4,256]{2,0,1,3:T(2,128)} %copy.1039), calls=%async_computation.3 | async-start | bytes 524288 | tf_op jit(solution)/shard_map/all_to_all | solution.py:164
  145.2 10.8 %all-to-all-start.7 = ((f32[2,1,128,8]{3,0,1,2:T(2,128)}), f32[2,1,128,8]{3,0,1,2:T(2,128)S(1)}, u32[]{:S(2)}, u32[]{:S(2)}) async-start(f32[2,1,128,8]{3,0,1,2:T(2,128)} %copy.1063), calls=%async_computation.7 | async-start | bytes 262144 | tf_op jit(solution)/shard_map/all_to_all | solution.py:136
  159.1 13.4 %collective-permute-start.15 = (f32[3,2,1,4,4,128]{5,4,3,2,1,0:T(4,128)S(1)}, f32[3,2,1,4,4,128]{5,4,3,2,1,0:T(4,128)S(1)}, u32[]{:S(2)}, u32[]{:S(2)}) collective-permute-start(f32[3,2,1,4,4,128]{5,4,3,2,1,0:T(4,128)S(1)} %get-tuple-element.239), channel_id=1, source_target_pairs={{1,0},{2,1},{3,2},{4,3},{5,4},{6,5},{7,6},{8,7},{9,8},{10,9},{11,1... | collective-permute-start | bytes 147464 | tf_op jit(solution)/shard_map/ppermute | solution.py:18
  160.4 12.1 %collective-permute-start.14 = (f32[3,2,1,4,4,128]{5,4,3,2,1,0:T(4,128)S(1)}, f32[3,2,1,4,4,128]{5,4,3,2,1,0:T(4,128)S(1)}, u32[]{:S(2)}, u32[]{:S(2)}) collective-permute-start(f32[3,2,1,4,4,128]{5,4,3,2,1,0:T(4,128)S(1)} %get-tuple-element.238), channel_id=1, source_target_pairs={{0,1},{1,2},{2,3},{3,4},{4,5},{5,6},{6,7},{7,8},{8,9},{9,10},{10,1... | collective-permute-start | bytes 147464 | tf_op jit(solution)/shard_map/ppermute | solution.py:17
  168.0 11.4 %collective-permute-start.24 = (f32[2,1,4,12,256]{4,2,3,1,0:T(4,128)S(1)}, f32[2,1,4,12,256]{4,2,3,1,0:T(4,128)S(1)}, u32[]{:S(2)}, u32[]{:S(2)}) collective-permute-start(f32[2,1,4,12,256]{4,2,3,1,0:T(4,128)S(1)} %fusion.1101), channel_id=1, source_target_pairs={{1,0},{2,1},{3,2},{4,3},{5,4},{6,5},{7,6},{8,7},{9,8},{10,9},{11,1... | collective-permute-start | bytes 294920 | tf_op jit(solution)/shard_map/ppermute | solution.py:18
  169.3 10.1 %collective-permute-start.25 = (f32[2,1,4,12,256]{4,2,3,1,0:T(4,128)S(1)}, f32[2,1,4,12,256]{4,2,3,1,0:T(4,128)S(1)}, u32[]{:S(2)}, u32[]{:S(2)}) collective-permute-start(f32[2,1,4,12,256]{4,2,3,1,0:T(4,128)S(1)} %fusion.1101), channel_id=1, source_target_pairs={{0,1},{1,2},{2,3},{3,4},{4,5},{5,6},{6,7},{7,8},{8,9},{9,10},{10,1... | collective-permute-start | bytes 294920 | tf_op jit(solution)/shard_map/ppermute | solution.py:17
  191.1 26.3 %all-to-all-start.6 = ((f32[2,1,4,256]{2,0,1,3:T(2,128)}), f32[2,1,4,256]{2,0,1,3:T(2,128)S(1)}, u32[]{:S(2)}, u32[]{:S(2)}) async-start(f32[2,1,4,256]{2,0,1,3:T(2,128)} %copy.1055), calls=%async_computation.6 | async-start | bytes 524288 | tf_op jit(solution)/shard_map/all_to_all | solution.py:164
  218.0 9.6 %all-to-all-start.8 = ((f32[32,1,128]{2,1,0:T(1,128)}), f32[32,1,128]{2,1,0:T(1,128)S(1)}, u32[]{:S(2)}, u32[]{:S(2)}) async-start(f32[32,1,128]{2,1,0:T(1,128)} %broadcast_in_dim.10), calls=%async_computation.8 | async-start | bytes 32768 | tf_op jit(solution)/shard_map/all_to_all | solution.py:25
  221.2 21.3 %collective-permute-start.23 = (f32[3,2,1,4,4,128]{5,4,3,2,1,0:T(4,128)S(1)}, f32[3,2,1,4,4,128]{5,4,3,2,1,0:T(4,128)S(1)}, u32[]{:S(2)}, u32[]{:S(2)}) collective-permute-start(f32[3,2,1,4,4,128]{5,4,3,2,1,0:T(4,128)S(1)} %get-tuple-element.235), channel_id=1, source_target_pairs={{1,0},{2,1},{3,2},{4,3},{5,4},{6,5},{7,6},{8,7},{9,8},{10,9},{11,1... | collective-permute-start | bytes 147464 | tf_op jit(solution)/shard_map/ppermute | solution.py:18
  222.5 20.0 %collective-permute-start.22 = (f32[3,2,1,4,4,128]{5,4,3,2,1,0:T(4,128)S(1)}, f32[3,2,1,4,4,128]{5,4,3,2,1,0:T(4,128)S(1)}, u32[]{:S(2)}, u32[]{:S(2)}) collective-permute-start(f32[3,2,1,4,4,128]{5,4,3,2,1,0:T(4,128)S(1)} %get-tuple-element.234), channel_id=1, source_target_pairs={{0,1},{1,2},{2,3},{3,4},{4,5},{5,6},{6,7},{7,8},{8,9},{9,10},{10,1... | collective-permute-start | bytes 147464 | tf_op jit(solution)/shard_map/ppermute | solution.py:17
  227.6 14.7 %all-to-all-start.9 = ((f32[2,1,128,8]{3,0,1,2:T(2,128)}), f32[2,1,128,8]{3,0,1,2:T(2,128)S(1)}, u32[]{:S(2)}, u32[]{:S(2)}) async-start(f32[2,1,128,8]{3,0,1,2:T(2,128)} %copy.1067), calls=%async_computation.9 | async-start | bytes 262144 | tf_op jit(solution)/shard_map/all_to_all | solution.py:136
  254.2 19.0 %all-to-all-start.10 = ((f32[32,1,128]{2,1,0:T(1,128)}), f32[32,1,128]{2,1,0:T(1,128)S(1)}, u32[]{:S(2)}, u32[]{:S(2)}) async-start(f32[32,1,128]{2,1,0:T(1,128)} %broadcast_in_dim.11), calls=%async_computation.10 | async-start | bytes 32768 | tf_op jit(solution)/shard_map/all_to_all | solution.py:25
  (30 other events, 138.8 us)

commit v2 on v1

v2 whole, which is shorter than its diff:
```python
import jax
import jax.numpy as jnp
from jax import lax
from jax.sharding import PartitionSpec as P

COEFF = (1225.0 / 1024.0, -245.0 / 3072.0, 49.0 / 5120.0, -5.0 / 7168.0)
TIME_STEP = 0.2
HALO = 4
ROW_AXIS = 2
DEPTH_AXIS = 3


def halo_rows(fields):
    devices = lax.axis_size("gx")
    up = [(i, i + 1) for i in range(devices - 1)]
    down = [(i + 1, i) for i in range(devices - 1)]
    packed = jnp.concatenate(fields, axis=DEPTH_AXIS)
    length = packed.shape[ROW_AXIS]
    before = lax.ppermute(
        lax.slice_in_dim(packed, length - HALO, length, axis=ROW_AXIS), "gx", up
    )
    after = lax.ppermute(lax.slice_in_dim(packed, 0, HALO, axis=ROW_AXIS), "gx", down)
    padded = jnp.concatenate([before, packed, after], axis=ROW_AXIS)
    out, start = [], 0
    for f in fields:
        depth = f.shape[DEPTH_AXIS]
        out.append(lax.slice_in_dim(padded, start, start + depth, axis=DEPTH_AXIS))
        start += depth
    return out


def gather_sum(partial, parts):
    copies = jnp.broadcast_to(partial[None], (parts,) + partial.shape)
    return jnp.sum(lax.all_to_all(copies, "gx", 0, 0, tiled=True), axis=0)


def stencil(padded, axis, forward):
    length = padded.shape[axis] - 8
    summed = None
    for offset in range(1, 5):
        if forward:
            front_at, back_at = (4 + offset, 5 - offset)
        else:
            front_at, back_at = (3 + offset, 4 - offset)
        front = lax.slice_in_dim(padded, front_at, front_at + length, axis=axis)
        back = lax.slice_in_dim(padded, back_at, back_at + length, axis=axis)
        addend = COEFF[offset - 1] * (front - back)
        summed = addend if summed is None else summed + addend
    return summed


def padded_zero(field, axis):
    widths = [(0, 0)] * field.ndim
    widths[axis] = (4, 4)
    return jnp.pad(field, widths)


def derive(field, axis, forward):
    return stencil(padded_zero(field, axis), axis, forward)


def on_device(
    solid_state,
    water_state,
    lame_lambda,
    shear_mu,
    solid_buoy,
    water_kappa,
    water_buoy,
    seafloor,
    source_cell,
    wavelet,
    receiver_column,
    observed,
):
    parts = lax.axis_size("gx")
    place = lax.axis_index("gx")
    n_fields, waves, shots, width_x, rock_z, total_y = solid_state.shape
    local_y = water_state.shape[3]
    depth_rows = water_state.shape[4]
    total_x = water_state.shape[5]
    anchor_y = place * local_y

    rock_in = jnp.concatenate(
        [
            solid_state.reshape(n_fields * waves * shots, width_x, rock_z, total_y),
            jnp.stack([lame_lambda, shear_mu, solid_buoy]),
        ],
        axis=0,
    )
    rock = lax.all_to_all(
        jnp.transpose(rock_in, (0, 3, 2, 1)), "gx", split_axis=1, concat_axis=3, tiled=True
    )
    rock_state = rock[: n_fields * waves * shots].reshape(
        n_fields, waves, shots, local_y, rock_z, total_x
    )
    lam, mu, buoy = rock[-3], rock[-2], rock[-1]

    vel_x, vel_y, vel_z = (rock_state[0], rock_state[1], rock_state[2])
    sig_xx, sig_yy, sig_zz = (rock_state[3], rock_state[4], rock_state[5])
    sig_xy, sig_xz, sig_yz = (rock_state[6], rock_state[7], rock_state[8])
    pressure, flow_x, flow_y, flow_z = (
        water_state[0],
        water_state[1],
        water_state[2],
        water_state[3],
    )
    depth_idx = lax.broadcasted_iota(jnp.int32, (1, depth_rows, 1), 1)
    floor_rows = seafloor[:, None, :]
    live = (depth_idx < floor_rows).astype(jnp.float32)
    bottom = (depth_idx == floor_rows - 1).astype(jnp.float32)
    above = (depth_idx < floor_rows - 1).astype(jnp.float32)
    rows_y = lax.broadcasted_iota(jnp.int32, (local_y, 1, 1), 0) + anchor_y
    cols_x = lax.broadcasted_iota(jnp.int32, (1, 1, total_x), 2)
    flat_cell = (depth_idx * total_y + rows_y) * total_x + cols_x
    source_hot = (flat_cell[None] == source_cell[:, None, None, None]).astype(jnp.float32)
    node_y = receiver_column // total_x
    node_x = receiver_column % total_x
    inside = (node_y >= anchor_y) & (node_y < anchor_y + local_y)
    local_col = (node_y - anchor_y) * total_x + node_x
    column_iota = lax.broadcasted_iota(jnp.int32, (1, local_y * total_x), 1)
    node_hot = ((column_iota == local_col[:, None]) & inside[:, None]).astype(jnp.float32)
    grad_lambda = jnp.zeros(lam.shape, jnp.float32)
    grad_mu = jnp.zeros(lam.shape, jnp.float32)
    grad_kappa = jnp.zeros(water_kappa.shape, jnp.float32)
    misfits = []
    for step in range(wavelet.shape[0]):
        floor_pressure = jnp.sum(pressure * bottom, axis=3)
        sxy_pad, syy_pad, syz_pad, p_pad = halo_rows([sig_xy, sig_yy, sig_yz, pressure])
        vel_x = vel_x + TIME_STEP * buoy * (
            derive(sig_xx, 4, True) + stencil(sxy_pad, 2, False) + derive(sig_xz, 3, False)
        )
        vel_y = vel_y + TIME_STEP * buoy * (
            derive(sig_xy, 4, False) + stencil(syy_pad, 2, True) + derive(sig_yz, 3, False)
        )
        vel_z = vel_z + TIME_STEP * buoy * (
            derive(sig_xz, 4, False) + stencil(syz_pad, 2, False) + derive(sig_zz, 3, True)
        )
        floor_velocity = vel_z[:, :, :, 0, :]
        flow_x = (flow_x - TIME_STEP * water_buoy * derive(pressure, 4, True)) * live
        flow_y = (flow_y - TIME_STEP * water_buoy * stencil(p_pad, 2, True)) * live
        flow_z = (
            flow_z - TIME_STEP * water_buoy * derive(pressure, 3, True)
        ) * above + floor_velocity[:, :, :, None, :] * bottom
        vx_pad, vy_pad, vz_pad, uy_pad = halo_rows([vel_x, vel_y, vel_z, flow_y])
        strain_x = derive(vel_x, 4, False)
        strain_y = stencil(vy_pad, 2, False)
        strain_z = derive(vel_z, 3, False)
        dilation = strain_x + strain_y + strain_z
        shear_xy = stencil(vx_pad, 2, True) + derive(vel_y, 4, True)
        shear_xz = derive(vel_x, 3, True) + derive(vel_z, 4, True)
        shear_yz = derive(vel_y, 3, True) + stencil(vz_pad, 2, True)
        lam_part = lam * dilation
        sig_xx = sig_xx + TIME_STEP * (lam_part + 2.0 * mu * strain_x)
        sig_yy = sig_yy + TIME_STEP * (lam_part + 2.0 * mu * strain_y)
        sig_zz = sig_zz + TIME_STEP * (lam_part + 2.0 * mu * strain_z)
        sig_xy = sig_xy + TIME_STEP * mu * shear_xy
        sig_xz = sig_xz + TIME_STEP * mu * shear_xz
        sig_yz = sig_yz + TIME_STEP * mu * shear_yz
        sig_zz = sig_zz.at[:, :, :, 0, :].set(-floor_pressure)
        grad_lambda = grad_lambda + jnp.sum(dilation[0] * dilation[1], axis=0)
        normal_part = (
            strain_x[0] * strain_x[1] + strain_y[0] * strain_y[1] + strain_z[0] * strain_z[1]
        )
        shear_part = (
            shear_xy[0] * shear_xy[1] + shear_xz[0] * shear_xz[1] + shear_yz[0] * shear_yz[1]
        )
        grad_mu = grad_mu + jnp.sum(2.0 * normal_part + shear_part, axis=0)
        pressure = (
            pressure
            - TIME_STEP
            * water_kappa
            * (derive(flow_x, 4, False) + stencil(uy_pad, 2, False) + derive(flow_z, 3, False))
        ) * live
        pressure = pressure.at[0].add(wavelet[step][:, None, None, None] * source_hot)
        surface = jnp.sum(pressure * bottom, axis=3)
        partial_record = jnp.einsum(
            "sc,rc->sr",
            surface[0].reshape(shots, local_y * total_x),
            node_hot,
            precision=lax.Precision.HIGHEST,
        )
        recorded = gather_sum(partial_record, parts)
        misfit = recorded - observed[step]
        scaled = misfit * lax.rsqrt(jnp.mean(misfit * misfit, axis=1, keepdims=True) + 1e-06)
        inject = jnp.dot(
            scaled, node_hot, precision=lax.Precision.HIGHEST, preferred_element_type=jnp.float32
        ).reshape(shots, local_y, total_x)
        pressure = pressure.at[1].add(inject[:, :, None, :] * bottom)
        grad_kappa = grad_kappa + jnp.sum(pressure[0] * pressure[1], axis=0)
        misfits.append(misfit)

    grads = lax.all_to_all(
        jnp.stack([grad_lambda, grad_mu]), "gx", split_axis=3, concat_axis=1, tiled=True
    )
    grads = jnp.transpose(grads, (0, 3, 2, 1))
    return (grads[0], grads[1], grad_kappa, jnp.stack(misfits))


def solution(mesh):
    placed = (
        P(None, None, "groups", "gx", None, None),
        P(None, None, "groups", "gx", None, None),
        P("gx", None, None),
        P("gx", None, None),
        P("gx", None, None),
        P("gx", None, None),
        P("gx", None, None),
        P("gx", None),
        P("groups"),
        P(None, "groups"),
        P(),
        P(None, "groups", None),
    )
    return jax.shard_map(
        on_device,
        mesh=mesh,
        in_specs=placed,
        out_specs=(
            P("gx", "groups", None),
            P("gx", "groups", None),
            P("gx", "groups", None),
            P(None, "groups", None),
        ),
        check_vma=False,
    )
```

time: 279 us -> 203 us (0.73)
  starting transfers between devices: 162 us -> 93 us
  waiting for transfers between devices: 70 us -> 33.6 us
  local copies, waits for them, and re-layouts: 17.7 us -> 34.8 us
  other arithmetic: 18.9 us -> 30.9 us
    all_to_all x7 -> x2, starting transfers between devices: 67.9 us -> 9.86 us  [the longest x1 7.3 us: on_device(): lax.all_to_all(jnp.transpose(rock_in, (0, 3, 2, 1)), 'gx', split_axis=1,...]
    all_to_all x7 -> x2, waiting for transfers between devices: 45.4 us -> 9.83 us  [the longest x1 6.37 us: on_device(): lax.all_to_all(jnp.transpose(rock_in, (0, 3, 2, 1)), 'gx', split_axis=1,...]
    ppermute x32 -> x16, starting transfers between devices: 74 us -> 42.5 us  [the longest x8 32.1 us: halo_rows(): lax.ppermute(lax.slice_in_dim(packed, length - HALO, length, axis=ROW_AXI...]
    all_to_all x4, starting transfers between devices: 19.6 us -> 40.7 us  [gather_sum(): return jnp.sum(lax.all_to_all(copies, 'gx', 0, 0, tiled=True), axis=0)]
    unnamed x34 -> x127, local copies, waits for them, and re-layouts: 4.87 us -> 15.7 us
    ppermute x32 -> x16, waiting for transfers between devices: 13.1 us -> 4.93 us  [the longest x8 4.91 us: halo_rows(): lax.ppermute(lax.slice_in_dim(packed, length - HALO, length, axis=ROW_AXI...]
    add x25 -> x27, other arithmetic: 4.39 us -> 12 us  [the longest x3 2.75 us: on_device(): sig_xz = sig_xz + TIME_STEP * mu * shear_xz]
    all_to_all x4, waiting for transfers between devices: 11.5 us -> 18.8 us  [gather_sum(): return jnp.sum(lax.all_to_all(copies, 'gx', 0, 0, tiled=True), axis=0)]
  transfers between devices with their start and end apart: 43 -> 22, of which waited for: 17 -> 13; matrix products, arithmetic and copies ran while one was open for 6% -> 12% of each run, Pallas kernels for 0% -> 0%
where the time goes in v2:
time: 203 us; the launch traced here: 201 us
  starting transfers between devices  93 us (46%)
  local copies, waits for them, and re-layouts  34.8 us (17%)
  waiting for transfers between devices  33.6 us (17%)
  other arithmetic  30.9 us (15%)
  between operations  5.73 us (3%)
  matrix products  3.42 us (2%)
    all_to_all x4, starting transfers between devices, gather_sum(): return jnp.sum(lax.all_to_all(copies, 'gx', 0, 0, tiled=True), axis=0)  40.7 us
    ppermute x8, starting transfers between devices, halo_rows(): lax.ppermute(lax.slice_in_dim(packed, length - HALO, length, axis=ROW_AXI...  32.1 us
    all_to_all x4, waiting for transfers between devices, gather_sum(): return jnp.sum(lax.all_to_all(copies, 'gx', 0, 0, tiled=True), axis=0)  18.8 us
    unnamed x127, local copies, waits for them, and re-layouts  15.7 us
    ppermute x8, starting transfers between devices, halo_rows(): lax.ppermute(lax.slice_in_dim(packed, 0, HALO, axis=ROW_AXIS), 'gx', down)  10.3 us
    all_to_all x1, starting transfers between devices, on_device(): lax.all_to_all(jnp.transpose(rock_in, (0, 3, 2, 1)), 'gx', split_axis=1,...  7.3 us
    all_to_all x1, waiting for transfers between devices, on_device(): lax.all_to_all(jnp.transpose(rock_in, (0, 3, 2, 1)), 'gx', split_axis=1,...  6.37 us
    ppermute x8, waiting for transfers between devices, halo_rows(): lax.ppermute(lax.slice_in_dim(packed, length - HALO, length, axis=ROW_AXI...  4.91 us
  transfers between devices with their start and end apart: 22, of which 13 were waited for; matrix products, arithmetic and copies ran while one was open for 12% of the time, Pallas kernels for 0%

profile of v2, /device:TPU:0, one launch (start us, length us, event | category | flops | bytes accessed | tf_op | source)
XLA Modules:
  0.0 201.5 jit_solution(6539396504415313993)
XLA Ops:
  3.1 1.9 copy.585
  6.6 4.0 %reshape.1873 = f32[32,1,2688]{2,1,0:T(1,128)} reshape(f32[128,4,8,21]{3,2,1,0:T(8,128)} %bitcast_bitcast_fusion) | data formatting | bytes 688128
  10.6 7.3 %all-to-all-start = ((f32[32,1,2688]{2,1,0:T(1,128)}), f32[32,1,2688]{2,1,0:T(1,128)S(1)}, u32[]{:S(2)}, u32[]{:S(2)}) async-start(f32[32,1,2688]{2,1,0:T(1,128)} %reshape.1873), calls=%async_computation | async-start | bytes 688128 | tf_op jit(solution)/shard_map/all_to_all | solution.py:91
  23.8 6.4 %all-to-all-done = f32[32,1,2688]{2,1,0:T(1,128)S(1)} async-done(((f32[32,1,2688]{2,1,0:T(1,128)}), f32[32,1,2688]{2,1,0:T(1,128)S(1)}, u32[]{:S(2)}, u32[]{:S(2)}) %all-to-all-start) | async-done | bytes 344096 | tf_op jit(solution)/shard_map/all_to_all | solution.py:91
  32.2 2.3 %reshape.1874 = f32[128,4,8,21]{3,2,1,0:T(8,128)S(1)} reshape(f32[32,2688]{1,0:T(8,128)S(1)} %reduce.41) | data formatting | bytes 688128
  40.1 3.7 %collective-permute-start = (f32[2,1,4,24,256]{4,3,2,1,0:T(8,128)}, f32[2,1,4,24,256]{4,3,2,1,0:T(8,128)}, u32[]{:S(2)}, u32[]{:S(2)}) collective-permute-start(f32[2,1,4,24,256]{4,3,2,1,0:T(8,128)} %pad_maximum_fusion.9), channel_id=1, source_target_pairs={{0,1},{1,2},{2,3},{3,4},{4,5},{5,6},{6,7},{7,8},{8,9},{9,10},{10,1... | collective-permute-start | bytes 589832 | tf_op jit(solution)/shard_map/ppermute | solution.py:19
  55.0 3.0 %collective-permute-start.2 = (f32[2,1,4,24,256]{4,3,2,1,0:T(8,128)S(1)}, f32[2,1,4,24,256]{4,3,2,1,0:T(8,128)S(1)}, u32[]{:S(2)}, u32[]{:S(2)}) collective-permute-start(f32[2,1,4,24,256]{4,3,2,1,0:T(8,128)S(1)} %pad_maximum_fusion.10), channel_id=1, source_target_pairs={{0,1},{1,2},{2,3},{3,4},{4,5},{5,6},{6,7},{7,8},{8,9},{9,10},{10,1... | collective-permute-start | bytes 589832 | tf_op jit(solution)/shard_map/ppermute | solution.py:19
  61.4 10.2 %all-to-all-start.1 = ((f32[32,1,128]{2,1,0:T(1,128)}), f32[32,1,128]{2,1,0:T(1,128)S(1)}, u32[]{:S(2)}, u32[]{:S(2)}) async-start(f32[32,1,128]{2,1,0:T(1,128)} %broadcast_in_dim.8), calls=%async_computation.1 | async-start | bytes 32768 | tf_op jit(solution)/shard_map/all_to_all | solution.py:34
  74.1 4.6 %all-to-all-done.1 = f32[32,1,128]{2,1,0:T(1,128)S(1)} async-done(((f32[32,1,128]{2,1,0:T(1,128)}), f32[32,1,128]{2,1,0:T(1,128)S(1)}, u32[]{:S(2)}, u32[]{:S(2)}) %all-to-all-start.1) | async-done | bytes 16416 | tf_op jit(solution)/shard_map/all_to_all | solution.py:34
  81.8 3.0 %collective-permute-start.4 = (f32[2,1,4,24,256]{4,3,2,1,0:T(8,128)S(1)}, f32[2,1,4,24,256]{4,3,2,1,0:T(8,128)S(1)}, u32[]{:S(2)}, u32[]{:S(2)}) collective-permute-start(f32[2,1,4,24,256]{4,3,2,1,0:T(8,128)S(1)} %pad_maximum_fusion.11), channel_id=1, source_target_pairs={{0,1},{1,2},{2,3},{3,4},{4,5},{5,6},{6,7},{7,8},{8,9},{9,10},{10,1... | collective-permute-start | bytes 589832 | tf_op jit(solution)/shard_map/ppermute | solution.py:19
  88.3 5.3 %collective-permute-start.6 = (f32[2,1,4,24,256]{4,3,2,1,0:T(8,128)S(1)}, f32[2,1,4,24,256]{4,3,2,1,0:T(8,128)S(1)}, u32[]{:S(2)}, u32[]{:S(2)}) collective-permute-start(f32[2,1,4,24,256]{4,3,2,1,0:T(8,128)S(1)} %pad_maximum_fusion.12), channel_id=1, source_target_pairs={{0,1},{1,2},{2,3},{3,4},{4,5},{5,6},{6,7},{7,8},{8,9},{9,10},{10,1... | collective-permute-start | bytes 589832 | tf_op jit(solution)/shard_map/ppermute | solution.py:19
  97.0 10.2 %all-to-all-start.2 = ((f32[32,1,128]{2,1,0:T(1,128)}), f32[32,1,128]{2,1,0:T(1,128)S(1)}, u32[]{:S(2)}, u32[]{:S(2)}) async-start(f32[32,1,128]{2,1,0:T(1,128)} %broadcast_in_dim.9), calls=%async_computation.2 | async-start | bytes 32768 | tf_op jit(solution)/shard_map/all_to_all | solution.py:34
  109.6 4.6 %all-to-all-done.2 = f32[32,1,128]{2,1,0:T(1,128)S(1)} async-done(((f32[32,1,128]{2,1,0:T(1,128)}), f32[32,1,128]{2,1,0:T(1,128)S(1)}, u32[]{:S(2)}, u32[]{:S(2)}) %all-to-all-start.2) | async-done | bytes 16416 | tf_op jit(solution)/shard_map/all_to_all | solution.py:34
  117.4 3.0 %collective-permute-start.8 = (f32[2,1,4,24,256]{4,3,2,1,0:T(8,128)S(1)}, f32[2,1,4,24,256]{4,3,2,1,0:T(8,128)S(1)}, u32[]{:S(2)}, u32[]{:S(2)}) collective-permute-start(f32[2,1,4,24,256]{4,3,2,1,0:T(8,128)S(1)} %pad_maximum_fusion.13), channel_id=1, source_target_pairs={{0,1},{1,2},{2,3},{3,4},{4,5},{5,6},{6,7},{7,8},{8,9},{9,10},{10,1... | collective-permute-start | bytes 589832 | tf_op jit(solution)/shard_map/ppermute | solution.py:19
  123.9 5.6 %collective-permute-start.10 = (f32[2,1,4,24,256]{4,3,2,1,0:T(8,128)S(1)}, f32[2,1,4,24,256]{4,3,2,1,0:T(8,128)S(1)}, u32[]{:S(2)}, u32[]{:S(2)}) collective-permute-start(f32[2,1,4,24,256]{4,3,2,1,0:T(8,128)S(1)} %pad_maximum_fusion.14), channel_id=1, source_target_pairs={{0,1},{1,2},{2,3},{3,4},{4,5},{5,6},{6,7},{7,8},{8,9},{9,10},{10,1... | collective-permute-start | bytes 589832 | tf_op jit(solution)/shard_map/ppermute | solution.py:19
  132.6 10.2 %all-to-all-start.3 = ((f32[32,1,128]{2,1,0:T(1,128)}), f32[32,1,128]{2,1,0:T(1,128)S(1)}, u32[]{:S(2)}, u32[]{:S(2)}) async-start(f32[32,1,128]{2,1,0:T(1,128)} %broadcast_in_dim.10), calls=%async_computation.3 | async-start | bytes 32768 | tf_op jit(solution)/shard_map/all_to_all | solution.py:34
  144.6 5.2 %all-to-all-done.3 = f32[32,1,128]{2,1,0:T(1,128)S(1)} async-done(((f32[32,1,128]{2,1,0:T(1,128)}), f32[32,1,128]{2,1,0:T(1,128)S(1)}, u32[]{:S(2)}, u32[]{:S(2)}) %all-to-all-start.3) | async-done | bytes 16416 | tf_op jit(solution)/shard_map/all_to_all | solution.py:34
  153.0 3.0 %collective-permute-start.12 = (f32[2,1,4,24,256]{4,3,2,1,0:T(8,128)S(1)}, f32[2,1,4,24,256]{4,3,2,1,0:T(8,128)S(1)}, u32[]{:S(2)}, u32[]{:S(2)}) collective-permute-start(f32[2,1,4,24,256]{4,3,2,1,0:T(8,128)S(1)} %pad_maximum_fusion.15), channel_id=1, source_target_pairs={{0,1},{1,2},{2,3},{3,4},{4,5},{5,6},{6,7},{7,8},{8,9},{9,10},{10,1... | collective-permute-start | bytes 589832 | tf_op jit(solution)/shard_map/ppermute | solution.py:19
  159.5 5.3 %collective-permute-start.14 = (f32[2,1,4,24,256]{4,3,2,1,0:T(8,128)S(1)}, f32[2,1,4,24,256]{4,3,2,1,0:T(8,128)S(1)}, u32[]{:S(2)}, u32[]{:S(2)}) collective-permute-start(f32[2,1,4,24,256]{4,3,2,1,0:T(8,128)S(1)} %pad_maximum_fusion.16), channel_id=1, source_target_pairs={{0,1},{1,2},{2,3},{3,4},{4,5},{5,6},{6,7},{7,8},{8,9},{9,10},{10,1... | collective-permute-start | bytes 589832 | tf_op jit(solution)/shard_map/ppermute | solution.py:19
  168.6 10.2 %all-to-all-start.5 = ((f32[32,1,128]{2,1,0:T(1,128)}), f32[32,1,128]{2,1,0:T(1,128)S(1)}, u32[]{:S(2)}, u32[]{:S(2)}) async-start(f32[32,1,128]{2,1,0:T(1,128)} %broadcast_in_dim.11), calls=%async_computation.5 | async-start | bytes 32768 | tf_op jit(solution)/shard_map/all_to_all | solution.py:34
  181.5 4.4 %all-to-all-done.5 = f32[32,1,128]{2,1,0:T(1,128)S(1)} async-done(((f32[32,1,128]{2,1,0:T(1,128)}), f32[32,1,128]{2,1,0:T(1,128)S(1)}, u32[]{:S(2)}, u32[]{:S(2)}) %all-to-all-start.5) | async-done | bytes 16416 | tf_op jit(solution)/shard_map/all_to_all | solution.py:34
  185.8 2.6 %all-to-all-start.4 = ((f32[32,1,256]{2,1,0:T(1,128)}), f32[32,1,256]{2,1,0:T(1,128)S(1)}, u32[]{:S(2)}, u32[]{:S(2)}) async-start(f32[32,1,256]{2,1,0:T(1,128)} %reshape.1875), calls=%async_computation.4 | async-start | bytes 65536 | tf_op jit(solution)/shard_map/all_to_all | solution.py:193
  192.2 3.5 %all-to-all-done.4 = f32[32,1,256]{2,1,0:T(1,128)S(1)} async-done(((f32[32,1,256]{2,1,0:T(1,128)}), f32[32,1,256]{2,1,0:T(1,128)S(1)}, u32[]{:S(2)}, u32[]{:S(2)}) %all-to-all-start.4) | async-done | bytes 32800 | tf_op jit(solution)/shard_map/all_to_all | solution.py:193
  197.7 1.9 copy.683
  (310 shorter events, 74.3 us)
Async XLA Ops:
  10.6 19.6 %all-to-all-start = ((f32[32,1,2688]{2,1,0:T(1,128)}), f32[32,1,2688]{2,1,0:T(1,128)S(1)}, u32[]{:S(2)}, u32[]{:S(2)}) async-start(f32[32,1,2688]{2,1,0:T(1,128)} %reshape.1873), calls=%async_computation | async-start | bytes 688128 | tf_op jit(solution)/shard_map/all_to_all | solution.py:91
  18.0 97.6 %copy-start.32 = (s32[4,256]{1,0:T(4,128)}, s32[4,256]{1,0:T(4,128)S(1)}, u32[]{:S(2)}) copy-start(s32[4,256]{1,0:T(4,128)S(1)} %multiply_add_fusion.24) | copy-start | bytes 12292
  38.8 9.1 %collective-permute-start.1 = (f32[2,1,4,24,256]{4,3,2,1,0:T(8,128)}, f32[2,1,4,24,256]{4,3,2,1,0:T(8,128)}, u32[]{:S(2)}, u32[]{:S(2)}) collective-permute-start(f32[2,1,4,24,256]{4,3,2,1,0:T(8,128)} %pad_maximum_fusion.9), channel_id=1, source_target_pairs={{1,0},{2,1},{3,2},{4,3},{5,4},{6,5},{7,6},{8,7},{9,8},{10,9},{11,1... | collective-permute-start | bytes 589832 | tf_op jit(solution)/shard_map/ppermute | solution.py:22
  40.1 7.9 %collective-permute-start = (f32[2,1,4,24,256]{4,3,2,1,0:T(8,128)}, f32[2,1,4,24,256]{4,3,2,1,0:T(8,128)}, u32[]{:S(2)}, u32[]{:S(2)}) collective-permute-start(f32[2,1,4,24,256]{4,3,2,1,0:T(8,128)} %pad_maximum_fusion.9), channel_id=1, source_target_pairs={{0,1},{1,2},{2,3},{3,4},{4,5},{5,6},{6,7},{7,8},{8,9},{9,10},{10,1... | collective-permute-start | bytes 589832 | tf_op jit(solution)/shard_map/ppermute | solution.py:19
  53.7 5.3 %collective-permute-start.3 = (f32[2,1,4,24,256]{4,3,2,1,0:T(8,128)S(1)}, f32[2,1,4,24,256]{4,3,2,1,0:T(8,128)S(1)}, u32[]{:S(2)}, u32[]{:S(2)}) collective-permute-start(f32[2,1,4,24,256]{4,3,2,1,0:T(8,128)S(1)} %pad_maximum_fusion.10), channel_id=1, source_target_pairs={{1,0},{2,1},{3,2},{4,3},{5,4},{6,5},{7,6},{8,7},{9,8},{10,9},{11,1... | collective-permute-start | bytes 589832 | tf_op jit(solution)/shard_map/ppermute | solution.py:22
  55.0 4.1 %collective-permute-start.2 = (f32[2,1,4,24,256]{4,3,2,1,0:T(8,128)S(1)}, f32[2,1,4,24,256]{4,3,2,1,0:T(8,128)S(1)}, u32[]{:S(2)}, u32[]{:S(2)}) collective-permute-start(f32[2,1,4,24,256]{4,3,2,1,0:T(8,128)S(1)} %pad_maximum_fusion.10), channel_id=1, source_target_pairs={{0,1},{1,2},{2,3},{3,4},{4,5},{5,6},{6,7},{7,8},{8,9},{9,10},{10,1... | collective-permute-start | bytes 589832 | tf_op jit(solution)/shard_map/ppermute | solution.py:19
  58.1 57.5 %copy-start.40 = (s32[128]{0:T(128)}, s32[128]{0:T(128)S(1)}, u32[]{:S(2)}) copy-start(s32[128]{0:T(128)S(1)} %fusion.1097) | copy-start | bytes 1540
  61.4 17.3 %all-to-all-start.1 = ((f32[32,1,128]{2,1,0:T(1,128)}), f32[32,1,128]{2,1,0:T(1,128)S(1)}, u32[]{:S(2)}, u32[]{:S(2)}) async-start(f32[32,1,128]{2,1,0:T(1,128)} %broadcast_in_dim.8), calls=%async_computation.1 | async-start | bytes 32768 | tf_op jit(solution)/shard_map/all_to_all | solution.py:34
  80.5 4.4 %collective-permute-start.5 = (f32[2,1,4,24,256]{4,3,2,1,0:T(8,128)S(1)}, f32[2,1,4,24,256]{4,3,2,1,0:T(8,128)S(1)}, u32[]{:S(2)}, u32[]{:S(2)}) collective-permute-start(f32[2,1,4,24,256]{4,3,2,1,0:T(8,128)S(1)} %pad_maximum_fusion.11), channel_id=1, source_target_pairs={{1,0},{2,1},{3,2},{4,3},{5,4},{6,5},{7,6},{8,7},{9,8},{10,9},{11,1... | collective-permute-start | bytes 589832 | tf_op jit(solution)/shard_map/ppermute | solution.py:22
  81.8 4.1 %collective-permute-start.4 = (f32[2,1,4,24,256]{4,3,2,1,0:T(8,128)S(1)}, f32[2,1,4,24,256]{4,3,2,1,0:T(8,128)S(1)}, u32[]{:S(2)}, u32[]{:S(2)}) collective-permute-start(f32[2,1,4,24,256]{4,3,2,1,0:T(8,128)S(1)} %pad_maximum_fusion.11), channel_id=1, source_target_pairs={{0,1},{1,2},{2,3},{3,4},{4,5},{5,6},{6,7},{7,8},{8,9},{9,10},{10,1... | collective-permute-start | bytes 589832 | tf_op jit(solution)/shard_map/ppermute | solution.py:19
  87.0 6.7 %collective-permute-start.7 = (f32[2,1,4,24,256]{4,3,2,1,0:T(8,128)S(1)}, f32[2,1,4,24,256]{4,3,2,1,0:T(8,128)S(1)}, u32[]{:S(2)}, u32[]{:S(2)}) collective-permute-start(f32[2,1,4,24,256]{4,3,2,1,0:T(8,128)S(1)} %pad_maximum_fusion.12), channel_id=1, source_target_pairs={{1,0},{2,1},{3,2},{4,3},{5,4},{6,5},{7,6},{8,7},{9,8},{10,9},{11,1... | collective-permute-start | bytes 589832 | tf_op jit(solution)/shard_map/ppermute | solution.py:22
  88.3 6.4 %collective-permute-start.6 = (f32[2,1,4,24,256]{4,3,2,1,0:T(8,128)S(1)}, f32[2,1,4,24,256]{4,3,2,1,0:T(8,128)S(1)}, u32[]{:S(2)}, u32[]{:S(2)}) collective-permute-start(f32[2,1,4,24,256]{4,3,2,1,0:T(8,128)S(1)} %pad_maximum_fusion.12), channel_id=1, source_target_pairs={{0,1},{1,2},{2,3},{3,4},{4,5},{5,6},{6,7},{7,8},{8,9},{9,10},{10,1... | collective-permute-start | bytes 589832 | tf_op jit(solution)/shard_map/ppermute | solution.py:19
  97.0 17.2 %all-to-all-start.2 = ((f32[32,1,128]{2,1,0:T(1,128)}), f32[32,1,128]{2,1,0:T(1,128)S(1)}, u32[]{:S(2)}, u32[]{:S(2)}) async-start(f32[32,1,128]{2,1,0:T(1,128)} %broadcast_in_dim.9), calls=%async_computation.2 | async-start | bytes 32768 | tf_op jit(solution)/shard_map/all_to_all | solution.py:34
  116.1 5.1 %collective-permute-start.9 = (f32[2,1,4,24,256]{4,3,2,1,0:T(8,128)S(1)}, f32[2,1,4,24,256]{4,3,2,1,0:T(8,128)S(1)}, u32[]{:S(2)}, u32[]{:S(2)}) collective-permute-start(f32[2,1,4,24,256]{4,3,2,1,0:T(8,128)S(1)} %pad_maximum_fusion.13), channel_id=1, source_target_pairs={{1,0},{2,1},{3,2},{4,3},{5,4},{6,5},{7,6},{8,7},{9,8},{10,9},{11,1... | collective-permute-start | bytes 589832 | tf_op jit(solution)/shard_map/ppermute | solution.py:22
  117.4 4.1 %collective-permute-start.8 = (f32[2,1,4,24,256]{4,3,2,1,0:T(8,128)S(1)}, f32[2,1,4,24,256]{4,3,2,1,0:T(8,128)S(1)}, u32[]{:S(2)}, u32[]{:S(2)}) collective-permute-start(f32[2,1,4,24,256]{4,3,2,1,0:T(8,128)S(1)} %pad_maximum_fusion.13), channel_id=1, source_target_pairs={{0,1},{1,2},{2,3},{3,4},{4,5},{5,6},{6,7},{7,8},{8,9},{9,10},{10,1... | collective-permute-start | bytes 589832 | tf_op jit(solution)/shard_map/ppermute | solution.py:19
  122.6 6.9 %collective-permute-start.11 = (f32[2,1,4,24,256]{4,3,2,1,0:T(8,128)S(1)}, f32[2,1,4,24,256]{4,3,2,1,0:T(8,128)S(1)}, u32[]{:S(2)}, u32[]{:S(2)}) collective-permute-start(f32[2,1,4,24,256]{4,3,2,1,0:T(8,128)S(1)} %pad_maximum_fusion.14), channel_id=1, source_target_pairs={{1,0},{2,1},{3,2},{4,3},{5,4},{6,5},{7,6},{8,7},{9,8},{10,9},{11,1... | collective-permute-start | bytes 589832 | tf_op jit(solution)/shard_map/ppermute | solution.py:22
  123.9 6.4 %collective-permute-start.10 = (f32[2,1,4,24,256]{4,3,2,1,0:T(8,128)S(1)}, f32[2,1,4,24,256]{4,3,2,1,0:T(8,128)S(1)}, u32[]{:S(2)}, u32[]{:S(2)}) collective-permute-start(f32[2,1,4,24,256]{4,3,2,1,0:T(8,128)S(1)} %pad_maximum_fusion.14), channel_id=1, source_target_pairs={{0,1},{1,2},{2,3},{3,4},{4,5},{5,6},{6,7},{7,8},{8,9},{9,10},{10,1... | collective-permute-start | bytes 589832 | tf_op jit(solution)/shard_map/ppermute | solution.py:19
  132.6 17.3 %all-to-all-start.3 = ((f32[32,1,128]{2,1,0:T(1,128)}), f32[32,1,128]{2,1,0:T(1,128)S(1)}, u32[]{:S(2)}, u32[]{:S(2)}) async-start(f32[32,1,128]{2,1,0:T(1,128)} %broadcast_in_dim.10), calls=%async_computation.3 | async-start | bytes 32768 | tf_op jit(solution)/shard_map/all_to_all | solution.py:34
  151.7 4.5 %collective-permute-start.13 = (f32[2,1,4,24,256]{4,3,2,1,0:T(8,128)S(1)}, f32[2,1,4,24,256]{4,3,2,1,0:T(8,128)S(1)}, u32[]{:S(2)}, u32[]{:S(2)}) collective-permute-start(f32[2,1,4,24,256]{4,3,2,1,0:T(8,128)S(1)} %pad_maximum_fusion.15), channel_id=1, source_target_pairs={{1,0},{2,1},{3,2},{4,3},{5,4},{6,5},{7,6},{8,7},{9,8},{10,9},{11,1... | collective-permute-start | bytes 589832 | tf_op jit(solution)/shard_map/ppermute | solution.py:22
  153.0 4.1 %collective-permute-start.12 = (f32[2,1,4,24,256]{4,3,2,1,0:T(8,128)S(1)}, f32[2,1,4,24,256]{4,3,2,1,0:T(8,128)S(1)}, u32[]{:S(2)}, u32[]{:S(2)}) collective-permute-start(f32[2,1,4,24,256]{4,3,2,1,0:T(8,128)S(1)} %pad_maximum_fusion.15), channel_id=1, source_target_pairs={{0,1},{1,2},{2,3},{3,4},{4,5},{5,6},{6,7},{7,8},{8,9},{9,10},{10,1... | collective-permute-start | bytes 589832 | tf_op jit(solution)/shard_map/ppermute | solution.py:19
  158.2 6.9 %collective-permute-start.15 = (f32[2,1,4,24,256]{4,3,2,1,0:T(8,128)S(1)}, f32[2,1,4,24,256]{4,3,2,1,0:T(8,128)S(1)}, u32[]{:S(2)}, u32[]{:S(2)}) collective-permute-start(f32[2,1,4,24,256]{4,3,2,1,0:T(8,128)S(1)} %pad_maximum_fusion.16), channel_id=1, source_target_pairs={{1,0},{2,1},{3,2},{4,3},{5,4},{6,5},{7,6},{8,7},{9,8},{10,9},{11,1... | collective-permute-start | bytes 589832 | tf_op jit(solution)/shard_map/ppermute | solution.py:22
  159.5 6.4 %collective-permute-start.14 = (f32[2,1,4,24,256]{4,3,2,1,0:T(8,128)S(1)}, f32[2,1,4,24,256]{4,3,2,1,0:T(8,128)S(1)}, u32[]{:S(2)}, u32[]{:S(2)}) collective-permute-start(f32[2,1,4,24,256]{4,3,2,1,0:T(8,128)S(1)} %pad_maximum_fusion.16), channel_id=1, source_target_pairs={{0,1},{1,2},{2,3},{3,4},{4,5},{5,6},{6,7},{7,8},{8,9},{9,10},{10,1... | collective-permute-start | bytes 589832 | tf_op jit(solution)/shard_map/ppermute | solution.py:19
  168.6 17.2 %all-to-all-start.5 = ((f32[32,1,128]{2,1,0:T(1,128)}), f32[32,1,128]{2,1,0:T(1,128)S(1)}, u32[]{:S(2)}, u32[]{:S(2)}) async-start(f32[32,1,128]{2,1,0:T(1,128)} %broadcast_in_dim.11), calls=%async_computation.5 | async-start | bytes 32768 | tf_op jit(solution)/shard_map/all_to_all | solution.py:34
  185.8 9.8 %all-to-all-start.4 = ((f32[32,1,256]{2,1,0:T(1,128)}), f32[32,1,256]{2,1,0:T(1,128)S(1)}, u32[]{:S(2)}, u32[]{:S(2)}) async-start(f32[32,1,256]{2,1,0:T(1,128)} %reshape.1875), calls=%async_computation.4 | async-start | bytes 65536 | tf_op jit(solution)/shard_map/all_to_all | solution.py:193
  (48 other events, 527.7 us)

commit v3 on v2

--- a/solution.py
+++ b/solution.py
@@ -120,11 +120,12 @@
     local_col = (node_y - anchor_y) * total_x + node_x
     column_iota = lax.broadcasted_iota(jnp.int32, (1, local_y * total_x), 1)
     node_hot = ((column_iota == local_col[:, None]) & inside[:, None]).astype(jnp.float32)
-    grad_lambda = jnp.zeros(lam.shape, jnp.float32)
-    grad_mu = jnp.zeros(lam.shape, jnp.float32)
-    grad_kappa = jnp.zeros(water_kappa.shape, jnp.float32)
-    misfits = []
-    for step in range(wavelet.shape[0]):
+    steps = wavelet.shape[0]
+    lam_acc = jnp.zeros((1, shots) + lam.shape, jnp.float32)
+    mu_acc = jnp.zeros((1, shots) + lam.shape, jnp.float32)
+    kappa_acc = jnp.zeros((1, shots) + water_kappa.shape, jnp.float32)
+    partial_records = []
+    for step in range(steps):
         floor_pressure = jnp.sum(pressure * bottom, axis=3)
         sxy_pad, syy_pad, syz_pad, p_pad = halo_rows([sig_xy, sig_yy, sig_yz, pressure])
         vel_x = vel_x + TIME_STEP * buoy * (
@@ -158,14 +159,14 @@
         sig_xz = sig_xz + TIME_STEP * mu * shear_xz
         sig_yz = sig_yz + TIME_STEP * mu * shear_yz
         sig_zz = sig_zz.at[:, :, :, 0, :].set(-floor_pressure)
-        grad_lambda = grad_lambda + jnp.sum(dilation[0] * dilation[1], axis=0)
+        lam_acc = lam_acc + dilation[:1] * dilation[1:]
         normal_part = (
-            strain_x[0] * strain_x[1] + strain_y[0] * strain_y[1] + strain_z[0] * strain_z[1]
+            strain_x[:1] * strain_x[1:] + strain_y[:1] * strain_y[1:] + strain_z[:1] * strain_z[1:]
         )
         shear_part = (
-            shear_xy[0] * shear_xy[1] + shear_xz[0] * shear_xz[1] + shear_yz[0] * shear_yz[1]
-        )
-        grad_mu = grad_mu + jnp.sum(2.0 * normal_part + shear_part, axis=0)
+            shear_xy[:1] * shear_xy[1:] + shear_xz[:1] * shear_xz[1:] + shear_yz[:1] * shear_yz[1:]
+        )
+        mu_acc = mu_acc + (2.0 * normal_part + shear_part)
         pressure = (
             pressure
             - TIME_STEP
@@ -173,28 +174,49 @@
             * (derive(flow_x, 4, False) + stencil(uy_pad, 2, False) + derive(flow_z, 3, False))
         ) * live
         pressure = pressure.at[0].add(wavelet[step][:, None, None, None] * source_hot)
-        surface = jnp.sum(pressure * bottom, axis=3)
+        surface = jnp.sum(pressure[0] * bottom, axis=2)
         partial_record = jnp.einsum(
             "sc,rc->sr",
-            surface[0].reshape(shots, local_y * total_x),
+            surface.reshape(shots, local_y * total_x),
             node_hot,
             precision=lax.Precision.HIGHEST,
         )
-        recorded = gather_sum(partial_record, parts)
-        misfit = recorded - observed[step]
-        scaled = misfit * lax.rsqrt(jnp.mean(misfit * misfit, axis=1, keepdims=True) + 1e-06)
+        partial_records.append(partial_record)
+        local_misfit = partial_record - observed[step]
         inject = jnp.dot(
-            scaled, node_hot, precision=lax.Precision.HIGHEST, preferred_element_type=jnp.float32
+            local_misfit, node_hot, precision=lax.Precision.HIGHEST, preferred_element_type=jnp.float32
         ).reshape(shots, local_y, total_x)
-        pressure = pressure.at[1].add(inject[:, :, None, :] * bottom)
-        grad_kappa = grad_kappa + jnp.sum(pressure[0] * pressure[1], axis=0)
-        misfits.append(misfit)
+        kick = inject[:, :, None, :] * bottom
+        kappa_acc = jnp.concatenate(
+            [kappa_acc + pressure[:1] * pressure[1:], (pressure[0] * kick)[None]], axis=0
+        )
+        if step + 1 < steps:
+            rock_zero = jnp.zeros((1,) + vel_x.shape[1:], jnp.float32)
+            water_zero = jnp.zeros((1,) + flow_x.shape[1:], jnp.float32)
+            vel_x, vel_y, vel_z = [jnp.concatenate([f, rock_zero]) for f in (vel_x, vel_y, vel_z)]
+            sig_xx, sig_yy, sig_zz, sig_xy, sig_xz, sig_yz = [
+                jnp.concatenate([f, rock_zero])
+                for f in (sig_xx, sig_yy, sig_zz, sig_xy, sig_xz, sig_yz)
+            ]
+            flow_x, flow_y, flow_z = [jnp.concatenate([f, water_zero]) for f in (flow_x, flow_y, flow_z)]
+            pressure = jnp.concatenate([pressure, kick[None]])
+            lam_acc = jnp.concatenate([lam_acc, jnp.zeros((1,) + lam_acc.shape[1:], jnp.float32)])
+            mu_acc = jnp.concatenate([mu_acc, jnp.zeros((1,) + mu_acc.shape[1:], jnp.float32)])
+
+    recorded = gather_sum(jnp.stack(partial_records), parts)
+    misfits = recorded - observed
+    scales = lax.rsqrt(jnp.mean(misfits * misfits, axis=2) + 1e-06)
+    weights = jnp.concatenate([jnp.ones((1, shots), jnp.float32), scales])
+    grad_kappa = jnp.sum(kappa_acc * weights[:, :, None, None, None], axis=(0, 1))
+    rock_weights = weights[: lam_acc.shape[0], :, None, None, None]
+    grad_lambda = jnp.sum(lam_acc * rock_weights, axis=(0, 1))
+    grad_mu = jnp.sum(mu_acc * rock_weights, axis=(0, 1))
 
     grads = lax.all_to_all(
         jnp.stack([grad_lambda, grad_mu]), "gx", split_axis=3, concat_axis=1, tiled=True
     )
     grads = jnp.transpose(grads, (0, 3, 2, 1))
-    return (grads[0], grads[1], grad_kappa, jnp.stack(misfits))
+    return (grads[0], grads[1], grad_kappa, misfits)
 
 
 def solution(mesh):

time: 203 us -> 206 us (1.015)
  waiting for transfers between devices: 33.6 us -> 25.5 us
  other arithmetic: 30.9 us -> 38.2 us
  local copies, waits for them, and re-layouts: 34.8 us -> 41 us
  between operations: 5.73 us -> 3.13 us
    all_to_all x4 -> x1, starting transfers between devices: 40.7 us -> 11.2 us  [gather_sum(): return jnp.sum(lax.all_to_all(copies, 'gx', 0, 0, tiled=True), axis=0)]
    ppermute x8, starting transfers between devices: 32.1 us -> 60 us  [halo_rows(): lax.ppermute(lax.slice_in_dim(packed, length - HALO, length, axis=ROW_AXI...]
    all_to_all x4 -> x1, waiting for transfers between devices: 18.8 us -> 6.34 us  [gather_sum(): return jnp.sum(lax.all_to_all(copies, 'gx', 0, 0, tiled=True), axis=0)]
    mul x3 -> x7, other arithmetic: 1.04 us -> 5.04 us  [the longest x4 4.28 us: on_device(): pressure[:1] * pressure[1:]]
    mul x0 -> x22, local copies, waits for them, and re-layouts: none -> 3.73 us  [the longest x3 0.67 us: on_device(): strain_z[:1] * strain_z[1:]]
    add x4 -> x11, other arithmetic: 1.07 us -> 4.73 us  [the longest x3 1.68 us: on_device(): kappa_acc + pressure[:1] * pressure[1:]]
    ppermute x8, waiting for transfers between devices: 0.02 us -> 3.42 us  [halo_rows(): lax.ppermute(lax.slice_in_dim(packed, 0, HALO, axis=ROW_AXIS), 'gx', down)]
    all_to_all x1, waiting for transfers between devices: 3.46 us -> 6.5 us  [on_device(): lax.all_to_all(jnp.stack([grad_lambda, grad_mu]), 'gx', split_axis=3, con...]
  transfers between devices with their start and end apart: 22 -> 19, of which waited for: 13 -> 7; matrix products, arithmetic and copies ran while one was open for 12% -> 12% of each run, Pallas kernels for 0% -> 0%
where the time goes in v3:
time: 206 us; the launch traced here: 205 us
  starting transfers between devices  91.3 us (44%)
  local copies, waits for them, and re-layouts  41 us (20%)
  other arithmetic  38.2 us (19%)
  waiting for transfers between devices  25.5 us (12%)
  matrix products  5.47 us (3%)
  between operations  3.13 us (2%)
    ppermute x8, starting transfers between devices, halo_rows(): lax.ppermute(lax.slice_in_dim(packed, length - HALO, length, axis=ROW_AXI...  60 us
    unnamed x128, local copies, waits for them, and re-layouts  15.7 us
    all_to_all x1, starting transfers between devices, gather_sum(): return jnp.sum(lax.all_to_all(copies, 'gx', 0, 0, tiled=True), axis=0)  11.2 us
    ppermute x8, starting transfers between devices, halo_rows(): lax.ppermute(lax.slice_in_dim(packed, 0, HALO, axis=ROW_AXIS), 'gx', down)  10.3 us
    all_to_all x1, starting transfers between devices, on_device(): lax.all_to_all(jnp.transpose(rock_in, (0, 3, 2, 1)), 'gx', split_axis=1,...  7.3 us
    all_to_all x1, waiting for transfers between devices, on_device(): lax.all_to_all(jnp.transpose(rock_in, (0, 3, 2, 1)), 'gx', split_axis=1,...  6.79 us
    all_to_all x1, waiting for transfers between devices, on_device(): lax.all_to_all(jnp.stack([grad_lambda, grad_mu]), 'gx', split_axis=3, con...  6.5 us
    all_to_all x1, waiting for transfers between devices, gather_sum(): return jnp.sum(lax.all_to_all(copies, 'gx', 0, 0, tiled=True), axis=0)  6.34 us
  transfers between devices with their start and end apart: 19, of which 7 were waited for; matrix products, arithmetic and copies ran while one was open for 12% of the time, Pallas kernels for 0%

profile of v3, /device:TPU:0, one launch (start us, length us, event | category | flops | bytes accessed | tf_op | source)
XLA Modules:
  0.0 204.6 jit_solution(4123726527828656755)
XLA Ops:
  3.1 1.9 copy.1089
  5.0 1.5 bitcast_bitcast_fusion
  6.5 4.0 %reshape.954 = f32[32,1,2688]{2,1,0:T(1,128)} reshape(f32[128,4,8,21]{3,2,1,0:T(8,128)} %bitcast_bitcast_fusion) | data formatting | bytes 688128
  10.6 7.3 %all-to-all-start = ((f32[32,1,2688]{2,1,0:T(1,128)}), f32[32,1,2688]{2,1,0:T(1,128)S(1)}, u32[]{:S(2)}, u32[]{:S(2)}) async-start(f32[32,1,2688]{2,1,0:T(1,128)} %reshape.954), calls=%async_computation | async-start | bytes 688128 | tf_op jit(solution)/shard_map/all_to_all | solution.py:91
  23.4 6.8 %all-to-all-done = f32[32,1,2688]{2,1,0:T(1,128)S(1)} async-done(((f32[32,1,2688]{2,1,0:T(1,128)}), f32[32,1,2688]{2,1,0:T(1,128)S(1)}, u32[]{:S(2)}, u32[]{:S(2)}) %all-to-all-start) | async-done | bytes 344096 | tf_op jit(solution)/shard_map/all_to_all | solution.py:91
  30.8 1.5 reduce.23
  32.2 2.3 %reshape.955 = f32[128,4,8,21]{3,2,1,0:T(8,128)S(1)} reshape(f32[32,2688]{1,0:T(8,128)S(1)} %reduce.23) | data formatting | bytes 688128
  34.5 1.9 copy.1090
  40.1 3.7 %collective-permute-start = (f32[2,1,4,24,256]{4,3,2,1,0:T(8,128)}, f32[2,1,4,24,256]{4,3,2,1,0:T(8,128)}, u32[]{:S(2)}, u32[]{:S(2)}) collective-permute-start(f32[2,1,4,24,256]{4,3,2,1,0:T(8,128)} %pad_maximum_fusion.18), channel_id=1, source_target_pairs={{0,1},{1,2},{2,3},{3,4},{4,5},{5,6},{6,7},{7,8},{8,9},{9,10},{10,1... | collective-permute-start | bytes 589832 | tf_op jit(solution)/shard_map/ppermute | solution.py:19
  53.2 3.0 %collective-permute-start.2 = (f32[2,1,4,24,256]{4,3,2,1,0:T(8,128)S(1)}, f32[2,1,4,24,256]{4,3,2,1,0:T(8,128)S(1)}, u32[]{:S(2)}, u32[]{:S(2)}) collective-permute-start(f32[2,1,4,24,256]{4,3,2,1,0:T(8,128)S(1)} %pad_maximum_fusion.19), channel_id=1, source_target_pairs={{0,1},{1,2},{2,3},{3,4},{4,5},{5,6},{6,7},{7,8},{8,9},{9,10},{10,1... | collective-permute-start | bytes 589832 | tf_op jit(solution)/shard_map/ppermute | solution.py:19
  63.6 8.1 %collective-permute-start.4 = (f32[3,1,4,24,256]{4,3,2,1,0:T(8,128)S(1)}, f32[3,1,4,24,256]{4,3,2,1,0:T(8,128)S(1)}, u32[]{:S(2)}, u32[]{:S(2)}) collective-permute-start(f32[3,1,4,24,256]{4,3,2,1,0:T(8,128)S(1)} %maximum_maximum_fusion.9), channel_id=1, source_target_pairs={{0,1},{1,2},{2,3},{3,4},{4,5},{5,6},{6,7},{7,8},{8,9},{9,10},{10,1... | collective-permute-start | bytes 884744 | tf_op jit(solution)/shard_map/ppermute | solution.py:19
  75.3 10.7 %collective-permute-start.6 = (f32[3,1,4,24,256]{4,3,2,1,0:T(8,128)S(1)}, f32[3,1,4,24,256]{4,3,2,1,0:T(8,128)S(1)}, u32[]{:S(2)}, u32[]{:S(2)}) collective-permute-start(f32[3,1,4,24,256]{4,3,2,1,0:T(8,128)S(1)} %pad_maximum_fusion.13), channel_id=1, source_target_pairs={{0,1},{1,2},{2,3},{3,4},{4,5},{5,6},{6,7},{7,8},{8,9},{9,10},{10,1... | collective-permute-start | bytes 884744 | tf_op jit(solution)/shard_map/ppermute | solution.py:19
  94.6 9.3 %collective-permute-start.8 = (f32[4,1,4,24,256]{4,3,2,1,0:T(8,128)}, f32[4,1,4,24,256]{4,3,2,1,0:T(8,128)S(1)}, u32[]{:S(2)}, u32[]{:S(2)}) collective-permute-start(f32[4,1,4,24,256]{4,3,2,1,0:T(8,128)} %maximum_maximum_fusion.8), channel_id=1, source_target_pairs={{0,1},{1,2},{2,3},{3,4},{4,5},{5,6},{6,7},{7,8},{8,9},{9,10},{10,1... | collective-permute-start | bytes 1179656 | tf_op jit(solution)/shard_map/ppermute | solution.py:19
  109.9 9.7 %collective-permute-start.10 = (f32[4,1,4,24,256]{4,3,2,1,0:T(8,128)S(1)}, f32[4,1,4,24,256]{4,3,2,1,0:T(8,128)S(1)}, u32[]{:S(2)}, u32[]{:S(2)}) collective-permute-start(f32[4,1,4,24,256]{4,3,2,1,0:T(8,128)S(1)} %pad_maximum_fusion.10), channel_id=1, source_target_pairs={{0,1},{1,2},{2,3},{3,4},{4,5},{5,6},{6,7},{7,8},{8,9},{9,10},{10,1... | collective-permute-start | bytes 1179656 | tf_op jit(solution)/shard_map/ppermute | solution.py:19
  131.6 10.1 %collective-permute-start.12 = (f32[5,1,4,24,256]{4,3,2,1,0:T(8,128)}, f32[5,1,4,24,256]{4,3,2,1,0:T(8,128)S(1)}, u32[]{:S(2)}, u32[]{:S(2)}) collective-permute-start(f32[5,1,4,24,256]{4,3,2,1,0:T(8,128)} %maximum_maximum_fusion.5), channel_id=1, source_target_pairs={{0,1},{1,2},{2,3},{3,4},{4,5},{5,6},{6,7},{7,8},{8,9},{9,10},{10,1... | collective-permute-start | bytes 1474568 | tf_op jit(solution)/shard_map/ppermute | solution.py:19
  144.7 1.5 scatter.14
  151.7 5.4 %collective-permute-start.14 = (f32[5,1,4,24,256]{4,3,2,1,0:T(8,128)S(1)}, f32[5,1,4,24,256]{4,3,2,1,0:T(8,128)S(1)}, u32[]{:S(2)}, u32[]{:S(2)}) collective-permute-start(f32[5,1,4,24,256]{4,3,2,1,0:T(8,128)S(1)} %pad_maximum_fusion.7), channel_id=1, source_target_pairs={{0,1},{1,2},{2,3},{3,4},{4,5},{5,6},{6,7},{7,8},{8,9},{9,10},{10,1... | collective-permute-start | bytes 1474568 | tf_op jit(solution)/shard_map/ppermute | solution.py:19
  159.2 3.4 %collective-permute-done.15 = f32[5,1,4,24,256]{4,3,2,0,1:T(8,128)S(1)} collective-permute-done((f32[5,1,4,24,256]{4,3,2,0,1:T(8,128)S(1)}, f32[5,1,4,24,256]{4,3,2,0,1:T(8,128)S(1)}, u32[]{:S(2)}, u32[]{:S(2)}) %collective-permute-start.15) | collective-permute-done | bytes 491552 | tf_op jit(solution)/shard_map/ppermute | solution.py:22
  167.3 11.2 %all-to-all-start.1 = ((f32[32,4,1,128]{3,2,1,0:T(1,128)}), f32[32,4,1,128]{3,2,1,0:T(1,128)S(1)}, u32[]{:S(2)}, u32[]{:S(2)}) async-start(f32[32,4,1,128]{3,2,1,0:T(1,128)} %broadcast_in_dim.5), calls=%async_computation.1 | async-start | bytes 131072 | tf_op jit(solution)/shard_map/all_to_all | solution.py:34
  179.3 6.3 %all-to-all-done.1 = f32[32,4,1,128]{3,2,1,0:T(1,128)S(1)} async-done(((f32[32,4,1,128]{3,2,1,0:T(1,128)}), f32[32,4,1,128]{3,2,1,0:T(1,128)S(1)}, u32[]{:S(2)}, u32[]{:S(2)}) %all-to-all-start.1) | async-done | bytes 65568 | tf_op jit(solution)/shard_map/all_to_all | solution.py:34
  187.2 1.7 reshape.956
  188.9 2.5 %all-to-all-start.2 = ((f32[32,1,256]{2,1,0:T(1,128)}), f32[32,1,256]{2,1,0:T(1,128)S(1)}, u32[]{:S(2)}, u32[]{:S(2)}) async-start(f32[32,1,256]{2,1,0:T(1,128)} %reshape.956), calls=%async_computation.2 | async-start | bytes 65536 | tf_op jit(solution)/shard_map/all_to_all | solution.py:215
  192.2 6.5 %all-to-all-done.2 = f32[32,1,256]{2,1,0:T(1,128)S(1)} async-done(((f32[32,1,256]{2,1,0:T(1,128)}), f32[32,1,256]{2,1,0:T(1,128)S(1)}, u32[]{:S(2)}, u32[]{:S(2)}) %all-to-all-start.2) | async-done | bytes 32800 | tf_op jit(solution)/shard_map/all_to_all | solution.py:215
  200.8 1.9 copy.1265
  (343 shorter events, 79.1 us)
Async XLA Ops:
  10.6 19.6 %all-to-all-start = ((f32[32,1,2688]{2,1,0:T(1,128)}), f32[32,1,2688]{2,1,0:T(1,128)S(1)}, u32[]{:S(2)}, u32[]{:S(2)}) async-start(f32[32,1,2688]{2,1,0:T(1,128)} %reshape.954), calls=%async_computation | async-start | bytes 688128 | tf_op jit(solution)/shard_map/all_to_all | solution.py:91
  38.8 9.1 %collective-permute-start.1 = (f32[2,1,4,24,256]{4,3,2,1,0:T(8,128)}, f32[2,1,4,24,256]{4,3,2,1,0:T(8,128)S(1)}, u32[]{:S(2)}, u32[]{:S(2)}) collective-permute-start(f32[2,1,4,24,256]{4,3,2,1,0:T(8,128)} %pad_maximum_fusion.18), channel_id=1, source_target_pairs={{1,0},{2,1},{3,2},{4,3},{5,4},{6,5},{7,6},{8,7},{9,8},{10,9},{11,1... | collective-permute-start | bytes 589832 | tf_op jit(solution)/shard_map/ppermute | solution.py:22
  40.1 7.8 %collective-permute-start = (f32[2,1,4,24,256]{4,3,2,1,0:T(8,128)}, f32[2,1,4,24,256]{4,3,2,1,0:T(8,128)}, u32[]{:S(2)}, u32[]{:S(2)}) collective-permute-start(f32[2,1,4,24,256]{4,3,2,1,0:T(8,128)} %pad_maximum_fusion.18), channel_id=1, source_target_pairs={{0,1},{1,2},{2,3},{3,4},{4,5},{5,6},{6,7},{7,8},{8,9},{9,10},{10,1... | collective-permute-start | bytes 589832 | tf_op jit(solution)/shard_map/ppermute | solution.py:19
  51.9 5.3 %collective-permute-start.3 = (f32[2,1,4,24,256]{4,3,2,1,0:T(8,128)S(1)}, f32[2,1,4,24,256]{4,3,2,1,0:T(8,128)S(1)}, u32[]{:S(2)}, u32[]{:S(2)}) collective-permute-start(f32[2,1,4,24,256]{4,3,2,1,0:T(8,128)S(1)} %pad_maximum_fusion.19), channel_id=1, source_target_pairs={{1,0},{2,1},{3,2},{4,3},{5,4},{6,5},{7,6},{8,7},{9,8},{10,9},{11,1... | collective-permute-start | bytes 589832 | tf_op jit(solution)/shard_map/ppermute | solution.py:22
  53.2 4.1 %collective-permute-start.2 = (f32[2,1,4,24,256]{4,3,2,1,0:T(8,128)S(1)}, f32[2,1,4,24,256]{4,3,2,1,0:T(8,128)S(1)}, u32[]{:S(2)}, u32[]{:S(2)}) collective-permute-start(f32[2,1,4,24,256]{4,3,2,1,0:T(8,128)S(1)} %pad_maximum_fusion.19), channel_id=1, source_target_pairs={{0,1},{1,2},{2,3},{3,4},{4,5},{5,6},{6,7},{7,8},{8,9},{9,10},{10,1... | collective-permute-start | bytes 589832 | tf_op jit(solution)/shard_map/ppermute | solution.py:19
  62.3 9.6 %collective-permute-start.5 = (f32[3,1,4,24,256]{4,3,2,1,0:T(8,128)S(1)}, f32[3,1,4,24,256]{4,3,2,1,0:T(8,128)S(1)}, u32[]{:S(2)}, u32[]{:S(2)}) collective-permute-start(f32[3,1,4,24,256]{4,3,2,1,0:T(8,128)S(1)} %maximum_maximum_fusion.9), channel_id=1, source_target_pairs={{1,0},{2,1},{3,2},{4,3},{5,4},{6,5},{7,6},{8,7},{9,8},{10,9},{11,1... | collective-permute-start | bytes 884744 | tf_op jit(solution)/shard_map/ppermute | solution.py:22
  63.6 9.3 %collective-permute-start.4 = (f32[3,1,4,24,256]{4,3,2,1,0:T(8,128)S(1)}, f32[3,1,4,24,256]{4,3,2,1,0:T(8,128)S(1)}, u32[]{:S(2)}, u32[]{:S(2)}) collective-permute-start(f32[3,1,4,24,256]{4,3,2,1,0:T(8,128)S(1)} %maximum_maximum_fusion.9), channel_id=1, source_target_pairs={{0,1},{1,2},{2,3},{3,4},{4,5},{5,6},{6,7},{7,8},{8,9},{9,10},{10,1... | collective-permute-start | bytes 884744 | tf_op jit(solution)/shard_map/ppermute | solution.py:19
  74.0 12.4 %collective-permute-start.7 = (f32[3,1,4,24,256]{4,3,2,1,0:T(8,128)S(1)}, f32[3,1,4,24,256]{4,3,2,1,0:T(8,128)S(1)}, u32[]{:S(2)}, u32[]{:S(2)}) collective-permute-start(f32[3,1,4,24,256]{4,3,2,1,0:T(8,128)S(1)} %pad_maximum_fusion.13), channel_id=1, source_target_pairs={{1,0},{2,1},{3,2},{4,3},{5,4},{6,5},{7,6},{8,7},{9,8},{10,9},{11,1... | collective-permute-start | bytes 884744 | tf_op jit(solution)/shard_map/ppermute | solution.py:22
  75.3 11.8 %collective-permute-start.6 = (f32[3,1,4,24,256]{4,3,2,1,0:T(8,128)S(1)}, f32[3,1,4,24,256]{4,3,2,1,0:T(8,128)S(1)}, u32[]{:S(2)}, u32[]{:S(2)}) collective-permute-start(f32[3,1,4,24,256]{4,3,2,1,0:T(8,128)S(1)} %pad_maximum_fusion.13), channel_id=1, source_target_pairs={{0,1},{1,2},{2,3},{3,4},{4,5},{5,6},{6,7},{7,8},{8,9},{9,10},{10,1... | collective-permute-start | bytes 884744 | tf_op jit(solution)/shard_map/ppermute | solution.py:19
  93.3 13.8 %collective-permute-start.9 = (f32[4,1,4,24,256]{4,3,2,1,0:T(8,128)}, f32[4,1,4,24,256]{4,3,2,1,0:T(8,128)S(1)}, u32[]{:S(2)}, u32[]{:S(2)}) collective-permute-start(f32[4,1,4,24,256]{4,3,2,1,0:T(8,128)} %maximum_maximum_fusion.8), channel_id=1, source_target_pairs={{1,0},{2,1},{3,2},{4,3},{5,4},{6,5},{7,6},{8,7},{9,8},{10,9},{11,1... | collective-permute-start | bytes 1179656 | tf_op jit(solution)/shard_map/ppermute | solution.py:22
  94.6 12.5 %collective-permute-start.8 = (f32[4,1,4,24,256]{4,3,2,1,0:T(8,128)}, f32[4,1,4,24,256]{4,3,2,1,0:T(8,128)S(1)}, u32[]{:S(2)}, u32[]{:S(2)}) collective-permute-start(f32[4,1,4,24,256]{4,3,2,1,0:T(8,128)} %maximum_maximum_fusion.8), channel_id=1, source_target_pairs={{0,1},{1,2},{2,3},{3,4},{4,5},{5,6},{6,7},{7,8},{8,9},{9,10},{10,1... | collective-permute-start | bytes 1179656 | tf_op jit(solution)/shard_map/ppermute | solution.py:19
  108.6 11.6 %collective-permute-start.11 = (f32[4,1,4,24,256]{4,3,2,1,0:T(8,128)S(1)}, f32[4,1,4,24,256]{4,3,2,1,0:T(8,128)S(1)}, u32[]{:S(2)}, u32[]{:S(2)}) collective-permute-start(f32[4,1,4,24,256]{4,3,2,1,0:T(8,128)S(1)} %pad_maximum_fusion.10), channel_id=1, source_target_pairs={{1,0},{2,1},{3,2},{4,3},{5,4},{6,5},{7,6},{8,7},{9,8},{10,9},{11,1... | collective-permute-start | bytes 1179656 | tf_op jit(solution)/shard_map/ppermute | solution.py:22
  109.9 11.0 %collective-permute-start.10 = (f32[4,1,4,24,256]{4,3,2,1,0:T(8,128)S(1)}, f32[4,1,4,24,256]{4,3,2,1,0:T(8,128)S(1)}, u32[]{:S(2)}, u32[]{:S(2)}) collective-permute-start(f32[4,1,4,24,256]{4,3,2,1,0:T(8,128)S(1)} %pad_maximum_fusion.10), channel_id=1, source_target_pairs={{0,1},{1,2},{2,3},{3,4},{4,5},{5,6},{6,7},{7,8},{8,9},{9,10},{10,1... | collective-permute-start | bytes 1179656 | tf_op jit(solution)/shard_map/ppermute | solution.py:19
  122.3 20.0 %copy-start.13 = (f32[4,1,4,4,256]{4,3,2,1,0:T(4,128)}, f32[4,1,4,4,256]{4,3,2,1,0:T(4,128)S(1)}, u32[]{:S(2)}) copy-start(f32[4,1,4,4,256]{4,3,2,1,0:T(4,128)S(1)} %get-tuple-element.229) | copy-start | bytes 196612
  127.3 20.7 %copy-start.25 = (f32[2,1,4,4,256]{4,3,2,1,0:T(4,128)S(1)}, f32[2,1,4,4,256]{4,3,2,1,0:T(4,128)}, u32[]{:S(2)}) copy-start(f32[2,1,4,4,256]{4,3,2,1,0:T(4,128)} %fusion.1027) | copy-start | bytes 98308
  127.5 21.1 %copy-start.15 = (f32[4,1,4,4,256]{4,3,2,1,0:T(4,128)}, f32[4,1,4,4,256]{4,3,2,1,0:T(4,128)S(1)}, u32[]{:S(2)}) copy-start(f32[4,1,4,4,256]{4,3,2,1,0:T(4,128)S(1)} %get-tuple-element.134) | copy-start | bytes 196612
  127.9 20.8 %copy-start.17 = (f32[4,1,4,4,256]{4,3,2,1,0:T(4,128)}, f32[4,1,4,4,256]{4,3,2,1,0:T(4,128)S(1)}, u32[]{:S(2)}) copy-start(f32[4,1,4,4,256]{4,3,2,1,0:T(4,128)S(1)} %get-tuple-element.132) | copy-start | bytes 196612
  130.3 19.3 %collective-permute-start.13 = (f32[5,1,4,24,256]{4,3,2,1,0:T(8,128)}, f32[5,1,4,24,256]{4,3,2,1,0:T(8,128)S(1)}, u32[]{:S(2)}, u32[]{:S(2)}) collective-permute-start(f32[5,1,4,24,256]{4,3,2,1,0:T(8,128)} %maximum_maximum_fusion.5), channel_id=1, source_target_pairs={{1,0},{2,1},{3,2},{4,3},{5,4},{6,5},{7,6},{8,7},{9,8},{10,9},{11,1... | collective-permute-start | bytes 1474568 | tf_op jit(solution)/shard_map/ppermute | solution.py:22
  131.6 18.1 %collective-permute-start.12 = (f32[5,1,4,24,256]{4,3,2,1,0:T(8,128)}, f32[5,1,4,24,256]{4,3,2,1,0:T(8,128)S(1)}, u32[]{:S(2)}, u32[]{:S(2)}) collective-permute-start(f32[5,1,4,24,256]{4,3,2,1,0:T(8,128)} %maximum_maximum_fusion.5), channel_id=1, source_target_pairs={{0,1},{1,2},{2,3},{3,4},{4,5},{5,6},{6,7},{7,8},{8,9},{9,10},{10,1... | collective-permute-start | bytes 1474568 | tf_op jit(solution)/shard_map/ppermute | solution.py:19
  151.7 7.6 %collective-permute-start.14 = (f32[5,1,4,24,256]{4,3,2,1,0:T(8,128)S(1)}, f32[5,1,4,24,256]{4,3,2,1,0:T(8,128)S(1)}, u32[]{:S(2)}, u32[]{:S(2)}) collective-permute-start(f32[5,1,4,24,256]{4,3,2,1,0:T(8,128)S(1)} %pad_maximum_fusion.7), channel_id=1, source_target_pairs={{0,1},{1,2},{2,3},{3,4},{4,5},{5,6},{6,7},{7,8},{8,9},{9,10},{10,1... | collective-permute-start | bytes 1474568 | tf_op jit(solution)/shard_map/ppermute | solution.py:19
  157.0 5.6 %collective-permute-start.15 = (f32[5,1,4,24,256]{4,3,2,0,1:T(8,128)S(1)}, f32[5,1,4,24,256]{4,3,2,0,1:T(8,128)S(1)}, u32[]{:S(2)}, u32[]{:S(2)}) collective-permute-start(f32[5,1,4,24,256]{4,3,2,0,1:T(8,128)S(1)} %fusion.1131), channel_id=1, source_target_pairs={{1,0},{2,1},{3,2},{4,3},{5,4},{6,5},{7,6},{8,7},{9,8},{10,9},{11,1... | collective-permute-start | bytes 1474568 | tf_op jit(solution)/shard_map/ppermute | solution.py:22
  164.4 22.1 %copy-start.23 = (f32[3,1,4,4,256]{4,3,2,1,0:T(4,128)S(1)}, f32[3,1,4,4,256]{4,3,2,1,0:T(4,128)}, u32[]{:S(2)}) copy-start(f32[3,1,4,4,256]{4,3,2,1,0:T(4,128)} %fusion.833) | copy-start | bytes 147460
  167.3 18.4 %all-to-all-start.1 = ((f32[32,4,1,128]{3,2,1,0:T(1,128)}), f32[32,4,1,128]{3,2,1,0:T(1,128)S(1)}, u32[]{:S(2)}, u32[]{:S(2)}) async-start(f32[32,4,1,128]{3,2,1,0:T(1,128)} %broadcast_in_dim.5), calls=%async_computation.1 | async-start | bytes 131072 | tf_op jit(solution)/shard_map/all_to_all | solution.py:34
  188.9 9.8 %all-to-all-start.2 = ((f32[32,1,256]{2,1,0:T(1,128)}), f32[32,1,256]{2,1,0:T(1,128)S(1)}, u32[]{:S(2)}, u32[]{:S(2)}) async-start(f32[32,1,256]{2,1,0:T(1,128)} %reshape.956), calls=%async_computation.2 | async-start | bytes 65536 | tf_op jit(solution)/shard_map/all_to_all | solution.py:215
  (49 other events, 336.8 us)

commit v4 on v3

--- a/solution.py
+++ b/solution.py
@@ -8,6 +8,7 @@
 HALO = 4
 ROW_AXIS = 2
 DEPTH_AXIS = 3
+DEFERRED = 2
 
 
 def halo_rows(fields):
@@ -121,10 +122,12 @@
     column_iota = lax.broadcasted_iota(jnp.int32, (1, local_y * total_x), 1)
     node_hot = ((column_iota == local_col[:, None]) & inside[:, None]).astype(jnp.float32)
     steps = wavelet.shape[0]
+    first_late = steps - min(DEFERRED, steps)
     lam_acc = jnp.zeros((1, shots) + lam.shape, jnp.float32)
     mu_acc = jnp.zeros((1, shots) + lam.shape, jnp.float32)
     kappa_acc = jnp.zeros((1, shots) + water_kappa.shape, jnp.float32)
-    partial_records = []
+    early_misfits = []
+    late_records = []
     for step in range(steps):
         floor_pressure = jnp.sum(pressure * bottom, axis=3)
         sxy_pad, syy_pad, syz_pad, p_pad = halo_rows([sig_xy, sig_yy, sig_yz, pressure])
@@ -181,7 +184,17 @@
             node_hot,
             precision=lax.Precision.HIGHEST,
         )
-        partial_records.append(partial_record)
+        if step < first_late:
+            misfit = gather_sum(partial_record, parts) - observed[step]
+            scaled = misfit * lax.rsqrt(jnp.mean(misfit * misfit, axis=1, keepdims=True) + 1e-06)
+            inject = jnp.dot(
+                scaled, node_hot, precision=lax.Precision.HIGHEST, preferred_element_type=jnp.float32
+            ).reshape(shots, local_y, total_x)
+            pressure = pressure.at[1].add(inject[:, :, None, :] * bottom)
+            kappa_acc = kappa_acc + pressure[:1] * pressure[1:]
+            early_misfits.append(misfit)
+            continue
+        late_records.append(partial_record)
         local_misfit = partial_record - observed[step]
         inject = jnp.dot(
             local_misfit, node_hot, precision=lax.Precision.HIGHEST, preferred_element_type=jnp.float32
@@ -203,20 +216,31 @@
             lam_acc = jnp.concatenate([lam_acc, jnp.zeros((1,) + lam_acc.shape[1:], jnp.float32)])
             mu_acc = jnp.concatenate([mu_acc, jnp.zeros((1,) + mu_acc.shape[1:], jnp.float32)])
 
-    recorded = gather_sum(jnp.stack(partial_records), parts)
-    misfits = recorded - observed
-    scales = lax.rsqrt(jnp.mean(misfits * misfits, axis=2) + 1e-06)
+    slots = lam_acc.shape[0]
+    rock_acc = jnp.concatenate([lam_acc, mu_acc]).reshape(
+        2 * slots * shots, local_y, rock_z, parts, width_x
+    )
+    rock_out = jnp.transpose(rock_acc, (3, 0, 1, 2, 4)).reshape(parts, -1)
+    records = jnp.stack(late_records).reshape(1, -1)
+    packed = jnp.concatenate([jnp.broadcast_to(records, (parts, records.shape[1])), rock_out], axis=1)
+    got = lax.all_to_all(packed, "gx", 0, 0, tiled=True)
+    late_count = len(late_records)
+    recorded = jnp.sum(got[:, : records.shape[1]], axis=0).reshape(late_count, shots, -1)
+    rock_back = got[:, records.shape[1] :].reshape(
+        parts, 2 * slots * shots, local_y, rock_z, width_x
+    )
+    rock_back = jnp.transpose(rock_back, (1, 4, 3, 0, 2)).reshape(
+        2, slots, shots, width_x, rock_z, parts * local_y
+    )
+    late_misfits = recorded - observed[first_late:]
+    scales = lax.rsqrt(jnp.mean(late_misfits * late_misfits, axis=2) + 1e-06)
     weights = jnp.concatenate([jnp.ones((1, shots), jnp.float32), scales])
     grad_kappa = jnp.sum(kappa_acc * weights[:, :, None, None, None], axis=(0, 1))
-    rock_weights = weights[: lam_acc.shape[0], :, None, None, None]
-    grad_lambda = jnp.sum(lam_acc * rock_weights, axis=(0, 1))
-    grad_mu = jnp.sum(mu_acc * rock_weights, axis=(0, 1))
-
-    grads = lax.all_to_all(
-        jnp.stack([grad_lambda, grad_mu]), "gx", split_axis=3, concat_axis=1, tiled=True
-    )
-    grads = jnp.transpose(grads, (0, 3, 2, 1))
-    return (grads[0], grads[1], grad_kappa, misfits)
+    rock_weights = weights[:slots, :, None, None, None]
+    grad_lambda = jnp.sum(rock_back[0] * rock_weights, axis=(0, 1))
+    grad_mu = jnp.sum(rock_back[1] * rock_weights, axis=(0, 1))
+    misfits = jnp.concatenate([jnp.stack(early_misfits), late_misfits]) if early_misfits else late_misfits
+    return (grad_lambda, grad_mu, grad_kappa, misfits)
 
 
 def solution(mesh):

time: 206 us -> 194 us (0.942)
  local copies, waits for them, and re-layouts: 41 us -> 30.5 us
  waiting for transfers between devices: 25.5 us -> 34.7 us
  other arithmetic: 38.2 us -> 30.3 us
    ppermute x8, starting transfers between devices: 60 us -> 34.9 us  [halo_rows(): lax.ppermute(lax.slice_in_dim(packed, length - HALO, length, axis=ROW_AXI...]
    all_to_all x1, starting transfers between devices: 2.52 us -> 16.4 us  [on_device(): got = lax.all_to_all(packed, 'gx', 0, 0, tiled=True)]
    all_to_all x1 -> x2, starting transfers between devices: 11.2 us -> 20.2 us  [gather_sum(): return jnp.sum(lax.all_to_all(copies, 'gx', 0, 0, tiled=True), axis=0)]
    ppermute x8, waiting for transfers between devices: 3.42 us -> 9.8 us  [halo_rows(): lax.ppermute(lax.slice_in_dim(packed, 0, HALO, axis=ROW_AXIS), 'gx', down)]
    mul x4 -> x1, other arithmetic: 4.28 us -> 0.69 us  [on_device(): pressure[:1] * pressure[1:]]
    unnamed x128 -> x124, local copies, waits for them, and re-layouts: 15.7 us -> 12.6 us
    dot_general x4 -> x2, matrix products: 3.82 us -> 0.89 us  [on_device(): jnp.dot(local_misfit, node_hot, precision=lax.Precision.HIGHEST, preferre...]
    all_to_all x1 -> x2, waiting for transfers between devices: 6.34 us -> 8.29 us  [gather_sum(): return jnp.sum(lax.all_to_all(copies, 'gx', 0, 0, tiled=True), axis=0)]
  transfers between devices with their start and end apart: 19 -> 20, of which waited for: 7 -> 11; matrix products, arithmetic and copies ran while one was open for 12% -> 9% of each run, Pallas kernels for 0% -> 0%
where the time goes in v4:
time: 194 us; the launch traced here: 193 us
  starting transfers between devices  89.4 us (46%)
  waiting for transfers between devices  34.7 us (18%)
  local copies, waits for them, and re-layouts  30.5 us (16%)
  other arithmetic  30.3 us (16%)
  between operations  4.41 us (2%)
  matrix products  3.42 us (2%)
    ppermute x8, starting transfers between devices, halo_rows(): lax.ppermute(lax.slice_in_dim(packed, length - HALO, length, axis=ROW_AXI...  34.9 us
    all_to_all x2, starting transfers between devices, gather_sum(): return jnp.sum(lax.all_to_all(copies, 'gx', 0, 0, tiled=True), axis=0)  20.2 us
    all_to_all x1, starting transfers between devices, on_device(): got = lax.all_to_all(packed, 'gx', 0, 0, tiled=True)  16.4 us
    unnamed x124, local copies, waits for them, and re-layouts  12.6 us
    ppermute x8, starting transfers between devices, halo_rows(): lax.ppermute(lax.slice_in_dim(packed, 0, HALO, axis=ROW_AXIS), 'gx', down)  10.5 us
    ppermute x8, waiting for transfers between devices, halo_rows(): lax.ppermute(lax.slice_in_dim(packed, 0, HALO, axis=ROW_AXIS), 'gx', down)  9.8 us
    all_to_all x2, waiting for transfers between devices, gather_sum(): return jnp.sum(lax.all_to_all(copies, 'gx', 0, 0, tiled=True), axis=0)  8.29 us
    all_to_all x1, starting transfers between devices, on_device(): lax.all_to_all(jnp.transpose(rock_in, (0, 3, 2, 1)), 'gx', split_axis=1,...  7.3 us
  transfers between devices with their start and end apart: 20, of which 11 were waited for; matrix products, arithmetic and copies ran while one was open for 9% of the time, Pallas kernels for 0%

profile of v4, /device:TPU:0, one launch (start us, length us, event | category | flops | bytes accessed | tf_op | source)
XLA Modules:
  0.0 192.8 jit_solution(5236456532530224276)
XLA Ops:
  3.1 1.9 copy.2326
  5.0 1.5 bitcast_bitcast_fusion
  6.6 4.0 %reshape.1004 = f32[32,1,2688]{2,1,0:T(1,128)} reshape(f32[128,4,8,21]{3,2,1,0:T(8,128)} %bitcast_bitcast_fusion) | data formatting | bytes 688128
  10.6 7.3 %all-to-all-start = ((f32[32,1,2688]{2,1,0:T(1,128)}), f32[32,1,2688]{2,1,0:T(1,128)S(1)}, u32[]{:S(2)}, u32[]{:S(2)}) async-start(f32[32,1,2688]{2,1,0:T(1,128)} %reshape.1004), calls=%async_computation | async-start | bytes 688128 | tf_op jit(solution)/shard_map/all_to_all | solution.py:92
  23.3 6.9 %all-to-all-done = f32[32,1,2688]{2,1,0:T(1,128)S(1)} async-done(((f32[32,1,2688]{2,1,0:T(1,128)}), f32[32,1,2688]{2,1,0:T(1,128)S(1)}, u32[]{:S(2)}, u32[]{:S(2)}) %all-to-all-start) | async-done | bytes 344096 | tf_op jit(solution)/shard_map/all_to_all | solution.py:92
  32.2 2.3 %reshape.1005 = f32[128,4,8,21]{3,2,1,0:T(8,128)S(1)} reshape(f32[32,2688]{1,0:T(8,128)S(1)} %reduce.34) | data formatting | bytes 688128
  34.5 1.9 copy.2327
  40.0 3.7 %collective-permute-start.1 = (f32[2,1,4,24,256]{4,3,2,1,0:T(8,128)}, f32[2,1,4,24,256]{4,3,2,1,0:T(8,128)}, u32[]{:S(2)}, u32[]{:S(2)}) collective-permute-start(f32[2,1,4,24,256]{4,3,2,1,0:T(8,128)} %pad_maximum_fusion.13), channel_id=1, source_target_pairs={{0,1},{1,2},{2,3},{3,4},{4,5},{5,6},{6,7},{7,8},{8,9},{9,10},{10,1... | collective-permute-start | bytes 589832 | tf_op jit(solution)/shard_map/ppermute | solution.py:20
  51.8 2.2 %collective-permute-start.2 = (f32[2,1,4,24,256]{4,3,2,1,0:T(8,128)S(1)}, f32[2,1,4,24,256]{4,3,2,1,0:T(8,128)S(1)}, u32[]{:S(2)}, u32[]{:S(2)}) collective-permute-start(f32[2,1,4,24,256]{4,3,2,1,0:T(8,128)S(1)} %pad_maximum_fusion.14), channel_id=1, source_target_pairs={{0,1},{1,2},{2,3},{3,4},{4,5},{5,6},{6,7},{7,8},{8,9},{9,10},{10,1... | collective-permute-start | bytes 589832 | tf_op jit(solution)/shard_map/ppermute | solution.py:20
  56.3 2.7 %collective-permute-done.3 = f32[2,1,4,24,256]{4,3,2,1,0:T(8,128)S(1)} collective-permute-done((f32[2,1,4,24,256]{4,3,2,1,0:T(8,128)S(1)}, f32[2,1,4,24,256]{4,3,2,1,0:T(8,128)S(1)}, u32[]{:S(2)}, u32[]{:S(2)}) %collective-permute-start.3) | collective-permute-done | bytes 196640 | tf_op jit(solution)/shard_map/ppermute | solution.py:23
  61.2 9.9 %all-to-all-start.1 = ((f32[32,1,128]{2,1,0:T(1,128)}), f32[32,1,128]{2,1,0:T(1,128)S(1)}, u32[]{:S(2)}, u32[]{:S(2)}) async-start(f32[32,1,128]{2,1,0:T(1,128)} %broadcast_in_dim.8), calls=%async_computation.1 | async-start | bytes 32768 | tf_op jit(solution)/shard_map/all_to_all | solution.py:35
  74.4 3.8 %all-to-all-done.1 = f32[32,1,128]{2,1,0:T(1,128)S(1)} async-done(((f32[32,1,128]{2,1,0:T(1,128)}), f32[32,1,128]{2,1,0:T(1,128)S(1)}, u32[]{:S(2)}, u32[]{:S(2)}) %all-to-all-start.1) | async-done | bytes 16416 | tf_op jit(solution)/shard_map/all_to_all | solution.py:35
  81.4 3.0 %collective-permute-start.5 = (f32[2,1,4,24,256]{4,3,2,1,0:T(8,128)S(1)}, f32[2,1,4,24,256]{4,3,2,1,0:T(8,128)S(1)}, u32[]{:S(2)}, u32[]{:S(2)}) collective-permute-start(f32[2,1,4,24,256]{4,3,2,1,0:T(8,128)S(1)} %pad_maximum_fusion.15), channel_id=1, source_target_pairs={{0,1},{1,2},{2,3},{3,4},{4,5},{5,6},{6,7},{7,8},{8,9},{9,10},{10,1... | collective-permute-start | bytes 589832 | tf_op jit(solution)/shard_map/ppermute | solution.py:20
  86.5 4.7 %collective-permute-start.6 = (f32[2,1,4,24,256]{4,3,2,1,0:T(8,128)S(1)}, f32[2,1,4,24,256]{4,3,2,1,0:T(8,128)S(1)}, u32[]{:S(2)}, u32[]{:S(2)}) collective-permute-start(f32[2,1,4,24,256]{4,3,2,1,0:T(8,128)S(1)} %pad_maximum_fusion.16), channel_id=1, source_target_pairs={{0,1},{1,2},{2,3},{3,4},{4,5},{5,6},{6,7},{7,8},{8,9},{9,10},{10,1... | collective-permute-start | bytes 589832 | tf_op jit(solution)/shard_map/ppermute | solution.py:20
  92.6 4.0 %collective-permute-done.7 = f32[2,1,4,24,256]{4,3,2,1,0:T(8,128)S(1)} collective-permute-done((f32[2,1,4,24,256]{4,3,2,1,0:T(8,128)S(1)}, f32[2,1,4,24,256]{4,3,2,1,0:T(8,128)S(1)}, u32[]{:S(2)}, u32[]{:S(2)}) %collective-permute-start.7) | collective-permute-done | bytes 196640 | tf_op jit(solution)/shard_map/ppermute | solution.py:23
  98.8 10.3 %all-to-all-start.2 = ((f32[32,1,128]{2,1,0:T(1,128)}), f32[32,1,128]{2,1,0:T(1,128)S(1)}, u32[]{:S(2)}, u32[]{:S(2)}) async-start(f32[32,1,128]{2,1,0:T(1,128)} %broadcast_in_dim.9), calls=%async_computation.2 | async-start | bytes 32768 | tf_op jit(solution)/shard_map/all_to_all | solution.py:35
  111.8 4.5 %all-to-all-done.2 = f32[32,1,128]{2,1,0:T(1,128)S(1)} async-done(((f32[32,1,128]{2,1,0:T(1,128)}), f32[32,1,128]{2,1,0:T(1,128)S(1)}, u32[]{:S(2)}, u32[]{:S(2)}) %all-to-all-start.2) | async-done | bytes 16416 | tf_op jit(solution)/shard_map/all_to_all | solution.py:35
  119.4 3.0 %collective-permute-start.9 = (f32[2,1,4,24,256]{4,3,2,1,0:T(8,128)S(1)}, f32[2,1,4,24,256]{4,3,2,1,0:T(8,128)S(1)}, u32[]{:S(2)}, u32[]{:S(2)}) collective-permute-start(f32[2,1,4,24,256]{4,3,2,1,0:T(8,128)S(1)} %pad_maximum_fusion.17), channel_id=1, source_target_pairs={{0,1},{1,2},{2,3},{3,4},{4,5},{5,6},{6,7},{7,8},{8,9},{9,10},{10,1... | collective-permute-start | bytes 589832 | tf_op jit(solution)/shard_map/ppermute | solution.py:20
  124.6 4.7 %collective-permute-start.10 = (f32[2,1,4,24,256]{4,3,2,1,0:T(8,128)S(1)}, f32[2,1,4,24,256]{4,3,2,1,0:T(8,128)S(1)}, u32[]{:S(2)}, u32[]{:S(2)}) collective-permute-start(f32[2,1,4,24,256]{4,3,2,1,0:T(8,128)S(1)} %pad_maximum_fusion.18), channel_id=1, source_target_pairs={{0,1},{1,2},{2,3},{3,4},{4,5},{5,6},{6,7},{7,8},{8,9},{9,10},{10,1... | collective-permute-start | bytes 589832 | tf_op jit(solution)/shard_map/ppermute | solution.py:20
  131.5 3.1 %collective-permute-done.11 = f32[2,1,4,24,256]{4,3,2,1,0:T(8,128)S(1)} collective-permute-done((f32[2,1,4,24,256]{4,3,2,1,0:T(8,128)S(1)}, f32[2,1,4,24,256]{4,3,2,1,0:T(8,128)S(1)}, u32[]{:S(2)}, u32[]{:S(2)}) %collective-permute-start.11) | collective-permute-done | bytes 196640 | tf_op jit(solution)/shard_map/ppermute | solution.py:23
  141.5 6.8 %collective-permute-start.13 = (f32[3,1,4,24,256]{4,3,2,0,1:T(8,128)S(1)}, f32[3,1,4,24,256]{4,3,2,0,1:T(8,128)S(1)}, u32[]{:S(2)}, u32[]{:S(2)}) collective-permute-start(f32[3,1,4,24,256]{4,3,2,0,1:T(8,128)S(1)} %maximum_bitcast_fusion), channel_id=1, source_target_pairs={{0,1},{1,2},{2,3},{3,4},{4,5},{5,6},{6,7},{7,8},{8,9},{9,10},{10,1... | collective-permute-start | bytes 884744 | tf_op jit(solution)/shard_map/ppermute | solution.py:20
  151.9 6.7 %collective-permute-start.14 = (f32[3,1,4,24,256]{4,3,2,1,0:T(8,128)S(1)}, f32[3,1,4,24,256]{4,3,2,1,0:T(8,128)S(1)}, u32[]{:S(2)}, u32[]{:S(2)}) collective-permute-start(f32[3,1,4,24,256]{4,3,2,1,0:T(8,128)S(1)} %pad_maximum_fusion.12), channel_id=1, source_target_pairs={{0,1},{1,2},{2,3},{3,4},{4,5},{5,6},{6,7},{7,8},{8,9},{9,10},{10,1... | collective-permute-start | bytes 884744 | tf_op jit(solution)/shard_map/ppermute | solution.py:20
  164.8 16.4 %all-to-all-start.3 = ((f32[32,1,768]{2,1,0:T(1,128)}), f32[32,1,768]{2,1,0:T(1,128)S(1)}, u32[]{:S(2)}, u32[]{:S(2)}) async-start(f32[32,1,768]{2,1,0:T(1,128)} %all_to_all.30), calls=%async_computation.3 | async-start | bytes 196608 | tf_op jit(solution)/shard_map/all_to_all | solution.py:226
  182.0 7.1 %all-to-all-done.3 = f32[32,1,768]{2,1,0:T(1,128)S(1)} async-done(((f32[32,1,768]{2,1,0:T(1,128)}), f32[32,1,768]{2,1,0:T(1,128)S(1)}, u32[]{:S(2)}, u32[]{:S(2)}) %all-to-all-start.3) | async-done | bytes 98336 | tf_op jit(solution)/shard_map/all_to_all | solution.py:226
  (326 shorter events, 65.8 us)
Async XLA Ops:
  10.6 19.6 %all-to-all-start = ((f32[32,1,2688]{2,1,0:T(1,128)}), f32[32,1,2688]{2,1,0:T(1,128)S(1)}, u32[]{:S(2)}, u32[]{:S(2)}) async-start(f32[32,1,2688]{2,1,0:T(1,128)} %reshape.1004), calls=%async_computation | async-start | bytes 688128 | tf_op jit(solution)/shard_map/all_to_all | solution.py:92
  18.0 99.6 %copy-start.35 = (s32[4,256]{1,0:T(4,128)}, s32[4,256]{1,0:T(4,128)S(1)}, u32[]{:S(2)}) copy-start(s32[4,256]{1,0:T(4,128)S(1)} %multiply_add_fusion.7) | copy-start | bytes 12292
  38.8 9.1 %collective-permute-start = (f32[2,1,4,24,256]{4,3,2,1,0:T(8,128)}, f32[2,1,4,24,256]{4,3,2,1,0:T(8,128)S(1)}, u32[]{:S(2)}, u32[]{:S(2)}) collective-permute-start(f32[2,1,4,24,256]{4,3,2,1,0:T(8,128)} %pad_maximum_fusion.13), channel_id=1, source_target_pairs={{1,0},{2,1},{3,2},{4,3},{5,4},{6,5},{7,6},{8,7},{9,8},{10,9},{11,1... | collective-permute-start | bytes 589832 | tf_op jit(solution)/shard_map/ppermute | solution.py:23
  40.0 7.8 %collective-permute-start.1 = (f32[2,1,4,24,256]{4,3,2,1,0:T(8,128)}, f32[2,1,4,24,256]{4,3,2,1,0:T(8,128)}, u32[]{:S(2)}, u32[]{:S(2)}) collective-permute-start(f32[2,1,4,24,256]{4,3,2,1,0:T(8,128)} %pad_maximum_fusion.13), channel_id=1, source_target_pairs={{0,1},{1,2},{2,3},{3,4},{4,5},{5,6},{6,7},{7,8},{8,9},{9,10},{10,1... | collective-permute-start | bytes 589832 | tf_op jit(solution)/shard_map/ppermute | solution.py:20
  51.8 4.4 %collective-permute-start.2 = (f32[2,1,4,24,256]{4,3,2,1,0:T(8,128)S(1)}, f32[2,1,4,24,256]{4,3,2,1,0:T(8,128)S(1)}, u32[]{:S(2)}, u32[]{:S(2)}) collective-permute-start(f32[2,1,4,24,256]{4,3,2,1,0:T(8,128)S(1)} %pad_maximum_fusion.14), channel_id=1, source_target_pairs={{0,1},{1,2},{2,3},{3,4},{4,5},{5,6},{6,7},{7,8},{8,9},{9,10},{10,1... | collective-permute-start | bytes 589832 | tf_op jit(solution)/shard_map/ppermute | solution.py:20
  54.0 4.9 %collective-permute-start.3 = (f32[2,1,4,24,256]{4,3,2,1,0:T(8,128)S(1)}, f32[2,1,4,24,256]{4,3,2,1,0:T(8,128)S(1)}, u32[]{:S(2)}, u32[]{:S(2)}) collective-permute-start(f32[2,1,4,24,256]{4,3,2,1,0:T(8,128)S(1)} %pad_maximum_fusion.14), channel_id=1, source_target_pairs={{1,0},{2,1},{3,2},{4,3},{5,4},{6,5},{7,6},{8,7},{9,8},{10,9},{11,1... | collective-permute-start | bytes 589832 | tf_op jit(solution)/shard_map/ppermute | solution.py:23
  55.3 80.9 %copy-start.44 = (s32[128]{0:T(128)}, s32[128]{0:T(128)S(1)}, u32[]{:S(2)}) copy-start(s32[128]{0:T(128)S(1)} %fusion.1017) | copy-start | bytes 1540
  61.2 17.0 %all-to-all-start.1 = ((f32[32,1,128]{2,1,0:T(1,128)}), f32[32,1,128]{2,1,0:T(1,128)S(1)}, u32[]{:S(2)}, u32[]{:S(2)}) async-start(f32[32,1,128]{2,1,0:T(1,128)} %broadcast_in_dim.8), calls=%async_computation.1 | async-start | bytes 32768 | tf_op jit(solution)/shard_map/all_to_all | solution.py:35
  80.1 4.4 %collective-permute-start.4 = (f32[2,1,4,24,256]{4,3,2,1,0:T(8,128)S(1)}, f32[2,1,4,24,256]{4,3,2,1,0:T(8,128)S(1)}, u32[]{:S(2)}, u32[]{:S(2)}) collective-permute-start(f32[2,1,4,24,256]{4,3,2,1,0:T(8,128)S(1)} %pad_maximum_fusion.15), channel_id=1, source_target_pairs={{1,0},{2,1},{3,2},{4,3},{5,4},{6,5},{7,6},{8,7},{9,8},{10,9},{11,1... | collective-permute-start | bytes 589832 | tf_op jit(solution)/shard_map/ppermute | solution.py:23
  81.4 4.1 %collective-permute-start.5 = (f32[2,1,4,24,256]{4,3,2,1,0:T(8,128)S(1)}, f32[2,1,4,24,256]{4,3,2,1,0:T(8,128)S(1)}, u32[]{:S(2)}, u32[]{:S(2)}) collective-permute-start(f32[2,1,4,24,256]{4,3,2,1,0:T(8,128)S(1)} %pad_maximum_fusion.15), channel_id=1, source_target_pairs={{0,1},{1,2},{2,3},{3,4},{4,5},{5,6},{6,7},{7,8},{8,9},{9,10},{10,1... | collective-permute-start | bytes 589832 | tf_op jit(solution)/shard_map/ppermute | solution.py:20
  86.5 6.0 %collective-permute-start.6 = (f32[2,1,4,24,256]{4,3,2,1,0:T(8,128)S(1)}, f32[2,1,4,24,256]{4,3,2,1,0:T(8,128)S(1)}, u32[]{:S(2)}, u32[]{:S(2)}) collective-permute-start(f32[2,1,4,24,256]{4,3,2,1,0:T(8,128)S(1)} %pad_maximum_fusion.16), channel_id=1, source_target_pairs={{0,1},{1,2},{2,3},{3,4},{4,5},{5,6},{6,7},{7,8},{8,9},{9,10},{10,1... | collective-permute-start | bytes 589832 | tf_op jit(solution)/shard_map/ppermute | solution.py:20
  91.3 5.3 %collective-permute-start.7 = (f32[2,1,4,24,256]{4,3,2,1,0:T(8,128)S(1)}, f32[2,1,4,24,256]{4,3,2,1,0:T(8,128)S(1)}, u32[]{:S(2)}, u32[]{:S(2)}) collective-permute-start(f32[2,1,4,24,256]{4,3,2,1,0:T(8,128)S(1)} %pad_maximum_fusion.16), channel_id=1, source_target_pairs={{1,0},{2,1},{3,2},{4,3},{5,4},{6,5},{7,6},{8,7},{9,8},{10,9},{11,1... | collective-permute-start | bytes 589832 | tf_op jit(solution)/shard_map/ppermute | solution.py:23
  98.8 17.4 %all-to-all-start.2 = ((f32[32,1,128]{2,1,0:T(1,128)}), f32[32,1,128]{2,1,0:T(1,128)S(1)}, u32[]{:S(2)}, u32[]{:S(2)}) async-start(f32[32,1,128]{2,1,0:T(1,128)} %broadcast_in_dim.9), calls=%async_computation.2 | async-start | bytes 32768 | tf_op jit(solution)/shard_map/all_to_all | solution.py:35
  118.1 4.5 %collective-permute-start.8 = (f32[2,1,4,24,256]{4,3,2,1,0:T(8,128)S(1)}, f32[2,1,4,24,256]{4,3,2,1,0:T(8,128)S(1)}, u32[]{:S(2)}, u32[]{:S(2)}) collective-permute-start(f32[2,1,4,24,256]{4,3,2,1,0:T(8,128)S(1)} %pad_maximum_fusion.17), channel_id=1, source_target_pairs={{1,0},{2,1},{3,2},{4,3},{5,4},{6,5},{7,6},{8,7},{9,8},{10,9},{11,1... | collective-permute-start | bytes 589832 | tf_op jit(solution)/shard_map/ppermute | solution.py:23
  119.4 4.1 %collective-permute-start.9 = (f32[2,1,4,24,256]{4,3,2,1,0:T(8,128)S(1)}, f32[2,1,4,24,256]{4,3,2,1,0:T(8,128)S(1)}, u32[]{:S(2)}, u32[]{:S(2)}) collective-permute-start(f32[2,1,4,24,256]{4,3,2,1,0:T(8,128)S(1)} %pad_maximum_fusion.17), channel_id=1, source_target_pairs={{0,1},{1,2},{2,3},{3,4},{4,5},{5,6},{6,7},{7,8},{8,9},{9,10},{10,1... | collective-permute-start | bytes 589832 | tf_op jit(solution)/shard_map/ppermute | solution.py:20
  124.6 6.9 %collective-permute-start.10 = (f32[2,1,4,24,256]{4,3,2,1,0:T(8,128)S(1)}, f32[2,1,4,24,256]{4,3,2,1,0:T(8,128)S(1)}, u32[]{:S(2)}, u32[]{:S(2)}) collective-permute-start(f32[2,1,4,24,256]{4,3,2,1,0:T(8,128)S(1)} %pad_maximum_fusion.18), channel_id=1, source_target_pairs={{0,1},{1,2},{2,3},{3,4},{4,5},{5,6},{6,7},{7,8},{8,9},{9,10},{10,1... | collective-permute-start | bytes 589832 | tf_op jit(solution)/shard_map/ppermute | solution.py:20
  129.3 5.3 %collective-permute-start.11 = (f32[2,1,4,24,256]{4,3,2,1,0:T(8,128)S(1)}, f32[2,1,4,24,256]{4,3,2,1,0:T(8,128)S(1)}, u32[]{:S(2)}, u32[]{:S(2)}) collective-permute-start(f32[2,1,4,24,256]{4,3,2,1,0:T(8,128)S(1)} %pad_maximum_fusion.18), channel_id=1, source_target_pairs={{1,0},{2,1},{3,2},{4,3},{5,4},{6,5},{7,6},{8,7},{9,8},{10,9},{11,1... | collective-permute-start | bytes 589832 | tf_op jit(solution)/shard_map/ppermute | solution.py:23
  140.2 9.0 %collective-permute-start.12 = (f32[3,1,4,24,256]{4,3,2,0,1:T(8,128)S(1)}, f32[3,1,4,24,256]{4,3,2,0,1:T(8,128)S(1)}, u32[]{:S(2)}, u32[]{:S(2)}) collective-permute-start(f32[3,1,4,24,256]{4,3,2,0,1:T(8,128)S(1)} %maximum_bitcast_fusion), channel_id=1, source_target_pairs={{1,0},{2,1},{3,2},{4,3},{5,4},{6,5},{7,6},{8,7},{9,8},{10,9},{11,1... | collective-permute-start | bytes 884744 | tf_op jit(solution)/shard_map/ppermute | solution.py:23
  141.5 7.9 %collective-permute-start.13 = (f32[3,1,4,24,256]{4,3,2,0,1:T(8,128)S(1)}, f32[3,1,4,24,256]{4,3,2,0,1:T(8,128)S(1)}, u32[]{:S(2)}, u32[]{:S(2)}) collective-permute-start(f32[3,1,4,24,256]{4,3,2,0,1:T(8,128)S(1)} %maximum_bitcast_fusion), channel_id=1, source_target_pairs={{0,1},{1,2},{2,3},{3,4},{4,5},{5,6},{6,7},{7,8},{8,9},{9,10},{10,1... | collective-permute-start | bytes 884744 | tf_op jit(solution)/shard_map/ppermute | solution.py:20
  150.6 8.5 %collective-permute-start.15 = (f32[3,1,4,24,256]{4,3,2,0,1:T(8,128)S(1)}, f32[3,1,4,24,256]{4,3,2,0,1:T(8,128)S(1)}, u32[]{:S(2)}, u32[]{:S(2)}) collective-permute-start(f32[3,1,4,24,256]{4,3,2,0,1:T(8,128)S(1)} %fusion.1063), channel_id=1, source_target_pairs={{1,0},{2,1},{3,2},{4,3},{5,4},{6,5},{7,6},{8,7},{9,8},{10,9},{11,1... | collective-permute-start | bytes 884744 | tf_op jit(solution)/shard_map/ppermute | solution.py:23
  151.9 7.9 %collective-permute-start.14 = (f32[3,1,4,24,256]{4,3,2,1,0:T(8,128)S(1)}, f32[3,1,4,24,256]{4,3,2,1,0:T(8,128)S(1)}, u32[]{:S(2)}, u32[]{:S(2)}) collective-permute-start(f32[3,1,4,24,256]{4,3,2,1,0:T(8,128)S(1)} %pad_maximum_fusion.12), channel_id=1, source_target_pairs={{0,1},{1,2},{2,3},{3,4},{4,5},{5,6},{6,7},{7,8},{8,9},{9,10},{10,1... | collective-permute-start | bytes 884744 | tf_op jit(solution)/shard_map/ppermute | solution.py:20
  163.2 26.3 %copy-start.49 = (f32[1,1,128]{2,1,0:T(1,128)S(1)}, f32[1,1,128]{2,1,0:T(1,128)}, u32[]{:S(2)}) copy-start(f32[1,1,128]{2,1,0:T(1,128)} %copy-done.48) | copy-start | bytes 1540
  163.2 26.3 %copy-start.51 = (f32[1,1,128]{2,1,0:T(1,128)S(1)}, f32[1,1,128]{2,1,0:T(1,128)}, u32[]{:S(2)}) copy-start(f32[1,1,128]{2,1,0:T(1,128)} %copy-done.50) | copy-start | bytes 1540
  164.8 24.2 %all-to-all-start.3 = ((f32[32,1,768]{2,1,0:T(1,128)}), f32[32,1,768]{2,1,0:T(1,128)S(1)}, u32[]{:S(2)}, u32[]{:S(2)}) async-start(f32[32,1,768]{2,1,0:T(1,128)} %all_to_all.30), calls=%async_computation.3 | async-start | bytes 196608 | tf_op jit(solution)/shard_map/all_to_all | solution.py:226
  (48 other events, 409.7 us)

commit v5 on v4

--- a/solution.py
+++ b/solution.py
@@ -89,8 +89,8 @@
         ],
         axis=0,
     )
-    rock = lax.all_to_all(
-        jnp.transpose(rock_in, (0, 3, 2, 1)), "gx", split_axis=1, concat_axis=3, tiled=True
+    rock = jnp.transpose(
+        lax.all_to_all(rock_in, "gx", split_axis=3, concat_axis=1, tiled=True), (0, 3, 2, 1)
     )
     rock_state = rock[: n_fields * waves * shots].reshape(
         n_fields, waves, shots, local_y, rock_z, total_x

time: 194 us -> 194 us (level)
  local copies, waits for them, and re-layouts: 30.5 us -> 21.9 us
  waiting for transfers between devices: 34.7 us -> 40.6 us
    all_to_all x2, waiting for transfers between devices: 8.29 us -> 11.6 us  [gather_sum(): return jnp.sum(lax.all_to_all(copies, 'gx', 0, 0, tiled=True), axis=0)]
    ppermute x8, starting transfers between devices: 34.9 us -> 38.1 us  [halo_rows(): lax.ppermute(lax.slice_in_dim(packed, length - HALO, length, axis=ROW_AXI...]
    ppermute x8, waiting for transfers between devices: 9.8 us -> 12.9 us  [halo_rows(): lax.ppermute(lax.slice_in_dim(packed, 0, HALO, axis=ROW_AXIS), 'gx', down)]
    all_to_all x1, waiting for transfers between devices: 6.89 us -> 9.96 us  [on_device(): lax.all_to_all(rock_in, 'gx', split_axis=3, concat_axis=1, tiled=True)]
    unnamed x124 -> x111, local copies, waits for them, and re-layouts: 12.6 us -> 9.62 us
    reduce_sum x4, other arithmetic: 2.97 us -> 0.2 us  [on_device(): surface = jnp.sum(pressure[0] * bottom, axis=2)]
    all_to_all x1, starting transfers between devices: 16.4 us -> 13.8 us  [on_device(): got = lax.all_to_all(packed, 'gx', 0, 0, tiled=True)]
    ppermute x8, waiting for transfers between devices: 2.66 us -> 0.02 us  [halo_rows(): lax.ppermute(lax.slice_in_dim(packed, length - HALO, length, axis=ROW_AXI...]
  transfers between devices with their start and end apart: 20 -> 20, of which waited for: 11 -> 11; matrix products, arithmetic and copies ran while one was open for 9% -> 4% of each run, Pallas kernels for 0% -> 0%
where the time goes in v5:
time: 194 us; the launch traced here: 193 us
  starting transfers between devices  89.7 us (46%)
  waiting for transfers between devices  40.6 us (21%)
  other arithmetic  32.1 us (17%)
  local copies, waits for them, and re-layouts  21.9 us (11%)
  between operations  4.27 us (2%)
  matrix products  4.08 us (2%)
    ppermute x8, starting transfers between devices, halo_rows(): lax.ppermute(lax.slice_in_dim(packed, length - HALO, length, axis=ROW_AXI...  38.1 us
    all_to_all x2, starting transfers between devices, gather_sum(): return jnp.sum(lax.all_to_all(copies, 'gx', 0, 0, tiled=True), axis=0)  20.1 us
    all_to_all x1, starting transfers between devices, on_device(): got = lax.all_to_all(packed, 'gx', 0, 0, tiled=True)  13.8 us
    ppermute x8, waiting for transfers between devices, halo_rows(): lax.ppermute(lax.slice_in_dim(packed, 0, HALO, axis=ROW_AXIS), 'gx', down)  12.9 us
    all_to_all x2, waiting for transfers between devices, gather_sum(): return jnp.sum(lax.all_to_all(copies, 'gx', 0, 0, tiled=True), axis=0)  11.6 us
    ppermute x8, starting transfers between devices, halo_rows(): lax.ppermute(lax.slice_in_dim(packed, 0, HALO, axis=ROW_AXIS), 'gx', down)  10.5 us
    all_to_all x1, waiting for transfers between devices, on_device(): lax.all_to_all(rock_in, 'gx', split_axis=3, concat_axis=1, tiled=True)  9.96 us
    unnamed x111, local copies, waits for them, and re-layouts  9.62 us
  transfers between devices with their start and end apart: 20, of which 11 were waited for; matrix products, arithmetic and copies ran while one was open for 4% of the time, Pallas kernels for 0%

profile of v5, /device:TPU:0, one launch (start us, length us, event | category | flops | bytes accessed | tf_op | source)
XLA Modules:
  0.0 192.7 jit_solution(3024546435368767049)
XLA Ops:
  3.1 1.9 copy.2099
  5.1 2.7 %reshape.996 = f32[32,1,2688]{2,1,0:T(1,128)} reshape(f32[128,4,8,21]{3,2,1,0:T(8,128)S(1)} %bitcast.544) | data formatting | bytes 688128
  7.7 7.3 %all-to-all-start = ((f32[32,1,2688]{2,1,0:T(1,128)}), f32[32,1,2688]{2,1,0:T(1,128)S(1)}, u32[]{:S(2)}, u32[]{:S(2)}) async-start(f32[32,1,2688]{2,1,0:T(1,128)} %reshape.996), calls=%async_computation | async-start | bytes 688128 | tf_op jit(solution)/shard_map/all_to_all | solution.py:93
  17.4 10.0 %all-to-all-done = f32[32,1,2688]{2,1,0:T(1,128)S(1)} async-done(((f32[32,1,2688]{2,1,0:T(1,128)}), f32[32,1,2688]{2,1,0:T(1,128)S(1)}, u32[]{:S(2)}, u32[]{:S(2)}) %all-to-all-start) | async-done | bytes 344096 | tf_op jit(solution)/shard_map/all_to_all | solution.py:93
  29.3 2.3 %reshape.997 = f32[128,4,8,21]{3,2,1,0:T(8,128)S(1)} reshape(f32[32,2688]{1,0:T(8,128)S(1)} %reduce.34) | data formatting | bytes 688128
  33.2 2.3 %copy.2102 = f32[21,256,4,4]{1,2,3,0:T(4,128)S(1)} copy(f32[21,256,4,4]{0,1,3,2:T(8,128)} %bitcast.546) | data formatting | bytes 688128 | tf_op jit(solution)/shard_map/all_to_all | solution.py:93
  38.3 2.4 %collective-permute-done = f32[2,1,4,24,256]{4,3,2,1,0:T(8,128)S(1)} collective-permute-done((f32[2,1,4,24,256]{4,3,2,1,0:T(8,128)S(1)}, f32[2,1,4,24,256]{4,3,2,1,0:T(8,128)S(1)}, u32[]{:S(2)}, u32[]{:S(2)}) %collective-permute-start) | collective-permute-done | bytes 196640 | tf_op jit(solution)/shard_map/ppermute | solution.py:23
  41.9 6.1 %collective-permute-start.2 = (f32[2,1,4,24,256]{4,3,2,1,0:T(8,128)S(1)}, f32[2,1,4,24,256]{4,3,2,1,0:T(8,128)S(1)}, u32[]{:S(2)}, u32[]{:S(2)}) collective-permute-start(f32[2,1,4,24,256]{4,3,2,1,0:T(8,128)S(1)} %pad_maximum_fusion.11), channel_id=1, source_target_pairs={{0,1},{1,2},{2,3},{3,4},{4,5},{5,6},{6,7},{7,8},{8,9},{9,10},{10,1... | collective-permute-start | bytes 589832 | tf_op jit(solution)/shard_map/ppermute | solution.py:20
  49.3 2.0 %collective-permute-done.3 = f32[2,1,4,24,256]{4,3,2,1,0:T(8,128)S(1)} collective-permute-done((f32[2,1,4,24,256]{4,3,2,1,0:T(8,128)S(1)}, f32[2,1,4,24,256]{4,3,2,1,0:T(8,128)S(1)}, u32[]{:S(2)}, u32[]{:S(2)}) %collective-permute-start.3) | collective-permute-done | bytes 196640 | tf_op jit(solution)/shard_map/ppermute | solution.py:23
  53.5 10.4 %all-to-all-start.1 = ((f32[32,1,128]{2,1,0:T(1,128)}), f32[32,1,128]{2,1,0:T(1,128)S(1)}, u32[]{:S(2)}, u32[]{:S(2)}) async-start(f32[32,1,128]{2,1,0:T(1,128)} %broadcast_in_dim.8), calls=%async_computation.1 | async-start | bytes 32768 | tf_op jit(solution)/shard_map/all_to_all | solution.py:35
  66.4 4.6 %all-to-all-done.1 = f32[32,1,128]{2,1,0:T(1,128)S(1)} async-done(((f32[32,1,128]{2,1,0:T(1,128)}), f32[32,1,128]{2,1,0:T(1,128)S(1)}, u32[]{:S(2)}, u32[]{:S(2)}) %all-to-all-start.1) | async-done | bytes 16416 | tf_op jit(solution)/shard_map/all_to_all | solution.py:35
  76.1 2.2 %collective-permute-done.4 = f32[2,1,4,24,256]{4,3,2,1,0:T(8,128)S(1)} collective-permute-done((f32[2,1,4,24,256]{4,3,2,1,0:T(8,128)S(1)}, f32[2,1,4,24,256]{4,3,2,1,0:T(8,128)S(1)}, u32[]{:S(2)}, u32[]{:S(2)}) %collective-permute-start.4) | collective-permute-done | bytes 196640 | tf_op jit(solution)/shard_map/ppermute | solution.py:23
  79.4 6.1 %collective-permute-start.6 = (f32[2,1,4,24,256]{4,3,2,1,0:T(8,128)S(1)}, f32[2,1,4,24,256]{4,3,2,1,0:T(8,128)S(1)}, u32[]{:S(2)}, u32[]{:S(2)}) collective-permute-start(f32[2,1,4,24,256]{4,3,2,1,0:T(8,128)S(1)} %pad_maximum_fusion.13), channel_id=1, source_target_pairs={{0,1},{1,2},{2,3},{3,4},{4,5},{5,6},{6,7},{7,8},{8,9},{9,10},{10,1... | collective-permute-start | bytes 589832 | tf_op jit(solution)/shard_map/ppermute | solution.py:20
  87.0 1.8 collective-permute-done.7
  93.5 9.6 %all-to-all-start.2 = ((f32[32,1,128]{2,1,0:T(1,128)}), f32[32,1,128]{2,1,0:T(1,128)S(1)}, u32[]{:S(2)}, u32[]{:S(2)}) async-start(f32[32,1,128]{2,1,0:T(1,128)} %broadcast_in_dim.9), calls=%async_computation.2 | async-start | bytes 32768 | tf_op jit(solution)/shard_map/all_to_all | solution.py:35
  103.2 7.0 %all-to-all-done.2 = f32[32,1,128]{2,1,0:T(1,128)S(1)} async-done(((f32[32,1,128]{2,1,0:T(1,128)}), f32[32,1,128]{2,1,0:T(1,128)S(1)}, u32[]{:S(2)}, u32[]{:S(2)}) %all-to-all-start.2) | async-done | bytes 16416 | tf_op jit(solution)/shard_map/all_to_all | solution.py:35
  115.4 2.1 %collective-permute-done.8 = f32[2,1,4,24,256]{4,3,2,1,0:T(8,128)S(1)} collective-permute-done((f32[2,1,4,24,256]{4,3,2,1,0:T(8,128)S(1)}, f32[2,1,4,24,256]{4,3,2,1,0:T(8,128)S(1)}, u32[]{:S(2)}, u32[]{:S(2)}) %collective-permute-start.8) | collective-permute-done | bytes 196640 | tf_op jit(solution)/shard_map/ppermute | solution.py:23
  118.7 6.1 %collective-permute-start.10 = (f32[2,1,4,24,256]{4,3,2,1,0:T(8,128)S(1)}, f32[2,1,4,24,256]{4,3,2,1,0:T(8,128)S(1)}, u32[]{:S(2)}, u32[]{:S(2)}) collective-permute-start(f32[2,1,4,24,256]{4,3,2,1,0:T(8,128)S(1)} %pad_maximum_fusion.15), channel_id=1, source_target_pairs={{0,1},{1,2},{2,3},{3,4},{4,5},{5,6},{6,7},{7,8},{8,9},{9,10},{10,1... | collective-permute-start | bytes 589832 | tf_op jit(solution)/shard_map/ppermute | solution.py:20
  126.0 2.0 %collective-permute-done.11 = f32[2,1,4,24,256]{4,3,2,1,0:T(8,128)S(1)} collective-permute-done((f32[2,1,4,24,256]{4,3,2,1,0:T(8,128)S(1)}, f32[2,1,4,24,256]{4,3,2,1,0:T(8,128)S(1)}, u32[]{:S(2)}, u32[]{:S(2)}) %collective-permute-start.11) | collective-permute-done | bytes 196640 | tf_op jit(solution)/shard_map/ppermute | solution.py:23
  133.5 6.3 %collective-permute-start.13 = (f32[3,1,4,24,256]{4,3,2,1,0:T(8,128)S(1)}, f32[3,1,4,24,256]{4,3,2,1,0:T(8,128)S(1)}, u32[]{:S(2)}, u32[]{:S(2)}) collective-permute-start(f32[3,1,4,24,256]{4,3,2,1,0:T(8,128)S(1)} %maximum_maximum_fusion.8), channel_id=1, source_target_pairs={{0,1},{1,2},{2,3},{3,4},{4,5},{5,6},{6,7},{7,8},{8,9},{9,10},{10,1... | collective-permute-start | bytes 884744 | tf_op jit(solution)/shard_map/ppermute | solution.py:20
  150.4 8.6 %collective-permute-start.14 = (f32[3,1,4,24,256]{4,3,2,1,0:T(8,128)S(1)}, f32[3,1,4,24,256]{4,3,2,1,0:T(8,128)S(1)}, u32[]{:S(2)}, u32[]{:S(2)}) collective-permute-start(f32[3,1,4,24,256]{4,3,2,1,0:T(8,128)S(1)} %pad_maximum_fusion.9), channel_id=1, source_target_pairs={{0,1},{1,2},{2,3},{3,4},{4,5},{5,6},{6,7},{7,8},{8,9},{9,10},{10,1... | collective-permute-start | bytes 884744 | tf_op jit(solution)/shard_map/ppermute | solution.py:20
  162.3 2.7 %fusion.54 = f32[3,1,4,12,256]{4,3,2,1,0:T(8,128)S(1)} fusion(f32[3,1,4,12,256]{4,3,2,1,0:T(8,128)} %get-tuple-element.231, f32[3,1,4,12,256]{4,3,2,1,0:T(8,128)S(1)} %get-tuple-element.230, f32[3,1,4,24,256]{4,3,2,1,0:T(8,128)} %copy-done, f32[3,1,8,24,256]{4,3,2,1,0:T(8,128)S(1)} %get-tuple-element.212, f32[3,1,8,24,256]{4,3,2,1,0:T(8,128)S(1)} %get-tuple-element.213, ...), kind=kLoop, calls=%fused_computation.330 | loop fusion | flops 1437696 | bytes 1867776 | tf_op jit(solution)/shard_map/mul | solution.py:173
  167.5 13.8 %all-to-all-start.3 = ((f32[32,1,768]{2,1,0:T(1,128)}), f32[32,1,768]{2,1,0:T(1,128)S(1)}, u32[]{:S(2)}, u32[]{:S(2)}) async-start(f32[32,1,768]{2,1,0:T(1,128)} %all_to_all.33), calls=%async_computation.3 | async-start | bytes 196608 | tf_op jit(solution)/shard_map/all_to_all | solution.py:226
  183.0 6.1 %all-to-all-done.3 = f32[32,1,768]{2,1,0:T(1,128)S(1)} async-done(((f32[32,1,768]{2,1,0:T(1,128)}), f32[32,1,768]{2,1,0:T(1,128)S(1)}, u32[]{:S(2)}, u32[]{:S(2)}) %all-to-all-start.3) | async-done | bytes 98336 | tf_op jit(solution)/shard_map/all_to_all | solution.py:226
  (287 shorter events, 62.2 us)
Async XLA Ops:
  7.7 19.6 %all-to-all-start = ((f32[32,1,2688]{2,1,0:T(1,128)}), f32[32,1,2688]{2,1,0:T(1,128)S(1)}, u32[]{:S(2)}, u32[]{:S(2)}) async-start(f32[32,1,2688]{2,1,0:T(1,128)} %reshape.996), calls=%async_computation | async-start | bytes 688128 | tf_op jit(solution)/shard_map/all_to_all | solution.py:93
  15.1 96.5 %copy-start.29 = (s32[4,256]{1,0:T(4,128)}, s32[4,256]{1,0:T(4,128)S(1)}, u32[]{:S(2)}) copy-start(s32[4,256]{1,0:T(4,128)S(1)} %multiply_add_fusion.25) | copy-start | bytes 12292
  17.3 94.2 %copy-start.35 = (pred[128]{0:T(512)(128)(4,1)}, pred[128]{0:T(512)(128)(4,1)S(1)}, u32[]{:S(2)}) copy-start(pred[128]{0:T(512)(128)(4,1)S(1)} %get-tuple-element.195) | copy-start | bytes 388
  35.5 2.8 %collective-permute-start.1 = (f32[2,1,4,24,256]{4,3,2,1,0:T(8,128)S(1)}, f32[2,1,4,24,256]{4,3,2,1,0:T(8,128)S(1)}, u32[]{:S(2)}, u32[]{:S(2)}) collective-permute-start(f32[2,1,4,24,256]{4,3,2,1,0:T(8,128)S(1)} %pad_maximum_fusion.10), channel_id=1, source_target_pairs={{0,1},{1,2},{2,3},{3,4},{4,5},{5,6},{6,7},{7,8},{8,9},{9,10},{10,1... | collective-permute-start | bytes 589832 | tf_op jit(solution)/shard_map/ppermute | solution.py:20
  37.0 3.7 %collective-permute-start = (f32[2,1,4,24,256]{4,3,2,1,0:T(8,128)S(1)}, f32[2,1,4,24,256]{4,3,2,1,0:T(8,128)S(1)}, u32[]{:S(2)}, u32[]{:S(2)}) collective-permute-start(f32[2,1,4,24,256]{4,3,2,1,0:T(8,128)S(1)} %pad_maximum_fusion.10), channel_id=1, source_target_pairs={{1,0},{2,1},{3,2},{4,3},{5,4},{6,5},{7,6},{8,7},{9,8},{10,9},{11,1... | collective-permute-start | bytes 589832 | tf_op jit(solution)/shard_map/ppermute | solution.py:23
  41.9 7.4 %collective-permute-start.2 = (f32[2,1,4,24,256]{4,3,2,1,0:T(8,128)S(1)}, f32[2,1,4,24,256]{4,3,2,1,0:T(8,128)S(1)}, u32[]{:S(2)}, u32[]{:S(2)}) collective-permute-start(f32[2,1,4,24,256]{4,3,2,1,0:T(8,128)S(1)} %pad_maximum_fusion.11), channel_id=1, source_target_pairs={{0,1},{1,2},{2,3},{3,4},{4,5},{5,6},{6,7},{7,8},{8,9},{9,10},{10,1... | collective-permute-start | bytes 589832 | tf_op jit(solution)/shard_map/ppermute | solution.py:20
  47.9 3.3 %collective-permute-start.3 = (f32[2,1,4,24,256]{4,3,2,1,0:T(8,128)S(1)}, f32[2,1,4,24,256]{4,3,2,1,0:T(8,128)S(1)}, u32[]{:S(2)}, u32[]{:S(2)}) collective-permute-start(f32[2,1,4,24,256]{4,3,2,1,0:T(8,128)S(1)} %pad_maximum_fusion.11), channel_id=1, source_target_pairs={{1,0},{2,1},{3,2},{4,3},{5,4},{6,5},{7,6},{8,7},{9,8},{10,9},{11,1... | collective-permute-start | bytes 589832 | tf_op jit(solution)/shard_map/ppermute | solution.py:23
  49.2 62.3 %copy-start.38 = (s32[128]{0:T(128)}, s32[128]{0:T(128)S(1)}, u32[]{:S(2)}) copy-start(s32[128]{0:T(128)S(1)} %fusion.1089) | copy-start | bytes 1540
  53.5 17.5 %all-to-all-start.1 = ((f32[32,1,128]{2,1,0:T(1,128)}), f32[32,1,128]{2,1,0:T(1,128)S(1)}, u32[]{:S(2)}, u32[]{:S(2)}) async-start(f32[32,1,128]{2,1,0:T(1,128)} %broadcast_in_dim.8), calls=%async_computation.1 | async-start | bytes 32768 | tf_op jit(solution)/shard_map/all_to_all | solution.py:35
  72.9 3.2 %collective-permute-start.5 = (f32[2,1,4,24,256]{4,3,2,1,0:T(8,128)S(1)}, f32[2,1,4,24,256]{4,3,2,1,0:T(8,128)S(1)}, u32[]{:S(2)}, u32[]{:S(2)}) collective-permute-start(f32[2,1,4,24,256]{4,3,2,1,0:T(8,128)S(1)} %pad_maximum_fusion.12), channel_id=1, source_target_pairs={{0,1},{1,2},{2,3},{3,4},{4,5},{5,6},{6,7},{7,8},{8,9},{9,10},{10,1... | collective-permute-start | bytes 589832 | tf_op jit(solution)/shard_map/ppermute | solution.py:20
  74.7 3.6 %collective-permute-start.4 = (f32[2,1,4,24,256]{4,3,2,1,0:T(8,128)S(1)}, f32[2,1,4,24,256]{4,3,2,1,0:T(8,128)S(1)}, u32[]{:S(2)}, u32[]{:S(2)}) collective-permute-start(f32[2,1,4,24,256]{4,3,2,1,0:T(8,128)S(1)} %pad_maximum_fusion.12), channel_id=1, source_target_pairs={{1,0},{2,1},{3,2},{4,3},{5,4},{6,5},{7,6},{8,7},{9,8},{10,9},{11,1... | collective-permute-start | bytes 589832 | tf_op jit(solution)/shard_map/ppermute | solution.py:23
  79.4 7.6 %collective-permute-start.6 = (f32[2,1,4,24,256]{4,3,2,1,0:T(8,128)S(1)}, f32[2,1,4,24,256]{4,3,2,1,0:T(8,128)S(1)}, u32[]{:S(2)}, u32[]{:S(2)}) collective-permute-start(f32[2,1,4,24,256]{4,3,2,1,0:T(8,128)S(1)} %pad_maximum_fusion.13), channel_id=1, source_target_pairs={{0,1},{1,2},{2,3},{3,4},{4,5},{5,6},{6,7},{7,8},{8,9},{9,10},{10,1... | collective-permute-start | bytes 589832 | tf_op jit(solution)/shard_map/ppermute | solution.py:20
  85.5 3.3 %collective-permute-start.7 = (f32[2,1,4,24,256]{4,3,2,1,0:T(8,128)S(1)}, f32[2,1,4,24,256]{4,3,2,1,0:T(8,128)S(1)}, u32[]{:S(2)}, u32[]{:S(2)}) collective-permute-start(f32[2,1,4,24,256]{4,3,2,1,0:T(8,128)S(1)} %pad_maximum_fusion.13), channel_id=1, source_target_pairs={{1,0},{2,1},{3,2},{4,3},{5,4},{6,5},{7,6},{8,7},{9,8},{10,9},{11,1... | collective-permute-start | bytes 589832 | tf_op jit(solution)/shard_map/ppermute | solution.py:23
  91.3 26.5 %copy-start.15 = (f32[2,1,4,4,256]{4,3,2,0,1:T(4,128)}, f32[2,1,4,4,256]{4,3,2,0,1:T(4,128)S(1)}, u32[]{:S(2)}) copy-start(f32[2,1,4,4,256]{4,3,2,0,1:T(4,128)S(1)} %get-tuple-element.268) | copy-start | bytes 98308
  93.5 16.7 %all-to-all-start.2 = ((f32[32,1,128]{2,1,0:T(1,128)}), f32[32,1,128]{2,1,0:T(1,128)S(1)}, u32[]{:S(2)}, u32[]{:S(2)}) async-start(f32[32,1,128]{2,1,0:T(1,128)} %broadcast_in_dim.9), calls=%async_computation.2 | async-start | bytes 32768 | tf_op jit(solution)/shard_map/all_to_all | solution.py:35
  112.1 3.3 %collective-permute-start.9 = (f32[2,1,4,24,256]{4,3,2,1,0:T(8,128)S(1)}, f32[2,1,4,24,256]{4,3,2,1,0:T(8,128)S(1)}, u32[]{:S(2)}, u32[]{:S(2)}) collective-permute-start(f32[2,1,4,24,256]{4,3,2,1,0:T(8,128)S(1)} %pad_maximum_fusion.14), channel_id=1, source_target_pairs={{0,1},{1,2},{2,3},{3,4},{4,5},{5,6},{6,7},{7,8},{8,9},{9,10},{10,1... | collective-permute-start | bytes 589832 | tf_op jit(solution)/shard_map/ppermute | solution.py:20
  113.9 3.6 %collective-permute-start.8 = (f32[2,1,4,24,256]{4,3,2,1,0:T(8,128)S(1)}, f32[2,1,4,24,256]{4,3,2,1,0:T(8,128)S(1)}, u32[]{:S(2)}, u32[]{:S(2)}) collective-permute-start(f32[2,1,4,24,256]{4,3,2,1,0:T(8,128)S(1)} %pad_maximum_fusion.14), channel_id=1, source_target_pairs={{1,0},{2,1},{3,2},{4,3},{5,4},{6,5},{7,6},{8,7},{9,8},{10,9},{11,1... | collective-permute-start | bytes 589832 | tf_op jit(solution)/shard_map/ppermute | solution.py:23
  118.7 7.4 %collective-permute-start.10 = (f32[2,1,4,24,256]{4,3,2,1,0:T(8,128)S(1)}, f32[2,1,4,24,256]{4,3,2,1,0:T(8,128)S(1)}, u32[]{:S(2)}, u32[]{:S(2)}) collective-permute-start(f32[2,1,4,24,256]{4,3,2,1,0:T(8,128)S(1)} %pad_maximum_fusion.15), channel_id=1, source_target_pairs={{0,1},{1,2},{2,3},{3,4},{4,5},{5,6},{6,7},{7,8},{8,9},{9,10},{10,1... | collective-permute-start | bytes 589832 | tf_op jit(solution)/shard_map/ppermute | solution.py:20
  124.7 3.3 %collective-permute-start.11 = (f32[2,1,4,24,256]{4,3,2,1,0:T(8,128)S(1)}, f32[2,1,4,24,256]{4,3,2,1,0:T(8,128)S(1)}, u32[]{:S(2)}, u32[]{:S(2)}) collective-permute-start(f32[2,1,4,24,256]{4,3,2,1,0:T(8,128)S(1)} %pad_maximum_fusion.15), channel_id=1, source_target_pairs={{1,0},{2,1},{3,2},{4,3},{5,4},{6,5},{7,6},{8,7},{9,8},{10,9},{11,1... | collective-permute-start | bytes 589832 | tf_op jit(solution)/shard_map/ppermute | solution.py:23
  133.5 8.8 %collective-permute-start.13 = (f32[3,1,4,24,256]{4,3,2,1,0:T(8,128)S(1)}, f32[3,1,4,24,256]{4,3,2,1,0:T(8,128)S(1)}, u32[]{:S(2)}, u32[]{:S(2)}) collective-permute-start(f32[3,1,4,24,256]{4,3,2,1,0:T(8,128)S(1)} %maximum_maximum_fusion.8), channel_id=1, source_target_pairs={{0,1},{1,2},{2,3},{3,4},{4,5},{5,6},{6,7},{7,8},{8,9},{9,10},{10,1... | collective-permute-start | bytes 884744 | tf_op jit(solution)/shard_map/ppermute | solution.py:20
  139.8 3.5 %collective-permute-start.12 = (f32[3,1,4,24,256]{4,3,2,1,0:T(8,128)S(1)}, f32[3,1,4,24,256]{4,3,2,1,0:T(8,128)S(1)}, u32[]{:S(2)}, u32[]{:S(2)}) collective-permute-start(f32[3,1,4,24,256]{4,3,2,1,0:T(8,128)S(1)} %maximum_maximum_fusion.8), channel_id=1, source_target_pairs={{1,0},{2,1},{3,2},{4,3},{5,4},{6,5},{7,6},{8,7},{9,8},{10,9},{11,1... | collective-permute-start | bytes 884744 | tf_op jit(solution)/shard_map/ppermute | solution.py:23
  149.1 11.1 %collective-permute-start.15 = (f32[3,1,4,24,256]{4,3,2,1,0:T(8,128)S(1)}, f32[3,1,4,24,256]{4,3,2,1,0:T(8,128)S(1)}, u32[]{:S(2)}, u32[]{:S(2)}) collective-permute-start(f32[3,1,4,24,256]{4,3,2,1,0:T(8,128)S(1)} %pad_maximum_fusion.9), channel_id=1, source_target_pairs={{1,0},{2,1},{3,2},{4,3},{5,4},{6,5},{7,6},{8,7},{9,8},{10,9},{11,1... | collective-permute-start | bytes 884744 | tf_op jit(solution)/shard_map/ppermute | solution.py:23
  150.4 9.8 %collective-permute-start.14 = (f32[3,1,4,24,256]{4,3,2,1,0:T(8,128)S(1)}, f32[3,1,4,24,256]{4,3,2,1,0:T(8,128)S(1)}, u32[]{:S(2)}, u32[]{:S(2)}) collective-permute-start(f32[3,1,4,24,256]{4,3,2,1,0:T(8,128)S(1)} %pad_maximum_fusion.9), channel_id=1, source_target_pairs={{0,1},{1,2},{2,3},{3,4},{4,5},{5,6},{6,7},{7,8},{8,9},{9,10},{10,1... | collective-permute-start | bytes 884744 | tf_op jit(solution)/shard_map/ppermute | solution.py:20
  167.5 21.6 %all-to-all-start.3 = ((f32[32,1,768]{2,1,0:T(1,128)}), f32[32,1,768]{2,1,0:T(1,128)S(1)}, u32[]{:S(2)}, u32[]{:S(2)}) async-start(f32[32,1,768]{2,1,0:T(1,128)} %all_to_all.33), calls=%async_computation.3 | async-start | bytes 196608 | tf_op jit(solution)/shard_map/all_to_all | solution.py:226
  (43 other events, 457.5 us)

commit v6 on v5

--- a/solution.py
+++ b/solution.py
@@ -130,7 +130,11 @@
     late_records = []
     for step in range(steps):
         floor_pressure = jnp.sum(pressure * bottom, axis=3)
-        sxy_pad, syy_pad, syz_pad, p_pad = halo_rows([sig_xy, sig_yy, sig_yz, pressure])
+        if step == 0:
+            (p_pad,) = halo_rows([pressure])
+            sxy_pad, syy_pad, syz_pad = halo_rows([sig_xy, sig_yy, sig_yz])
+        else:
+            sxy_pad, syy_pad, syz_pad, p_pad = halo_rows([sig_xy, sig_yy, sig_yz, pressure])
         vel_x = vel_x + TIME_STEP * buoy * (
             derive(sig_xx, 4, True) + stencil(sxy_pad, 2, False) + derive(sig_xz, 3, False)
         )

time: 194 us -> 203 us (1.046)
  starting transfers between devices: 89.7 us -> 95 us
  other arithmetic: 32.1 us -> 35.9 us
  waiting for transfers between devices: 40.6 us -> 37.6 us
  local copies, waits for them, and re-layouts: 21.9 us -> 24.4 us
    all_to_all x2, waiting for transfers between devices: 11.6 us -> 8.47 us  [gather_sum(): return jnp.sum(lax.all_to_all(copies, 'gx', 0, 0, tiled=True), axis=0)]
    reduce_sum x4, other arithmetic: 0.2 us -> 2.91 us  [on_device(): surface = jnp.sum(pressure[0] * bottom, axis=2)]
    mul x2 -> x4, other arithmetic: 0.7 us -> 3.26 us  [on_device(): (flow_x - TIME_STEP * water_buoy * derive(pressure, 4, True)) * live]
    ppermute x8 -> x9, starting transfers between devices: 38.1 us -> 40.4 us  [halo_rows(): lax.ppermute(lax.slice_in_dim(packed, length - HALO, length, axis=ROW_AXI...]
    add x3 -> x0, other arithmetic: 2.26 us -> none  [the longest x2 1.51 us: on_device(): (flow_z - TIME_STEP * water_buoy * derive(pressure, 3, True)) * above]
    ppermute x8 -> x9, starting transfers between devices: 10.5 us -> 11.6 us  [halo_rows(): lax.ppermute(lax.slice_in_dim(packed, 0, HALO, axis=ROW_AXIS), 'gx', down)]
    ppermute x8 -> x9, waiting for transfers between devices: 12.9 us -> 13.2 us  [halo_rows(): lax.ppermute(lax.slice_in_dim(packed, 0, HALO, axis=ROW_AXIS), 'gx', down)]
    unnamed x111 -> x127, local copies, waits for them, and re-layouts: 9.62 us -> 9.55 us
  transfers between devices with their start and end apart: 20 -> 22, of which waited for: 11 -> 11; matrix products, arithmetic and copies ran while one was open for 4% -> 9% of each run, Pallas kernels for 0% -> 0%
where the time goes in v6:
time: 203 us; the launch traced here: 202 us
  starting transfers between devices  95 us (47%)
  waiting for transfers between devices  37.6 us (19%)
  other arithmetic  35.9 us (18%)
  local copies, waits for them, and re-layouts  24.4 us (12%)
  between operations  4.63 us (2%)
  matrix products  4.08 us (2%)
    ppermute x9, starting transfers between devices, halo_rows(): lax.ppermute(lax.slice_in_dim(packed, length - HALO, length, axis=ROW_AXI...  40.4 us
    all_to_all x2, starting transfers between devices, gather_sum(): return jnp.sum(lax.all_to_all(copies, 'gx', 0, 0, tiled=True), axis=0)  20.9 us
    all_to_all x1, starting transfers between devices, on_device(): got = lax.all_to_all(packed, 'gx', 0, 0, tiled=True)  13.4 us
    ppermute x9, waiting for transfers between devices, halo_rows(): lax.ppermute(lax.slice_in_dim(packed, 0, HALO, axis=ROW_AXIS), 'gx', down)  13.2 us
    ppermute x9, starting transfers between devices, halo_rows(): lax.ppermute(lax.slice_in_dim(packed, 0, HALO, axis=ROW_AXIS), 'gx', down)  11.6 us
    all_to_all x1, waiting for transfers between devices, on_device(): lax.all_to_all(rock_in, 'gx', split_axis=3, concat_axis=1, tiled=True)  9.57 us
    unnamed x127, local copies, waits for them, and re-layouts  9.55 us
    all_to_all x1, starting transfers between devices, on_device(): lax.all_to_all(rock_in, 'gx', split_axis=3, concat_axis=1, tiled=True)  8.76 us
  transfers between devices with their start and end apart: 22, of which 11 were waited for; matrix products, arithmetic and copies ran while one was open for 9% of the time, Pallas kernels for 0%

profile of v6, /device:TPU:0, one launch (start us, length us, event | category | flops | bytes accessed | tf_op | source)
XLA Modules:
  0.0 201.7 jit_solution(17358009067566458261)
XLA Ops:
  2.8 3.0 %collective-permute-start.1 = (f32[2,1,4,12,256]{4,2,3,1,0:T(4,128)S(1)}, f32[2,1,4,12,256]{4,2,3,1,0:T(4,128)S(1)}, u32[]{:S(2)}, u32[]{:S(2)}) collective-permute-start(f32[2,1,4,12,256]{4,2,3,1,0:T(4,128)S(1)} %slice_bitcast_fusion.3), channel_id=1, source_target_pairs={{0,1},{1,2},{2,3},{3,4},{4,5},{5,6},{6,7},{7,8},{8,9},{9,10},{10,1... | collective-permute-start | bytes 294920 | tf_op jit(solution)/shard_map/ppermute | solution.py:20
  8.4 1.9 copy.2222
  10.3 2.7 %reshape.996 = f32[32,1,2688]{2,1,0:T(1,128)} reshape(f32[128,4,8,21]{3,2,1,0:T(8,128)S(1)} %bitcast.524) | data formatting | bytes 688128
  13.0 8.8 %all-to-all-start = ((f32[32,1,2688]{2,1,0:T(1,128)}), f32[32,1,2688]{2,1,0:T(1,128)S(1)}, u32[]{:S(2)}, u32[]{:S(2)}) async-start(f32[32,1,2688]{2,1,0:T(1,128)} %reshape.996), calls=%async_computation | async-start | bytes 688128 | tf_op jit(solution)/shard_map/all_to_all | solution.py:93
  24.5 9.6 %all-to-all-done = f32[32,1,2688]{2,1,0:T(1,128)S(1)} async-done(((f32[32,1,2688]{2,1,0:T(1,128)}), f32[32,1,2688]{2,1,0:T(1,128)S(1)}, u32[]{:S(2)}, u32[]{:S(2)}) %all-to-all-start) | async-done | bytes 344096 | tf_op jit(solution)/shard_map/all_to_all | solution.py:93
  36.0 2.3 %reshape.997 = f32[128,4,8,21]{3,2,1,0:T(8,128)S(1)} reshape(f32[32,2688]{1,0:T(8,128)S(1)} %reduce.34) | data formatting | bytes 688128
  39.8 2.3 %copy.2225 = f32[21,256,4,4]{1,2,3,0:T(4,128)S(1)} copy(f32[21,256,4,4]{0,1,3,2:T(8,128)} %bitcast.526) | data formatting | bytes 688128 | tf_op jit(solution)/shard_map/all_to_all | solution.py:93
  45.1 2.2 %collective-permute-done.3 = f32[2,1,4,12,256]{4,2,3,1,0:T(4,128)S(1)} collective-permute-done((f32[2,1,4,12,256]{4,2,3,1,0:T(4,128)S(1)}, f32[2,1,4,12,256]{4,2,3,1,0:T(4,128)S(1)}, u32[]{:S(2)}, u32[]{:S(2)}) %collective-permute-start.3) | collective-permute-done | bytes 98336 | tf_op jit(solution)/shard_map/ppermute | solution.py:23
  48.0 5.2 %collective-permute-start.4 = (f32[2,1,4,24,256]{4,3,2,1,0:T(8,128)S(1)}, f32[2,1,4,24,256]{4,3,2,1,0:T(8,128)S(1)}, u32[]{:S(2)}, u32[]{:S(2)}) collective-permute-start(f32[2,1,4,24,256]{4,3,2,1,0:T(8,128)S(1)} %pad_maximum_fusion.10), channel_id=1, source_target_pairs={{0,1},{1,2},{2,3},{3,4},{4,5},{5,6},{6,7},{7,8},{8,9},{9,10},{10,1... | collective-permute-start | bytes 589832 | tf_op jit(solution)/shard_map/ppermute | solution.py:20
  59.8 10.4 %all-to-all-start.1 = ((f32[32,1,128]{2,1,0:T(1,128)}), f32[32,1,128]{2,1,0:T(1,128)S(1)}, u32[]{:S(2)}, u32[]{:S(2)}) async-start(f32[32,1,128]{2,1,0:T(1,128)} %broadcast_in_dim.8), calls=%async_computation.1 | async-start | bytes 32768 | tf_op jit(solution)/shard_map/all_to_all | solution.py:35
  75.0 2.2 %all-to-all-done.1 = f32[32,1,128]{2,1,0:T(1,128)S(1)} async-done(((f32[32,1,128]{2,1,0:T(1,128)}), f32[32,1,128]{2,1,0:T(1,128)S(1)}, u32[]{:S(2)}, u32[]{:S(2)}) %all-to-all-start.1) | async-done | bytes 16416 | tf_op jit(solution)/shard_map/all_to_all | solution.py:35
  82.6 2.0 collective-permute-done.6
  86.3 6.1 %collective-permute-start.8 = (f32[2,1,4,24,256]{4,3,2,1,0:T(8,128)S(1)}, f32[2,1,4,24,256]{4,3,2,1,0:T(8,128)S(1)}, u32[]{:S(2)}, u32[]{:S(2)}) collective-permute-start(f32[2,1,4,24,256]{4,3,2,1,0:T(8,128)S(1)} %pad_maximum_fusion.12), channel_id=1, source_target_pairs={{0,1},{1,2},{2,3},{3,4},{4,5},{5,6},{6,7},{7,8},{8,9},{9,10},{10,1... | collective-permute-start | bytes 589832 | tf_op jit(solution)/shard_map/ppermute | solution.py:20
  93.7 2.0 %collective-permute-done.9 = f32[2,1,4,24,256]{4,3,2,1,0:T(8,128)S(1)} collective-permute-done((f32[2,1,4,24,256]{4,3,2,1,0:T(8,128)S(1)}, f32[2,1,4,24,256]{4,3,2,1,0:T(8,128)S(1)}, u32[]{:S(2)}, u32[]{:S(2)}) %collective-permute-start.9) | collective-permute-done | bytes 196640 | tf_op jit(solution)/shard_map/ppermute | solution.py:23
  100.9 10.4 %all-to-all-start.2 = ((f32[32,1,128]{2,1,0:T(1,128)}), f32[32,1,128]{2,1,0:T(1,128)S(1)}, u32[]{:S(2)}, u32[]{:S(2)}) async-start(f32[32,1,128]{2,1,0:T(1,128)} %broadcast_in_dim.9), calls=%async_computation.2 | async-start | bytes 32768 | tf_op jit(solution)/shard_map/all_to_all | solution.py:35
  112.2 6.2 %all-to-all-done.2 = f32[32,1,128]{2,1,0:T(1,128)S(1)} async-done(((f32[32,1,128]{2,1,0:T(1,128)}), f32[32,1,128]{2,1,0:T(1,128)S(1)}, u32[]{:S(2)}, u32[]{:S(2)}) %all-to-all-start.2) | async-done | bytes 16416 | tf_op jit(solution)/shard_map/all_to_all | solution.py:35
  123.6 2.2 %collective-permute-done.10 = f32[2,1,4,24,256]{4,3,2,1,0:T(8,128)S(1)} collective-permute-done((f32[2,1,4,24,256]{4,3,2,1,0:T(8,128)S(1)}, f32[2,1,4,24,256]{4,3,2,1,0:T(8,128)S(1)}, u32[]{:S(2)}, u32[]{:S(2)}) %collective-permute-start.10) | collective-permute-done | bytes 196640 | tf_op jit(solution)/shard_map/ppermute | solution.py:23
  127.4 6.1 %collective-permute-start.12 = (f32[2,1,4,24,256]{4,3,2,1,0:T(8,128)S(1)}, f32[2,1,4,24,256]{4,3,2,1,0:T(8,128)S(1)}, u32[]{:S(2)}, u32[]{:S(2)}) collective-permute-start(f32[2,1,4,24,256]{4,3,2,1,0:T(8,128)S(1)} %pad_maximum_fusion.14), channel_id=1, source_target_pairs={{0,1},{1,2},{2,3},{3,4},{4,5},{5,6},{6,7},{7,8},{8,9},{9,10},{10,1... | collective-permute-start | bytes 589832 | tf_op jit(solution)/shard_map/ppermute | solution.py:20
  134.8 2.0 %collective-permute-done.13 = f32[2,1,4,24,256]{4,3,2,1,0:T(8,128)S(1)} collective-permute-done((f32[2,1,4,24,256]{4,3,2,1,0:T(8,128)S(1)}, f32[2,1,4,24,256]{4,3,2,1,0:T(8,128)S(1)}, u32[]{:S(2)}, u32[]{:S(2)}) %collective-permute-start.13) | collective-permute-done | bytes 196640 | tf_op jit(solution)/shard_map/ppermute | solution.py:23
  144.2 6.3 %collective-permute-start.15 = (f32[3,1,4,24,256]{4,3,2,1,0:T(8,128)S(1)}, f32[3,1,4,24,256]{4,3,2,1,0:T(8,128)S(1)}, u32[]{:S(2)}, u32[]{:S(2)}) collective-permute-start(f32[3,1,4,24,256]{4,3,2,1,0:T(8,128)S(1)} %pad_maximum_fusion.8), channel_id=1, source_target_pairs={{0,1},{1,2},{2,3},{3,4},{4,5},{5,6},{6,7},{7,8},{8,9},{9,10},{10,1... | collective-permute-start | bytes 884744 | tf_op jit(solution)/shard_map/ppermute | solution.py:20
  157.3 8.8 %collective-permute-start.16 = (f32[3,1,4,24,256]{4,3,2,1,0:T(8,128)S(1)}, f32[3,1,4,24,256]{4,3,2,1,0:T(8,128)S(1)}, u32[]{:S(2)}, u32[]{:S(2)}) collective-permute-start(f32[3,1,4,24,256]{4,3,2,1,0:T(8,128)S(1)} %pad_maximum_fusion.9), channel_id=1, source_target_pairs={{0,1},{1,2},{2,3},{3,4},{4,5},{5,6},{6,7},{7,8},{8,9},{9,10},{10,1... | collective-permute-start | bytes 884744 | tf_op jit(solution)/shard_map/ppermute | solution.py:20
  171.2 3.2 %subtract_multiply_fusion = f32[3,1,4,12,256]{4,2,3,1,0:T(4,128)S(1)} fusion(f32[3,1,4,12,256]{4,2,3,1,0:T(4,128)} %get-tuple-element.275, f32[3,1,4,12,256]{4,3,2,1,0:T(8,128)S(1)} %slice.4182, f32[3,1,4,12,256]{4,3,2,1,0:T(8,128)} %get-tuple-element.200, f32[3,1,4,12,256]{4,3,2,1,0:T(8,128)} %get-tuple-element.197, ...), kind=kLoop, calls=%fused_computation.437 | loop fusion | flops 1437696 | bytes 1867776 | tf_op jit(solution)/shard_map/mul | solution.py:177
  176.9 13.4 %all-to-all-start.3 = ((f32[32,1,768]{2,1,0:T(1,128)}), f32[32,1,768]{2,1,0:T(1,128)S(1)}, u32[]{:S(2)}, u32[]{:S(2)}) async-start(f32[32,1,768]{2,1,0:T(1,128)} %all_to_all.33), calls=%async_computation.3 | async-start | bytes 196608 | tf_op jit(solution)/shard_map/all_to_all | solution.py:230
  191.6 6.4 %all-to-all-done.3 = f32[32,1,768]{2,1,0:T(1,128)S(1)} async-done(((f32[32,1,768]{2,1,0:T(1,128)}), f32[32,1,768]{2,1,0:T(1,128)S(1)}, u32[]{:S(2)}, u32[]{:S(2)}) %all-to-all-start.3) | async-done | bytes 98336 | tf_op jit(solution)/shard_map/all_to_all | solution.py:230
  (333 shorter events, 71.5 us)
Async XLA Ops:
  1.5 22.4 %collective-permute-start = (f32[2,1,4,12,256]{4,2,3,1,0:T(4,128)S(1)}, f32[2,1,4,12,256]{4,2,3,1,0:T(4,128)S(1)}, u32[]{:S(2)}, u32[]{:S(2)}) collective-permute-start(f32[2,1,4,12,256]{4,2,3,1,0:T(4,128)S(1)} %slice_bitcast_fusion.3), channel_id=1, source_target_pairs={{1,0},{2,1},{3,2},{4,3},{5,4},{6,5},{7,6},{8,7},{9,8},{10,9},{11,1... | collective-permute-start | bytes 294920 | tf_op jit(solution)/shard_map/ppermute | solution.py:23
  2.8 21.1 %collective-permute-start.1 = (f32[2,1,4,12,256]{4,2,3,1,0:T(4,128)S(1)}, f32[2,1,4,12,256]{4,2,3,1,0:T(4,128)S(1)}, u32[]{:S(2)}, u32[]{:S(2)}) collective-permute-start(f32[2,1,4,12,256]{4,2,3,1,0:T(4,128)S(1)} %slice_bitcast_fusion.3), channel_id=1, source_target_pairs={{0,1},{1,2},{2,3},{3,4},{4,5},{5,6},{6,7},{7,8},{8,9},{9,10},{10,1... | collective-permute-start | bytes 294920 | tf_op jit(solution)/shard_map/ppermute | solution.py:20
  13.0 21.1 %all-to-all-start = ((f32[32,1,2688]{2,1,0:T(1,128)}), f32[32,1,2688]{2,1,0:T(1,128)S(1)}, u32[]{:S(2)}, u32[]{:S(2)}) async-start(f32[32,1,2688]{2,1,0:T(1,128)} %reshape.996), calls=%async_computation | async-start | bytes 688128 | tf_op jit(solution)/shard_map/all_to_all | solution.py:93
  22.6 97.2 %copy-start.41 = (pred[128]{0:T(512)(128)(4,1)}, pred[128]{0:T(512)(128)(4,1)S(1)}, u32[]{:S(2)}) copy-start(pred[128]{0:T(512)(128)(4,1)S(1)} %get-tuple-element.191) | copy-start | bytes 388
  23.9 95.8 %copy-start.35 = (s32[4,256]{1,0:T(4,128)}, s32[4,256]{1,0:T(4,128)S(1)}, u32[]{:S(2)}) copy-start(s32[4,256]{1,0:T(4,128)S(1)} %multiply_add_fusion.30) | copy-start | bytes 12292
  42.2 2.8 %collective-permute-start.2 = (f32[2,1,4,12,256]{4,2,3,1,0:T(4,128)S(1)}, f32[2,1,4,12,256]{4,2,3,1,0:T(4,128)S(1)}, u32[]{:S(2)}, u32[]{:S(2)}) collective-permute-start(f32[2,1,4,12,256]{4,2,3,1,0:T(4,128)S(1)} %copy_dynamic-update-slice_fusion), channel_id=1, source_target_pairs={{0,1},{1,2},{2,3},{3,4},{4,5},{5,6},{6,7},{7,8},{8,9},{9,10},{10,1... | collective-permute-start | bytes 294920 | tf_op jit(solution)/shard_map/ppermute | solution.py:20
  43.6 3.6 %collective-permute-start.3 = (f32[2,1,4,12,256]{4,2,3,1,0:T(4,128)S(1)}, f32[2,1,4,12,256]{4,2,3,1,0:T(4,128)S(1)}, u32[]{:S(2)}, u32[]{:S(2)}) collective-permute-start(f32[2,1,4,12,256]{4,2,3,1,0:T(4,128)S(1)} %copy_dynamic-update-slice_fusion), channel_id=1, source_target_pairs={{1,0},{2,1},{3,2},{4,3},{5,4},{6,5},{7,6},{8,7},{9,8},{10,9},{11,1... | collective-permute-start | bytes 294920 | tf_op jit(solution)/shard_map/ppermute | solution.py:23
  48.0 6.6 %collective-permute-start.4 = (f32[2,1,4,24,256]{4,3,2,1,0:T(8,128)S(1)}, f32[2,1,4,24,256]{4,3,2,1,0:T(8,128)S(1)}, u32[]{:S(2)}, u32[]{:S(2)}) collective-permute-start(f32[2,1,4,24,256]{4,3,2,1,0:T(8,128)S(1)} %pad_maximum_fusion.10), channel_id=1, source_target_pairs={{0,1},{1,2},{2,3},{3,4},{4,5},{5,6},{6,7},{7,8},{8,9},{9,10},{10,1... | collective-permute-start | bytes 589832 | tf_op jit(solution)/shard_map/ppermute | solution.py:20
  53.2 3.3 %collective-permute-start.5 = (f32[2,1,4,24,256]{4,3,2,1,0:T(8,128)S(1)}, f32[2,1,4,24,256]{4,3,2,1,0:T(8,128)S(1)}, u32[]{:S(2)}, u32[]{:S(2)}) collective-permute-start(f32[2,1,4,24,256]{4,3,2,1,0:T(8,128)S(1)} %pad_maximum_fusion.10), channel_id=1, source_target_pairs={{1,0},{2,1},{3,2},{4,3},{5,4},{6,5},{7,6},{8,7},{9,8},{10,9},{11,1... | collective-permute-start | bytes 589832 | tf_op jit(solution)/shard_map/ppermute | solution.py:23
  59.8 17.5 %all-to-all-start.1 = ((f32[32,1,128]{2,1,0:T(1,128)}), f32[32,1,128]{2,1,0:T(1,128)S(1)}, u32[]{:S(2)}, u32[]{:S(2)}) async-start(f32[32,1,128]{2,1,0:T(1,128)} %broadcast_in_dim.8), calls=%async_computation.1 | async-start | bytes 32768 | tf_op jit(solution)/shard_map/all_to_all | solution.py:35
  79.2 3.4 %collective-permute-start.7 = (f32[2,1,4,24,256]{4,3,2,1,0:T(8,128)S(1)}, f32[2,1,4,24,256]{4,3,2,1,0:T(8,128)S(1)}, u32[]{:S(2)}, u32[]{:S(2)}) collective-permute-start(f32[2,1,4,24,256]{4,3,2,1,0:T(8,128)S(1)} %pad_maximum_fusion.11), channel_id=1, source_target_pairs={{0,1},{1,2},{2,3},{3,4},{4,5},{5,6},{6,7},{7,8},{8,9},{9,10},{10,1... | collective-permute-start | bytes 589832 | tf_op jit(solution)/shard_map/ppermute | solution.py:20
  81.0 3.6 %collective-permute-start.6 = (f32[2,1,4,24,256]{4,3,2,1,0:T(8,128)S(1)}, f32[2,1,4,24,256]{4,3,2,1,0:T(8,128)S(1)}, u32[]{:S(2)}, u32[]{:S(2)}) collective-permute-start(f32[2,1,4,24,256]{4,3,2,1,0:T(8,128)S(1)} %pad_maximum_fusion.11), channel_id=1, source_target_pairs={{1,0},{2,1},{3,2},{4,3},{5,4},{6,5},{7,6},{8,7},{9,8},{10,9},{11,1... | collective-permute-start | bytes 589832 | tf_op jit(solution)/shard_map/ppermute | solution.py:23
  86.3 7.4 %collective-permute-start.8 = (f32[2,1,4,24,256]{4,3,2,1,0:T(8,128)S(1)}, f32[2,1,4,24,256]{4,3,2,1,0:T(8,128)S(1)}, u32[]{:S(2)}, u32[]{:S(2)}) collective-permute-start(f32[2,1,4,24,256]{4,3,2,1,0:T(8,128)S(1)} %pad_maximum_fusion.12), channel_id=1, source_target_pairs={{0,1},{1,2},{2,3},{3,4},{4,5},{5,6},{6,7},{7,8},{8,9},{9,10},{10,1... | collective-permute-start | bytes 589832 | tf_op jit(solution)/shard_map/ppermute | solution.py:20
  92.4 3.3 %collective-permute-start.9 = (f32[2,1,4,24,256]{4,3,2,1,0:T(8,128)S(1)}, f32[2,1,4,24,256]{4,3,2,1,0:T(8,128)S(1)}, u32[]{:S(2)}, u32[]{:S(2)}) collective-permute-start(f32[2,1,4,24,256]{4,3,2,1,0:T(8,128)S(1)} %pad_maximum_fusion.12), channel_id=1, source_target_pairs={{1,0},{2,1},{3,2},{4,3},{5,4},{6,5},{7,6},{8,7},{9,8},{10,9},{11,1... | collective-permute-start | bytes 589832 | tf_op jit(solution)/shard_map/ppermute | solution.py:23
  100.9 17.5 %all-to-all-start.2 = ((f32[32,1,128]{2,1,0:T(1,128)}), f32[32,1,128]{2,1,0:T(1,128)S(1)}, u32[]{:S(2)}, u32[]{:S(2)}) async-start(f32[32,1,128]{2,1,0:T(1,128)} %broadcast_in_dim.9), calls=%async_computation.2 | async-start | bytes 32768 | tf_op jit(solution)/shard_map/all_to_all | solution.py:35
  120.3 3.2 %collective-permute-start.11 = (f32[2,1,4,24,256]{4,3,2,1,0:T(8,128)S(1)}, f32[2,1,4,24,256]{4,3,2,1,0:T(8,128)S(1)}, u32[]{:S(2)}, u32[]{:S(2)}) collective-permute-start(f32[2,1,4,24,256]{4,3,2,1,0:T(8,128)S(1)} %pad_maximum_fusion.13), channel_id=1, source_target_pairs={{0,1},{1,2},{2,3},{3,4},{4,5},{5,6},{6,7},{7,8},{8,9},{9,10},{10,1... | collective-permute-start | bytes 589832 | tf_op jit(solution)/shard_map/ppermute | solution.py:20
  122.1 3.6 %collective-permute-start.10 = (f32[2,1,4,24,256]{4,3,2,1,0:T(8,128)S(1)}, f32[2,1,4,24,256]{4,3,2,1,0:T(8,128)S(1)}, u32[]{:S(2)}, u32[]{:S(2)}) collective-permute-start(f32[2,1,4,24,256]{4,3,2,1,0:T(8,128)S(1)} %pad_maximum_fusion.13), channel_id=1, source_target_pairs={{1,0},{2,1},{3,2},{4,3},{5,4},{6,5},{7,6},{8,7},{9,8},{10,9},{11,1... | collective-permute-start | bytes 589832 | tf_op jit(solution)/shard_map/ppermute | solution.py:23
  127.4 7.4 %collective-permute-start.12 = (f32[2,1,4,24,256]{4,3,2,1,0:T(8,128)S(1)}, f32[2,1,4,24,256]{4,3,2,1,0:T(8,128)S(1)}, u32[]{:S(2)}, u32[]{:S(2)}) collective-permute-start(f32[2,1,4,24,256]{4,3,2,1,0:T(8,128)S(1)} %pad_maximum_fusion.14), channel_id=1, source_target_pairs={{0,1},{1,2},{2,3},{3,4},{4,5},{5,6},{6,7},{7,8},{8,9},{9,10},{10,1... | collective-permute-start | bytes 589832 | tf_op jit(solution)/shard_map/ppermute | solution.py:20
  133.5 3.3 %collective-permute-start.13 = (f32[2,1,4,24,256]{4,3,2,1,0:T(8,128)S(1)}, f32[2,1,4,24,256]{4,3,2,1,0:T(8,128)S(1)}, u32[]{:S(2)}, u32[]{:S(2)}) collective-permute-start(f32[2,1,4,24,256]{4,3,2,1,0:T(8,128)S(1)} %pad_maximum_fusion.14), channel_id=1, source_target_pairs={{1,0},{2,1},{3,2},{4,3},{5,4},{6,5},{7,6},{8,7},{9,8},{10,9},{11,1... | collective-permute-start | bytes 589832 | tf_op jit(solution)/shard_map/ppermute | solution.py:23
  144.2 8.9 %collective-permute-start.15 = (f32[3,1,4,24,256]{4,3,2,1,0:T(8,128)S(1)}, f32[3,1,4,24,256]{4,3,2,1,0:T(8,128)S(1)}, u32[]{:S(2)}, u32[]{:S(2)}) collective-permute-start(f32[3,1,4,24,256]{4,3,2,1,0:T(8,128)S(1)} %pad_maximum_fusion.8), channel_id=1, source_target_pairs={{0,1},{1,2},{2,3},{3,4},{4,5},{5,6},{6,7},{7,8},{8,9},{9,10},{10,1... | collective-permute-start | bytes 884744 | tf_op jit(solution)/shard_map/ppermute | solution.py:20
  150.5 3.5 %collective-permute-start.14 = (f32[3,1,4,24,256]{4,3,2,1,0:T(8,128)S(1)}, f32[3,1,4,24,256]{4,3,2,1,0:T(8,128)S(1)}, u32[]{:S(2)}, u32[]{:S(2)}) collective-permute-start(f32[3,1,4,24,256]{4,3,2,1,0:T(8,128)S(1)} %pad_maximum_fusion.8), channel_id=1, source_target_pairs={{1,0},{2,1},{3,2},{4,3},{5,4},{6,5},{7,6},{8,7},{9,8},{10,9},{11,1... | collective-permute-start | bytes 884744 | tf_op jit(solution)/shard_map/ppermute | solution.py:23
  156.0 11.4 %collective-permute-start.17 = (f32[3,1,4,24,256]{4,3,2,1,0:T(8,128)S(1)}, f32[3,1,4,24,256]{4,3,2,1,0:T(8,128)S(1)}, u32[]{:S(2)}, u32[]{:S(2)}) collective-permute-start(f32[3,1,4,24,256]{4,3,2,1,0:T(8,128)S(1)} %pad_maximum_fusion.9), channel_id=1, source_target_pairs={{1,0},{2,1},{3,2},{4,3},{5,4},{6,5},{7,6},{8,7},{9,8},{10,9},{11,1... | collective-permute-start | bytes 884744 | tf_op jit(solution)/shard_map/ppermute | solution.py:23
  157.3 10.2 %collective-permute-start.16 = (f32[3,1,4,24,256]{4,3,2,1,0:T(8,128)S(1)}, f32[3,1,4,24,256]{4,3,2,1,0:T(8,128)S(1)}, u32[]{:S(2)}, u32[]{:S(2)}) collective-permute-start(f32[3,1,4,24,256]{4,3,2,1,0:T(8,128)S(1)} %pad_maximum_fusion.9), channel_id=1, source_target_pairs={{0,1},{1,2},{2,3},{3,4},{4,5},{5,6},{6,7},{7,8},{8,9},{9,10},{10,1... | collective-permute-start | bytes 884744 | tf_op jit(solution)/shard_map/ppermute | solution.py:20
  176.9 21.2 %all-to-all-start.3 = ((f32[32,1,768]{2,1,0:T(1,128)}), f32[32,1,768]{2,1,0:T(1,128)S(1)}, u32[]{:S(2)}, u32[]{:S(2)}) async-start(f32[32,1,768]{2,1,0:T(1,128)} %all_to_all.33), calls=%async_computation.3 | async-start | bytes 196608 | tf_op jit(solution)/shard_map/all_to_all | solution.py:230
  (52 other events, 562.6 us)

commit v7 on v5

--- a/solution.py
+++ b/solution.py
@@ -28,6 +28,13 @@
         out.append(lax.slice_in_dim(padded, start, start + depth, axis=DEPTH_AXIS))
         start += depth
     return out
+
+
+def fill_waves(field, waves):
+    extra = waves - field.shape[0]
+    if extra == 0:
+        return field
+    return jnp.concatenate([field, jnp.zeros((extra,) + field.shape[1:], field.dtype)])
 
 
 def gather_sum(partial, parts):
@@ -128,9 +135,26 @@
     kappa_acc = jnp.zeros((1, shots) + water_kappa.shape, jnp.float32)
     early_misfits = []
     late_records = []
+    pending = []
     for step in range(steps):
+        if pending and pending[0][0] == step - 2:
+            _, saved_floor = pending.pop(0)
+            rock_zero = jnp.zeros((1,) + vel_x.shape[1:], jnp.float32)
+            vel_x, vel_y, vel_z = [jnp.concatenate([f, rock_zero]) for f in (vel_x, vel_y, vel_z)]
+            sig_xx, sig_yy, sig_xy, sig_xz, sig_yz = [
+                jnp.concatenate([f, rock_zero]) for f in (sig_xx, sig_yy, sig_xy, sig_xz, sig_yz)
+            ]
+            sig_zz = jnp.concatenate([sig_zz, rock_zero.at[:, :, :, 0, :].set(-saved_floor)])
+            lam_acc = jnp.concatenate([lam_acc, jnp.zeros((1,) + lam_acc.shape[1:], jnp.float32)])
+            mu_acc = jnp.concatenate([mu_acc, jnp.zeros((1,) + mu_acc.shape[1:], jnp.float32)])
+        rock_waves = vel_x.shape[0]
+        water_waves = pressure.shape[0]
         floor_pressure = jnp.sum(pressure * bottom, axis=3)
-        sxy_pad, syy_pad, syz_pad, p_pad = halo_rows([sig_xy, sig_yy, sig_yz, pressure])
+        pending = [(at, floor_pressure[rock_waves + i : rock_waves + i + 1]) for i, (at, _) in enumerate(pending)]
+        sxy_pad, syy_pad, syz_pad, p_pad = halo_rows(
+            [fill_waves(f, water_waves) for f in (sig_xy, sig_yy, sig_yz)] + [pressure]
+        )
+        sxy_pad, syy_pad, syz_pad = [f[:rock_waves] for f in (sxy_pad, syy_pad, syz_pad)]
         vel_x = vel_x + TIME_STEP * buoy * (
             derive(sig_xx, 4, True) + stencil(sxy_pad, 2, False) + derive(sig_xz, 3, False)
         )
@@ -140,13 +164,16 @@
         vel_z = vel_z + TIME_STEP * buoy * (
             derive(sig_xz, 4, False) + stencil(syz_pad, 2, False) + derive(sig_zz, 3, True)
         )
-        floor_velocity = vel_z[:, :, :, 0, :]
+        floor_velocity = fill_waves(vel_z[:, :, :, 0, :], water_waves)
         flow_x = (flow_x - TIME_STEP * water_buoy * derive(pressure, 4, True)) * live
         flow_y = (flow_y - TIME_STEP * water_buoy * stencil(p_pad, 2, True)) * live
         flow_z = (
             flow_z - TIME_STEP * water_buoy * derive(pressure, 3, True)
         ) * above + floor_velocity[:, :, :, None, :] * bottom
-        vx_pad, vy_pad, vz_pad, uy_pad = halo_rows([vel_x, vel_y, vel_z, flow_y])
+        vx_pad, vy_pad, vz_pad, uy_pad = halo_rows(
+            [fill_waves(f, water_waves) for f in (vel_x, vel_y, vel_z)] + [flow_y]
+        )
+        vx_pad, vy_pad, vz_pad = [f[:rock_waves] for f in (vx_pad, vy_pad, vz_pad)]
         strain_x = derive(vel_x, 4, False)
         strain_y = stencil(vy_pad, 2, False)
         strain_z = derive(vel_z, 3, False)
@@ -161,7 +188,7 @@
         sig_xy = sig_xy + TIME_STEP * mu * shear_xy
         sig_xz = sig_xz + TIME_STEP * mu * shear_xz
         sig_yz = sig_yz + TIME_STEP * mu * shear_yz
-        sig_zz = sig_zz.at[:, :, :, 0, :].set(-floor_pressure)
+        sig_zz = sig_zz.at[:, :, :, 0, :].set(-floor_pressure[:rock_waves])
         lam_acc = lam_acc + dilation[:1] * dilation[1:]
         normal_part = (
             strain_x[:1] * strain_x[1:] + strain_y[:1] * strain_y[1:] + strain_z[:1] * strain_z[1:]
@@ -204,17 +231,10 @@
             [kappa_acc + pressure[:1] * pressure[1:], (pressure[0] * kick)[None]], axis=0
         )
         if step + 1 < steps:
-            rock_zero = jnp.zeros((1,) + vel_x.shape[1:], jnp.float32)
             water_zero = jnp.zeros((1,) + flow_x.shape[1:], jnp.float32)
-            vel_x, vel_y, vel_z = [jnp.concatenate([f, rock_zero]) for f in (vel_x, vel_y, vel_z)]
-            sig_xx, sig_yy, sig_zz, sig_xy, sig_xz, sig_yz = [
-                jnp.concatenate([f, rock_zero])
-                for f in (sig_xx, sig_yy, sig_zz, sig_xy, sig_xz, sig_yz)
-            ]
             flow_x, flow_y, flow_z = [jnp.concatenate([f, water_zero]) for f in (flow_x, flow_y, flow_z)]
             pressure = jnp.concatenate([pressure, kick[None]])
-            lam_acc = jnp.concatenate([lam_acc, jnp.zeros((1,) + lam_acc.shape[1:], jnp.float32)])
-            mu_acc = jnp.concatenate([mu_acc, jnp.zeros((1,) + mu_acc.shape[1:], jnp.float32)])
+            pending.append((step, None))
 
     slots = lam_acc.shape[0]
     rock_acc = jnp.concatenate([lam_acc, mu_acc]).reshape(

time: 194 us -> 186 us (0.959)
  other arithmetic: 32.1 us -> 27.1 us
  waiting for transfers between devices: 40.6 us -> 36.1 us
  starting transfers between devices: 89.7 us -> 92.6 us
    ppermute x8, waiting for transfers between devices: 12.9 us -> 3.99 us  [halo_rows(): lax.ppermute(lax.slice_in_dim(packed, 0, HALO, axis=ROW_AXIS), 'gx', down)]
    ppermute x8, starting transfers between devices: 38.1 us -> 44.6 us  [halo_rows(): lax.ppermute(lax.slice_in_dim(packed, length - HALO, length, axis=ROW_AXI...]
    ppermute x8, waiting for transfers between devices: 0.02 us -> 5.66 us  [halo_rows(): lax.ppermute(lax.slice_in_dim(packed, length - HALO, length, axis=ROW_AXI...]
    all_to_all x1, starting transfers between devices: 13.8 us -> 10.1 us  [on_device(): got = lax.all_to_all(packed, 'gx', 0, 0, tiled=True)]
    mul x4, other arithmetic: 3.63 us -> 1.44 us  [on_device(): (pressure - TIME_STEP * water_kappa * (derive(flow_x, 4, False) + stencil...]
    unnamed x111 -> x130, local copies, waits for them, and re-layouts: 9.62 us -> 10.1 us
  transfers between devices with their start and end apart: 20 -> 20, of which waited for: 11 -> 12; matrix products, arithmetic and copies ran while one was open for 4% -> 4% of each run, Pallas kernels for 0% -> 0%
where the time goes in v7:
time: 186 us; the launch traced here: 185 us
  starting transfers between devices  92.6 us (50%)
  waiting for transfers between devices  36.1 us (19%)
  other arithmetic  27.1 us (15%)
  local copies, waits for them, and re-layouts  21.1 us (11%)
  between operations  4.35 us (2%)
  matrix products  3.43 us (2%)
    ppermute x8, starting transfers between devices, halo_rows(): lax.ppermute(lax.slice_in_dim(packed, length - HALO, length, axis=ROW_AXI...  44.6 us
    all_to_all x2, starting transfers between devices, gather_sum(): return jnp.sum(lax.all_to_all(copies, 'gx', 0, 0, tiled=True), axis=0)  20.3 us
    all_to_all x1, waiting for transfers between devices, on_device(): lax.all_to_all(rock_in, 'gx', split_axis=3, concat_axis=1, tiled=True)  10.6 us
    ppermute x8, starting transfers between devices, halo_rows(): lax.ppermute(lax.slice_in_dim(packed, 0, HALO, axis=ROW_AXIS), 'gx', down)  10.3 us
    all_to_all x1, starting transfers between devices, on_device(): got = lax.all_to_all(packed, 'gx', 0, 0, tiled=True)  10.1 us
    all_to_all x2, waiting for transfers between devices, gather_sum(): return jnp.sum(lax.all_to_all(copies, 'gx', 0, 0, tiled=True), axis=0)  10.1 us
    unnamed x130, local copies, waits for them, and re-layouts  10.1 us
    all_to_all x1, starting transfers between devices, on_device(): lax.all_to_all(rock_in, 'gx', split_axis=3, concat_axis=1, tiled=True)  7.3 us
  transfers between devices with their start and end apart: 20, of which 12 were waited for; matrix products, arithmetic and copies ran while one was open for 4% of the time, Pallas kernels for 0%

profile of v7, /device:TPU:0, one launch (start us, length us, event | category | flops | bytes accessed | tf_op | source)
XLA Modules:
  0.0 184.7 jit_solution(18311607117074692580)
XLA Ops:
  3.1 1.9 %copy.2465 = f32[21,8,4,128]{0,1,2,3:T(8,128)S(1)} copy(f32[21,8,4,128]{3,1,2,0:T(8,128)S(1)} %pad_maximum_fusion.8) | data formatting | bytes 688128 | tf_op jit(solution)/shard_map/concatenate | solution.py:92
  5.1 2.7 %reshape.974 = f32[32,1,2688]{2,1,0:T(1,128)} reshape(f32[128,4,8,21]{3,2,1,0:T(8,128)S(1)} %bitcast.595) | data formatting | bytes 688128
  7.7 7.3 %all-to-all-start = ((f32[32,1,2688]{2,1,0:T(1,128)}), f32[32,1,2688]{2,1,0:T(1,128)S(1)}, u32[]{:S(2)}, u32[]{:S(2)}) async-start(f32[32,1,2688]{2,1,0:T(1,128)} %reshape.974), calls=%async_computation | async-start | bytes 688128 | tf_op jit(solution)/shard_map/all_to_all | solution.py:100
  16.8 10.6 %all-to-all-done = f32[32,1,2688]{2,1,0:T(1,128)S(1)} async-done(((f32[32,1,2688]{2,1,0:T(1,128)}), f32[32,1,2688]{2,1,0:T(1,128)S(1)}, u32[]{:S(2)}, u32[]{:S(2)}) %all-to-all-start) | async-done | bytes 344096 | tf_op jit(solution)/shard_map/all_to_all | solution.py:100
  27.8 1.5 reduce.32
  29.3 2.3 %reshape.975 = f32[128,4,8,21]{3,2,1,0:T(8,128)S(1)} reshape(f32[32,2688]{1,0:T(8,128)S(1)} %reduce.32) | data formatting | bytes 688128
  31.6 1.5 copy.2758
  33.1 2.3 %copy.2468 = f32[21,256,4,4]{1,2,3,0:T(4,128)S(1)} copy(f32[21,256,4,4]{0,1,3,2:T(8,128)} %bitcast.597) | data formatting | bytes 688128 | tf_op jit(solution)/shard_map/all_to_all | solution.py:100
  36.8 3.0 %collective-permute-start.1 = (f32[2,1,4,24,256]{4,3,2,1,0:T(8,128)S(1)}, f32[2,1,4,24,256]{4,3,2,1,0:T(8,128)S(1)}, u32[]{:S(2)}, u32[]{:S(2)}) collective-permute-start(f32[2,1,4,24,256]{4,3,2,1,0:T(8,128)S(1)} %pad_maximum_fusion.10), channel_id=1, source_target_pairs={{0,1},{1,2},{2,3},{3,4},{4,5},{5,6},{6,7},{7,8},{8,9},{9,10},{10,1... | collective-permute-start | bytes 589832 | tf_op jit(solution)/shard_map/ppermute | solution.py:20
  42.0 5.3 %collective-permute-start.2 = (f32[2,1,4,24,256]{4,3,2,1,0:T(8,128)S(1)}, f32[2,1,4,24,256]{4,3,2,1,0:T(8,128)S(1)}, u32[]{:S(2)}, u32[]{:S(2)}) collective-permute-start(f32[2,1,4,24,256]{4,3,2,1,0:T(8,128)S(1)} %pad_maximum_fusion.11), channel_id=1, source_target_pairs={{0,1},{1,2},{2,3},{3,4},{4,5},{5,6},{6,7},{7,8},{8,9},{9,10},{10,1... | collective-permute-start | bytes 589832 | tf_op jit(solution)/shard_map/ppermute | solution.py:20
  48.6 4.0 %collective-permute-done.3 = f32[2,1,4,24,256]{4,3,2,1,0:T(8,128)S(1)} collective-permute-done((f32[2,1,4,24,256]{4,3,2,1,0:T(8,128)S(1)}, f32[2,1,4,24,256]{4,3,2,1,0:T(8,128)S(1)}, u32[]{:S(2)}, u32[]{:S(2)}) %collective-permute-start.3) | collective-permute-done | bytes 196640 | tf_op jit(solution)/shard_map/ppermute | solution.py:23
  54.9 9.9 %all-to-all-start.1 = ((f32[32,1,128]{2,1,0:T(1,128)}), f32[32,1,128]{2,1,0:T(1,128)S(1)}, u32[]{:S(2)}, u32[]{:S(2)}) async-start(f32[32,1,128]{2,1,0:T(1,128)} %broadcast_in_dim.8), calls=%async_computation.1 | async-start | bytes 32768 | tf_op jit(solution)/shard_map/all_to_all | solution.py:42
  67.8 4.0 %all-to-all-done.1 = f32[32,1,128]{2,1,0:T(1,128)S(1)} async-done(((f32[32,1,128]{2,1,0:T(1,128)}), f32[32,1,128]{2,1,0:T(1,128)S(1)}, u32[]{:S(2)}, u32[]{:S(2)}) %all-to-all-start.1) | async-done | bytes 16416 | tf_op jit(solution)/shard_map/all_to_all | solution.py:42
  75.0 3.0 %collective-permute-start.5 = (f32[2,1,4,24,256]{4,3,2,1,0:T(8,128)S(1)}, f32[2,1,4,24,256]{4,3,2,1,0:T(8,128)S(1)}, u32[]{:S(2)}, u32[]{:S(2)}) collective-permute-start(f32[2,1,4,24,256]{4,3,2,1,0:T(8,128)S(1)} %pad_maximum_fusion.12), channel_id=1, source_target_pairs={{0,1},{1,2},{2,3},{3,4},{4,5},{5,6},{6,7},{7,8},{8,9},{9,10},{10,1... | collective-permute-start | bytes 589832 | tf_op jit(solution)/shard_map/ppermute | solution.py:20
  81.5 5.5 %collective-permute-start.6 = (f32[2,1,4,24,256]{4,3,2,1,0:T(8,128)S(1)}, f32[2,1,4,24,256]{4,3,2,1,0:T(8,128)S(1)}, u32[]{:S(2)}, u32[]{:S(2)}) collective-permute-start(f32[2,1,4,24,256]{4,3,2,1,0:T(8,128)S(1)} %pad_maximum_fusion.13), channel_id=1, source_target_pairs={{0,1},{1,2},{2,3},{3,4},{4,5},{5,6},{6,7},{7,8},{8,9},{9,10},{10,1... | collective-permute-start | bytes 589832 | tf_op jit(solution)/shard_map/ppermute | solution.py:20
  91.7 10.4 %all-to-all-start.2 = ((f32[32,1,128]{2,1,0:T(1,128)}), f32[32,1,128]{2,1,0:T(1,128)S(1)}, u32[]{:S(2)}, u32[]{:S(2)}) async-start(f32[32,1,128]{2,1,0:T(1,128)} %broadcast_in_dim.9), calls=%async_computation.2 | async-start | bytes 32768 | tf_op jit(solution)/shard_map/all_to_all | solution.py:42
  103.1 6.1 %all-to-all-done.2 = f32[32,1,128]{2,1,0:T(1,128)S(1)} async-done(((f32[32,1,128]{2,1,0:T(1,128)}), f32[32,1,128]{2,1,0:T(1,128)S(1)}, u32[]{:S(2)}, u32[]{:S(2)}) %all-to-all-start.2) | async-done | bytes 16416 | tf_op jit(solution)/shard_map/all_to_all | solution.py:42
  112.4 3.0 %collective-permute-start.9 = (f32[2,1,4,24,256]{4,3,2,1,0:T(8,128)S(1)}, f32[2,1,4,24,256]{4,3,2,1,0:T(8,128)S(1)}, u32[]{:S(2)}, u32[]{:S(2)}) collective-permute-start(f32[2,1,4,24,256]{4,3,2,1,0:T(8,128)S(1)} %pad_maximum_fusion.14), channel_id=1, source_target_pairs={{0,1},{1,2},{2,3},{3,4},{4,5},{5,6},{6,7},{7,8},{8,9},{9,10},{10,1... | collective-permute-start | bytes 589832 | tf_op jit(solution)/shard_map/ppermute | solution.py:20
  117.6 1.3 collective-permute-start.11
  118.9 5.3 %collective-permute-start.10 = (f32[2,1,4,24,256]{4,3,2,1,0:T(8,128)S(1)}, f32[2,1,4,24,256]{4,3,2,1,0:T(8,128)S(1)}, u32[]{:S(2)}, u32[]{:S(2)}) collective-permute-start(f32[2,1,4,24,256]{4,3,2,1,0:T(8,128)S(1)} %pad_maximum_fusion.15), channel_id=1, source_target_pairs={{0,1},{1,2},{2,3},{3,4},{4,5},{5,6},{6,7},{7,8},{8,9},{9,10},{10,1... | collective-permute-start | bytes 589832 | tf_op jit(solution)/shard_map/ppermute | solution.py:20
  133.1 9.1 %collective-permute-start.13 = (f32[3,1,4,24,256]{4,3,2,1,0:T(8,128)S(1)}, f32[3,1,4,24,256]{4,3,2,1,0:T(8,128)}, u32[]{:S(2)}, u32[]{:S(2)}) collective-permute-start(f32[3,1,4,24,256]{4,3,2,1,0:T(8,128)S(1)} %maximum_maximum_fusion.8), channel_id=1, source_target_pairs={{0,1},{1,2},{2,3},{3,4},{4,5},{5,6},{6,7},{7,8},{8,9},{9,10},{10,1... | collective-permute-start | bytes 884744 | tf_op jit(solution)/shard_map/ppermute | solution.py:20
  147.7 10.2 %collective-permute-start.14 = (f32[3,1,4,24,256]{4,3,2,1,0:T(8,128)S(1)}, f32[3,1,4,24,256]{4,3,2,1,0:T(8,128)S(1)}, u32[]{:S(2)}, u32[]{:S(2)}) collective-permute-start(f32[3,1,4,24,256]{4,3,2,1,0:T(8,128)S(1)} %pad_maximum_fusion.9), channel_id=1, source_target_pairs={{0,1},{1,2},{2,3},{3,4},{4,5},{5,6},{6,7},{7,8},{8,9},{9,10},{10,1... | collective-permute-start | bytes 884744 | tf_op jit(solution)/shard_map/ppermute | solution.py:20
  163.7 10.1 %all-to-all-start.3 = ((f32[32,1,512]{2,1,0:T(1,128)}), f32[32,1,512]{2,1,0:T(1,128)S(1)}, u32[]{:S(2)}, u32[]{:S(2)}) async-start(f32[32,1,512]{2,1,0:T(1,128)} %all_to_all.33), calls=%async_computation.3 | async-start | bytes 131072 | tf_op jit(solution)/shard_map/all_to_all | solution.py:246
  175.4 5.8 %all-to-all-done.3 = f32[32,1,512]{2,1,0:T(1,128)S(1)} async-done(((f32[32,1,512]{2,1,0:T(1,128)}), f32[32,1,512]{2,1,0:T(1,128)S(1)}, u32[]{:S(2)}, u32[]{:S(2)}) %all-to-all-start.3) | async-done | bytes 65568 | tf_op jit(solution)/shard_map/all_to_all | solution.py:246
  (295 shorter events, 54.3 us)
Async XLA Ops:
  7.7 19.6 %all-to-all-start = ((f32[32,1,2688]{2,1,0:T(1,128)}), f32[32,1,2688]{2,1,0:T(1,128)S(1)}, u32[]{:S(2)}, u32[]{:S(2)}) async-start(f32[32,1,2688]{2,1,0:T(1,128)} %reshape.974), calls=%async_computation | async-start | bytes 688128 | tf_op jit(solution)/shard_map/all_to_all | solution.py:100
  15.1 113.3 %copy-start.41 = (s32[4,256]{1,0:T(4,128)}, s32[4,256]{1,0:T(4,128)S(1)}, u32[]{:S(2)}) copy-start(s32[4,256]{1,0:T(4,128)S(1)} %multiply_add_fusion.18) | copy-start | bytes 12292
  16.7 110.5 %copy-start.35 = (s32[4,12]{1,0:T(4,128)}, s32[4,12]{1,0:T(4,128)S(1)}, u32[]{:S(2)}) copy-start(s32[4,12]{1,0:T(4,128)S(1)} %add_multiply_fusion) | copy-start | bytes 580
  16.7 111.7 %copy-start.46 = (pred[128]{0:T(512)(128)(4,1)}, pred[128]{0:T(512)(128)(4,1)S(1)}, u32[]{:S(2)}) copy-start(pred[128]{0:T(512)(128)(4,1)S(1)} %get-tuple-element.191) | copy-start | bytes 388
  16.7 114.3 %copy-start = (s32[4,256]{1,0:T(4,128)}, s32[4,256]{1,0:T(4,128)S(1)}, u32[]{:S(2)}) copy-start(s32[4,256]{1,0:T(4,128)S(1)} %broadcast_add_fusion) | copy-start | bytes 12292
  35.5 4.4 %collective-permute-start = (f32[2,1,4,24,256]{4,3,2,1,0:T(8,128)S(1)}, f32[2,1,4,24,256]{4,3,2,1,0:T(8,128)S(1)}, u32[]{:S(2)}, u32[]{:S(2)}) collective-permute-start(f32[2,1,4,24,256]{4,3,2,1,0:T(8,128)S(1)} %pad_maximum_fusion.10), channel_id=1, source_target_pairs={{1,0},{2,1},{3,2},{4,3},{5,4},{6,5},{7,6},{8,7},{9,8},{10,9},{11,1... | collective-permute-start | bytes 589832 | tf_op jit(solution)/shard_map/ppermute | solution.py:23
  36.8 4.1 %collective-permute-start.1 = (f32[2,1,4,24,256]{4,3,2,1,0:T(8,128)S(1)}, f32[2,1,4,24,256]{4,3,2,1,0:T(8,128)S(1)}, u32[]{:S(2)}, u32[]{:S(2)}) collective-permute-start(f32[2,1,4,24,256]{4,3,2,1,0:T(8,128)S(1)} %pad_maximum_fusion.10), channel_id=1, source_target_pairs={{0,1},{1,2},{2,3},{3,4},{4,5},{5,6},{6,7},{7,8},{8,9},{9,10},{10,1... | collective-permute-start | bytes 589832 | tf_op jit(solution)/shard_map/ppermute | solution.py:20
  42.0 6.6 %collective-permute-start.2 = (f32[2,1,4,24,256]{4,3,2,1,0:T(8,128)S(1)}, f32[2,1,4,24,256]{4,3,2,1,0:T(8,128)S(1)}, u32[]{:S(2)}, u32[]{:S(2)}) collective-permute-start(f32[2,1,4,24,256]{4,3,2,1,0:T(8,128)S(1)} %pad_maximum_fusion.11), channel_id=1, source_target_pairs={{0,1},{1,2},{2,3},{3,4},{4,5},{5,6},{6,7},{7,8},{8,9},{9,10},{10,1... | collective-permute-start | bytes 589832 | tf_op jit(solution)/shard_map/ppermute | solution.py:20
  47.3 5.3 %collective-permute-start.3 = (f32[2,1,4,24,256]{4,3,2,1,0:T(8,128)S(1)}, f32[2,1,4,24,256]{4,3,2,1,0:T(8,128)S(1)}, u32[]{:S(2)}, u32[]{:S(2)}) collective-permute-start(f32[2,1,4,24,256]{4,3,2,1,0:T(8,128)S(1)} %pad_maximum_fusion.11), channel_id=1, source_target_pairs={{1,0},{2,1},{3,2},{4,3},{5,4},{6,5},{7,6},{8,7},{9,8},{10,9},{11,1... | collective-permute-start | bytes 589832 | tf_op jit(solution)/shard_map/ppermute | solution.py:23
  54.9 17.0 %all-to-all-start.1 = ((f32[32,1,128]{2,1,0:T(1,128)}), f32[32,1,128]{2,1,0:T(1,128)S(1)}, u32[]{:S(2)}, u32[]{:S(2)}) async-start(f32[32,1,128]{2,1,0:T(1,128)} %broadcast_in_dim.8), calls=%async_computation.1 | async-start | bytes 32768 | tf_op jit(solution)/shard_map/all_to_all | solution.py:42
  73.7 4.5 %collective-permute-start.4 = (f32[2,1,4,24,256]{4,3,2,1,0:T(8,128)S(1)}, f32[2,1,4,24,256]{4,3,2,1,0:T(8,128)S(1)}, u32[]{:S(2)}, u32[]{:S(2)}) collective-permute-start(f32[2,1,4,24,256]{4,3,2,1,0:T(8,128)S(1)} %pad_maximum_fusion.12), channel_id=1, source_target_pairs={{1,0},{2,1},{3,2},{4,3},{5,4},{6,5},{7,6},{8,7},{9,8},{10,9},{11,1... | collective-permute-start | bytes 589832 | tf_op jit(solution)/shard_map/ppermute | solution.py:23
  75.0 4.1 %collective-permute-start.5 = (f32[2,1,4,24,256]{4,3,2,1,0:T(8,128)S(1)}, f32[2,1,4,24,256]{4,3,2,1,0:T(8,128)S(1)}, u32[]{:S(2)}, u32[]{:S(2)}) collective-permute-start(f32[2,1,4,24,256]{4,3,2,1,0:T(8,128)S(1)} %pad_maximum_fusion.12), channel_id=1, source_target_pairs={{0,1},{1,2},{2,3},{3,4},{4,5},{5,6},{6,7},{7,8},{8,9},{9,10},{10,1... | collective-permute-start | bytes 589832 | tf_op jit(solution)/shard_map/ppermute | solution.py:20
  80.2 6.8 %collective-permute-start.7 = (f32[2,1,4,24,256]{4,3,2,1,0:T(8,128)S(1)}, f32[2,1,4,24,256]{4,3,2,1,0:T(8,128)S(1)}, u32[]{:S(2)}, u32[]{:S(2)}) collective-permute-start(f32[2,1,4,24,256]{4,3,2,1,0:T(8,128)S(1)} %pad_maximum_fusion.13), channel_id=1, source_target_pairs={{1,0},{2,1},{3,2},{4,3},{5,4},{6,5},{7,6},{8,7},{9,8},{10,9},{11,1... | collective-permute-start | bytes 589832 | tf_op jit(solution)/shard_map/ppermute | solution.py:23
  81.5 6.4 %collective-permute-start.6 = (f32[2,1,4,24,256]{4,3,2,1,0:T(8,128)S(1)}, f32[2,1,4,24,256]{4,3,2,1,0:T(8,128)S(1)}, u32[]{:S(2)}, u32[]{:S(2)}) collective-permute-start(f32[2,1,4,24,256]{4,3,2,1,0:T(8,128)S(1)} %pad_maximum_fusion.13), channel_id=1, source_target_pairs={{0,1},{1,2},{2,3},{3,4},{4,5},{5,6},{6,7},{7,8},{8,9},{9,10},{10,1... | collective-permute-start | bytes 589832 | tf_op jit(solution)/shard_map/ppermute | solution.py:20
  91.7 17.5 %all-to-all-start.2 = ((f32[32,1,128]{2,1,0:T(1,128)}), f32[32,1,128]{2,1,0:T(1,128)S(1)}, u32[]{:S(2)}, u32[]{:S(2)}) async-start(f32[32,1,128]{2,1,0:T(1,128)} %broadcast_in_dim.9), calls=%async_computation.2 | async-start | bytes 32768 | tf_op jit(solution)/shard_map/all_to_all | solution.py:42
  111.1 4.5 %collective-permute-start.8 = (f32[2,1,4,24,256]{4,3,2,1,0:T(8,128)S(1)}, f32[2,1,4,24,256]{4,3,2,1,0:T(8,128)S(1)}, u32[]{:S(2)}, u32[]{:S(2)}) collective-permute-start(f32[2,1,4,24,256]{4,3,2,1,0:T(8,128)S(1)} %pad_maximum_fusion.14), channel_id=1, source_target_pairs={{1,0},{2,1},{3,2},{4,3},{5,4},{6,5},{7,6},{8,7},{9,8},{10,9},{11,1... | collective-permute-start | bytes 589832 | tf_op jit(solution)/shard_map/ppermute | solution.py:23
  112.4 4.1 %collective-permute-start.9 = (f32[2,1,4,24,256]{4,3,2,1,0:T(8,128)S(1)}, f32[2,1,4,24,256]{4,3,2,1,0:T(8,128)S(1)}, u32[]{:S(2)}, u32[]{:S(2)}) collective-permute-start(f32[2,1,4,24,256]{4,3,2,1,0:T(8,128)S(1)} %pad_maximum_fusion.14), channel_id=1, source_target_pairs={{0,1},{1,2},{2,3},{3,4},{4,5},{5,6},{6,7},{7,8},{8,9},{9,10},{10,1... | collective-permute-start | bytes 589832 | tf_op jit(solution)/shard_map/ppermute | solution.py:20
  117.6 6.7 %collective-permute-start.11 = (f32[2,1,4,24,256]{4,3,2,1,0:T(8,128)S(1)}, f32[2,1,4,24,256]{4,3,2,1,0:T(8,128)S(1)}, u32[]{:S(2)}, u32[]{:S(2)}) collective-permute-start(f32[2,1,4,24,256]{4,3,2,1,0:T(8,128)S(1)} %pad_maximum_fusion.15), channel_id=1, source_target_pairs={{1,0},{2,1},{3,2},{4,3},{5,4},{6,5},{7,6},{8,7},{9,8},{10,9},{11,1... | collective-permute-start | bytes 589832 | tf_op jit(solution)/shard_map/ppermute | solution.py:23
  118.9 6.4 %collective-permute-start.10 = (f32[2,1,4,24,256]{4,3,2,1,0:T(8,128)S(1)}, f32[2,1,4,24,256]{4,3,2,1,0:T(8,128)S(1)}, u32[]{:S(2)}, u32[]{:S(2)}) collective-permute-start(f32[2,1,4,24,256]{4,3,2,1,0:T(8,128)S(1)} %pad_maximum_fusion.15), channel_id=1, source_target_pairs={{0,1},{1,2},{2,3},{3,4},{4,5},{5,6},{6,7},{7,8},{8,9},{9,10},{10,1... | collective-permute-start | bytes 589832 | tf_op jit(solution)/shard_map/ppermute | solution.py:20
  131.8 10.5 %collective-permute-start.12 = (f32[3,1,4,24,256]{4,3,2,1,0:T(8,128)S(1)}, f32[3,1,4,24,256]{4,3,2,1,0:T(8,128)S(1)}, u32[]{:S(2)}, u32[]{:S(2)}) collective-permute-start(f32[3,1,4,24,256]{4,3,2,1,0:T(8,128)S(1)} %maximum_maximum_fusion.8), channel_id=1, source_target_pairs={{1,0},{2,1},{3,2},{4,3},{5,4},{6,5},{7,6},{8,7},{9,8},{10,9},{11,1... | collective-permute-start | bytes 884744 | tf_op jit(solution)/shard_map/ppermute | solution.py:23
  133.1 9.7 %collective-permute-start.13 = (f32[3,1,4,24,256]{4,3,2,1,0:T(8,128)S(1)}, f32[3,1,4,24,256]{4,3,2,1,0:T(8,128)}, u32[]{:S(2)}, u32[]{:S(2)}) collective-permute-start(f32[3,1,4,24,256]{4,3,2,1,0:T(8,128)S(1)} %maximum_maximum_fusion.8), channel_id=1, source_target_pairs={{0,1},{1,2},{2,3},{3,4},{4,5},{5,6},{6,7},{7,8},{8,9},{9,10},{10,1... | collective-permute-start | bytes 884744 | tf_op jit(solution)/shard_map/ppermute | solution.py:20
  146.4 12.2 %collective-permute-start.15 = (f32[3,1,4,24,256]{4,3,2,1,0:T(8,128)S(1)}, f32[3,1,4,24,256]{4,3,2,1,0:T(8,128)S(1)}, u32[]{:S(2)}, u32[]{:S(2)}) collective-permute-start(f32[3,1,4,24,256]{4,3,2,1,0:T(8,128)S(1)} %pad_maximum_fusion.9), channel_id=1, source_target_pairs={{1,0},{2,1},{3,2},{4,3},{5,4},{6,5},{7,6},{8,7},{9,8},{10,9},{11,1... | collective-permute-start | bytes 884744 | tf_op jit(solution)/shard_map/ppermute | solution.py:23
  147.7 11.4 %collective-permute-start.14 = (f32[3,1,4,24,256]{4,3,2,1,0:T(8,128)S(1)}, f32[3,1,4,24,256]{4,3,2,1,0:T(8,128)S(1)}, u32[]{:S(2)}, u32[]{:S(2)}) collective-permute-start(f32[3,1,4,24,256]{4,3,2,1,0:T(8,128)S(1)} %pad_maximum_fusion.9), channel_id=1, source_target_pairs={{0,1},{1,2},{2,3},{3,4},{4,5},{5,6},{6,7},{7,8},{8,9},{9,10},{10,1... | collective-permute-start | bytes 884744 | tf_op jit(solution)/shard_map/ppermute | solution.py:20
  163.7 17.6 %all-to-all-start.3 = ((f32[32,1,512]{2,1,0:T(1,128)}), f32[32,1,512]{2,1,0:T(1,128)S(1)}, u32[]{:S(2)}, u32[]{:S(2)}) async-start(f32[32,1,512]{2,1,0:T(1,128)} %all_to_all.33), calls=%async_computation.3 | async-start | bytes 131072 | tf_op jit(solution)/shard_map/all_to_all | solution.py:246
  (52 other events, 389.0 us)

commit v8 on v7

--- a/solution.py
+++ b/solution.py
@@ -8,7 +8,7 @@
 HALO = 4
 ROW_AXIS = 2
 DEPTH_AXIS = 3
-DEFERRED = 2
+DEFERRED = 3
 
 
 def halo_rows(fields):

time: 186 us -> 184 us (0.989)
  other arithmetic: 27.1 us -> 21.4 us
  starting transfers between devices: 92.6 us -> 98.2 us
    all_to_all x1, starting transfers between devices: 10.1 us -> 20.5 us  [on_device(): got = lax.all_to_all(packed, 'gx', 0, 0, tiled=True)]
    all_to_all x2 -> x1, starting transfers between devices: 20.3 us -> 12.2 us  [gather_sum(): return jnp.sum(lax.all_to_all(copies, 'gx', 0, 0, tiled=True), axis=0)]
    ppermute x8, waiting for transfers between devices: 3.99 us -> 8.56 us  [halo_rows(): lax.ppermute(lax.slice_in_dim(packed, 0, HALO, axis=ROW_AXIS), 'gx', down)]
    all_to_all x2 -> x1, waiting for transfers between devices: 10.1 us -> 6.42 us  [gather_sum(): return jnp.sum(lax.all_to_all(copies, 'gx', 0, 0, tiled=True), axis=0)]
    ppermute x8, starting transfers between devices: 44.6 us -> 47.8 us  [halo_rows(): lax.ppermute(lax.slice_in_dim(packed, length - HALO, length, axis=ROW_AXI...]
    unnamed x130 -> x64, local copies, waits for them, and re-layouts: 10.1 us -> 8.81 us
  transfers between devices with their start and end apart: 20 -> 19, of which waited for: 12 -> 11; matrix products, arithmetic and copies ran while one was open for 4% -> 2% of each run, Pallas kernels for 0% -> 0%
where the time goes in v8:
time: 184 us
  starting transfers between devices  98.2 us (53%)
  waiting for transfers between devices  37.2 us (20%)
  other arithmetic  21.4 us (12%)
  local copies, waits for them, and re-layouts  20 us (11%)
  matrix products  3.44 us (2%)
  between operations  3.4 us (2%)
    ppermute x8, starting transfers between devices, halo_rows(): lax.ppermute(lax.slice_in_dim(packed, length - HALO, length, axis=ROW_AXI...  47.8 us
    all_to_all x1, starting transfers between devices, on_device(): got = lax.all_to_all(packed, 'gx', 0, 0, tiled=True)  20.5 us
    all_to_all x1, starting transfers between devices, gather_sum(): return jnp.sum(lax.all_to_all(copies, 'gx', 0, 0, tiled=True), axis=0)  12.2 us
    all_to_all x1, waiting for transfers between devices, on_device(): lax.all_to_all(rock_in, 'gx', split_axis=3, concat_axis=1, tiled=True)  10.7 us
    ppermute x8, starting transfers between devices, halo_rows(): lax.ppermute(lax.slice_in_dim(packed, 0, HALO, axis=ROW_AXIS), 'gx', down)  10.3 us
    unnamed x64, local copies, waits for them, and re-layouts  8.81 us
    ppermute x8, waiting for transfers between devices, halo_rows(): lax.ppermute(lax.slice_in_dim(packed, 0, HALO, axis=ROW_AXIS), 'gx', down)  8.56 us
    all_to_all x1, starting transfers between devices, on_device(): lax.all_to_all(rock_in, 'gx', split_axis=3, concat_axis=1, tiled=True)  7.3 us
  transfers between devices with their start and end apart: 19, of which 11 were waited for; matrix products, arithmetic and copies ran while one was open for 2% of the time, Pallas kernels for 0%

profile of v8, /device:TPU:0, one launch (start us, length us, event | category | flops | bytes accessed | tf_op | source)
XLA Modules:
  0.0 183.5 jit_solution(13426830352071359334)
XLA Ops:
  3.1 1.9 %copy.2275 = f32[21,8,4,128]{0,1,2,3:T(8,128)S(1)} copy(f32[21,8,4,128]{3,1,2,0:T(8,128)S(1)} %pad_maximum_fusion.9) | data formatting | bytes 688128 | tf_op jit(solution)/shard_map/concatenate | solution.py:92
  5.1 2.7 %reshape.1017 = f32[32,1,2688]{2,1,0:T(1,128)} reshape(f32[128,4,8,21]{3,2,1,0:T(8,128)S(1)} %bitcast.558) | data formatting | bytes 688128
  7.7 7.3 %all-to-all-start = ((f32[32,1,2688]{2,1,0:T(1,128)}), f32[32,1,2688]{2,1,0:T(1,128)S(1)}, u32[]{:S(2)}, u32[]{:S(2)}) async-start(f32[32,1,2688]{2,1,0:T(1,128)} %reshape.1017), calls=%async_computation | async-start | bytes 688128 | tf_op jit(solution)/shard_map/all_to_all | solution.py:100
  16.7 10.7 %all-to-all-done = f32[32,1,2688]{2,1,0:T(1,128)S(1)} async-done(((f32[32,1,2688]{2,1,0:T(1,128)}), f32[32,1,2688]{2,1,0:T(1,128)S(1)}, u32[]{:S(2)}, u32[]{:S(2)}) %all-to-all-start) | async-done | bytes 344096 | tf_op jit(solution)/shard_map/all_to_all | solution.py:100
  27.8 1.5 reduce.33
  29.3 2.3 %reshape.1018 = f32[128,4,8,21]{3,2,1,0:T(8,128)S(1)} reshape(f32[32,2688]{1,0:T(8,128)S(1)} %reduce.33) | data formatting | bytes 688128
  31.6 1.6 copy.2561
  33.2 2.3 %copy.2278 = f32[21,256,4,4]{1,2,3,0:T(4,128)S(1)} copy(f32[21,256,4,4]{0,1,3,2:T(8,128)} %bitcast.560) | data formatting | bytes 688128 | tf_op jit(solution)/shard_map/all_to_all | solution.py:100
  35.6 1.4 collective-permute-start.1
  38.3 2.4 %collective-permute-done = f32[2,1,4,24,256]{4,3,2,1,0:T(8,128)S(1)} collective-permute-done((f32[2,1,4,24,256]{4,3,2,1,0:T(8,128)S(1)}, f32[2,1,4,24,256]{4,3,2,1,0:T(8,128)S(1)}, u32[]{:S(2)}, u32[]{:S(2)}) %collective-permute-start) | collective-permute-done | bytes 196640 | tf_op jit(solution)/shard_map/ppermute | solution.py:23
  43.2 6.7 %collective-permute-start.2 = (f32[2,1,4,24,256]{4,3,2,1,0:T(8,128)S(1)}, f32[2,1,4,24,256]{4,3,2,1,0:T(8,128)S(1)}, u32[]{:S(2)}, u32[]{:S(2)}) collective-permute-start(f32[2,1,4,24,256]{4,3,2,1,0:T(8,128)S(1)} %pad_maximum_fusion.15), channel_id=1, source_target_pairs={{0,1},{1,2},{2,3},{3,4},{4,5},{5,6},{6,7},{7,8},{8,9},{9,10},{10,1... | collective-permute-start | bytes 589832 | tf_op jit(solution)/shard_map/ppermute | solution.py:20
  53.2 12.2 %all-to-all-start.1 = ((f32[32,1,128]{2,1,0:T(1,128)}), f32[32,1,128]{2,1,0:T(1,128)S(1)}, u32[]{:S(2)}, u32[]{:S(2)}) async-start(f32[32,1,128]{2,1,0:T(1,128)} %broadcast_in_dim.6), calls=%async_computation.1 | async-start | bytes 32768 | tf_op jit(solution)/shard_map/all_to_all | solution.py:42
  66.1 6.4 %all-to-all-done.1 = f32[32,1,128]{2,1,0:T(1,128)S(1)} async-done(((f32[32,1,128]{2,1,0:T(1,128)}), f32[32,1,128]{2,1,0:T(1,128)S(1)}, u32[]{:S(2)}, u32[]{:S(2)}) %all-to-all-start.1) | async-done | bytes 16416 | tf_op jit(solution)/shard_map/all_to_all | solution.py:42
  74.4 1.8 collective-permute-start.5
  77.6 2.1 %collective-permute-done.4 = f32[2,1,4,24,256]{4,3,2,1,0:T(8,128)S(1)} collective-permute-done((f32[2,1,4,24,256]{4,3,2,1,0:T(8,128)S(1)}, f32[2,1,4,24,256]{4,3,2,1,0:T(8,128)S(1)}, u32[]{:S(2)}, u32[]{:S(2)}) %collective-permute-start.4) | collective-permute-done | bytes 196640 | tf_op jit(solution)/shard_map/ppermute | solution.py:23
  82.2 6.9 %collective-permute-start.6 = (f32[2,1,4,24,256]{4,3,2,1,0:T(8,128)S(1)}, f32[2,1,4,24,256]{4,3,2,1,0:T(8,128)S(1)}, u32[]{:S(2)}, u32[]{:S(2)}) collective-permute-start(f32[2,1,4,24,256]{4,3,2,1,0:T(8,128)S(1)} %pad_maximum_fusion.17), channel_id=1, source_target_pairs={{0,1},{1,2},{2,3},{3,4},{4,5},{5,6},{6,7},{7,8},{8,9},{9,10},{10,1... | collective-permute-start | bytes 589832 | tf_op jit(solution)/shard_map/ppermute | solution.py:20
  93.5 7.3 %collective-permute-start.9 = (f32[3,1,4,24,256]{4,3,2,1,0:T(8,128)S(1)}, f32[3,1,4,24,256]{4,3,2,1,0:T(8,128)S(1)}, u32[]{:S(2)}, u32[]{:S(2)}) collective-permute-start(f32[3,1,4,24,256]{4,3,2,1,0:T(8,128)S(1)} %maximum_maximum_fusion.9), channel_id=1, source_target_pairs={{0,1},{1,2},{2,3},{3,4},{4,5},{5,6},{6,7},{7,8},{8,9},{9,10},{10,1... | collective-permute-start | bytes 884744 | tf_op jit(solution)/shard_map/ppermute | solution.py:20
  100.8 1.3 collective-permute-start.8
  102.2 4.0 %collective-permute-done.8 = f32[3,1,4,24,256]{4,3,2,1,0:T(8,128)S(1)} collective-permute-done((f32[3,1,4,24,256]{4,3,2,1,0:T(8,128)S(1)}, f32[3,1,4,24,256]{4,3,2,1,0:T(8,128)S(1)}, u32[]{:S(2)}, u32[]{:S(2)}) %collective-permute-start.8) | collective-permute-done | bytes 294944 | tf_op jit(solution)/shard_map/ppermute | solution.py:23
  108.5 8.6 %collective-permute-start.10 = (f32[3,1,4,24,256]{4,3,2,1,0:T(8,128)S(1)}, f32[3,1,4,24,256]{4,3,2,1,0:T(8,128)S(1)}, u32[]{:S(2)}, u32[]{:S(2)}) collective-permute-start(f32[3,1,4,24,256]{4,3,2,1,0:T(8,128)S(1)} %pad_maximum_fusion.10), channel_id=1, source_target_pairs={{0,1},{1,2},{2,3},{3,4},{4,5},{5,6},{6,7},{7,8},{8,9},{9,10},{10,1... | collective-permute-start | bytes 884744 | tf_op jit(solution)/shard_map/ppermute | solution.py:20
  124.6 6.7 %collective-permute-start.13 = (f32[4,1,4,24,256]{4,3,2,1,0:T(8,128)S(1)}, f32[4,1,4,24,256]{4,3,2,1,0:T(8,128)S(1)}, u32[]{:S(2)}, u32[]{:S(2)}) collective-permute-start(f32[4,1,4,24,256]{4,3,2,1,0:T(8,128)S(1)} %maximum_maximum_fusion.8), channel_id=1, source_target_pairs={{0,1},{1,2},{2,3},{3,4},{4,5},{5,6},{6,7},{7,8},{8,9},{9,10},{10,1... | collective-permute-start | bytes 1179656 | tf_op jit(solution)/shard_map/ppermute | solution.py:20
  135.3 8.4 %collective-permute-start.14 = (f32[4,1,4,24,256]{4,3,2,1,0:T(8,128)S(1)}, f32[4,1,4,24,256]{4,3,2,1,0:T(8,128)S(1)}, u32[]{:S(2)}, u32[]{:S(2)}) collective-permute-start(f32[4,1,4,24,256]{4,3,2,1,0:T(8,128)S(1)} %pad_maximum_fusion.8), channel_id=1, source_target_pairs={{0,1},{1,2},{2,3},{3,4},{4,5},{5,6},{6,7},{7,8},{8,9},{9,10},{10,1... | collective-permute-start | bytes 1179656 | tf_op jit(solution)/shard_map/ppermute | solution.py:20
  151.3 20.5 %all-to-all-start.2 = ((f32[32,1,896]{2,1,0:T(1,128)}), f32[32,1,896]{2,1,0:T(1,128)S(1)}, u32[]{:S(2)}, u32[]{:S(2)}) async-start(f32[32,1,896]{2,1,0:T(1,128)} %all_to_all.29), calls=%async_computation.2 | async-start | bytes 229376 | tf_op jit(solution)/shard_map/all_to_all | solution.py:246
  172.5 7.2 %all-to-all-done.2 = f32[32,1,896]{2,1,0:T(1,128)S(1)} async-done(((f32[32,1,896]{2,1,0:T(1,128)}), f32[32,1,896]{2,1,0:T(1,128)S(1)}, u32[]{:S(2)}, u32[]{:S(2)}) %all-to-all-start.2) | async-done | bytes 114720 | tf_op jit(solution)/shard_map/all_to_all | solution.py:246
  (252 shorter events, 45.9 us)
Async XLA Ops:
  7.7 19.6 %all-to-all-start = ((f32[32,1,2688]{2,1,0:T(1,128)}), f32[32,1,2688]{2,1,0:T(1,128)S(1)}, u32[]{:S(2)}, u32[]{:S(2)}) async-start(f32[32,1,2688]{2,1,0:T(1,128)} %reshape.1017), calls=%async_computation | async-start | bytes 688128 | tf_op jit(solution)/shard_map/all_to_all | solution.py:100
  16.6 75.3 %copy-start.11 = (pred[128]{0:T(512)(128)(4,1)}, pred[128]{0:T(512)(128)(4,1)S(1)}, u32[]{:S(2)}) copy-start(pred[128]{0:T(512)(128)(4,1)S(1)} %get-tuple-element.197) | copy-start | bytes 388
  35.6 2.8 %collective-permute-start.1 = (f32[2,1,4,24,256]{4,3,2,1,0:T(8,128)S(1)}, f32[2,1,4,24,256]{4,3,2,1,0:T(8,128)S(1)}, u32[]{:S(2)}, u32[]{:S(2)}) collective-permute-start(f32[2,1,4,24,256]{4,3,2,1,0:T(8,128)S(1)} %pad_maximum_fusion.14), channel_id=1, source_target_pairs={{0,1},{1,2},{2,3},{3,4},{4,5},{5,6},{6,7},{7,8},{8,9},{9,10},{10,1... | collective-permute-start | bytes 589832 | tf_op jit(solution)/shard_map/ppermute | solution.py:20
  37.0 3.7 %collective-permute-start = (f32[2,1,4,24,256]{4,3,2,1,0:T(8,128)S(1)}, f32[2,1,4,24,256]{4,3,2,1,0:T(8,128)S(1)}, u32[]{:S(2)}, u32[]{:S(2)}) collective-permute-start(f32[2,1,4,24,256]{4,3,2,1,0:T(8,128)S(1)} %pad_maximum_fusion.14), channel_id=1, source_target_pairs={{1,0},{2,1},{3,2},{4,3},{5,4},{6,5},{7,6},{8,7},{9,8},{10,9},{11,1... | collective-permute-start | bytes 589832 | tf_op jit(solution)/shard_map/ppermute | solution.py:23
  41.9 8.0 %collective-permute-start.3 = (f32[2,1,4,24,256]{4,3,2,1,0:T(8,128)S(1)}, f32[2,1,4,24,256]{4,3,2,1,0:T(8,128)S(1)}, u32[]{:S(2)}, u32[]{:S(2)}) collective-permute-start(f32[2,1,4,24,256]{4,3,2,1,0:T(8,128)S(1)} %pad_maximum_fusion.15), channel_id=1, source_target_pairs={{1,0},{2,1},{3,2},{4,3},{5,4},{6,5},{7,6},{8,7},{9,8},{10,9},{11,1... | collective-permute-start | bytes 589832 | tf_op jit(solution)/shard_map/ppermute | solution.py:23
  43.2 7.7 %collective-permute-start.2 = (f32[2,1,4,24,256]{4,3,2,1,0:T(8,128)S(1)}, f32[2,1,4,24,256]{4,3,2,1,0:T(8,128)S(1)}, u32[]{:S(2)}, u32[]{:S(2)}) collective-permute-start(f32[2,1,4,24,256]{4,3,2,1,0:T(8,128)S(1)} %pad_maximum_fusion.15), channel_id=1, source_target_pairs={{0,1},{1,2},{2,3},{3,4},{4,5},{5,6},{6,7},{7,8},{8,9},{9,10},{10,1... | collective-permute-start | bytes 589832 | tf_op jit(solution)/shard_map/ppermute | solution.py:20
  49.9 42.0 %copy-start.18 = (s32[128]{0:T(128)}, s32[128]{0:T(128)S(1)}, u32[]{:S(2)}) copy-start(s32[128]{0:T(128)S(1)} %fusion.1093) | copy-start | bytes 1540
  51.0 21.5 %copy-start.10 = (f32[4,1,128]{2,1,0:T(1,128)S(1)}, f32[4,1,128]{2,1,0:T(1,128)}, u32[]{:S(2)}) copy-start(f32[4,1,128]{2,1,0:T(1,128)} %param.41) | copy-start | bytes 6148
  53.2 19.3 %all-to-all-start.1 = ((f32[32,1,128]{2,1,0:T(1,128)}), f32[32,1,128]{2,1,0:T(1,128)S(1)}, u32[]{:S(2)}, u32[]{:S(2)}) async-start(f32[32,1,128]{2,1,0:T(1,128)} %broadcast_in_dim.6), calls=%async_computation.1 | async-start | bytes 32768 | tf_op jit(solution)/shard_map/all_to_all | solution.py:42
  74.4 3.3 %collective-permute-start.5 = (f32[2,1,4,24,256]{4,3,2,1,0:T(8,128)S(1)}, f32[2,1,4,24,256]{4,3,2,1,0:T(8,128)S(1)}, u32[]{:S(2)}, u32[]{:S(2)}) collective-permute-start(f32[2,1,4,24,256]{4,3,2,1,0:T(8,128)S(1)} %pad_maximum_fusion.16), channel_id=1, source_target_pairs={{0,1},{1,2},{2,3},{3,4},{4,5},{5,6},{6,7},{7,8},{8,9},{9,10},{10,1... | collective-permute-start | bytes 589832 | tf_op jit(solution)/shard_map/ppermute | solution.py:20
  76.2 3.6 %collective-permute-start.4 = (f32[2,1,4,24,256]{4,3,2,1,0:T(8,128)S(1)}, f32[2,1,4,24,256]{4,3,2,1,0:T(8,128)S(1)}, u32[]{:S(2)}, u32[]{:S(2)}) collective-permute-start(f32[2,1,4,24,256]{4,3,2,1,0:T(8,128)S(1)} %pad_maximum_fusion.16), channel_id=1, source_target_pairs={{1,0},{2,1},{3,2},{4,3},{5,4},{6,5},{7,6},{8,7},{9,8},{10,9},{11,1... | collective-permute-start | bytes 589832 | tf_op jit(solution)/shard_map/ppermute | solution.py:23
  80.9 8.2 %collective-permute-start.7 = (f32[2,1,4,24,256]{4,3,2,1,0:T(8,128)S(1)}, f32[2,1,4,24,256]{4,3,2,1,0:T(8,128)S(1)}, u32[]{:S(2)}, u32[]{:S(2)}) collective-permute-start(f32[2,1,4,24,256]{4,3,2,1,0:T(8,128)S(1)} %pad_maximum_fusion.17), channel_id=1, source_target_pairs={{1,0},{2,1},{3,2},{4,3},{5,4},{6,5},{7,6},{8,7},{9,8},{10,9},{11,1... | collective-permute-start | bytes 589832 | tf_op jit(solution)/shard_map/ppermute | solution.py:23
  82.2 7.7 %collective-permute-start.6 = (f32[2,1,4,24,256]{4,3,2,1,0:T(8,128)S(1)}, f32[2,1,4,24,256]{4,3,2,1,0:T(8,128)S(1)}, u32[]{:S(2)}, u32[]{:S(2)}) collective-permute-start(f32[2,1,4,24,256]{4,3,2,1,0:T(8,128)S(1)} %pad_maximum_fusion.17), channel_id=1, source_target_pairs={{0,1},{1,2},{2,3},{3,4},{4,5},{5,6},{6,7},{7,8},{8,9},{9,10},{10,1... | collective-permute-start | bytes 589832 | tf_op jit(solution)/shard_map/ppermute | solution.py:20
  91.9 14.4 %copy-start.14 = (f32[1,128]{1,0:T(1,128)}, f32[1,128]{1,0:T(1,128)S(1)}, u32[]{:S(2)}) copy-start(f32[1,128]{1,0:T(1,128)S(1)} %fusion.5) | copy-start | bytes 1540
  93.5 8.7 %collective-permute-start.9 = (f32[3,1,4,24,256]{4,3,2,1,0:T(8,128)S(1)}, f32[3,1,4,24,256]{4,3,2,1,0:T(8,128)S(1)}, u32[]{:S(2)}, u32[]{:S(2)}) collective-permute-start(f32[3,1,4,24,256]{4,3,2,1,0:T(8,128)S(1)} %maximum_maximum_fusion.9), channel_id=1, source_target_pairs={{0,1},{1,2},{2,3},{3,4},{4,5},{5,6},{6,7},{7,8},{8,9},{9,10},{10,1... | collective-permute-start | bytes 884744 | tf_op jit(solution)/shard_map/ppermute | solution.py:20
  100.8 5.4 %collective-permute-start.8 = (f32[3,1,4,24,256]{4,3,2,1,0:T(8,128)S(1)}, f32[3,1,4,24,256]{4,3,2,1,0:T(8,128)S(1)}, u32[]{:S(2)}, u32[]{:S(2)}) collective-permute-start(f32[3,1,4,24,256]{4,3,2,1,0:T(8,128)S(1)} %maximum_maximum_fusion.9), channel_id=1, source_target_pairs={{1,0},{2,1},{3,2},{4,3},{5,4},{6,5},{7,6},{8,7},{9,8},{10,9},{11,1... | collective-permute-start | bytes 884744 | tf_op jit(solution)/shard_map/ppermute | solution.py:23
  107.2 10.4 %collective-permute-start.11 = (f32[3,1,4,24,256]{4,3,2,1,0:T(8,128)S(1)}, f32[3,1,4,24,256]{4,3,2,1,0:T(8,128)S(1)}, u32[]{:S(2)}, u32[]{:S(2)}) collective-permute-start(f32[3,1,4,24,256]{4,3,2,1,0:T(8,128)S(1)} %pad_maximum_fusion.10), channel_id=1, source_target_pairs={{1,0},{2,1},{3,2},{4,3},{5,4},{6,5},{7,6},{8,7},{9,8},{10,9},{11,1... | collective-permute-start | bytes 884744 | tf_op jit(solution)/shard_map/ppermute | solution.py:23
  108.5 9.8 %collective-permute-start.10 = (f32[3,1,4,24,256]{4,3,2,1,0:T(8,128)S(1)}, f32[3,1,4,24,256]{4,3,2,1,0:T(8,128)S(1)}, u32[]{:S(2)}, u32[]{:S(2)}) collective-permute-start(f32[3,1,4,24,256]{4,3,2,1,0:T(8,128)S(1)} %pad_maximum_fusion.10), channel_id=1, source_target_pairs={{0,1},{1,2},{2,3},{3,4},{4,5},{5,6},{6,7},{7,8},{8,9},{9,10},{10,1... | collective-permute-start | bytes 884744 | tf_op jit(solution)/shard_map/ppermute | solution.py:20
  122.6 8.9 %collective-permute-start.12 = (f32[4,1,4,24,256]{4,3,2,1,0:T(8,128)S(1)}, f32[4,1,4,24,256]{4,3,2,1,0:T(8,128)S(1)}, u32[]{:S(2)}, u32[]{:S(2)}) collective-permute-start(f32[4,1,4,24,256]{4,3,2,1,0:T(8,128)S(1)} %maximum_maximum_fusion.8), channel_id=1, source_target_pairs={{1,0},{2,1},{3,2},{4,3},{5,4},{6,5},{7,6},{8,7},{9,8},{10,9},{11,1... | collective-permute-start | bytes 1179656 | tf_op jit(solution)/shard_map/ppermute | solution.py:23
  124.6 8.1 %collective-permute-start.13 = (f32[4,1,4,24,256]{4,3,2,1,0:T(8,128)S(1)}, f32[4,1,4,24,256]{4,3,2,1,0:T(8,128)S(1)}, u32[]{:S(2)}, u32[]{:S(2)}) collective-permute-start(f32[4,1,4,24,256]{4,3,2,1,0:T(8,128)S(1)} %maximum_maximum_fusion.8), channel_id=1, source_target_pairs={{0,1},{1,2},{2,3},{3,4},{4,5},{5,6},{6,7},{7,8},{8,9},{9,10},{10,1... | collective-permute-start | bytes 1179656 | tf_op jit(solution)/shard_map/ppermute | solution.py:20
  134.0 10.3 %collective-permute-start.15 = (f32[4,1,4,24,256]{4,3,2,1,0:T(8,128)S(1)}, f32[4,1,4,24,256]{4,3,2,1,0:T(8,128)S(1)}, u32[]{:S(2)}, u32[]{:S(2)}) collective-permute-start(f32[4,1,4,24,256]{4,3,2,1,0:T(8,128)S(1)} %pad_maximum_fusion.8), channel_id=1, source_target_pairs={{1,0},{2,1},{3,2},{4,3},{5,4},{6,5},{7,6},{8,7},{9,8},{10,9},{11,1... | collective-permute-start | bytes 1179656 | tf_op jit(solution)/shard_map/ppermute | solution.py:23
  135.3 9.7 %collective-permute-start.14 = (f32[4,1,4,24,256]{4,3,2,1,0:T(8,128)S(1)}, f32[4,1,4,24,256]{4,3,2,1,0:T(8,128)S(1)}, u32[]{:S(2)}, u32[]{:S(2)}) collective-permute-start(f32[4,1,4,24,256]{4,3,2,1,0:T(8,128)S(1)} %pad_maximum_fusion.8), channel_id=1, source_target_pairs={{0,1},{1,2},{2,3},{3,4},{4,5},{5,6},{6,7},{7,8},{8,9},{9,10},{10,1... | collective-permute-start | bytes 1179656 | tf_op jit(solution)/shard_map/ppermute | solution.py:20
  150.0 30.3 %copy-start.22 = (f32[1,1,128]{2,1,0:T(1,128)S(1)}, f32[1,1,128]{2,1,0:T(1,128)}, u32[]{:S(2)}) copy-start(f32[1,1,128]{2,1,0:T(1,128)} %copy-done.21) | copy-start | bytes 1540
  151.3 28.5 %all-to-all-start.2 = ((f32[32,1,896]{2,1,0:T(1,128)}), f32[32,1,896]{2,1,0:T(1,128)S(1)}, u32[]{:S(2)}, u32[]{:S(2)}) async-start(f32[32,1,896]{2,1,0:T(1,128)} %all_to_all.29), calls=%async_computation.2 | async-start | bytes 229376 | tf_op jit(solution)/shard_map/all_to_all | solution.py:246
  (18 other events, 121.4 us)

commit v9 on v8

--- a/solution.py
+++ b/solution.py
@@ -8,7 +8,7 @@
 HALO = 4
 ROW_AXIS = 2
 DEPTH_AXIS = 3
-DEFERRED = 3
+DEFERRED = 4
 
 
 def halo_rows(fields):

time: 184 us -> 193 us (1.049)
  waiting for transfers between devices: 37.2 us -> 27.3 us
  other arithmetic: 21.4 us -> 30.9 us
  local copies, waits for them, and re-layouts: 20 us -> 23.9 us
  starting transfers between devices: 98.2 us -> 102 us
    ppermute x8, starting transfers between devices: 47.8 us -> 64.1 us  [halo_rows(): lax.ppermute(lax.slice_in_dim(packed, length - HALO, length, axis=ROW_AXI...]
    all_to_all x1 -> x0, starting transfers between devices: 12.2 us -> none  [gather_sum(): return jnp.sum(lax.all_to_all(copies, 'gx', 0, 0, tiled=True), axis=0)]
    all_to_all x1 -> x0, waiting for transfers between devices: 6.42 us -> none  [gather_sum(): return jnp.sum(lax.all_to_all(copies, 'gx', 0, 0, tiled=True), axis=0)]
    unnamed x64 -> x174, local copies, waits for them, and re-layouts: 8.81 us -> 10.1 us
  transfers between devices with their start and end apart: 19 -> 18, of which waited for: 11 -> 9; matrix products, arithmetic and copies ran while one was open for 2% -> 5% of each run, Pallas kernels for 0% -> 0%
where the time goes in v9:
time: 193 us; the launch traced here: 192 us
  starting transfers between devices  102 us (53%)
  other arithmetic  30.9 us (16%)
  waiting for transfers between devices  27.3 us (14%)
  local copies, waits for them, and re-layouts  23.9 us (12%)
  matrix products  4.07 us (2%)
  between operations  3.52 us (2%)
    ppermute x8, starting transfers between devices, halo_rows(): lax.ppermute(lax.slice_in_dim(packed, length - HALO, length, axis=ROW_AXI...  64.1 us
    all_to_all x1, starting transfers between devices, on_device(): got = lax.all_to_all(packed, 'gx', 0, 0, tiled=True)  20.4 us
    all_to_all x1, waiting for transfers between devices, on_device(): lax.all_to_all(rock_in, 'gx', split_axis=3, concat_axis=1, tiled=True)  10.6 us
    ppermute x8, starting transfers between devices, halo_rows(): lax.ppermute(lax.slice_in_dim(packed, 0, HALO, axis=ROW_AXIS), 'gx', down)  10.5 us
    unnamed x174, local copies, waits for them, and re-layouts  10.1 us
    all_to_all x1, starting transfers between devices, on_device(): lax.all_to_all(rock_in, 'gx', split_axis=3, concat_axis=1, tiled=True)  7.3 us
    all_to_all x1, waiting for transfers between devices, on_device(): got = lax.all_to_all(packed, 'gx', 0, 0, tiled=True)  7.12 us
    ppermute x8, waiting for transfers between devices, halo_rows(): lax.ppermute(lax.slice_in_dim(packed, 0, HALO, axis=ROW_AXIS), 'gx', down)  6.94 us
  transfers between devices with their start and end apart: 18, of which 9 were waited for; matrix products, arithmetic and copies ran while one was open for 5% of the time, Pallas kernels for 0%

profile of v9, /device:TPU:0, one launch (start us, length us, event | category | flops | bytes accessed | tf_op | source)
XLA Modules:
  0.0 191.9 jit_solution(17331790434904845663)
XLA Ops:
  3.1 1.9 copy.1956
  5.1 2.7 %reshape.1054 = f32[32,1,2688]{2,1,0:T(1,128)} reshape(f32[128,4,8,21]{3,2,1,0:T(8,128)S(1)} %bitcast.554) | data formatting | bytes 688128
  7.7 7.3 %all-to-all-start = ((f32[32,1,2688]{2,1,0:T(1,128)}), f32[32,1,2688]{2,1,0:T(1,128)S(1)}, u32[]{:S(2)}, u32[]{:S(2)}) async-start(f32[32,1,2688]{2,1,0:T(1,128)} %reshape.1054), calls=%async_computation | async-start | bytes 688128 | tf_op jit(solution)/shard_map/all_to_all | solution.py:100
  16.7 10.6 %all-to-all-done = f32[32,1,2688]{2,1,0:T(1,128)S(1)} async-done(((f32[32,1,2688]{2,1,0:T(1,128)}), f32[32,1,2688]{2,1,0:T(1,128)S(1)}, u32[]{:S(2)}, u32[]{:S(2)}) %all-to-all-start) | async-done | bytes 344096 | tf_op jit(solution)/shard_map/all_to_all | solution.py:100
  27.8 1.5 reduce.28
  29.3 2.3 %reshape.1055 = f32[128,4,8,21]{3,2,1,0:T(8,128)S(1)} reshape(f32[32,2688]{1,0:T(8,128)S(1)} %reduce.28) | data formatting | bytes 688128
  31.6 1.5 copy.2244
  33.1 2.3 %copy.1959 = f32[21,256,4,4]{1,2,3,0:T(4,128)S(1)} copy(f32[21,256,4,4]{0,1,3,2:T(8,128)} %bitcast.556) | data formatting | bytes 688128 | tf_op jit(solution)/shard_map/all_to_all | solution.py:100
  35.5 1.4 collective-permute-start.1
  36.9 1.3 collective-permute-start
  38.3 2.4 %collective-permute-done = f32[2,1,4,24,256]{4,3,2,1,0:T(8,128)S(1)} collective-permute-done((f32[2,1,4,24,256]{4,3,2,1,0:T(8,128)S(1)}, f32[2,1,4,24,256]{4,3,2,1,0:T(8,128)S(1)}, u32[]{:S(2)}, u32[]{:S(2)}) %collective-permute-start) | collective-permute-done | bytes 196640 | tf_op jit(solution)/shard_map/ppermute | solution.py:23
  41.8 1.3 collective-permute-start.3
  43.1 6.7 %collective-permute-start.2 = (f32[2,1,4,24,256]{4,3,2,1,0:T(8,128)S(1)}, f32[2,1,4,24,256]{4,3,2,1,0:T(8,128)S(1)}, u32[]{:S(2)}, u32[]{:S(2)}) collective-permute-start(f32[2,1,4,24,256]{4,3,2,1,0:T(8,128)S(1)} %pad_maximum_fusion.18), channel_id=1, source_target_pairs={{0,1},{1,2},{2,3},{3,4},{4,5},{5,6},{6,7},{7,8},{8,9},{9,10},{10,1... | collective-permute-start | bytes 589832 | tf_op jit(solution)/shard_map/ppermute | solution.py:20
  56.6 5.2 %collective-permute-start.5 = (f32[3,1,4,24,256]{4,3,2,1,0:T(8,128)S(1)}, f32[3,1,4,24,256]{4,3,2,1,0:T(8,128)S(1)}, u32[]{:S(2)}, u32[]{:S(2)}) collective-permute-start(f32[3,1,4,24,256]{4,3,2,1,0:T(8,128)S(1)} %maximum_maximum_fusion.10), channel_id=1, source_target_pairs={{0,1},{1,2},{2,3},{3,4},{4,5},{5,6},{6,7},{7,8},{8,9},{9,10},{10,1... | collective-permute-start | bytes 884744 | tf_op jit(solution)/shard_map/ppermute | solution.py:20
  61.8 1.3 collective-permute-start.4
  63.9 3.4 %collective-permute-done.4 = f32[3,1,4,24,256]{4,3,2,1,0:T(8,128)S(1)} collective-permute-done((f32[3,1,4,24,256]{4,3,2,1,0:T(8,128)S(1)}, f32[3,1,4,24,256]{4,3,2,1,0:T(8,128)S(1)}, u32[]{:S(2)}, u32[]{:S(2)}) %collective-permute-start.4) | collective-permute-done | bytes 294944 | tf_op jit(solution)/shard_map/ppermute | solution.py:23
  68.3 1.4 collective-permute-start.7
  69.7 11.0 %collective-permute-start.6 = (f32[3,1,4,24,256]{4,3,2,1,0:T(8,128)S(1)}, f32[3,1,4,24,256]{4,3,2,1,0:T(8,128)S(1)}, u32[]{:S(2)}, u32[]{:S(2)}) collective-permute-start(f32[3,1,4,24,256]{4,3,2,1,0:T(8,128)S(1)} %pad_maximum_fusion.12), channel_id=1, source_target_pairs={{0,1},{1,2},{2,3},{3,4},{4,5},{5,6},{6,7},{7,8},{8,9},{9,10},{10,1... | collective-permute-start | bytes 884744 | tf_op jit(solution)/shard_map/ppermute | solution.py:20
  90.2 6.7 %collective-permute-start.9 = (f32[4,1,4,24,256]{4,3,2,1,0:T(8,128)}, f32[4,1,4,24,256]{4,3,2,1,0:T(8,128)S(1)}, u32[]{:S(2)}, u32[]{:S(2)}) collective-permute-start(f32[4,1,4,24,256]{4,3,2,1,0:T(8,128)} %maximum_maximum_fusion.9), channel_id=1, source_target_pairs={{0,1},{1,2},{2,3},{3,4},{4,5},{5,6},{6,7},{7,8},{8,9},{9,10},{10,1... | collective-permute-start | bytes 1179656 | tf_op jit(solution)/shard_map/ppermute | solution.py:20
  101.4 8.3 %collective-permute-start.10 = (f32[4,1,4,24,256]{4,3,2,1,0:T(8,128)S(1)}, f32[4,1,4,24,256]{4,3,2,1,0:T(8,128)S(1)}, u32[]{:S(2)}, u32[]{:S(2)}) collective-permute-start(f32[4,1,4,24,256]{4,3,2,1,0:T(8,128)S(1)} %pad_maximum_fusion.9), channel_id=1, source_target_pairs={{0,1},{1,2},{2,3},{3,4},{4,5},{5,6},{6,7},{7,8},{8,9},{9,10},{10,1... | collective-permute-start | bytes 1179656 | tf_op jit(solution)/shard_map/ppermute | solution.py:20
  117.4 7.7 %collective-permute-start.13 = (f32[5,1,4,24,256]{4,3,2,1,0:T(8,128)}, f32[5,1,4,24,256]{4,3,2,1,0:T(8,128)S(1)}, u32[]{:S(2)}, u32[]{:S(2)}) collective-permute-start(f32[5,1,4,24,256]{4,3,2,1,0:T(8,128)} %maximum_maximum_fusion.6), channel_id=1, source_target_pairs={{0,1},{1,2},{2,3},{3,4},{4,5},{5,6},{6,7},{7,8},{8,9},{9,10},{10,1... | collective-permute-start | bytes 1474568 | tf_op jit(solution)/shard_map/ppermute | solution.py:20
  134.3 17.2 %collective-permute-start.14 = (f32[5,1,4,24,256]{4,3,2,1,0:T(8,128)S(1)}, f32[5,1,4,24,256]{4,3,2,1,0:T(8,128)S(1)}, u32[]{:S(2)}, u32[]{:S(2)}) collective-permute-start(f32[5,1,4,24,256]{4,3,2,1,0:T(8,128)S(1)} %pad_maximum_fusion.6), channel_id=1, source_target_pairs={{0,1},{1,2},{2,3},{3,4},{4,5},{5,6},{6,7},{7,8},{8,9},{9,10},{10,1... | collective-permute-start | bytes 1474568 | tf_op jit(solution)/shard_map/ppermute | solution.py:20
  159.2 20.4 %all-to-all-start.1 = ((f32[32,1,1280]{2,1,0:T(1,128)}), f32[32,1,1280]{2,1,0:T(1,128)S(1)}, u32[]{:S(2)}, u32[]{:S(2)}) async-start(f32[32,1,1280]{2,1,0:T(1,128)} %all_to_all.25), calls=%async_computation.1 | async-start | bytes 327680 | tf_op jit(solution)/shard_map/all_to_all | solution.py:246
  181.0 7.1 %all-to-all-done.1 = f32[32,1,1280]{2,1,0:T(1,128)S(1)} async-done(((f32[32,1,1280]{2,1,0:T(1,128)}), f32[32,1,1280]{2,1,0:T(1,128)S(1)}, u32[]{:S(2)}, u32[]{:S(2)}) %all-to-all-start.1) | async-done | bytes 163872 | tf_op jit(solution)/shard_map/all_to_all | solution.py:246
  (377 shorter events, 55.7 us)
Async XLA Ops:
  7.7 19.6 %all-to-all-start = ((f32[32,1,2688]{2,1,0:T(1,128)}), f32[32,1,2688]{2,1,0:T(1,128)S(1)}, u32[]{:S(2)}, u32[]{:S(2)}) async-start(f32[32,1,2688]{2,1,0:T(1,128)} %reshape.1054), calls=%async_computation | async-start | bytes 688128 | tf_op jit(solution)/shard_map/all_to_all | solution.py:100
  15.1 69.0 %copy-start.60 = (s32[4,256]{1,0:T(4,128)}, s32[4,256]{1,0:T(4,128)S(1)}, u32[]{:S(2)}) copy-start(s32[4,256]{1,0:T(4,128)S(1)} %multiply_add_fusion.19) | copy-start | bytes 12292
  16.4 95.8 %copy-start.4 = (f32[4,12,256]{2,1,0:T(8,128)}, f32[4,12,256]{2,1,0:T(8,128)S(1)}, u32[]{:S(2)}) copy-start(f32[4,12,256]{2,1,0:T(8,128)S(1)} %copy.1948) | copy-start | bytes 147460
  16.7 66.1 %copy-start.51 = (s32[4,12]{1,0:T(4,128)}, s32[4,12]{1,0:T(4,128)S(1)}, u32[]{:S(2)}) copy-start(s32[4,12]{1,0:T(4,128)S(1)} %add_multiply_fusion) | copy-start | bytes 580
  16.7 67.4 %copy-start.66 = (pred[128]{0:T(512)(128)(4,1)}, pred[128]{0:T(512)(128)(4,1)S(1)}, u32[]{:S(2)}) copy-start(pred[128]{0:T(512)(128)(4,1)S(1)} %get-tuple-element.197) | copy-start | bytes 388
  16.7 69.0 %copy-start.15 = (s32[4,256]{1,0:T(4,128)}, s32[4,256]{1,0:T(4,128)S(1)}, u32[]{:S(2)}) copy-start(s32[4,256]{1,0:T(4,128)S(1)} %broadcast_add_fusion) | copy-start | bytes 12292
  16.7 93.0 %copy-start.2 = (f32[4,12,256]{2,1,0:T(8,128)}, f32[4,12,256]{2,1,0:T(8,128)S(1)}, u32[]{:S(2)}) copy-start(f32[4,12,256]{2,1,0:T(8,128)S(1)} %get-tuple-element.290) | copy-start | bytes 147460
  35.5 2.8 %collective-permute-start.1 = (f32[2,1,4,24,256]{4,3,2,1,0:T(8,128)S(1)}, f32[2,1,4,24,256]{4,3,2,1,0:T(8,128)S(1)}, u32[]{:S(2)}, u32[]{:S(2)}) collective-permute-start(f32[2,1,4,24,256]{4,3,2,1,0:T(8,128)S(1)} %pad_maximum_fusion.17), channel_id=1, source_target_pairs={{0,1},{1,2},{2,3},{3,4},{4,5},{5,6},{6,7},{7,8},{8,9},{9,10},{10,1... | collective-permute-start | bytes 589832 | tf_op jit(solution)/shard_map/ppermute | solution.py:20
  36.9 3.7 %collective-permute-start = (f32[2,1,4,24,256]{4,3,2,1,0:T(8,128)S(1)}, f32[2,1,4,24,256]{4,3,2,1,0:T(8,128)S(1)}, u32[]{:S(2)}, u32[]{:S(2)}) collective-permute-start(f32[2,1,4,24,256]{4,3,2,1,0:T(8,128)S(1)} %pad_maximum_fusion.17), channel_id=1, source_target_pairs={{1,0},{2,1},{3,2},{4,3},{5,4},{6,5},{7,6},{8,7},{9,8},{10,9},{11,1... | collective-permute-start | bytes 589832 | tf_op jit(solution)/shard_map/ppermute | solution.py:23
  41.8 8.0 %collective-permute-start.3 = (f32[2,1,4,24,256]{4,3,2,1,0:T(8,128)S(1)}, f32[2,1,4,24,256]{4,3,2,1,0:T(8,128)S(1)}, u32[]{:S(2)}, u32[]{:S(2)}) collective-permute-start(f32[2,1,4,24,256]{4,3,2,1,0:T(8,128)S(1)} %pad_maximum_fusion.18), channel_id=1, source_target_pairs={{1,0},{2,1},{3,2},{4,3},{5,4},{6,5},{7,6},{8,7},{9,8},{10,9},{11,1... | collective-permute-start | bytes 589832 | tf_op jit(solution)/shard_map/ppermute | solution.py:23
  43.1 7.7 %collective-permute-start.2 = (f32[2,1,4,24,256]{4,3,2,1,0:T(8,128)S(1)}, f32[2,1,4,24,256]{4,3,2,1,0:T(8,128)S(1)}, u32[]{:S(2)}, u32[]{:S(2)}) collective-permute-start(f32[2,1,4,24,256]{4,3,2,1,0:T(8,128)S(1)} %pad_maximum_fusion.18), channel_id=1, source_target_pairs={{0,1},{1,2},{2,3},{3,4},{4,5},{5,6},{6,7},{7,8},{8,9},{9,10},{10,1... | collective-permute-start | bytes 589832 | tf_op jit(solution)/shard_map/ppermute | solution.py:20
  56.6 7.3 %collective-permute-start.5 = (f32[3,1,4,24,256]{4,3,2,1,0:T(8,128)S(1)}, f32[3,1,4,24,256]{4,3,2,1,0:T(8,128)S(1)}, u32[]{:S(2)}, u32[]{:S(2)}) collective-permute-start(f32[3,1,4,24,256]{4,3,2,1,0:T(8,128)S(1)} %maximum_maximum_fusion.10), channel_id=1, source_target_pairs={{0,1},{1,2},{2,3},{3,4},{4,5},{5,6},{6,7},{7,8},{8,9},{9,10},{10,1... | collective-permute-start | bytes 884744 | tf_op jit(solution)/shard_map/ppermute | solution.py:20
  61.8 5.4 %collective-permute-start.4 = (f32[3,1,4,24,256]{4,3,2,1,0:T(8,128)S(1)}, f32[3,1,4,24,256]{4,3,2,1,0:T(8,128)S(1)}, u32[]{:S(2)}, u32[]{:S(2)}) collective-permute-start(f32[3,1,4,24,256]{4,3,2,1,0:T(8,128)S(1)} %maximum_maximum_fusion.10), channel_id=1, source_target_pairs={{1,0},{2,1},{3,2},{4,3},{5,4},{6,5},{7,6},{8,7},{9,8},{10,9},{11,1... | collective-permute-start | bytes 884744 | tf_op jit(solution)/shard_map/ppermute | solution.py:23
  68.3 12.9 %collective-permute-start.7 = (f32[3,1,4,24,256]{4,3,2,1,0:T(8,128)S(1)}, f32[3,1,4,24,256]{4,3,2,1,0:T(8,128)S(1)}, u32[]{:S(2)}, u32[]{:S(2)}) collective-permute-start(f32[3,1,4,24,256]{4,3,2,1,0:T(8,128)S(1)} %pad_maximum_fusion.12), channel_id=1, source_target_pairs={{1,0},{2,1},{3,2},{4,3},{5,4},{6,5},{7,6},{8,7},{9,8},{10,9},{11,1... | collective-permute-start | bytes 884744 | tf_op jit(solution)/shard_map/ppermute | solution.py:23
  69.7 12.0 %collective-permute-start.6 = (f32[3,1,4,24,256]{4,3,2,1,0:T(8,128)S(1)}, f32[3,1,4,24,256]{4,3,2,1,0:T(8,128)S(1)}, u32[]{:S(2)}, u32[]{:S(2)}) collective-permute-start(f32[3,1,4,24,256]{4,3,2,1,0:T(8,128)S(1)} %pad_maximum_fusion.12), channel_id=1, source_target_pairs={{0,1},{1,2},{2,3},{3,4},{4,5},{5,6},{6,7},{7,8},{8,9},{9,10},{10,1... | collective-permute-start | bytes 884744 | tf_op jit(solution)/shard_map/ppermute | solution.py:20
  88.2 10.4 %collective-permute-start.8 = (f32[4,1,4,24,256]{4,3,2,1,0:T(8,128)}, f32[4,1,4,24,256]{4,3,2,1,0:T(8,128)S(1)}, u32[]{:S(2)}, u32[]{:S(2)}) collective-permute-start(f32[4,1,4,24,256]{4,3,2,1,0:T(8,128)} %maximum_maximum_fusion.9), channel_id=1, source_target_pairs={{1,0},{2,1},{3,2},{4,3},{5,4},{6,5},{7,6},{8,7},{9,8},{10,9},{11,1... | collective-permute-start | bytes 1179656 | tf_op jit(solution)/shard_map/ppermute | solution.py:23
  90.2 8.5 %collective-permute-start.9 = (f32[4,1,4,24,256]{4,3,2,1,0:T(8,128)}, f32[4,1,4,24,256]{4,3,2,1,0:T(8,128)S(1)}, u32[]{:S(2)}, u32[]{:S(2)}) collective-permute-start(f32[4,1,4,24,256]{4,3,2,1,0:T(8,128)} %maximum_maximum_fusion.9), channel_id=1, source_target_pairs={{0,1},{1,2},{2,3},{3,4},{4,5},{5,6},{6,7},{7,8},{8,9},{9,10},{10,1... | collective-permute-start | bytes 1179656 | tf_op jit(solution)/shard_map/ppermute | solution.py:20
  100.1 10.2 %collective-permute-start.11 = (f32[4,1,4,24,256]{4,3,2,1,0:T(8,128)S(1)}, f32[4,1,4,24,256]{4,3,2,1,0:T(8,128)S(1)}, u32[]{:S(2)}, u32[]{:S(2)}) collective-permute-start(f32[4,1,4,24,256]{4,3,2,1,0:T(8,128)S(1)} %pad_maximum_fusion.9), channel_id=1, source_target_pairs={{1,0},{2,1},{3,2},{4,3},{5,4},{6,5},{7,6},{8,7},{9,8},{10,9},{11,1... | collective-permute-start | bytes 1179656 | tf_op jit(solution)/shard_map/ppermute | solution.py:23
  101.4 9.6 %collective-permute-start.10 = (f32[4,1,4,24,256]{4,3,2,1,0:T(8,128)S(1)}, f32[4,1,4,24,256]{4,3,2,1,0:T(8,128)S(1)}, u32[]{:S(2)}, u32[]{:S(2)}) collective-permute-start(f32[4,1,4,24,256]{4,3,2,1,0:T(8,128)S(1)} %pad_maximum_fusion.9), channel_id=1, source_target_pairs={{0,1},{1,2},{2,3},{3,4},{4,5},{5,6},{6,7},{7,8},{8,9},{9,10},{10,1... | collective-permute-start | bytes 1179656 | tf_op jit(solution)/shard_map/ppermute | solution.py:20
  117.4 13.7 %collective-permute-start.13 = (f32[5,1,4,24,256]{4,3,2,1,0:T(8,128)}, f32[5,1,4,24,256]{4,3,2,1,0:T(8,128)S(1)}, u32[]{:S(2)}, u32[]{:S(2)}) collective-permute-start(f32[5,1,4,24,256]{4,3,2,1,0:T(8,128)} %maximum_maximum_fusion.6), channel_id=1, source_target_pairs={{0,1},{1,2},{2,3},{3,4},{4,5},{5,6},{6,7},{7,8},{8,9},{9,10},{10,1... | collective-permute-start | bytes 1474568 | tf_op jit(solution)/shard_map/ppermute | solution.py:20
  125.1 5.9 %collective-permute-start.12 = (f32[5,1,4,24,256]{4,3,2,1,0:T(8,128)}, f32[5,1,4,24,256]{4,3,2,1,0:T(8,128)S(1)}, u32[]{:S(2)}, u32[]{:S(2)}) collective-permute-start(f32[5,1,4,24,256]{4,3,2,1,0:T(8,128)} %maximum_maximum_fusion.6), channel_id=1, source_target_pairs={{1,0},{2,1},{3,2},{4,3},{5,4},{6,5},{7,6},{8,7},{9,8},{10,9},{11,1... | collective-permute-start | bytes 1474568 | tf_op jit(solution)/shard_map/ppermute | solution.py:23
  133.0 19.2 %collective-permute-start.15 = (f32[5,1,4,24,256]{4,3,2,1,0:T(8,128)S(1)}, f32[5,1,4,24,256]{4,3,2,1,0:T(8,128)S(1)}, u32[]{:S(2)}, u32[]{:S(2)}) collective-permute-start(f32[5,1,4,24,256]{4,3,2,1,0:T(8,128)S(1)} %pad_maximum_fusion.6), channel_id=1, source_target_pairs={{1,0},{2,1},{3,2},{4,3},{5,4},{6,5},{7,6},{8,7},{9,8},{10,9},{11,1... | collective-permute-start | bytes 1474568 | tf_op jit(solution)/shard_map/ppermute | solution.py:23
  134.3 18.4 %collective-permute-start.14 = (f32[5,1,4,24,256]{4,3,2,1,0:T(8,128)S(1)}, f32[5,1,4,24,256]{4,3,2,1,0:T(8,128)S(1)}, u32[]{:S(2)}, u32[]{:S(2)}) collective-permute-start(f32[5,1,4,24,256]{4,3,2,1,0:T(8,128)S(1)} %pad_maximum_fusion.6), channel_id=1, source_target_pairs={{0,1},{1,2},{2,3},{3,4},{4,5},{5,6},{6,7},{7,8},{8,9},{9,10},{10,1... | collective-permute-start | bytes 1474568 | tf_op jit(solution)/shard_map/ppermute | solution.py:20
  159.2 29.0 %all-to-all-start.1 = ((f32[32,1,1280]{2,1,0:T(1,128)}), f32[32,1,1280]{2,1,0:T(1,128)S(1)}, u32[]{:S(2)}, u32[]{:S(2)}) async-start(f32[32,1,1280]{2,1,0:T(1,128)} %all_to_all.25), calls=%async_computation.1 | async-start | bytes 327680 | tf_op jit(solution)/shard_map/all_to_all | solution.py:246
  (72 other events, 629.7 us)

commit v10 on v8

--- a/solution.py
+++ b/solution.py
@@ -13,14 +13,17 @@
 
 def halo_rows(fields):
     devices = lax.axis_size("gx")
-    up = [(i, i + 1) for i in range(devices - 1)]
-    down = [(i + 1, i) for i in range(devices - 1)]
+    odd = lax.axis_index("gx") % 2 == 1
+    within = [(i, i ^ 1) for i in range(devices) if i ^ 1 < devices]
+    across = [(i, i + 1) for i in range(1, devices - 1, 2)] + [(i + 1, i) for i in range(1, devices - 1, 2)]
     packed = jnp.concatenate(fields, axis=DEPTH_AXIS)
     length = packed.shape[ROW_AXIS]
-    before = lax.ppermute(
-        lax.slice_in_dim(packed, length - HALO, length, axis=ROW_AXIS), "gx", up
-    )
-    after = lax.ppermute(lax.slice_in_dim(packed, 0, HALO, axis=ROW_AXIS), "gx", down)
+    last = lax.slice_in_dim(packed, length - HALO, length, axis=ROW_AXIS)
+    first = lax.slice_in_dim(packed, 0, HALO, axis=ROW_AXIS)
+    got_within = lax.ppermute(jnp.where(odd, first, last), "gx", within)
+    got_across = lax.ppermute(jnp.where(odd, last, first), "gx", across)
+    before = jnp.where(odd, got_within, got_across)
+    after = jnp.where(odd, got_across, got_within)
     padded = jnp.concatenate([before, packed, after], axis=ROW_AXIS)
     out, start = [], 0
     for f in fields:

time: 184 us -> 176 us (0.957)
  other arithmetic: 21.4 us -> 32.5 us
  waiting for transfers between devices: 37.2 us -> 26.8 us
  starting transfers between devices: 98.2 us -> 89.7 us
    all_to_all x1, starting transfers between devices: 20.5 us -> 10.7 us  [on_device(): got = lax.all_to_all(packed, 'gx', 0, 0, tiled=True)]
    ppermute x16, waiting for transfers between devices: 12.8 us -> 4.94 us  [the longest x8 4.92 us: halo_rows(): got_within = lax.ppermute(jnp.where(odd, first, last), 'gx', within)]
    ppermute x16, starting transfers between devices: 58.2 us -> 63.9 us  [the longest x8 58.1 us: halo_rows(): got_within = lax.ppermute(jnp.where(odd, first, last), 'gx', within)]
    all_to_all x1, starting transfers between devices: 12.2 us -> 7.81 us  [gather_sum(): return jnp.sum(lax.all_to_all(copies, 'gx', 0, 0, tiled=True), axis=0)]
    mul x3, other arithmetic: 1.33 us -> 4.4 us  [on_device(): (pressure - TIME_STEP * water_kappa * (derive(flow_x, 4, False) + stencil...]
    reduce_sum x4, other arithmetic: 0.2 us -> 2.93 us  [on_device(): surface = jnp.sum(pressure[0] * bottom, axis=2)]
    mul x1 -> x4, other arithmetic: 0.38 us -> 2.98 us  [on_device(): (flow_x - TIME_STEP * water_buoy * derive(pressure, 4, True)) * live]
    unnamed x64 -> x60, local copies, waits for them, and re-layouts: 8.81 us -> 8.74 us
  transfers between devices with their start and end apart: 19 -> 19, of which waited for: 11 -> 10; matrix products, arithmetic and copies ran while one was open for 2% -> 4% of each run, Pallas kernels for 0% -> 0%
where the time goes in v10:
time: 176 us
  starting transfers between devices  89.7 us (51%)
  other arithmetic  32.5 us (18%)
  waiting for transfers between devices  26.8 us (15%)
  local copies, waits for them, and re-layouts  20 us (11%)
  matrix products  3.46 us (2%)
  between operations  3.19 us (2%)
    ppermute x8, starting transfers between devices, halo_rows(): got_within = lax.ppermute(jnp.where(odd, first, last), 'gx', within)  58.1 us
    all_to_all x1, waiting for transfers between devices, on_device(): lax.all_to_all(rock_in, 'gx', split_axis=3, concat_axis=1, tiled=True)  10.7 us
    all_to_all x1, starting transfers between devices, on_device(): got = lax.all_to_all(packed, 'gx', 0, 0, tiled=True)  10.7 us
    unnamed x60, local copies, waits for them, and re-layouts  8.74 us
    all_to_all x1, starting transfers between devices, gather_sum(): return jnp.sum(lax.all_to_all(copies, 'gx', 0, 0, tiled=True), axis=0)  7.81 us
    all_to_all x1, starting transfers between devices, on_device(): lax.all_to_all(rock_in, 'gx', split_axis=3, concat_axis=1, tiled=True)  7.3 us
    all_to_all x1, waiting for transfers between devices, on_device(): got = lax.all_to_all(packed, 'gx', 0, 0, tiled=True)  6.45 us
    ppermute x8, starting transfers between devices, halo_rows(): got_across = lax.ppermute(jnp.where(odd, last, first), 'gx', across)  5.8 us
  transfers between devices with their start and end apart: 19, of which 10 were waited for; matrix products, arithmetic and copies ran while one was open for 4% of the time, Pallas kernels for 0%

profile of v10, /device:TPU:0, one launch (start us, length us, event | category | flops | bytes accessed | tf_op | source)
XLA Modules:
  0.0 175.6 jit_solution(17505844004298466910)
XLA Ops:
  3.1 1.9 %copy.4731 = f32[21,8,4,128]{0,1,2,3:T(8,128)S(1)} copy(f32[21,8,4,128]{3,1,2,0:T(8,128)S(1)} %pad_maximum_fusion.9) | data formatting | bytes 688128 | tf_op jit(solution)/shard_map/concatenate | solution.py:95
  5.1 2.6 %reshape.1017 = f32[32,1,2688]{2,1,0:T(1,128)} reshape(f32[128,4,8,21]{3,2,1,0:T(8,128)S(1)} %bitcast.311) | data formatting | bytes 688128
  7.7 7.3 %all-to-all-start = ((f32[32,1,2688]{2,1,0:T(1,128)}), f32[32,1,2688]{2,1,0:T(1,128)S(1)}, u32[]{:S(2)}, u32[]{:S(2)}) async-start(f32[32,1,2688]{2,1,0:T(1,128)} %reshape.1017), calls=%async_computation | async-start | bytes 688128 | tf_op jit(solution)/shard_map/all_to_all | solution.py:103
  16.6 10.7 %all-to-all-done = f32[32,1,2688]{2,1,0:T(1,128)S(1)} async-done(((f32[32,1,2688]{2,1,0:T(1,128)}), f32[32,1,2688]{2,1,0:T(1,128)S(1)}, u32[]{:S(2)}, u32[]{:S(2)}) %all-to-all-start) | async-done | bytes 344096 | tf_op jit(solution)/shard_map/all_to_all | solution.py:103
  27.8 1.5 reduce.33
  29.3 2.3 %reshape.1018 = f32[128,4,8,21]{3,2,1,0:T(8,128)S(1)} reshape(f32[32,2688]{1,0:T(8,128)S(1)} %reduce.33) | data formatting | bytes 688128
  31.6 1.6 copy.5010
  33.1 2.3 %copy.4734 = f32[21,256,4,4]{1,3,2,0:T(4,128)S(1)} copy(f32[21,256,4,4]{0,1,3,2:T(8,128)} %bitcast.313) | data formatting | bytes 688128 | tf_op jit(solution)/shard_map/all_to_all | solution.py:103
  39.3 9.9 %collective-permute-start.2 = (f32[2,1,4,24,256]{4,3,2,1,0:T(8,128)S(1)}, f32[2,1,4,24,256]{4,3,2,1,0:T(8,128)S(1)}, u32[]{:S(2)}, u32[]{:S(2)}) collective-permute-start(f32[2,1,4,24,256]{4,3,2,1,0:T(8,128)S(1)} %copy.4758), channel_id=1, source_target_pairs={{0,1},{1,0},{2,3},{3,2},{4,5},{5,4},{6,7},{7,6},{8,9},{9,8},{10,11... | collective-permute-start | bytes 589832 | tf_op jit(solution)/shard_map/ppermute | solution.py:23
  53.6 7.8 %all-to-all-start.1 = ((f32[32,1,128]{2,1,0:T(1,128)}), f32[32,1,128]{2,1,0:T(1,128)S(1)}, u32[]{:S(2)}, u32[]{:S(2)}) async-start(f32[32,1,128]{2,1,0:T(1,128)} %broadcast_in_dim.6), calls=%async_computation.1 | async-start | bytes 32768 | tf_op jit(solution)/shard_map/all_to_all | solution.py:45
  63.8 4.7 %all-to-all-done.1 = f32[32,1,128]{2,1,0:T(1,128)S(1)} async-done(((f32[32,1,128]{2,1,0:T(1,128)}), f32[32,1,128]{2,1,0:T(1,128)S(1)}, u32[]{:S(2)}, u32[]{:S(2)}) %all-to-all-start.1) | async-done | bytes 16416 | tf_op jit(solution)/shard_map/all_to_all | solution.py:45
  74.1 9.6 %collective-permute-start.6 = (f32[2,1,4,24,256]{4,3,2,1,0:T(8,128)S(1)}, f32[2,1,4,24,256]{4,3,2,1,0:T(8,128)S(1)}, u32[]{:S(2)}, u32[]{:S(2)}) collective-permute-start(f32[2,1,4,24,256]{4,3,2,1,0:T(8,128)S(1)} %copy.4784), channel_id=1, source_target_pairs={{0,1},{1,0},{2,3},{3,2},{4,5},{5,4},{6,7},{7,6},{8,9},{9,8},{10,11... | collective-permute-start | bytes 589832 | tf_op jit(solution)/shard_map/ppermute | solution.py:23
  83.7 1.1 collective-permute-done.6
  88.9 5.0 %collective-permute-start.9 = (f32[3,1,4,24,256]{4,3,2,1,0:T(8,128)S(1)}, f32[3,1,4,24,256]{4,3,2,1,0:T(8,128)S(1)}, u32[]{:S(2)}, u32[]{:S(2)}) collective-permute-start(f32[3,1,4,24,256]{4,3,2,1,0:T(8,128)S(1)} %copy.4791), channel_id=1, source_target_pairs={{0,1},{1,0},{2,3},{3,2},{4,5},{5,4},{6,7},{7,6},{8,9},{9,8},{10,11... | collective-permute-start | bytes 884744 | tf_op jit(solution)/shard_map/ppermute | solution.py:23
  97.6 12.4 %collective-permute-start.10 = (f32[3,1,4,24,256]{4,3,2,1,0:T(8,128)S(1)}, f32[3,1,4,24,256]{4,3,2,1,0:T(8,128)S(1)}, u32[]{:S(2)}, u32[]{:S(2)}) collective-permute-start(f32[3,1,4,24,256]{4,3,2,1,0:T(8,128)S(1)} %copy.4799), channel_id=1, source_target_pairs={{0,1},{1,0},{2,3},{3,2},{4,5},{5,4},{6,7},{7,6},{8,9},{9,8},{10,11... | collective-permute-start | bytes 884744 | tf_op jit(solution)/shard_map/ppermute | solution.py:23
  115.1 1.3 fusion.1143
  116.6 5.6 %collective-permute-start.13 = (f32[4,1,4,24,256]{4,3,2,1,0:T(8,128)S(1)}, f32[4,1,4,24,256]{4,3,2,1,0:T(8,128)S(1)}, u32[]{:S(2)}, u32[]{:S(2)}) collective-permute-start(f32[4,1,4,24,256]{4,3,2,1,0:T(8,128)S(1)} %copy.4806), channel_id=1, source_target_pairs={{0,1},{1,0},{2,3},{3,2},{4,5},{5,4},{6,7},{7,6},{8,9},{9,8},{10,11... | collective-permute-start | bytes 1179656 | tf_op jit(solution)/shard_map/ppermute | solution.py:23
  126.7 15.5 %collective-permute-start.14 = (f32[4,1,4,24,256]{4,3,2,1,0:T(8,128)S(1)}, f32[4,1,4,24,256]{4,3,2,1,0:T(8,128)S(1)}, u32[]{:S(2)}, u32[]{:S(2)}) collective-permute-start(f32[4,1,4,24,256]{4,3,2,1,0:T(8,128)S(1)} %copy.4814), channel_id=1, source_target_pairs={{0,1},{1,0},{2,3},{3,2},{4,5},{5,4},{6,7},{7,6},{8,9},{9,8},{10,11... | collective-permute-start | bytes 1179656 | tf_op jit(solution)/shard_map/ppermute | solution.py:23
  142.2 1.5 fusion.100
  144.7 1.2 maximum_maximum_fusion.1
  147.1 3.5 %subtract_multiply_fusion = f32[4,1,4,12,256]{4,2,3,1,0:T(4,128)S(1)} fusion(f32[4,1,4,12,256]{4,2,3,1,0:T(4,128)} %get-tuple-element.262, f32[4,1,4,24,256]{4,2,3,1,0:T(4,128)S(1)} %get-tuple-element.214, f32[4,1,8,24,256]{4,2,3,1,0:T(8,128)} %get-tuple-element.232, f32[4,1,8,24,256]{4,2,3,1,0:T(8,128)S(1)} %get-tuple-element.231, ...), kind=kLoop, calls=%fused_computation.372 | loop fusion | flops 1916928 | bytes 2457600 | tf_op jit(solution)/shard_map/mul | solution.py:203
  153.1 10.7 %all-to-all-start.2 = ((f32[32,1,896]{2,1,0:T(1,128)}), f32[32,1,896]{2,1,0:T(1,128)S(1)}, u32[]{:S(2)}, u32[]{:S(2)}) async-start(f32[32,1,896]{2,1,0:T(1,128)} %all_to_all.29), calls=%async_computation.2 | async-start | bytes 229376 | tf_op jit(solution)/shard_map/all_to_all | solution.py:249
  163.8 1.4 fusion.506
  165.3 6.4 %all-to-all-done.2 = f32[32,1,896]{2,1,0:T(1,128)S(1)} async-done(((f32[32,1,896]{2,1,0:T(1,128)}), f32[32,1,896]{2,1,0:T(1,128)S(1)}, u32[]{:S(2)}, u32[]{:S(2)}) %all-to-all-start.2) | async-done | bytes 114720 | tf_op jit(solution)/shard_map/all_to_all | solution.py:249
  (257 shorter events, 44.7 us)
Async XLA Ops:
  7.7 19.6 %all-to-all-start = ((f32[32,1,2688]{2,1,0:T(1,128)}), f32[32,1,2688]{2,1,0:T(1,128)S(1)}, u32[]{:S(2)}, u32[]{:S(2)}) async-start(f32[32,1,2688]{2,1,0:T(1,128)} %reshape.1017), calls=%async_computation | async-start | bytes 688128 | tf_op jit(solution)/shard_map/all_to_all | solution.py:103
  35.5 1.5 collective-permute-start.1
  35.6 1.4 collective-permute-start
  38.6 10.6 %collective-permute-start.3 = (f32[2,1,4,24,256]{4,3,2,1,0:T(8,128)S(1)}, f32[2,1,4,24,256]{4,3,2,1,0:T(8,128)S(1)}, u32[]{:S(2)}, u32[]{:S(2)}) collective-permute-start(f32[2,1,4,24,256]{4,3,2,1,0:T(8,128)S(1)} %copy.4758), channel_id=1, source_target_pairs={{1,2},{3,4},{5,6},{7,8},{9,10},{11,12},{13,14},{15,16},{17,18},{19... | collective-permute-start | bytes 589832 | tf_op jit(solution)/shard_map/ppermute | solution.py:24
  39.3 11.0 %collective-permute-start.2 = (f32[2,1,4,24,256]{4,3,2,1,0:T(8,128)S(1)}, f32[2,1,4,24,256]{4,3,2,1,0:T(8,128)S(1)}, u32[]{:S(2)}, u32[]{:S(2)}) collective-permute-start(f32[2,1,4,24,256]{4,3,2,1,0:T(8,128)S(1)} %copy.4758), channel_id=1, source_target_pairs={{0,1},{1,0},{2,3},{3,2},{4,5},{5,4},{6,7},{7,6},{8,9},{9,8},{10,11... | collective-permute-start | bytes 589832 | tf_op jit(solution)/shard_map/ppermute | solution.py:23
  49.1 38.3 %copy-start.19 = (s32[128]{0:T(128)}, s32[128]{0:T(128)S(1)}, u32[]{:S(2)}) copy-start(s32[128]{0:T(128)S(1)} %fusion.1127) | copy-start | bytes 1540
  50.5 18.0 %copy-start.14 = (f32[4,1,128]{2,1,0:T(1,128)S(1)}, f32[4,1,128]{2,1,0:T(1,128)}, u32[]{:S(2)}) copy-start(f32[4,1,128]{2,1,0:T(1,128)} %param.41) | copy-start | bytes 6148
  53.6 14.9 %all-to-all-start.1 = ((f32[32,1,128]{2,1,0:T(1,128)}), f32[32,1,128]{2,1,0:T(1,128)S(1)}, u32[]{:S(2)}, u32[]{:S(2)}) async-start(f32[32,1,128]{2,1,0:T(1,128)} %broadcast_in_dim.6), calls=%async_computation.1 | async-start | bytes 32768 | tf_op jit(solution)/shard_map/all_to_all | solution.py:45
  70.5 1.5 collective-permute-start.5
  70.5 1.4 collective-permute-start.4
  73.4 10.3 %collective-permute-start.7 = (f32[2,1,4,24,256]{4,3,2,1,0:T(8,128)S(1)}, f32[2,1,4,24,256]{4,3,2,1,0:T(8,128)S(1)}, u32[]{:S(2)}, u32[]{:S(2)}) collective-permute-start(f32[2,1,4,24,256]{4,3,2,1,0:T(8,128)S(1)} %copy.4784), channel_id=1, source_target_pairs={{1,2},{3,4},{5,6},{7,8},{9,10},{11,12},{13,14},{15,16},{17,18},{19... | collective-permute-start | bytes 589832 | tf_op jit(solution)/shard_map/ppermute | solution.py:24
  74.1 10.7 %collective-permute-start.6 = (f32[2,1,4,24,256]{4,3,2,1,0:T(8,128)S(1)}, f32[2,1,4,24,256]{4,3,2,1,0:T(8,128)S(1)}, u32[]{:S(2)}, u32[]{:S(2)}) collective-permute-start(f32[2,1,4,24,256]{4,3,2,1,0:T(8,128)S(1)} %copy.4784), channel_id=1, source_target_pairs={{0,1},{1,0},{2,3},{3,2},{4,5},{5,4},{6,7},{7,6},{8,9},{9,8},{10,11... | collective-permute-start | bytes 589832 | tf_op jit(solution)/shard_map/ppermute | solution.py:23
  88.9 6.2 %collective-permute-start.9 = (f32[3,1,4,24,256]{4,3,2,1,0:T(8,128)S(1)}, f32[3,1,4,24,256]{4,3,2,1,0:T(8,128)S(1)}, u32[]{:S(2)}, u32[]{:S(2)}) collective-permute-start(f32[3,1,4,24,256]{4,3,2,1,0:T(8,128)S(1)} %copy.4791), channel_id=1, source_target_pairs={{0,1},{1,0},{2,3},{3,2},{4,5},{5,4},{6,7},{7,6},{8,9},{9,8},{10,11... | collective-permute-start | bytes 884744 | tf_op jit(solution)/shard_map/ppermute | solution.py:23
  93.9 1.2 collective-permute-start.8
  96.9 13.7 %collective-permute-start.11 = (f32[3,1,4,24,256]{4,3,2,1,0:T(8,128)S(1)}, f32[3,1,4,24,256]{4,3,2,1,0:T(8,128)S(1)}, u32[]{:S(2)}, u32[]{:S(2)}) collective-permute-start(f32[3,1,4,24,256]{4,3,2,1,0:T(8,128)S(1)} %copy.4799), channel_id=1, source_target_pairs={{1,2},{3,4},{5,6},{7,8},{9,10},{11,12},{13,14},{15,16},{17,18},{19... | collective-permute-start | bytes 884744 | tf_op jit(solution)/shard_map/ppermute | solution.py:24
  97.6 13.6 %collective-permute-start.10 = (f32[3,1,4,24,256]{4,3,2,1,0:T(8,128)S(1)}, f32[3,1,4,24,256]{4,3,2,1,0:T(8,128)S(1)}, u32[]{:S(2)}, u32[]{:S(2)}) collective-permute-start(f32[3,1,4,24,256]{4,3,2,1,0:T(8,128)S(1)} %copy.4799), channel_id=1, source_target_pairs={{0,1},{1,0},{2,3},{3,2},{4,5},{5,4},{6,7},{7,6},{8,9},{9,8},{10,11... | collective-permute-start | bytes 884744 | tf_op jit(solution)/shard_map/ppermute | solution.py:23
  116.6 6.9 %collective-permute-start.13 = (f32[4,1,4,24,256]{4,3,2,1,0:T(8,128)S(1)}, f32[4,1,4,24,256]{4,3,2,1,0:T(8,128)S(1)}, u32[]{:S(2)}, u32[]{:S(2)}) collective-permute-start(f32[4,1,4,24,256]{4,3,2,1,0:T(8,128)S(1)} %copy.4806), channel_id=1, source_target_pairs={{0,1},{1,0},{2,3},{3,2},{4,5},{5,4},{6,7},{7,6},{8,9},{9,8},{10,11... | collective-permute-start | bytes 1179656 | tf_op jit(solution)/shard_map/ppermute | solution.py:23
  122.1 1.4 collective-permute-start.12
  125.8 17.9 %collective-permute-start.15 = (f32[4,1,4,24,256]{4,3,2,1,0:T(8,128)S(1)}, f32[4,1,4,24,256]{4,3,2,1,0:T(8,128)S(1)}, u32[]{:S(2)}, u32[]{:S(2)}) collective-permute-start(f32[4,1,4,24,256]{4,3,2,1,0:T(8,128)S(1)} %copy.4814), channel_id=1, source_target_pairs={{1,2},{3,4},{5,6},{7,8},{9,10},{11,12},{13,14},{15,16},{17,18},{19... | collective-permute-start | bytes 1179656 | tf_op jit(solution)/shard_map/ppermute | solution.py:24
  126.7 17.0 %collective-permute-start.14 = (f32[4,1,4,24,256]{4,3,2,1,0:T(8,128)S(1)}, f32[4,1,4,24,256]{4,3,2,1,0:T(8,128)S(1)}, u32[]{:S(2)}, u32[]{:S(2)}) collective-permute-start(f32[4,1,4,24,256]{4,3,2,1,0:T(8,128)S(1)} %copy.4814), channel_id=1, source_target_pairs={{0,1},{1,0},{2,3},{3,2},{4,5},{5,4},{6,7},{7,6},{8,9},{9,8},{10,11... | collective-permute-start | bytes 1179656 | tf_op jit(solution)/shard_map/ppermute | solution.py:23
  147.1 18.1 %copy-start.3 = (f32[4,12,256]{2,0,1:T(4,128)S(1)}, f32[4,12,256]{2,0,1:T(4,128)}, u32[]{:S(2)}) copy-start(f32[4,12,256]{2,0,1:T(4,128)} %get-tuple-element.277) | copy-start | bytes 147460
  147.1 18.2 %copy-start.4 = (f32[1,1,4,12,256]{4,2,3,1,0:T(4,128)S(1)}, f32[1,1,4,12,256]{4,2,3,1,0:T(4,128)}, u32[]{:S(2)}) copy-start(f32[1,1,4,12,256]{4,2,3,1,0:T(4,128)} %get-tuple-element.279) | copy-start | bytes 147460
  150.7 21.7 %copy-start.23 = (f32[1,1,128]{2,1,0:T(1,128)S(1)}, f32[1,1,128]{2,1,0:T(1,128)}, u32[]{:S(2)}) copy-start(f32[1,1,128]{2,1,0:T(1,128)} %copy-done.22) | copy-start | bytes 1540
  153.1 18.7 %all-to-all-start.2 = ((f32[32,1,896]{2,1,0:T(1,128)}), f32[32,1,896]{2,1,0:T(1,128)S(1)}, u32[]{:S(2)}, u32[]{:S(2)}) async-start(f32[32,1,896]{2,1,0:T(1,128)} %all_to_all.29), calls=%async_computation.2 | async-start | bytes 229376 | tf_op jit(solution)/shard_map/all_to_all | solution.py:249
  (19 other events, 163.6 us)

commit v11 on v10

--- a/solution.py
+++ b/solution.py
@@ -154,36 +154,47 @@
         water_waves = pressure.shape[0]
         floor_pressure = jnp.sum(pressure * bottom, axis=3)
         pending = [(at, floor_pressure[rock_waves + i : rock_waves + i + 1]) for i, (at, _) in enumerate(pending)]
+        (dx_sxx, dz_sxz, dx_sxy, dz_syz, dx_sxz, dz_szz, flow_x, flow_z_part) = lax.optimization_barrier(
+            (
+                derive(sig_xx, 4, True),
+                derive(sig_xz, 3, False),
+                derive(sig_xy, 4, False),
+                derive(sig_yz, 3, False),
+                derive(sig_xz, 4, False),
+                derive(sig_zz, 3, True),
+                (flow_x - TIME_STEP * water_buoy * derive(pressure, 4, True)) * live,
+                (flow_z - TIME_STEP * water_buoy * derive(pressure, 3, True)) * above,
+            )
+        )
         sxy_pad, syy_pad, syz_pad, p_pad = halo_rows(
             [fill_waves(f, water_waves) for f in (sig_xy, sig_yy, sig_yz)] + [pressure]
         )
         sxy_pad, syy_pad, syz_pad = [f[:rock_waves] for f in (sxy_pad, syy_pad, syz_pad)]
-        vel_x = vel_x + TIME_STEP * buoy * (
-            derive(sig_xx, 4, True) + stencil(sxy_pad, 2, False) + derive(sig_xz, 3, False)
-        )
-        vel_y = vel_y + TIME_STEP * buoy * (
-            derive(sig_xy, 4, False) + stencil(syy_pad, 2, True) + derive(sig_yz, 3, False)
-        )
-        vel_z = vel_z + TIME_STEP * buoy * (
-            derive(sig_xz, 4, False) + stencil(syz_pad, 2, False) + derive(sig_zz, 3, True)
-        )
+        vel_x = vel_x + TIME_STEP * buoy * (dx_sxx + stencil(sxy_pad, 2, False) + dz_sxz)
+        vel_y = vel_y + TIME_STEP * buoy * (dx_sxy + stencil(syy_pad, 2, True) + dz_syz)
+        vel_z = vel_z + TIME_STEP * buoy * (dx_sxz + stencil(syz_pad, 2, False) + dz_szz)
         floor_velocity = fill_waves(vel_z[:, :, :, 0, :], water_waves)
-        flow_x = (flow_x - TIME_STEP * water_buoy * derive(pressure, 4, True)) * live
         flow_y = (flow_y - TIME_STEP * water_buoy * stencil(p_pad, 2, True)) * live
-        flow_z = (
-            flow_z - TIME_STEP * water_buoy * derive(pressure, 3, True)
-        ) * above + floor_velocity[:, :, :, None, :] * bottom
+        flow_z = flow_z_part + floor_velocity[:, :, :, None, :] * bottom
+        (strain_x, strain_z, dx_vy, dz_vy, shear_xz, dx_ux, dz_uz) = lax.optimization_barrier(
+            (
+                derive(vel_x, 4, False),
+                derive(vel_z, 3, False),
+                derive(vel_y, 4, True),
+                derive(vel_y, 3, True),
+                derive(vel_x, 3, True) + derive(vel_z, 4, True),
+                derive(flow_x, 4, False),
+                derive(flow_z, 3, False),
+            )
+        )
         vx_pad, vy_pad, vz_pad, uy_pad = halo_rows(
             [fill_waves(f, water_waves) for f in (vel_x, vel_y, vel_z)] + [flow_y]
         )
         vx_pad, vy_pad, vz_pad = [f[:rock_waves] for f in (vx_pad, vy_pad, vz_pad)]
-        strain_x = derive(vel_x, 4, False)
         strain_y = stencil(vy_pad, 2, False)
-        strain_z = derive(vel_z, 3, False)
         dilation = strain_x + strain_y + strain_z
-        shear_xy = stencil(vx_pad, 2, True) + derive(vel_y, 4, True)
-        shear_xz = derive(vel_x, 3, True) + derive(vel_z, 4, True)
-        shear_yz = derive(vel_y, 3, True) + stencil(vz_pad, 2, True)
+        shear_xy = stencil(vx_pad, 2, True) + dx_vy
+        shear_yz = dz_vy + stencil(vz_pad, 2, True)
         lam_part = lam * dilation
         sig_xx = sig_xx + TIME_STEP * (lam_part + 2.0 * mu * strain_x)
         sig_yy = sig_yy + TIME_STEP * (lam_part + 2.0 * mu * strain_y)
@@ -204,7 +215,7 @@
             pressure
             - TIME_STEP
             * water_kappa
-            * (derive(flow_x, 4, False) + stencil(uy_pad, 2, False) + derive(flow_z, 3, False))
+            * (dx_ux + stencil(uy_pad, 2, False) + dz_uz)
         ) * live
         pressure = pressure.at[0].add(wavelet[step][:, None, None, None] * source_hot)
         surface = jnp.sum(pressure[0] * bottom, axis=2)

time: 176 us -> 172 us (0.977)
  starting transfers between devices: 89.7 us -> 79.2 us
  other arithmetic: 32.5 us -> 38.6 us
  waiting for transfers between devices: 26.8 us -> 23.9 us
  local copies, waits for them, and re-layouts: 20 us -> 22.5 us
    add x16 -> x58, other arithmetic: 3.44 us -> 13.6 us  [the longest x32 8.58 us: stencil(): summed = addend if summed is None else summed + addend]
    ppermute x8, starting transfers between devices: 58.1 us -> 48.9 us  [halo_rows(): got_within = lax.ppermute(jnp.where(odd, first, last), 'gx', within)]
    ppermute x8, waiting for transfers between devices: 4.92 us -> 1.92 us  [halo_rows(): got_within = lax.ppermute(jnp.where(odd, first, last), 'gx', within)]
    reduce_sum x4, other arithmetic: 2.93 us -> 0.2 us  [on_device(): surface = jnp.sum(pressure[0] * bottom, axis=2)]
    mul x10 -> x14, other arithmetic: 7.44 us -> 6.04 us  [the longest x4 2.07 us: on_device(): (pressure - TIME_STEP * water_kappa * (dx_ux + stencil(uy_pad, 2, False)...]
    unnamed x60 -> x88, local copies, waits for them, and re-layouts: 8.74 us -> 9.95 us
  transfers between devices with their start and end apart: 19 -> 19, of which waited for: 10 -> 7; matrix products, arithmetic and copies ran while one was open for 4% -> 10% of each run, Pallas kernels for 0% -> 0%
where the time goes in v11:
time: 172 us; the launch traced here: 171 us
  starting transfers between devices  79.2 us (46%)
  other arithmetic  38.6 us (22%)
  waiting for transfers between devices  23.9 us (14%)
  local copies, waits for them, and re-layouts  22.5 us (13%)
  between operations  3.5 us (2%)
  matrix products  3.44 us (2%)
    ppermute x8, starting transfers between devices, halo_rows(): got_within = lax.ppermute(jnp.where(odd, first, last), 'gx', within)  48.9 us
    all_to_all x1, waiting for transfers between devices, on_device(): lax.all_to_all(rock_in, 'gx', split_axis=3, concat_axis=1, tiled=True)  9.99 us
    unnamed x88, local copies, waits for them, and re-layouts  9.95 us
    all_to_all x1, starting transfers between devices, on_device(): got = lax.all_to_all(packed, 'gx', 0, 0, tiled=True)  9.15 us
    add x32, other arithmetic, stencil(): summed = addend if summed is None else summed + addend  8.58 us
    all_to_all x1, starting transfers between devices, gather_sum(): return jnp.sum(lax.all_to_all(copies, 'gx', 0, 0, tiled=True), axis=0)  8.06 us
    all_to_all x1, waiting for transfers between devices, on_device(): got = lax.all_to_all(packed, 'gx', 0, 0, tiled=True)  7.33 us
    all_to_all x1, starting transfers between devices, on_device(): lax.all_to_all(rock_in, 'gx', split_axis=3, concat_axis=1, tiled=True)  7.3 us
  transfers between devices with their start and end apart: 19, of which 7 were waited for; matrix products, arithmetic and copies ran while one was open for 10% of the time, Pallas kernels for 0%

profile of v11, /device:TPU:0, one launch (start us, length us, event | category | flops | bytes accessed | tf_op | source)
XLA Modules:
  0.0 171.1 jit_solution(9135316262266205042)
XLA Ops:
  3.1 1.9 %copy.3405 = f32[21,8,4,128]{0,1,2,3:T(8,128)S(1)} copy(f32[21,8,4,128]{3,1,2,0:T(8,128)S(1)} %pad_maximum_fusion.8) | data formatting | bytes 688128 | tf_op jit(solution)/shard_map/concatenate | solution.py:95
  5.1 2.7 %reshape.1017 = f32[32,1,2688]{2,1,0:T(1,128)} reshape(f32[128,4,8,21]{3,2,1,0:T(8,128)S(1)} %bitcast.357) | data formatting | bytes 688128
  7.7 7.3 %all-to-all-start = ((f32[32,1,2688]{2,1,0:T(1,128)}), f32[32,1,2688]{2,1,0:T(1,128)S(1)}, u32[]{:S(2)}, u32[]{:S(2)}) async-start(f32[32,1,2688]{2,1,0:T(1,128)} %reshape.1017), calls=%async_computation | async-start | bytes 688128 | tf_op jit(solution)/shard_map/all_to_all | solution.py:103
  17.3 10.0 %all-to-all-done = f32[32,1,2688]{2,1,0:T(1,128)S(1)} async-done(((f32[32,1,2688]{2,1,0:T(1,128)}), f32[32,1,2688]{2,1,0:T(1,128)S(1)}, u32[]{:S(2)}, u32[]{:S(2)}) %all-to-all-start) | async-done | bytes 344096 | tf_op jit(solution)/shard_map/all_to_all | solution.py:103
  27.8 1.5 reduce.33
  29.3 2.3 %reshape.1018 = f32[128,4,8,21]{3,2,1,0:T(8,128)S(1)} reshape(f32[32,2688]{1,0:T(8,128)S(1)} %reduce.33) | data formatting | bytes 688128
  31.6 1.6 copy.3545
  33.2 2.3 %copy.3408 = f32[21,256,4,4]{1,2,3,0:T(4,128)S(1)} copy(f32[21,256,4,4]{0,1,3,2:T(8,128)} %bitcast.359) | data formatting | bytes 688128 | tf_op jit(solution)/shard_map/all_to_all | solution.py:103
  36.5 1.7 %collective-permute-start = (f32[2,1,4,24,256]{4,3,2,1,0:T(8,128)S(1)}, f32[2,1,4,24,256]{4,3,2,1,0:T(8,128)S(1)}, u32[]{:S(2)}, u32[]{:S(2)}) collective-permute-start(f32[2,1,4,24,256]{4,3,2,1,0:T(8,128)S(1)} %maximum_bitcast_fusion.4), channel_id=1, source_target_pairs={{0,1},{1,0},{2,3},{3,2},{4,5},{5,4},{6,7},{7,6},{8,9},{9,8},{10,11... | collective-permute-start | bytes 589832 | tf_op jit(solution)/shard_map/ppermute | solution.py:23
  41.0 7.3 %collective-permute-start.2 = (f32[2,1,4,24,256]{4,3,2,1,0:T(8,128)S(1)}, f32[2,1,4,24,256]{4,3,2,1,0:T(8,128)S(1)}, u32[]{:S(2)}, u32[]{:S(2)}) collective-permute-start(f32[2,1,4,24,256]{4,3,2,1,0:T(8,128)S(1)} %maximum_bitcast_fusion.5), channel_id=1, source_target_pairs={{0,1},{1,0},{2,3},{3,2},{4,5},{5,4},{6,7},{7,6},{8,9},{9,8},{10,11... | collective-permute-start | bytes 589832 | tf_op jit(solution)/shard_map/ppermute | solution.py:23
  51.6 8.1 %all-to-all-start.1 = ((f32[32,1,128]{2,1,0:T(1,128)}), f32[32,1,128]{2,1,0:T(1,128)S(1)}, u32[]{:S(2)}, u32[]{:S(2)}) async-start(f32[32,1,128]{2,1,0:T(1,128)} %broadcast_in_dim.6), calls=%async_computation.1 | async-start | bytes 32768 | tf_op jit(solution)/shard_map/all_to_all | solution.py:45
  62.1 4.6 %all-to-all-done.1 = f32[32,1,128]{2,1,0:T(1,128)S(1)} async-done(((f32[32,1,128]{2,1,0:T(1,128)}), f32[32,1,128]{2,1,0:T(1,128)S(1)}, u32[]{:S(2)}, u32[]{:S(2)}) %all-to-all-start.1) | async-done | bytes 16416 | tf_op jit(solution)/shard_map/all_to_all | solution.py:45
  70.0 1.9 %collective-permute-start.4 = (f32[2,1,4,24,256]{4,3,2,1,0:T(8,128)S(1)}, f32[2,1,4,24,256]{4,3,2,1,0:T(8,128)S(1)}, u32[]{:S(2)}, u32[]{:S(2)}) collective-permute-start(f32[2,1,4,24,256]{4,3,2,1,0:T(8,128)S(1)} %maximum_bitcast_fusion.6), channel_id=1, source_target_pairs={{0,1},{1,0},{2,3},{3,2},{4,5},{5,4},{6,7},{7,6},{8,9},{9,8},{10,11... | collective-permute-start | bytes 589832 | tf_op jit(solution)/shard_map/ppermute | solution.py:23
  75.4 7.2 %collective-permute-start.6 = (f32[2,1,4,24,256]{4,3,2,1,0:T(8,128)S(1)}, f32[2,1,4,24,256]{4,3,2,1,0:T(8,128)S(1)}, u32[]{:S(2)}, u32[]{:S(2)}) collective-permute-start(f32[2,1,4,24,256]{4,3,2,1,0:T(8,128)S(1)} %maximum_bitcast_fusion.7), channel_id=1, source_target_pairs={{0,1},{1,0},{2,3},{3,2},{4,5},{5,4},{6,7},{7,6},{8,9},{9,8},{10,11... | collective-permute-start | bytes 589832 | tf_op jit(solution)/shard_map/ppermute | solution.py:23
  90.2 7.0 %collective-permute-start.8 = (f32[3,1,4,24,256]{4,3,2,1,0:T(8,128)S(1)}, f32[3,1,4,24,256]{4,3,2,1,0:T(8,128)S(1)}, u32[]{:S(2)}, u32[]{:S(2)}) collective-permute-start(f32[3,1,4,24,256]{4,3,2,1,0:T(8,128)S(1)} %maximum_bitcast_fusion.2), channel_id=1, source_target_pairs={{0,1},{1,0},{2,3},{3,2},{4,5},{5,4},{6,7},{7,6},{8,9},{9,8},{10,11... | collective-permute-start | bytes 884744 | tf_op jit(solution)/shard_map/ppermute | solution.py:23
  100.8 9.3 %collective-permute-start.10 = (f32[3,1,4,24,256]{4,3,2,1,0:T(8,128)S(1)}, f32[3,1,4,24,256]{4,3,2,1,0:T(8,128)S(1)}, u32[]{:S(2)}, u32[]{:S(2)}) collective-permute-start(f32[3,1,4,24,256]{4,3,2,1,0:T(8,128)S(1)} %maximum_bitcast_fusion.3), channel_id=1, source_target_pairs={{0,1},{1,0},{2,3},{3,2},{4,5},{5,4},{6,7},{7,6},{8,9},{9,8},{10,11... | collective-permute-start | bytes 884744 | tf_op jit(solution)/shard_map/ppermute | solution.py:23
  117.7 8.2 %collective-permute-start.12 = (f32[4,1,4,24,256]{4,3,2,1,0:T(8,128)S(1)}, f32[4,1,4,24,256]{4,3,2,1,0:T(8,128)S(1)}, u32[]{:S(2)}, u32[]{:S(2)}) collective-permute-start(f32[4,1,4,24,256]{4,3,2,1,0:T(8,128)S(1)} %maximum_bitcast_fusion), channel_id=1, source_target_pairs={{0,1},{1,0},{2,3},{3,2},{4,5},{5,4},{6,7},{7,6},{8,9},{9,8},{10,11... | collective-permute-start | bytes 1179656 | tf_op jit(solution)/shard_map/ppermute | solution.py:23
  127.2 1.4 scatter.16
  134.3 6.1 %collective-permute-start.14 = (f32[4,1,4,24,256]{4,3,2,1,0:T(8,128)S(1)}, f32[4,1,4,24,256]{4,3,2,1,0:T(8,128)S(1)}, u32[]{:S(2)}, u32[]{:S(2)}) collective-permute-start(f32[4,1,4,24,256]{4,3,2,1,0:T(8,128)S(1)} %maximum_bitcast_fusion.1), channel_id=1, source_target_pairs={{0,1},{1,0},{2,3},{3,2},{4,5},{5,4},{6,7},{7,6},{8,9},{9,8},{10,11... | collective-permute-start | bytes 1179656 | tf_op jit(solution)/shard_map/ppermute | solution.py:23
  141.4 1.2 fusion.44
  142.9 1.1 maximum_maximum_fusion.1
  145.3 1.6 fusion.68
  150.2 9.2 %all-to-all-start.2 = ((f32[32,1,896]{2,1,0:T(1,128)}), f32[32,1,896]{2,1,0:T(1,128)S(1)}, u32[]{:S(2)}, u32[]{:S(2)}) async-start(f32[32,1,896]{2,1,0:T(1,128)} %all_to_all.29), calls=%async_computation.2 | async-start | bytes 229376 | tf_op jit(solution)/shard_map/all_to_all | solution.py:260
  160.0 7.3 %all-to-all-done.2 = f32[32,1,896]{2,1,0:T(1,128)S(1)} async-done(((f32[32,1,896]{2,1,0:T(1,128)}), f32[32,1,896]{2,1,0:T(1,128)S(1)}, u32[]{:S(2)}, u32[]{:S(2)}) %all-to-all-start.2) | async-done | bytes 114720 | tf_op jit(solution)/shard_map/all_to_all | solution.py:260
  (326 shorter events, 54.8 us)
Async XLA Ops:
  7.7 19.6 %all-to-all-start = ((f32[32,1,2688]{2,1,0:T(1,128)}), f32[32,1,2688]{2,1,0:T(1,128)S(1)}, u32[]{:S(2)}, u32[]{:S(2)}) async-start(f32[32,1,2688]{2,1,0:T(1,128)} %reshape.1017), calls=%async_computation | async-start | bytes 688128 | tf_op jit(solution)/shard_map/all_to_all | solution.py:103
  17.2 33.3 %copy-start.19 = (pred[128]{0:T(512)(128)(4,1)}, pred[128]{0:T(512)(128)(4,1)S(1)}, u32[]{:S(2)}) copy-start(pred[128]{0:T(512)(128)(4,1)S(1)} %get-tuple-element.317) | copy-start | bytes 388
  17.3 33.2 %copy-start.28 = (s32[128]{0:T(128)}, s32[128]{0:T(128)S(1)}, u32[]{:S(2)}) copy-start(s32[128]{0:T(128)S(1)} %fusion.1154) | copy-start | bytes 1540
  35.8 2.9 %collective-permute-start.1 = (f32[2,1,4,24,256]{4,3,2,1,0:T(8,128)S(1)}, f32[2,1,4,24,256]{4,3,2,1,0:T(8,128)S(1)}, u32[]{:S(2)}, u32[]{:S(2)}) collective-permute-start(f32[2,1,4,24,256]{4,3,2,1,0:T(8,128)S(1)} %maximum_bitcast_fusion.4), channel_id=1, source_target_pairs={{1,2},{3,4},{5,6},{7,8},{9,10},{11,12},{13,14},{15,16},{17,18},{19... | collective-permute-start | bytes 589832 | tf_op jit(solution)/shard_map/ppermute | solution.py:24
  36.5 2.8 %collective-permute-start = (f32[2,1,4,24,256]{4,3,2,1,0:T(8,128)S(1)}, f32[2,1,4,24,256]{4,3,2,1,0:T(8,128)S(1)}, u32[]{:S(2)}, u32[]{:S(2)}) collective-permute-start(f32[2,1,4,24,256]{4,3,2,1,0:T(8,128)S(1)} %maximum_bitcast_fusion.4), channel_id=1, source_target_pairs={{0,1},{1,0},{2,3},{3,2},{4,5},{5,4},{6,7},{7,6},{8,9},{9,8},{10,11... | collective-permute-start | bytes 589832 | tf_op jit(solution)/shard_map/ppermute | solution.py:23
  40.3 8.7 %collective-permute-start.3 = (f32[2,1,4,24,256]{4,3,2,1,0:T(8,128)S(1)}, f32[2,1,4,24,256]{4,3,2,1,0:T(8,128)S(1)}, u32[]{:S(2)}, u32[]{:S(2)}) collective-permute-start(f32[2,1,4,24,256]{4,3,2,1,0:T(8,128)S(1)} %maximum_bitcast_fusion.5), channel_id=1, source_target_pairs={{1,2},{3,4},{5,6},{7,8},{9,10},{11,12},{13,14},{15,16},{17,18},{19... | collective-permute-start | bytes 589832 | tf_op jit(solution)/shard_map/ppermute | solution.py:24
  41.0 8.4 %collective-permute-start.2 = (f32[2,1,4,24,256]{4,3,2,1,0:T(8,128)S(1)}, f32[2,1,4,24,256]{4,3,2,1,0:T(8,128)S(1)}, u32[]{:S(2)}, u32[]{:S(2)}) collective-permute-start(f32[2,1,4,24,256]{4,3,2,1,0:T(8,128)S(1)} %maximum_bitcast_fusion.5), channel_id=1, source_target_pairs={{0,1},{1,0},{2,3},{3,2},{4,5},{5,4},{6,7},{7,6},{8,9},{9,8},{10,11... | collective-permute-start | bytes 589832 | tf_op jit(solution)/shard_map/ppermute | solution.py:23
  49.5 17.2 %copy-start.17 = (f32[4,1,128]{2,1,0:T(1,128)S(1)}, f32[4,1,128]{2,1,0:T(1,128)}, u32[]{:S(2)}) copy-start(f32[4,1,128]{2,1,0:T(1,128)} %param.41) | copy-start | bytes 6148
  49.5 18.5 %copy-start.14 = (s32[4,256]{1,0:T(4,128)S(1)}, s32[4,256]{1,0:T(4,128)}, u32[]{:S(2)}) copy-start(s32[4,256]{1,0:T(4,128)} %multiply_add_fusion.24) | copy-start | bytes 12292
  51.6 15.1 %all-to-all-start.1 = ((f32[32,1,128]{2,1,0:T(1,128)}), f32[32,1,128]{2,1,0:T(1,128)S(1)}, u32[]{:S(2)}, u32[]{:S(2)}) async-start(f32[32,1,128]{2,1,0:T(1,128)} %broadcast_in_dim.6), calls=%async_computation.1 | async-start | bytes 32768 | tf_op jit(solution)/shard_map/all_to_all | solution.py:45
  69.2 3.6 %collective-permute-start.5 = (f32[2,1,4,24,256]{4,3,2,1,0:T(8,128)S(1)}, f32[2,1,4,24,256]{4,3,2,1,0:T(8,128)S(1)}, u32[]{:S(2)}, u32[]{:S(2)}) collective-permute-start(f32[2,1,4,24,256]{4,3,2,1,0:T(8,128)S(1)} %maximum_bitcast_fusion.6), channel_id=1, source_target_pairs={{1,2},{3,4},{5,6},{7,8},{9,10},{11,12},{13,14},{15,16},{17,18},{19... | collective-permute-start | bytes 589832 | tf_op jit(solution)/shard_map/ppermute | solution.py:24
  70.0 3.0 %collective-permute-start.4 = (f32[2,1,4,24,256]{4,3,2,1,0:T(8,128)S(1)}, f32[2,1,4,24,256]{4,3,2,1,0:T(8,128)S(1)}, u32[]{:S(2)}, u32[]{:S(2)}) collective-permute-start(f32[2,1,4,24,256]{4,3,2,1,0:T(8,128)S(1)} %maximum_bitcast_fusion.6), channel_id=1, source_target_pairs={{0,1},{1,0},{2,3},{3,2},{4,5},{5,4},{6,7},{7,6},{8,9},{9,8},{10,11... | collective-permute-start | bytes 589832 | tf_op jit(solution)/shard_map/ppermute | solution.py:23
  74.8 9.2 %collective-permute-start.7 = (f32[2,1,4,24,256]{4,3,2,1,0:T(8,128)S(1)}, f32[2,1,4,24,256]{4,3,2,1,0:T(8,128)S(1)}, u32[]{:S(2)}, u32[]{:S(2)}) collective-permute-start(f32[2,1,4,24,256]{4,3,2,1,0:T(8,128)S(1)} %maximum_bitcast_fusion.7), channel_id=1, source_target_pairs={{1,2},{3,4},{5,6},{7,8},{9,10},{11,12},{13,14},{15,16},{17,18},{19... | collective-permute-start | bytes 589832 | tf_op jit(solution)/shard_map/ppermute | solution.py:24
  75.4 8.5 %collective-permute-start.6 = (f32[2,1,4,24,256]{4,3,2,1,0:T(8,128)S(1)}, f32[2,1,4,24,256]{4,3,2,1,0:T(8,128)S(1)}, u32[]{:S(2)}, u32[]{:S(2)}) collective-permute-start(f32[2,1,4,24,256]{4,3,2,1,0:T(8,128)S(1)} %maximum_bitcast_fusion.7), channel_id=1, source_target_pairs={{0,1},{1,0},{2,3},{3,2},{4,5},{5,4},{6,7},{7,6},{8,9},{9,8},{10,11... | collective-permute-start | bytes 589832 | tf_op jit(solution)/shard_map/ppermute | solution.py:23
  89.5 8.3 %collective-permute-start.9 = (f32[3,1,4,24,256]{4,3,2,1,0:T(8,128)S(1)}, f32[3,1,4,24,256]{4,3,2,1,0:T(8,128)S(1)}, u32[]{:S(2)}, u32[]{:S(2)}) collective-permute-start(f32[3,1,4,24,256]{4,3,2,1,0:T(8,128)S(1)} %maximum_bitcast_fusion.2), channel_id=1, source_target_pairs={{1,2},{3,4},{5,6},{7,8},{9,10},{11,12},{13,14},{15,16},{17,18},{19... | collective-permute-start | bytes 884744 | tf_op jit(solution)/shard_map/ppermute | solution.py:24
  90.2 8.2 %collective-permute-start.8 = (f32[3,1,4,24,256]{4,3,2,1,0:T(8,128)S(1)}, f32[3,1,4,24,256]{4,3,2,1,0:T(8,128)S(1)}, u32[]{:S(2)}, u32[]{:S(2)}) collective-permute-start(f32[3,1,4,24,256]{4,3,2,1,0:T(8,128)S(1)} %maximum_bitcast_fusion.2), channel_id=1, source_target_pairs={{0,1},{1,0},{2,3},{3,2},{4,5},{5,4},{6,7},{7,6},{8,9},{9,8},{10,11... | collective-permute-start | bytes 884744 | tf_op jit(solution)/shard_map/ppermute | solution.py:23
  100.1 11.5 %collective-permute-start.11 = (f32[3,1,4,24,256]{4,3,2,1,0:T(8,128)S(1)}, f32[3,1,4,24,256]{4,3,2,1,0:T(8,128)S(1)}, u32[]{:S(2)}, u32[]{:S(2)}) collective-permute-start(f32[3,1,4,24,256]{4,3,2,1,0:T(8,128)S(1)} %maximum_bitcast_fusion.3), channel_id=1, source_target_pairs={{1,2},{3,4},{5,6},{7,8},{9,10},{11,12},{13,14},{15,16},{17,18},{19... | collective-permute-start | bytes 884744 | tf_op jit(solution)/shard_map/ppermute | solution.py:24
  100.8 10.9 %collective-permute-start.10 = (f32[3,1,4,24,256]{4,3,2,1,0:T(8,128)S(1)}, f32[3,1,4,24,256]{4,3,2,1,0:T(8,128)S(1)}, u32[]{:S(2)}, u32[]{:S(2)}) collective-permute-start(f32[3,1,4,24,256]{4,3,2,1,0:T(8,128)S(1)} %maximum_bitcast_fusion.3), channel_id=1, source_target_pairs={{0,1},{1,0},{2,3},{3,2},{4,5},{5,4},{6,7},{7,6},{8,9},{9,8},{10,11... | collective-permute-start | bytes 884744 | tf_op jit(solution)/shard_map/ppermute | solution.py:23
  117.0 14.2 %collective-permute-start.13 = (f32[4,1,4,24,256]{4,3,2,1,0:T(8,128)S(1)}, f32[4,1,4,24,256]{4,3,2,1,0:T(8,128)S(1)}, u32[]{:S(2)}, u32[]{:S(2)}) collective-permute-start(f32[4,1,4,24,256]{4,3,2,1,0:T(8,128)S(1)} %maximum_bitcast_fusion), channel_id=1, source_target_pairs={{1,2},{3,4},{5,6},{7,8},{9,10},{11,12},{13,14},{15,16},{17,18},{19... | collective-permute-start | bytes 1179656 | tf_op jit(solution)/shard_map/ppermute | solution.py:24
  117.7 13.5 %collective-permute-start.12 = (f32[4,1,4,24,256]{4,3,2,1,0:T(8,128)S(1)}, f32[4,1,4,24,256]{4,3,2,1,0:T(8,128)S(1)}, u32[]{:S(2)}, u32[]{:S(2)}) collective-permute-start(f32[4,1,4,24,256]{4,3,2,1,0:T(8,128)S(1)} %maximum_bitcast_fusion), channel_id=1, source_target_pairs={{0,1},{1,0},{2,3},{3,2},{4,5},{5,4},{6,7},{7,6},{8,9},{9,8},{10,11... | collective-permute-start | bytes 1179656 | tf_op jit(solution)/shard_map/ppermute | solution.py:23
  133.4 9.3 %collective-permute-start.15 = (f32[4,1,4,24,256]{4,3,2,1,0:T(8,128)S(1)}, f32[4,1,4,24,256]{4,3,2,1,0:T(8,128)S(1)}, u32[]{:S(2)}, u32[]{:S(2)}) collective-permute-start(f32[4,1,4,24,256]{4,3,2,1,0:T(8,128)S(1)} %maximum_bitcast_fusion.1), channel_id=1, source_target_pairs={{1,2},{3,4},{5,6},{7,8},{9,10},{11,12},{13,14},{15,16},{17,18},{19... | collective-permute-start | bytes 1179656 | tf_op jit(solution)/shard_map/ppermute | solution.py:24
  134.3 8.3 %collective-permute-start.14 = (f32[4,1,4,24,256]{4,3,2,1,0:T(8,128)S(1)}, f32[4,1,4,24,256]{4,3,2,1,0:T(8,128)S(1)}, u32[]{:S(2)}, u32[]{:S(2)}) collective-permute-start(f32[4,1,4,24,256]{4,3,2,1,0:T(8,128)S(1)} %maximum_bitcast_fusion.1), channel_id=1, source_target_pairs={{0,1},{1,0},{2,3},{3,2},{4,5},{5,4},{6,7},{7,6},{8,9},{9,8},{10,11... | collective-permute-start | bytes 1179656 | tf_op jit(solution)/shard_map/ppermute | solution.py:23
  146.9 21.0 %copy-start.34 = (f32[1,1,128]{2,1,0:T(1,128)S(1)}, f32[1,1,128]{2,1,0:T(1,128)}, u32[]{:S(2)}) copy-start(f32[1,1,128]{2,1,0:T(1,128)} %copy-done.33) | copy-start | bytes 1540
  150.2 17.2 %all-to-all-start.2 = ((f32[32,1,896]{2,1,0:T(1,128)}), f32[32,1,896]{2,1,0:T(1,128)S(1)}, u32[]{:S(2)}, u32[]{:S(2)}) async-start(f32[32,1,896]{2,1,0:T(1,128)} %all_to_all.29), calls=%async_computation.2 | async-start | bytes 229376 | tf_op jit(solution)/shard_map/all_to_all | solution.py:260
  (30 other events, 188.7 us)

commit v12 on v11

--- a/solution.py
+++ b/solution.py
@@ -154,7 +154,13 @@
         water_waves = pressure.shape[0]
         floor_pressure = jnp.sum(pressure * bottom, axis=3)
         pending = [(at, floor_pressure[rock_waves + i : rock_waves + i + 1]) for i, (at, _) in enumerate(pending)]
-        (dx_sxx, dz_sxz, dx_sxy, dz_syz, dx_sxz, dz_szz, flow_x, flow_z_part) = lax.optimization_barrier(
+        (flow_x, flow_z_part) = lax.optimization_barrier(
+            (
+                (flow_x - TIME_STEP * water_buoy * derive(pressure, 4, True)) * live,
+                (flow_z - TIME_STEP * water_buoy * derive(pressure, 3, True)) * above,
+            )
+        )
+        (dx_sxx, dz_sxz, dx_sxy, dz_syz, dx_sxz, dz_szz) = lax.optimization_barrier(
             (
                 derive(sig_xx, 4, True),
                 derive(sig_xz, 3, False),
@@ -162,8 +168,6 @@
                 derive(sig_yz, 3, False),
                 derive(sig_xz, 4, False),
                 derive(sig_zz, 3, True),
-                (flow_x - TIME_STEP * water_buoy * derive(pressure, 4, True)) * live,
-                (flow_z - TIME_STEP * water_buoy * derive(pressure, 3, True)) * above,
             )
         )
         sxy_pad, syy_pad, syz_pad, p_pad = halo_rows(
@@ -176,15 +180,16 @@
         floor_velocity = fill_waves(vel_z[:, :, :, 0, :], water_waves)
         flow_y = (flow_y - TIME_STEP * water_buoy * stencil(p_pad, 2, True)) * live
         flow_z = flow_z_part + floor_velocity[:, :, :, None, :] * bottom
-        (strain_x, strain_z, dx_vy, dz_vy, shear_xz, dx_ux, dz_uz) = lax.optimization_barrier(
+        (dx_ux, dz_uz) = lax.optimization_barrier(
+            (derive(flow_x, 4, False), derive(flow_z, 3, False))
+        )
+        (strain_x, strain_z, dx_vy, dz_vy, shear_xz) = lax.optimization_barrier(
             (
                 derive(vel_x, 4, False),
                 derive(vel_z, 3, False),
                 derive(vel_y, 4, True),
                 derive(vel_y, 3, True),
                 derive(vel_x, 3, True) + derive(vel_z, 4, True),
-                derive(flow_x, 4, False),
-                derive(flow_z, 3, False),
             )
         )
         vx_pad, vy_pad, vz_pad, uy_pad = halo_rows(

time: 172 us -> 170 us (0.988)
  other arithmetic: 38.6 us -> 35.5 us
  starting transfers between devices: 79.2 us -> 81.9 us
    ppermute x8, starting transfers between devices: 48.9 us -> 52 us  [halo_rows(): got_within = lax.ppermute(jnp.where(odd, first, last), 'gx', within)]
    unnamed x88 -> x76, local copies, waits for them, and re-layouts: 9.95 us -> 8.88 us
  transfers between devices with their start and end apart: 19 -> 19, of which waited for: 7 -> 8; matrix products, arithmetic and copies ran while one was open for 10% -> 8% of each run, Pallas kernels for 0% -> 0%
where the time goes in v12:
time: 170 us; the launch traced here: 169 us
  starting transfers between devices  81.9 us (48%)
  other arithmetic  35.5 us (21%)
  waiting for transfers between devices  24 us (14%)
  local copies, waits for them, and re-layouts  20.8 us (12%)
  between operations  3.59 us (2%)
  matrix products  3.46 us (2%)
    ppermute x8, starting transfers between devices, halo_rows(): got_within = lax.ppermute(jnp.where(odd, first, last), 'gx', within)  52 us
    all_to_all x1, waiting for transfers between devices, on_device(): lax.all_to_all(rock_in, 'gx', split_axis=3, concat_axis=1, tiled=True)  9.85 us
    unnamed x76, local copies, waits for them, and re-layouts  8.88 us
    all_to_all x1, starting transfers between devices, on_device(): got = lax.all_to_all(packed, 'gx', 0, 0, tiled=True)  8.53 us
    all_to_all x1, starting transfers between devices, gather_sum(): return jnp.sum(lax.all_to_all(copies, 'gx', 0, 0, tiled=True), axis=0)  8.06 us
    add x32, other arithmetic, stencil(): summed = addend if summed is None else summed + addend  7.37 us
    all_to_all x1, starting transfers between devices, on_device(): lax.all_to_all(rock_in, 'gx', split_axis=3, concat_axis=1, tiled=True)  7.3 us
    all_to_all x1, waiting for transfers between devices, on_device(): got = lax.all_to_all(packed, 'gx', 0, 0, tiled=True)  6.33 us
  transfers between devices with their start and end apart: 19, of which 8 were waited for; matrix products, arithmetic and copies ran while one was open for 8% of the time, Pallas kernels for 0%

profile of v12, /device:TPU:0, one launch (start us, length us, event | category | flops | bytes accessed | tf_op | source)
XLA Modules:
  0.0 169.3 jit_solution(8871124676195889542)
XLA Ops:
  3.1 1.9 %copy.3390 = f32[21,8,4,128]{0,1,2,3:T(8,128)S(1)} copy(f32[21,8,4,128]{3,1,2,0:T(8,128)S(1)} %pad_maximum_fusion.8) | data formatting | bytes 688128 | tf_op jit(solution)/shard_map/concatenate | solution.py:95
  5.1 2.6 %reshape.1017 = f32[32,1,2688]{2,1,0:T(1,128)} reshape(f32[128,4,8,21]{3,2,1,0:T(8,128)S(1)} %bitcast.357) | data formatting | bytes 688128
  7.7 7.3 %all-to-all-start = ((f32[32,1,2688]{2,1,0:T(1,128)}), f32[32,1,2688]{2,1,0:T(1,128)S(1)}, u32[]{:S(2)}, u32[]{:S(2)}) async-start(f32[32,1,2688]{2,1,0:T(1,128)} %reshape.1017), calls=%async_computation | async-start | bytes 688128 | tf_op jit(solution)/shard_map/all_to_all | solution.py:103
  17.5 9.9 %all-to-all-done = f32[32,1,2688]{2,1,0:T(1,128)S(1)} async-done(((f32[32,1,2688]{2,1,0:T(1,128)}), f32[32,1,2688]{2,1,0:T(1,128)S(1)}, u32[]{:S(2)}, u32[]{:S(2)}) %all-to-all-start) | async-done | bytes 344096 | tf_op jit(solution)/shard_map/all_to_all | solution.py:103
  27.8 1.5 reduce.33
  29.3 2.3 %reshape.1018 = f32[128,4,8,21]{3,2,1,0:T(8,128)S(1)} reshape(f32[32,2688]{1,0:T(8,128)S(1)} %reduce.33) | data formatting | bytes 688128
  31.6 1.6 copy.3527
  33.2 2.3 %copy.3393 = f32[21,256,4,4]{1,2,3,0:T(4,128)S(1)} copy(f32[21,256,4,4]{0,1,3,2:T(8,128)} %bitcast.359) | data formatting | bytes 688128 | tf_op jit(solution)/shard_map/all_to_all | solution.py:103
  36.6 1.7 %collective-permute-start = (f32[2,1,4,24,256]{4,3,2,1,0:T(8,128)S(1)}, f32[2,1,4,24,256]{4,3,2,1,0:T(8,128)S(1)}, u32[]{:S(2)}, u32[]{:S(2)}) collective-permute-start(f32[2,1,4,24,256]{4,3,2,1,0:T(8,128)S(1)} %maximum_bitcast_fusion.4), channel_id=1, source_target_pairs={{0,1},{1,0},{2,3},{3,2},{4,5},{5,4},{6,7},{7,6},{8,9},{9,8},{10,11... | collective-permute-start | bytes 589832 | tf_op jit(solution)/shard_map/ppermute | solution.py:23
  41.3 7.3 %collective-permute-start.2 = (f32[2,1,4,24,256]{4,3,2,1,0:T(8,128)S(1)}, f32[2,1,4,24,256]{4,3,2,1,0:T(8,128)S(1)}, u32[]{:S(2)}, u32[]{:S(2)}) collective-permute-start(f32[2,1,4,24,256]{4,3,2,1,0:T(8,128)S(1)} %maximum_bitcast_fusion.5), channel_id=1, source_target_pairs={{0,1},{1,0},{2,3},{3,2},{4,5},{5,4},{6,7},{7,6},{8,9},{9,8},{10,11... | collective-permute-start | bytes 589832 | tf_op jit(solution)/shard_map/ppermute | solution.py:23
  51.8 8.1 %all-to-all-start.1 = ((f32[32,1,128]{2,1,0:T(1,128)}), f32[32,1,128]{2,1,0:T(1,128)S(1)}, u32[]{:S(2)}, u32[]{:S(2)}) async-start(f32[32,1,128]{2,1,0:T(1,128)} %broadcast_in_dim.6), calls=%async_computation.1 | async-start | bytes 32768 | tf_op jit(solution)/shard_map/all_to_all | solution.py:45
  62.4 4.6 %all-to-all-done.1 = f32[32,1,128]{2,1,0:T(1,128)S(1)} async-done(((f32[32,1,128]{2,1,0:T(1,128)}), f32[32,1,128]{2,1,0:T(1,128)S(1)}, u32[]{:S(2)}, u32[]{:S(2)}) %all-to-all-start.1) | async-done | bytes 16416 | tf_op jit(solution)/shard_map/all_to_all | solution.py:45
  69.7 1.9 %collective-permute-start.4 = (f32[2,1,4,24,256]{4,3,2,1,0:T(8,128)S(1)}, f32[2,1,4,24,256]{4,3,2,1,0:T(8,128)S(1)}, u32[]{:S(2)}, u32[]{:S(2)}) collective-permute-start(f32[2,1,4,24,256]{4,3,2,1,0:T(8,128)S(1)} %maximum_bitcast_fusion.6), channel_id=1, source_target_pairs={{0,1},{1,0},{2,3},{3,2},{4,5},{5,4},{6,7},{7,6},{8,9},{9,8},{10,11... | collective-permute-start | bytes 589832 | tf_op jit(solution)/shard_map/ppermute | solution.py:23
  74.8 7.2 %collective-permute-start.6 = (f32[2,1,4,24,256]{4,3,2,1,0:T(8,128)S(1)}, f32[2,1,4,24,256]{4,3,2,1,0:T(8,128)S(1)}, u32[]{:S(2)}, u32[]{:S(2)}) collective-permute-start(f32[2,1,4,24,256]{4,3,2,1,0:T(8,128)S(1)} %maximum_bitcast_fusion.7), channel_id=1, source_target_pairs={{0,1},{1,0},{2,3},{3,2},{4,5},{5,4},{6,7},{7,6},{8,9},{9,8},{10,11... | collective-permute-start | bytes 589832 | tf_op jit(solution)/shard_map/ppermute | solution.py:23
  88.8 7.3 %collective-permute-start.8 = (f32[3,1,4,24,256]{4,3,2,1,0:T(8,128)S(1)}, f32[3,1,4,24,256]{4,3,2,1,0:T(8,128)S(1)}, u32[]{:S(2)}, u32[]{:S(2)}) collective-permute-start(f32[3,1,4,24,256]{4,3,2,1,0:T(8,128)S(1)} %maximum_bitcast_fusion.2), channel_id=1, source_target_pairs={{0,1},{1,0},{2,3},{3,2},{4,5},{5,4},{6,7},{7,6},{8,9},{9,8},{10,11... | collective-permute-start | bytes 884744 | tf_op jit(solution)/shard_map/ppermute | solution.py:23
  99.2 9.3 %collective-permute-start.10 = (f32[3,1,4,24,256]{4,3,2,1,0:T(8,128)S(1)}, f32[3,1,4,24,256]{4,3,2,1,0:T(8,128)S(1)}, u32[]{:S(2)}, u32[]{:S(2)}) collective-permute-start(f32[3,1,4,24,256]{4,3,2,1,0:T(8,128)S(1)} %maximum_bitcast_fusion.3), channel_id=1, source_target_pairs={{0,1},{1,0},{2,3},{3,2},{4,5},{5,4},{6,7},{7,6},{8,9},{9,8},{10,11... | collective-permute-start | bytes 884744 | tf_op jit(solution)/shard_map/ppermute | solution.py:23
  116.0 8.4 %collective-permute-start.12 = (f32[4,1,4,24,256]{4,3,2,1,0:T(8,128)S(1)}, f32[4,1,4,24,256]{4,3,2,1,0:T(8,128)}, u32[]{:S(2)}, u32[]{:S(2)}) collective-permute-start(f32[4,1,4,24,256]{4,3,2,1,0:T(8,128)S(1)} %maximum_bitcast_fusion), channel_id=1, source_target_pairs={{0,1},{1,0},{2,3},{3,2},{4,5},{5,4},{6,7},{7,6},{8,9},{9,8},{10,11... | collective-permute-start | bytes 1179656 | tf_op jit(solution)/shard_map/ppermute | solution.py:23
  126.9 1.1 bitcast_select_fusion.2
  130.4 8.8 %collective-permute-start.14 = (f32[4,1,4,24,256]{4,3,2,1,0:T(8,128)S(1)}, f32[4,1,4,24,256]{4,3,2,1,0:T(8,128)S(1)}, u32[]{:S(2)}, u32[]{:S(2)}) collective-permute-start(f32[4,1,4,24,256]{4,3,2,1,0:T(8,128)S(1)} %maximum_bitcast_fusion.1), channel_id=1, source_target_pairs={{0,1},{1,0},{2,3},{3,2},{4,5},{5,4},{6,7},{7,6},{8,9},{9,8},{10,11... | collective-permute-start | bytes 1179656 | tf_op jit(solution)/shard_map/ppermute | solution.py:23
  139.8 1.3 fusion.44
  142.3 1.1 maximum_maximum_fusion.1
  144.8 1.7 fusion.68
  148.9 8.5 %all-to-all-start.2 = ((f32[32,1,896]{2,1,0:T(1,128)}), f32[32,1,896]{2,1,0:T(1,128)S(1)}, u32[]{:S(2)}, u32[]{:S(2)}) async-start(f32[32,1,896]{2,1,0:T(1,128)} %all_to_all.29), calls=%async_computation.2 | async-start | bytes 229376 | tf_op jit(solution)/shard_map/all_to_all | solution.py:265
  159.2 6.3 %all-to-all-done.2 = f32[32,1,896]{2,1,0:T(1,128)S(1)} async-done(((f32[32,1,896]{2,1,0:T(1,128)}), f32[32,1,896]{2,1,0:T(1,128)S(1)}, u32[]{:S(2)}, u32[]{:S(2)}) %all-to-all-start.2) | async-done | bytes 114720 | tf_op jit(solution)/shard_map/all_to_all | solution.py:265
  (314 shorter events, 51.7 us)
Async XLA Ops:
  7.7 19.6 %all-to-all-start = ((f32[32,1,2688]{2,1,0:T(1,128)}), f32[32,1,2688]{2,1,0:T(1,128)S(1)}, u32[]{:S(2)}, u32[]{:S(2)}) async-start(f32[32,1,2688]{2,1,0:T(1,128)} %reshape.1017), calls=%async_computation | async-start | bytes 688128 | tf_op jit(solution)/shard_map/all_to_all | solution.py:103
  17.4 50.9 %copy-start.15 = (pred[128]{0:T(512)(128)(4,1)}, pred[128]{0:T(512)(128)(4,1)S(1)}, u32[]{:S(2)}) copy-start(pred[128]{0:T(512)(128)(4,1)S(1)} %get-tuple-element.317) | copy-start | bytes 388
  17.4 50.9 %copy-start.23 = (s32[128]{0:T(128)}, s32[128]{0:T(128)S(1)}, u32[]{:S(2)}) copy-start(s32[128]{0:T(128)S(1)} %fusion.1154) | copy-start | bytes 1540
  35.8 3.0 %collective-permute-start.1 = (f32[2,1,4,24,256]{4,3,2,1,0:T(8,128)S(1)}, f32[2,1,4,24,256]{4,3,2,1,0:T(8,128)S(1)}, u32[]{:S(2)}, u32[]{:S(2)}) collective-permute-start(f32[2,1,4,24,256]{4,3,2,1,0:T(8,128)S(1)} %maximum_bitcast_fusion.4), channel_id=1, source_target_pairs={{1,2},{3,4},{5,6},{7,8},{9,10},{11,12},{13,14},{15,16},{17,18},{19... | collective-permute-start | bytes 589832 | tf_op jit(solution)/shard_map/ppermute | solution.py:24
  36.6 2.8 %collective-permute-start = (f32[2,1,4,24,256]{4,3,2,1,0:T(8,128)S(1)}, f32[2,1,4,24,256]{4,3,2,1,0:T(8,128)S(1)}, u32[]{:S(2)}, u32[]{:S(2)}) collective-permute-start(f32[2,1,4,24,256]{4,3,2,1,0:T(8,128)S(1)} %maximum_bitcast_fusion.4), channel_id=1, source_target_pairs={{0,1},{1,0},{2,3},{3,2},{4,5},{5,4},{6,7},{7,6},{8,9},{9,8},{10,11... | collective-permute-start | bytes 589832 | tf_op jit(solution)/shard_map/ppermute | solution.py:23
  40.6 8.5 %collective-permute-start.3 = (f32[2,1,4,24,256]{4,3,2,1,0:T(8,128)S(1)}, f32[2,1,4,24,256]{4,3,2,1,0:T(8,128)S(1)}, u32[]{:S(2)}, u32[]{:S(2)}) collective-permute-start(f32[2,1,4,24,256]{4,3,2,1,0:T(8,128)S(1)} %maximum_bitcast_fusion.5), channel_id=1, source_target_pairs={{1,2},{3,4},{5,6},{7,8},{9,10},{11,12},{13,14},{15,16},{17,18},{19... | collective-permute-start | bytes 589832 | tf_op jit(solution)/shard_map/ppermute | solution.py:24
  41.3 8.4 %collective-permute-start.2 = (f32[2,1,4,24,256]{4,3,2,1,0:T(8,128)S(1)}, f32[2,1,4,24,256]{4,3,2,1,0:T(8,128)S(1)}, u32[]{:S(2)}, u32[]{:S(2)}) collective-permute-start(f32[2,1,4,24,256]{4,3,2,1,0:T(8,128)S(1)} %maximum_bitcast_fusion.5), channel_id=1, source_target_pairs={{0,1},{1,0},{2,3},{3,2},{4,5},{5,4},{6,7},{7,6},{8,9},{9,8},{10,11... | collective-permute-start | bytes 589832 | tf_op jit(solution)/shard_map/ppermute | solution.py:23
  49.8 17.2 %copy-start.14 = (f32[4,1,128]{2,1,0:T(1,128)S(1)}, f32[4,1,128]{2,1,0:T(1,128)}, u32[]{:S(2)}) copy-start(f32[4,1,128]{2,1,0:T(1,128)} %param.41) | copy-start | bytes 6148
  51.8 15.1 %all-to-all-start.1 = ((f32[32,1,128]{2,1,0:T(1,128)}), f32[32,1,128]{2,1,0:T(1,128)S(1)}, u32[]{:S(2)}, u32[]{:S(2)}) async-start(f32[32,1,128]{2,1,0:T(1,128)} %broadcast_in_dim.6), calls=%async_computation.1 | async-start | bytes 32768 | tf_op jit(solution)/shard_map/all_to_all | solution.py:45
  68.9 3.0 %collective-permute-start.5 = (f32[2,1,4,24,256]{4,3,2,1,0:T(8,128)S(1)}, f32[2,1,4,24,256]{4,3,2,1,0:T(8,128)S(1)}, u32[]{:S(2)}, u32[]{:S(2)}) collective-permute-start(f32[2,1,4,24,256]{4,3,2,1,0:T(8,128)S(1)} %maximum_bitcast_fusion.6), channel_id=1, source_target_pairs={{1,2},{3,4},{5,6},{7,8},{9,10},{11,12},{13,14},{15,16},{17,18},{19... | collective-permute-start | bytes 589832 | tf_op jit(solution)/shard_map/ppermute | solution.py:24
  69.7 3.0 %collective-permute-start.4 = (f32[2,1,4,24,256]{4,3,2,1,0:T(8,128)S(1)}, f32[2,1,4,24,256]{4,3,2,1,0:T(8,128)S(1)}, u32[]{:S(2)}, u32[]{:S(2)}) collective-permute-start(f32[2,1,4,24,256]{4,3,2,1,0:T(8,128)S(1)} %maximum_bitcast_fusion.6), channel_id=1, source_target_pairs={{0,1},{1,0},{2,3},{3,2},{4,5},{5,4},{6,7},{7,6},{8,9},{9,8},{10,11... | collective-permute-start | bytes 589832 | tf_op jit(solution)/shard_map/ppermute | solution.py:23
  74.1 8.3 %collective-permute-start.7 = (f32[2,1,4,24,256]{4,3,2,1,0:T(8,128)S(1)}, f32[2,1,4,24,256]{4,3,2,1,0:T(8,128)S(1)}, u32[]{:S(2)}, u32[]{:S(2)}) collective-permute-start(f32[2,1,4,24,256]{4,3,2,1,0:T(8,128)S(1)} %maximum_bitcast_fusion.7), channel_id=1, source_target_pairs={{1,2},{3,4},{5,6},{7,8},{9,10},{11,12},{13,14},{15,16},{17,18},{19... | collective-permute-start | bytes 589832 | tf_op jit(solution)/shard_map/ppermute | solution.py:24
  74.8 8.2 %collective-permute-start.6 = (f32[2,1,4,24,256]{4,3,2,1,0:T(8,128)S(1)}, f32[2,1,4,24,256]{4,3,2,1,0:T(8,128)S(1)}, u32[]{:S(2)}, u32[]{:S(2)}) collective-permute-start(f32[2,1,4,24,256]{4,3,2,1,0:T(8,128)S(1)} %maximum_bitcast_fusion.7), channel_id=1, source_target_pairs={{0,1},{1,0},{2,3},{3,2},{4,5},{5,4},{6,7},{7,6},{8,9},{9,8},{10,11... | collective-permute-start | bytes 589832 | tf_op jit(solution)/shard_map/ppermute | solution.py:23
  88.1 8.6 %collective-permute-start.9 = (f32[3,1,4,24,256]{4,3,2,1,0:T(8,128)S(1)}, f32[3,1,4,24,256]{4,3,2,1,0:T(8,128)S(1)}, u32[]{:S(2)}, u32[]{:S(2)}) collective-permute-start(f32[3,1,4,24,256]{4,3,2,1,0:T(8,128)S(1)} %maximum_bitcast_fusion.2), channel_id=1, source_target_pairs={{1,2},{3,4},{5,6},{7,8},{9,10},{11,12},{13,14},{15,16},{17,18},{19... | collective-permute-start | bytes 884744 | tf_op jit(solution)/shard_map/ppermute | solution.py:24
  88.8 8.6 %collective-permute-start.8 = (f32[3,1,4,24,256]{4,3,2,1,0:T(8,128)S(1)}, f32[3,1,4,24,256]{4,3,2,1,0:T(8,128)S(1)}, u32[]{:S(2)}, u32[]{:S(2)}) collective-permute-start(f32[3,1,4,24,256]{4,3,2,1,0:T(8,128)S(1)} %maximum_bitcast_fusion.2), channel_id=1, source_target_pairs={{0,1},{1,0},{2,3},{3,2},{4,5},{5,4},{6,7},{7,6},{8,9},{9,8},{10,11... | collective-permute-start | bytes 884744 | tf_op jit(solution)/shard_map/ppermute | solution.py:23
  98.5 11.4 %collective-permute-start.11 = (f32[3,1,4,24,256]{4,3,2,1,0:T(8,128)S(1)}, f32[3,1,4,24,256]{4,3,2,1,0:T(8,128)S(1)}, u32[]{:S(2)}, u32[]{:S(2)}) collective-permute-start(f32[3,1,4,24,256]{4,3,2,1,0:T(8,128)S(1)} %maximum_bitcast_fusion.3), channel_id=1, source_target_pairs={{1,2},{3,4},{5,6},{7,8},{9,10},{11,12},{13,14},{15,16},{17,18},{19... | collective-permute-start | bytes 884744 | tf_op jit(solution)/shard_map/ppermute | solution.py:24
  99.2 10.7 %collective-permute-start.10 = (f32[3,1,4,24,256]{4,3,2,1,0:T(8,128)S(1)}, f32[3,1,4,24,256]{4,3,2,1,0:T(8,128)S(1)}, u32[]{:S(2)}, u32[]{:S(2)}) collective-permute-start(f32[3,1,4,24,256]{4,3,2,1,0:T(8,128)S(1)} %maximum_bitcast_fusion.3), channel_id=1, source_target_pairs={{0,1},{1,0},{2,3},{3,2},{4,5},{5,4},{6,7},{7,6},{8,9},{9,8},{10,11... | collective-permute-start | bytes 884744 | tf_op jit(solution)/shard_map/ppermute | solution.py:23
  115.3 11.6 %collective-permute-start.13 = (f32[4,1,4,24,256]{4,3,2,1,0:T(8,128)S(1)}, f32[4,1,4,24,256]{4,3,2,1,0:T(8,128)S(1)}, u32[]{:S(2)}, u32[]{:S(2)}) collective-permute-start(f32[4,1,4,24,256]{4,3,2,1,0:T(8,128)S(1)} %maximum_bitcast_fusion), channel_id=1, source_target_pairs={{1,2},{3,4},{5,6},{7,8},{9,10},{11,12},{13,14},{15,16},{17,18},{19... | collective-permute-start | bytes 1179656 | tf_op jit(solution)/shard_map/ppermute | solution.py:24
  116.0 10.9 %collective-permute-start.12 = (f32[4,1,4,24,256]{4,3,2,1,0:T(8,128)S(1)}, f32[4,1,4,24,256]{4,3,2,1,0:T(8,128)}, u32[]{:S(2)}, u32[]{:S(2)}) collective-permute-start(f32[4,1,4,24,256]{4,3,2,1,0:T(8,128)S(1)} %maximum_bitcast_fusion), channel_id=1, source_target_pairs={{0,1},{1,0},{2,3},{3,2},{4,5},{5,4},{6,7},{7,6},{8,9},{9,8},{10,11... | collective-permute-start | bytes 1179656 | tf_op jit(solution)/shard_map/ppermute | solution.py:23
  129.5 12.6 %collective-permute-start.15 = (f32[4,1,4,24,256]{4,3,2,1,0:T(8,128)S(1)}, f32[4,1,4,24,256]{4,3,2,1,0:T(8,128)S(1)}, u32[]{:S(2)}, u32[]{:S(2)}) collective-permute-start(f32[4,1,4,24,256]{4,3,2,1,0:T(8,128)S(1)} %maximum_bitcast_fusion.1), channel_id=1, source_target_pairs={{1,2},{3,4},{5,6},{7,8},{9,10},{11,12},{13,14},{15,16},{17,18},{19... | collective-permute-start | bytes 1179656 | tf_op jit(solution)/shard_map/ppermute | solution.py:24
  130.4 11.7 %collective-permute-start.14 = (f32[4,1,4,24,256]{4,3,2,1,0:T(8,128)S(1)}, f32[4,1,4,24,256]{4,3,2,1,0:T(8,128)S(1)}, u32[]{:S(2)}, u32[]{:S(2)}) collective-permute-start(f32[4,1,4,24,256]{4,3,2,1,0:T(8,128)S(1)} %maximum_bitcast_fusion.1), channel_id=1, source_target_pairs={{0,1},{1,0},{2,3},{3,2},{4,5},{5,4},{6,7},{7,6},{8,9},{9,8},{10,11... | collective-permute-start | bytes 1179656 | tf_op jit(solution)/shard_map/ppermute | solution.py:23
  144.8 14.2 %copy-start = (f32[2,1,4,12,256]{4,3,2,0,1:T(8,128)S(1)}, f32[2,1,4,12,256]{4,3,2,0,1:T(8,128)}, u32[]{:S(2)}) copy-start(f32[2,1,4,12,256]{4,3,2,0,1:T(8,128)} %fusion.280) | copy-start | bytes 294916
  144.8 14.2 %copy-start.4 = (f32[1,1,4,12,256]{4,3,2,0,1:T(8,128)S(1)}, f32[1,1,4,12,256]{4,3,2,0,1:T(8,128)}, u32[]{:S(2)}) copy-start(f32[1,1,4,12,256]{4,3,2,0,1:T(8,128)} %get-tuple-element.428) | copy-start | bytes 147460
  148.9 16.6 %all-to-all-start.2 = ((f32[32,1,896]{2,1,0:T(1,128)}), f32[32,1,896]{2,1,0:T(1,128)S(1)}, u32[]{:S(2)}, u32[]{:S(2)}) async-start(f32[32,1,896]{2,1,0:T(1,128)} %all_to_all.29), calls=%async_computation.2 | async-start | bytes 229376 | tf_op jit(solution)/shard_map/all_to_all | solution.py:265
  (24 other events, 165.8 us)

commit v13 on v12

--- a/solution.py
+++ b/solution.py
@@ -8,7 +8,7 @@
 HALO = 4
 ROW_AXIS = 2
 DEPTH_AXIS = 3
-DEFERRED = 3
+DEFERRED = 2
 
 
 def halo_rows(fields):

time: 170 us -> 175 us (1.029)
  waiting for transfers between devices: 24 us -> 33.8 us
  other arithmetic: 35.5 us -> 29.5 us
    all_to_all x1 -> x2, waiting for transfers between devices: 4.61 us -> 13.9 us  [gather_sum(): return jnp.sum(lax.all_to_all(copies, 'gx', 0, 0, tiled=True), axis=0)]
    ppermute x8, starting transfers between devices: 52 us -> 44.1 us  [halo_rows(): got_within = lax.ppermute(jnp.where(odd, first, last), 'gx', within)]
    all_to_all x1 -> x2, starting transfers between devices: 8.06 us -> 15.3 us  [gather_sum(): return jnp.sum(lax.all_to_all(copies, 'gx', 0, 0, tiled=True), axis=0)]
    unnamed x76 -> x110, local copies, waits for them, and re-layouts: 8.88 us -> 9.87 us
  transfers between devices with their start and end apart: 19 -> 20, of which waited for: 8 -> 11; matrix products, arithmetic and copies ran while one was open for 8% -> 4% of each run, Pallas kernels for 0% -> 0%
where the time goes in v13:
time: 175 us; the launch traced here: 174 us
  starting transfers between devices  80.7 us (46%)
  waiting for transfers between devices  33.8 us (19%)
  other arithmetic  29.5 us (17%)
  local copies, waits for them, and re-layouts  21.5 us (12%)
  between operations  4.3 us (2%)
  matrix products  4.05 us (2%)
    ppermute x8, starting transfers between devices, halo_rows(): got_within = lax.ppermute(jnp.where(odd, first, last), 'gx', within)  44.1 us
    all_to_all x2, starting transfers between devices, gather_sum(): return jnp.sum(lax.all_to_all(copies, 'gx', 0, 0, tiled=True), axis=0)  15.3 us
    all_to_all x2, waiting for transfers between devices, gather_sum(): return jnp.sum(lax.all_to_all(copies, 'gx', 0, 0, tiled=True), axis=0)  13.9 us
    all_to_all x1, waiting for transfers between devices, on_device(): lax.all_to_all(rock_in, 'gx', split_axis=3, concat_axis=1, tiled=True)  9.93 us
    unnamed x110, local copies, waits for them, and re-layouts  9.87 us
    all_to_all x1, starting transfers between devices, on_device(): got = lax.all_to_all(packed, 'gx', 0, 0, tiled=True)  8.21 us
    add x32, other arithmetic, stencil(): summed = addend if summed is None else summed + addend  7.75 us
    all_to_all x1, starting transfers between devices, on_device(): lax.all_to_all(rock_in, 'gx', split_axis=3, concat_axis=1, tiled=True)  7.3 us
  transfers between devices with their start and end apart: 20, of which 11 were waited for; matrix products, arithmetic and copies ran while one was open for 4% of the time, Pallas kernels for 0%

profile of v13, /device:TPU:0, one launch (start us, length us, event | category | flops | bytes accessed | tf_op | source)
XLA Modules:
  0.0 173.9 jit_solution(1588996644560110588)
XLA Ops:
  3.1 1.9 %copy.2320 = f32[21,8,4,128]{0,1,2,3:T(8,128)S(1)} copy(f32[21,8,4,128]{3,1,2,0:T(8,128)S(1)} %pad_maximum_fusion.8) | data formatting | bytes 688128 | tf_op jit(solution)/shard_map/concatenate | solution.py:95
  5.1 2.7 %reshape.974 = f32[32,1,2688]{2,1,0:T(1,128)} reshape(f32[128,4,8,21]{3,2,1,0:T(8,128)S(1)} %bitcast.334) | data formatting | bytes 688128
  7.7 7.3 %all-to-all-start = ((f32[32,1,2688]{2,1,0:T(1,128)}), f32[32,1,2688]{2,1,0:T(1,128)S(1)}, u32[]{:S(2)}, u32[]{:S(2)}) async-start(f32[32,1,2688]{2,1,0:T(1,128)} %reshape.974), calls=%async_computation | async-start | bytes 688128 | tf_op jit(solution)/shard_map/all_to_all | solution.py:103
  17.4 9.9 %all-to-all-done = f32[32,1,2688]{2,1,0:T(1,128)S(1)} async-done(((f32[32,1,2688]{2,1,0:T(1,128)}), f32[32,1,2688]{2,1,0:T(1,128)S(1)}, u32[]{:S(2)}, u32[]{:S(2)}) %all-to-all-start) | async-done | bytes 344096 | tf_op jit(solution)/shard_map/all_to_all | solution.py:103
  27.8 1.5 reduce.32
  29.3 2.3 %reshape.975 = f32[128,4,8,21]{3,2,1,0:T(8,128)S(1)} reshape(f32[32,2688]{1,0:T(8,128)S(1)} %reduce.32) | data formatting | bytes 688128
  31.6 1.5 copy.2448
  33.1 2.3 %copy.2323 = f32[21,256,4,4]{1,2,3,0:T(4,128)S(1)} copy(f32[21,256,4,4]{0,1,3,2:T(8,128)} %bitcast.336) | data formatting | bytes 688128 | tf_op jit(solution)/shard_map/all_to_all | solution.py:103
  36.5 1.7 collective-permute-start
  41.3 7.3 %collective-permute-start.2 = (f32[2,1,4,24,256]{4,3,2,1,0:T(8,128)S(1)}, f32[2,1,4,24,256]{4,3,2,1,0:T(8,128)S(1)}, u32[]{:S(2)}, u32[]{:S(2)}) collective-permute-start(f32[2,1,4,24,256]{4,3,2,1,0:T(8,128)S(1)} %maximum_bitcast_fusion.3), channel_id=1, source_target_pairs={{0,1},{1,0},{2,3},{3,2},{4,5},{5,4},{6,7},{7,6},{8,9},{9,8},{10,11... | collective-permute-start | bytes 589832 | tf_op jit(solution)/shard_map/ppermute | solution.py:23
  55.0 8.1 %all-to-all-start.1 = ((f32[32,1,128]{2,1,0:T(1,128)}), f32[32,1,128]{2,1,0:T(1,128)S(1)}, u32[]{:S(2)}, u32[]{:S(2)}) async-start(f32[32,1,128]{2,1,0:T(1,128)} %broadcast_in_dim.8), calls=%async_computation.1 | async-start | bytes 32768 | tf_op jit(solution)/shard_map/all_to_all | solution.py:45
  63.2 6.9 %all-to-all-done.1 = f32[32,1,128]{2,1,0:T(1,128)S(1)} async-done(((f32[32,1,128]{2,1,0:T(1,128)}), f32[32,1,128]{2,1,0:T(1,128)S(1)}, u32[]{:S(2)}, u32[]{:S(2)}) %all-to-all-start.1) | async-done | bytes 16416 | tf_op jit(solution)/shard_map/all_to_all | solution.py:45
  71.5 1.1 fusion.10
  73.5 1.9 %collective-permute-start.4 = (f32[2,1,4,24,256]{4,3,2,1,0:T(8,128)S(1)}, f32[2,1,4,24,256]{4,3,2,1,0:T(8,128)S(1)}, u32[]{:S(2)}, u32[]{:S(2)}) collective-permute-start(f32[2,1,4,24,256]{4,3,2,1,0:T(8,128)S(1)} %maximum_bitcast_fusion.4), channel_id=1, source_target_pairs={{0,1},{1,0},{2,3},{3,2},{4,5},{5,4},{6,7},{7,6},{8,9},{9,8},{10,11... | collective-permute-start | bytes 589832 | tf_op jit(solution)/shard_map/ppermute | solution.py:23
  75.5 1.0 collective-permute-done.4
  78.4 7.2 %collective-permute-start.6 = (f32[2,1,4,24,256]{4,3,2,1,0:T(8,128)S(1)}, f32[2,1,4,24,256]{4,3,2,1,0:T(8,128)S(1)}, u32[]{:S(2)}, u32[]{:S(2)}) collective-permute-start(f32[2,1,4,24,256]{4,3,2,1,0:T(8,128)S(1)} %maximum_bitcast_fusion.5), channel_id=1, source_target_pairs={{0,1},{1,0},{2,3},{3,2},{4,5},{5,4},{6,7},{7,6},{8,9},{9,8},{10,11... | collective-permute-start | bytes 589832 | tf_op jit(solution)/shard_map/ppermute | solution.py:23
  91.2 7.3 %all-to-all-start.2 = ((f32[32,1,128]{2,1,0:T(1,128)}), f32[32,1,128]{2,1,0:T(1,128)S(1)}, u32[]{:S(2)}, u32[]{:S(2)}) async-start(f32[32,1,128]{2,1,0:T(1,128)} %broadcast_in_dim.9), calls=%async_computation.2 | async-start | bytes 32768 | tf_op jit(solution)/shard_map/all_to_all | solution.py:45
  98.5 7.0 %all-to-all-done.2 = f32[32,1,128]{2,1,0:T(1,128)S(1)} async-done(((f32[32,1,128]{2,1,0:T(1,128)}), f32[32,1,128]{2,1,0:T(1,128)S(1)}, u32[]{:S(2)}, u32[]{:S(2)}) %all-to-all-start.2) | async-done | bytes 16416 | tf_op jit(solution)/shard_map/all_to_all | solution.py:45
  108.1 1.9 %collective-permute-start.8 = (f32[2,1,4,24,256]{4,3,2,1,0:T(8,128)S(1)}, f32[2,1,4,24,256]{4,3,2,1,0:T(8,128)S(1)}, u32[]{:S(2)}, u32[]{:S(2)}) collective-permute-start(f32[2,1,4,24,256]{4,3,2,1,0:T(8,128)S(1)} %maximum_bitcast_fusion.6), channel_id=1, source_target_pairs={{0,1},{1,0},{2,3},{3,2},{4,5},{5,4},{6,7},{7,6},{8,9},{9,8},{10,11... | collective-permute-start | bytes 589832 | tf_op jit(solution)/shard_map/ppermute | solution.py:23
  113.4 7.3 %collective-permute-start.10 = (f32[2,1,4,24,256]{4,3,2,1,0:T(8,128)S(1)}, f32[2,1,4,24,256]{4,3,2,1,0:T(8,128)S(1)}, u32[]{:S(2)}, u32[]{:S(2)}) collective-permute-start(f32[2,1,4,24,256]{4,3,2,1,0:T(8,128)S(1)} %maximum_bitcast_fusion.7), channel_id=1, source_target_pairs={{0,1},{1,0},{2,3},{3,2},{4,5},{5,4},{6,7},{7,6},{8,9},{9,8},{10,11... | collective-permute-start | bytes 589832 | tf_op jit(solution)/shard_map/ppermute | solution.py:23
  129.2 7.3 %collective-permute-start.12 = (f32[3,1,4,24,256]{4,3,2,1,0:T(8,128)S(1)}, f32[3,1,4,24,256]{4,3,2,1,0:T(8,128)S(1)}, u32[]{:S(2)}, u32[]{:S(2)}) collective-permute-start(f32[3,1,4,24,256]{4,3,2,1,0:T(8,128)S(1)} %maximum_bitcast_fusion), channel_id=1, source_target_pairs={{0,1},{1,0},{2,3},{3,2},{4,5},{5,4},{6,7},{7,6},{8,9},{9,8},{10,11... | collective-permute-start | bytes 884744 | tf_op jit(solution)/shard_map/ppermute | solution.py:23
  139.6 9.3 %collective-permute-start.14 = (f32[3,1,4,24,256]{4,3,2,1,0:T(8,128)S(1)}, f32[3,1,4,24,256]{4,3,2,1,0:T(8,128)S(1)}, u32[]{:S(2)}, u32[]{:S(2)}) collective-permute-start(f32[3,1,4,24,256]{4,3,2,1,0:T(8,128)S(1)} %maximum_bitcast_fusion.1), channel_id=1, source_target_pairs={{0,1},{1,0},{2,3},{3,2},{4,5},{5,4},{6,7},{7,6},{8,9},{9,8},{10,11... | collective-permute-start | bytes 884744 | tf_op jit(solution)/shard_map/ppermute | solution.py:23
  154.8 8.2 %all-to-all-start.3 = ((f32[32,1,512]{2,1,0:T(1,128)}), f32[32,1,512]{2,1,0:T(1,128)S(1)}, u32[]{:S(2)}, u32[]{:S(2)}) async-start(f32[32,1,512]{2,1,0:T(1,128)} %all_to_all.33), calls=%async_computation.3 | async-start | bytes 131072 | tf_op jit(solution)/shard_map/all_to_all | solution.py:265
  164.6 5.8 %all-to-all-done.3 = f32[32,1,512]{2,1,0:T(1,128)S(1)} async-done(((f32[32,1,512]{2,1,0:T(1,128)}), f32[32,1,512]{2,1,0:T(1,128)S(1)}, u32[]{:S(2)}, u32[]{:S(2)}) %all-to-all-start.3) | async-done | bytes 65568 | tf_op jit(solution)/shard_map/all_to_all | solution.py:265
  (323 shorter events, 50.9 us)
Async XLA Ops:
  7.7 19.6 %all-to-all-start = ((f32[32,1,2688]{2,1,0:T(1,128)}), f32[32,1,2688]{2,1,0:T(1,128)S(1)}, u32[]{:S(2)}, u32[]{:S(2)}) async-start(f32[32,1,2688]{2,1,0:T(1,128)} %reshape.974), calls=%async_computation | async-start | bytes 688128 | tf_op jit(solution)/shard_map/all_to_all | solution.py:103
  17.3 89.5 %copy-start.33 = (pred[128]{0:T(512)(128)(4,1)}, pred[128]{0:T(512)(128)(4,1)S(1)}, u32[]{:S(2)}) copy-start(pred[128]{0:T(512)(128)(4,1)S(1)} %get-tuple-element.299) | copy-start | bytes 388
  17.3 36.6 %copy-start.36 = (s32[128]{0:T(128)}, s32[128]{0:T(128)S(1)}, u32[]{:S(2)}) copy-start(s32[128]{0:T(128)S(1)} %fusion.1111) | copy-start | bytes 1540
  35.7 3.0 %collective-permute-start.1 = (f32[2,1,4,24,256]{4,3,2,1,0:T(8,128)S(1)}, f32[2,1,4,24,256]{4,3,2,1,0:T(8,128)S(1)}, u32[]{:S(2)}, u32[]{:S(2)}) collective-permute-start(f32[2,1,4,24,256]{4,3,2,1,0:T(8,128)S(1)} %maximum_bitcast_fusion.2), channel_id=1, source_target_pairs={{1,2},{3,4},{5,6},{7,8},{9,10},{11,12},{13,14},{15,16},{17,18},{19... | collective-permute-start | bytes 589832 | tf_op jit(solution)/shard_map/ppermute | solution.py:24
  36.5 2.8 %collective-permute-start = (f32[2,1,4,24,256]{4,3,2,1,0:T(8,128)S(1)}, f32[2,1,4,24,256]{4,3,2,1,0:T(8,128)S(1)}, u32[]{:S(2)}, u32[]{:S(2)}) collective-permute-start(f32[2,1,4,24,256]{4,3,2,1,0:T(8,128)S(1)} %maximum_bitcast_fusion.2), channel_id=1, source_target_pairs={{0,1},{1,0},{2,3},{3,2},{4,5},{5,4},{6,7},{7,6},{8,9},{9,8},{10,11... | collective-permute-start | bytes 589832 | tf_op jit(solution)/shard_map/ppermute | solution.py:23
  40.6 8.5 %collective-permute-start.3 = (f32[2,1,4,24,256]{4,3,2,1,0:T(8,128)S(1)}, f32[2,1,4,24,256]{4,3,2,1,0:T(8,128)S(1)}, u32[]{:S(2)}, u32[]{:S(2)}) collective-permute-start(f32[2,1,4,24,256]{4,3,2,1,0:T(8,128)S(1)} %maximum_bitcast_fusion.3), channel_id=1, source_target_pairs={{1,2},{3,4},{5,6},{7,8},{9,10},{11,12},{13,14},{15,16},{17,18},{19... | collective-permute-start | bytes 589832 | tf_op jit(solution)/shard_map/ppermute | solution.py:24
  41.3 8.4 %collective-permute-start.2 = (f32[2,1,4,24,256]{4,3,2,1,0:T(8,128)S(1)}, f32[2,1,4,24,256]{4,3,2,1,0:T(8,128)S(1)}, u32[]{:S(2)}, u32[]{:S(2)}) collective-permute-start(f32[2,1,4,24,256]{4,3,2,1,0:T(8,128)S(1)} %maximum_bitcast_fusion.3), channel_id=1, source_target_pairs={{0,1},{1,0},{2,3},{3,2},{4,5},{5,4},{6,7},{7,6},{8,9},{9,8},{10,11... | collective-permute-start | bytes 589832 | tf_op jit(solution)/shard_map/ppermute | solution.py:23
  55.0 15.1 %all-to-all-start.1 = ((f32[32,1,128]{2,1,0:T(1,128)}), f32[32,1,128]{2,1,0:T(1,128)S(1)}, u32[]{:S(2)}, u32[]{:S(2)}) async-start(f32[32,1,128]{2,1,0:T(1,128)} %broadcast_in_dim.8), calls=%async_computation.1 | async-start | bytes 32768 | tf_op jit(solution)/shard_map/all_to_all | solution.py:45
  72.6 2.9 %collective-permute-start.5 = (f32[2,1,4,24,256]{4,3,2,1,0:T(8,128)S(1)}, f32[2,1,4,24,256]{4,3,2,1,0:T(8,128)S(1)}, u32[]{:S(2)}, u32[]{:S(2)}) collective-permute-start(f32[2,1,4,24,256]{4,3,2,1,0:T(8,128)S(1)} %maximum_bitcast_fusion.4), channel_id=1, source_target_pairs={{1,2},{3,4},{5,6},{7,8},{9,10},{11,12},{13,14},{15,16},{17,18},{19... | collective-permute-start | bytes 589832 | tf_op jit(solution)/shard_map/ppermute | solution.py:24
  73.5 3.0 %collective-permute-start.4 = (f32[2,1,4,24,256]{4,3,2,1,0:T(8,128)S(1)}, f32[2,1,4,24,256]{4,3,2,1,0:T(8,128)S(1)}, u32[]{:S(2)}, u32[]{:S(2)}) collective-permute-start(f32[2,1,4,24,256]{4,3,2,1,0:T(8,128)S(1)} %maximum_bitcast_fusion.4), channel_id=1, source_target_pairs={{0,1},{1,0},{2,3},{3,2},{4,5},{5,4},{6,7},{7,6},{8,9},{9,8},{10,11... | collective-permute-start | bytes 589832 | tf_op jit(solution)/shard_map/ppermute | solution.py:23
  77.7 8.3 %collective-permute-start.7 = (f32[2,1,4,24,256]{4,3,2,1,0:T(8,128)S(1)}, f32[2,1,4,24,256]{4,3,2,1,0:T(8,128)S(1)}, u32[]{:S(2)}, u32[]{:S(2)}) collective-permute-start(f32[2,1,4,24,256]{4,3,2,1,0:T(8,128)S(1)} %maximum_bitcast_fusion.5), channel_id=1, source_target_pairs={{1,2},{3,4},{5,6},{7,8},{9,10},{11,12},{13,14},{15,16},{17,18},{19... | collective-permute-start | bytes 589832 | tf_op jit(solution)/shard_map/ppermute | solution.py:24
  78.4 8.2 %collective-permute-start.6 = (f32[2,1,4,24,256]{4,3,2,1,0:T(8,128)S(1)}, f32[2,1,4,24,256]{4,3,2,1,0:T(8,128)S(1)}, u32[]{:S(2)}, u32[]{:S(2)}) collective-permute-start(f32[2,1,4,24,256]{4,3,2,1,0:T(8,128)S(1)} %maximum_bitcast_fusion.5), channel_id=1, source_target_pairs={{0,1},{1,0},{2,3},{3,2},{4,5},{5,4},{6,7},{7,6},{8,9},{9,8},{10,11... | collective-permute-start | bytes 589832 | tf_op jit(solution)/shard_map/ppermute | solution.py:23
  87.4 19.9 %copy-start.8 = (f32[2,1,4,4,256]{4,3,2,0,1:T(4,128)}, f32[2,1,4,4,256]{4,3,2,0,1:T(4,128)S(1)}, u32[]{:S(2)}) copy-start(f32[2,1,4,4,256]{4,3,2,0,1:T(4,128)S(1)} %get-tuple-element.288) | copy-start | bytes 98308
  87.4 22.6 %copy-start.4 = (f32[2,1,4,4,256]{4,3,2,0,1:T(4,128)}, f32[2,1,4,4,256]{4,3,2,0,1:T(4,128)S(1)}, u32[]{:S(2)}) copy-start(f32[2,1,4,4,256]{4,3,2,0,1:T(4,128)S(1)} %get-tuple-element.383) | copy-start | bytes 98308
  91.2 14.4 %all-to-all-start.2 = ((f32[32,1,128]{2,1,0:T(1,128)}), f32[32,1,128]{2,1,0:T(1,128)S(1)}, u32[]{:S(2)}, u32[]{:S(2)}) async-start(f32[32,1,128]{2,1,0:T(1,128)} %broadcast_in_dim.9), calls=%async_computation.2 | async-start | bytes 32768 | tf_op jit(solution)/shard_map/all_to_all | solution.py:45
  107.4 3.4 %collective-permute-start.9 = (f32[2,1,4,24,256]{4,3,2,1,0:T(8,128)S(1)}, f32[2,1,4,24,256]{4,3,2,1,0:T(8,128)S(1)}, u32[]{:S(2)}, u32[]{:S(2)}) collective-permute-start(f32[2,1,4,24,256]{4,3,2,1,0:T(8,128)S(1)} %maximum_bitcast_fusion.6), channel_id=1, source_target_pairs={{1,2},{3,4},{5,6},{7,8},{9,10},{11,12},{13,14},{15,16},{17,18},{19... | collective-permute-start | bytes 589832 | tf_op jit(solution)/shard_map/ppermute | solution.py:24
  108.1 3.0 %collective-permute-start.8 = (f32[2,1,4,24,256]{4,3,2,1,0:T(8,128)S(1)}, f32[2,1,4,24,256]{4,3,2,1,0:T(8,128)S(1)}, u32[]{:S(2)}, u32[]{:S(2)}) collective-permute-start(f32[2,1,4,24,256]{4,3,2,1,0:T(8,128)S(1)} %maximum_bitcast_fusion.6), channel_id=1, source_target_pairs={{0,1},{1,0},{2,3},{3,2},{4,5},{5,4},{6,7},{7,6},{8,9},{9,8},{10,11... | collective-permute-start | bytes 589832 | tf_op jit(solution)/shard_map/ppermute | solution.py:23
  112.7 8.5 %collective-permute-start.11 = (f32[2,1,4,24,256]{4,3,2,1,0:T(8,128)S(1)}, f32[2,1,4,24,256]{4,3,2,1,0:T(8,128)S(1)}, u32[]{:S(2)}, u32[]{:S(2)}) collective-permute-start(f32[2,1,4,24,256]{4,3,2,1,0:T(8,128)S(1)} %maximum_bitcast_fusion.7), channel_id=1, source_target_pairs={{1,2},{3,4},{5,6},{7,8},{9,10},{11,12},{13,14},{15,16},{17,18},{19... | collective-permute-start | bytes 589832 | tf_op jit(solution)/shard_map/ppermute | solution.py:24
  113.4 8.4 %collective-permute-start.10 = (f32[2,1,4,24,256]{4,3,2,1,0:T(8,128)S(1)}, f32[2,1,4,24,256]{4,3,2,1,0:T(8,128)S(1)}, u32[]{:S(2)}, u32[]{:S(2)}) collective-permute-start(f32[2,1,4,24,256]{4,3,2,1,0:T(8,128)S(1)} %maximum_bitcast_fusion.7), channel_id=1, source_target_pairs={{0,1},{1,0},{2,3},{3,2},{4,5},{5,4},{6,7},{7,6},{8,9},{9,8},{10,11... | collective-permute-start | bytes 589832 | tf_op jit(solution)/shard_map/ppermute | solution.py:23
  128.5 8.6 %collective-permute-start.13 = (f32[3,1,4,24,256]{4,3,2,1,0:T(8,128)S(1)}, f32[3,1,4,24,256]{4,3,2,1,0:T(8,128)S(1)}, u32[]{:S(2)}, u32[]{:S(2)}) collective-permute-start(f32[3,1,4,24,256]{4,3,2,1,0:T(8,128)S(1)} %maximum_bitcast_fusion), channel_id=1, source_target_pairs={{1,2},{3,4},{5,6},{7,8},{9,10},{11,12},{13,14},{15,16},{17,18},{19... | collective-permute-start | bytes 884744 | tf_op jit(solution)/shard_map/ppermute | solution.py:24
  129.2 8.6 %collective-permute-start.12 = (f32[3,1,4,24,256]{4,3,2,1,0:T(8,128)S(1)}, f32[3,1,4,24,256]{4,3,2,1,0:T(8,128)S(1)}, u32[]{:S(2)}, u32[]{:S(2)}) collective-permute-start(f32[3,1,4,24,256]{4,3,2,1,0:T(8,128)S(1)} %maximum_bitcast_fusion), channel_id=1, source_target_pairs={{0,1},{1,0},{2,3},{3,2},{4,5},{5,4},{6,7},{7,6},{8,9},{9,8},{10,11... | collective-permute-start | bytes 884744 | tf_op jit(solution)/shard_map/ppermute | solution.py:23
  138.9 11.3 %collective-permute-start.15 = (f32[3,1,4,24,256]{4,3,2,1,0:T(8,128)S(1)}, f32[3,1,4,24,256]{4,3,2,1,0:T(8,128)S(1)}, u32[]{:S(2)}, u32[]{:S(2)}) collective-permute-start(f32[3,1,4,24,256]{4,3,2,1,0:T(8,128)S(1)} %maximum_bitcast_fusion.1), channel_id=1, source_target_pairs={{1,2},{3,4},{5,6},{7,8},{9,10},{11,12},{13,14},{15,16},{17,18},{19... | collective-permute-start | bytes 884744 | tf_op jit(solution)/shard_map/ppermute | solution.py:24
  139.6 10.6 %collective-permute-start.14 = (f32[3,1,4,24,256]{4,3,2,1,0:T(8,128)S(1)}, f32[3,1,4,24,256]{4,3,2,1,0:T(8,128)S(1)}, u32[]{:S(2)}, u32[]{:S(2)}) collective-permute-start(f32[3,1,4,24,256]{4,3,2,1,0:T(8,128)S(1)} %maximum_bitcast_fusion.1), channel_id=1, source_target_pairs={{0,1},{1,0},{2,3},{3,2},{4,5},{5,4},{6,7},{7,6},{8,9},{9,8},{10,11... | collective-permute-start | bytes 884744 | tf_op jit(solution)/shard_map/ppermute | solution.py:23
  154.8 15.6 %all-to-all-start.3 = ((f32[32,1,512]{2,1,0:T(1,128)}), f32[32,1,512]{2,1,0:T(1,128)S(1)}, u32[]{:S(2)}, u32[]{:S(2)}) async-start(f32[32,1,512]{2,1,0:T(1,128)} %all_to_all.33), calls=%async_computation.3 | async-start | bytes 131072 | tf_op jit(solution)/shard_map/all_to_all | solution.py:265
  (42 other events, 234.0 us)

commit v14 on v13

--- a/solution.py
+++ b/solution.py
@@ -8,7 +8,7 @@
 HALO = 4
 ROW_AXIS = 2
 DEPTH_AXIS = 3
-DEFERRED = 2
+DEFERRED = 4
 
 
 def halo_rows(fields):

time: 175 us -> 175 us (level)
  waiting for transfers between devices: 33.8 us -> 18.2 us
  other arithmetic: 29.5 us -> 40.6 us
  starting transfers between devices: 80.7 us -> 84 us
  local copies, waits for them, and re-layouts: 21.5 us -> 24.4 us
    all_to_all x2 -> x0, starting transfers between devices: 15.3 us -> none  [gather_sum(): return jnp.sum(lax.all_to_all(copies, 'gx', 0, 0, tiled=True), axis=0)]
    all_to_all x2 -> x0, waiting for transfers between devices: 13.9 us -> none  [gather_sum(): return jnp.sum(lax.all_to_all(copies, 'gx', 0, 0, tiled=True), axis=0)]
    ppermute x8, starting transfers between devices: 44.1 us -> 57.4 us  [halo_rows(): got_within = lax.ppermute(jnp.where(odd, first, last), 'gx', within)]
    all_to_all x1, starting transfers between devices: 8.21 us -> 13.6 us  [on_device(): got = lax.all_to_all(packed, 'gx', 0, 0, tiled=True)]
    ppermute x8, waiting for transfers between devices: 4.21 us -> 2.03 us  [halo_rows(): got_within = lax.ppermute(jnp.where(odd, first, last), 'gx', within)]
    mul x0 -> x15, local copies, waits for them, and re-layouts: none -> 1.84 us  [the longest x2 0.61 us: on_device(): shear_xz[:1] * shear_xz[1:]]
    add x32, other arithmetic: 7.75 us -> 9.51 us  [stencil(): summed = addend if summed is None else summed + addend]
    unnamed x110 -> x116, local copies, waits for them, and re-layouts: 9.87 us -> 9.53 us
  transfers between devices with their start and end apart: 20 -> 18, of which waited for: 11 -> 6; matrix products, arithmetic and copies ran while one was open for 4% -> 11% of each run, Pallas kernels for 0% -> 0%
where the time goes in v14:
time: 175 us; the launch traced here: 174 us
  starting transfers between devices  84 us (48%)
  other arithmetic  40.6 us (23%)
  local copies, waits for them, and re-layouts  24.4 us (14%)
  waiting for transfers between devices  18.2 us (10%)
  matrix products  3.44 us (2%)
  between operations  3.15 us (2%)
    ppermute x8, starting transfers between devices, halo_rows(): got_within = lax.ppermute(jnp.where(odd, first, last), 'gx', within)  57.4 us
    all_to_all x1, starting transfers between devices, on_device(): got = lax.all_to_all(packed, 'gx', 0, 0, tiled=True)  13.6 us
    unnamed x116, local copies, waits for them, and re-layouts  9.53 us
    add x32, other arithmetic, stencil(): summed = addend if summed is None else summed + addend  9.51 us
    all_to_all x1, waiting for transfers between devices, on_device(): lax.all_to_all(rock_in, 'gx', split_axis=3, concat_axis=1, tiled=True)  8.95 us
    all_to_all x1, starting transfers between devices, on_device(): lax.all_to_all(rock_in, 'gx', split_axis=3, concat_axis=1, tiled=True)  7.3 us
    all_to_all x1, waiting for transfers between devices, on_device(): got = lax.all_to_all(packed, 'gx', 0, 0, tiled=True)  7.21 us
    ppermute x8, starting transfers between devices, halo_rows(): got_across = lax.ppermute(jnp.where(odd, last, first), 'gx', across)  5.71 us
  transfers between devices with their start and end apart: 18, of which 6 were waited for; matrix products, arithmetic and copies ran while one was open for 11% of the time, Pallas kernels for 0%

profile of v14, /device:TPU:0, one launch (start us, length us, event | category | flops | bytes accessed | tf_op | source)
XLA Modules:
  0.0 173.9 jit_solution(9570497049488646804)
XLA Ops:
  1.4 1.0 copy.3217
  3.1 1.9 %copy.3221 = f32[21,8,4,128]{0,1,2,3:T(8,128)S(1)} copy(f32[21,8,4,128]{3,1,2,0:T(8,128)S(1)} %pad_maximum_fusion.8) | data formatting | bytes 688128 | tf_op jit(solution)/shard_map/concatenate | solution.py:95
  5.1 2.6 %reshape.1054 = f32[32,1,2688]{2,1,0:T(1,128)} reshape(f32[128,4,8,21]{3,2,1,0:T(8,128)S(1)} %bitcast.376) | data formatting | bytes 688128
  7.7 7.3 %all-to-all-start = ((f32[32,1,2688]{2,1,0:T(1,128)}), f32[32,1,2688]{2,1,0:T(1,128)S(1)}, u32[]{:S(2)}, u32[]{:S(2)}) async-start(f32[32,1,2688]{2,1,0:T(1,128)} %reshape.1054), calls=%async_computation | async-start | bytes 688128 | tf_op jit(solution)/shard_map/all_to_all | solution.py:103
  18.4 9.0 %all-to-all-done = f32[32,1,2688]{2,1,0:T(1,128)S(1)} async-done(((f32[32,1,2688]{2,1,0:T(1,128)}), f32[32,1,2688]{2,1,0:T(1,128)S(1)}, u32[]{:S(2)}, u32[]{:S(2)}) %all-to-all-start) | async-done | bytes 344096 | tf_op jit(solution)/shard_map/all_to_all | solution.py:103
  27.8 1.5 reduce.28
  29.3 2.3 %reshape.1055 = f32[128,4,8,21]{3,2,1,0:T(8,128)S(1)} reshape(f32[32,2688]{1,0:T(8,128)S(1)} %reduce.28) | data formatting | bytes 688128
  31.6 1.5 copy.3367
  33.1 2.3 %copy.3224 = f32[21,256,4,4]{1,2,3,0:T(4,128)S(1)} copy(f32[21,256,4,4]{0,1,3,2:T(8,128)} %bitcast.378) | data formatting | bytes 688128 | tf_op jit(solution)/shard_map/all_to_all | solution.py:103
  36.5 1.7 collective-permute-start
  41.3 7.3 %collective-permute-start.2 = (f32[2,1,4,24,256]{4,3,2,1,0:T(8,128)S(1)}, f32[2,1,4,24,256]{4,3,2,1,0:T(8,128)S(1)}, u32[]{:S(2)}, u32[]{:S(2)}) collective-permute-start(f32[2,1,4,24,256]{4,3,2,1,0:T(8,128)S(1)} %maximum_bitcast_fusion.7), channel_id=1, source_target_pairs={{0,1},{1,0},{2,3},{3,2},{4,5},{5,4},{6,7},{7,6},{8,9},{9,8},{10,11... | collective-permute-start | bytes 589832 | tf_op jit(solution)/shard_map/ppermute | solution.py:23
  55.4 7.3 %collective-permute-start.4 = (f32[3,1,4,24,256]{4,3,2,1,0:T(8,128)S(1)}, f32[3,1,4,24,256]{4,3,2,1,0:T(8,128)S(1)}, u32[]{:S(2)}, u32[]{:S(2)}) collective-permute-start(f32[3,1,4,24,256]{4,3,2,1,0:T(8,128)S(1)} %maximum_bitcast_fusion.4), channel_id=1, source_target_pairs={{0,1},{1,0},{2,3},{3,2},{4,5},{5,4},{6,7},{7,6},{8,9},{9,8},{10,11... | collective-permute-start | bytes 884744 | tf_op jit(solution)/shard_map/ppermute | solution.py:23
  65.9 9.3 %collective-permute-start.6 = (f32[3,1,4,24,256]{4,3,2,1,0:T(8,128)S(1)}, f32[3,1,4,24,256]{4,3,2,1,0:T(8,128)S(1)}, u32[]{:S(2)}, u32[]{:S(2)}) collective-permute-start(f32[3,1,4,24,256]{4,3,2,1,0:T(8,128)S(1)} %maximum_bitcast_fusion.5), channel_id=1, source_target_pairs={{0,1},{1,0},{2,3},{3,2},{4,5},{5,4},{6,7},{7,6},{8,9},{9,8},{10,11... | collective-permute-start | bytes 884744 | tf_op jit(solution)/shard_map/ppermute | solution.py:23
  83.9 8.5 %collective-permute-start.8 = (f32[4,1,4,24,256]{4,3,2,1,0:T(8,128)S(1)}, f32[4,1,4,24,256]{4,3,2,1,0:T(8,128)S(1)}, u32[]{:S(2)}, u32[]{:S(2)}) collective-permute-start(f32[4,1,4,24,256]{4,3,2,1,0:T(8,128)S(1)} %maximum_bitcast_fusion.2), channel_id=1, source_target_pairs={{0,1},{1,0},{2,3},{3,2},{4,5},{5,4},{6,7},{7,6},{8,9},{9,8},{10,11... | collective-permute-start | bytes 1179656 | tf_op jit(solution)/shard_map/ppermute | solution.py:23
  95.3 1.5 fusion.1202
  98.2 0.9 multiply_add_fusion.12
  101.9 5.6 %collective-permute-start.10 = (f32[4,1,4,24,256]{4,3,2,1,0:T(8,128)S(1)}, f32[4,1,4,24,256]{4,3,2,1,0:T(8,128)S(1)}, u32[]{:S(2)}, u32[]{:S(2)}) collective-permute-start(f32[4,1,4,24,256]{4,3,2,1,0:T(8,128)S(1)} %maximum_bitcast_fusion.3), channel_id=1, source_target_pairs={{0,1},{1,0},{2,3},{3,2},{4,5},{5,4},{6,7},{7,6},{8,9},{9,8},{10,11... | collective-permute-start | bytes 1179656 | tf_op jit(solution)/shard_map/ppermute | solution.py:23
  110.1 0.9 fusion.415
  115.7 0.9 maximum_bitcast_fusion
  117.4 6.8 %collective-permute-start.12 = (f32[5,1,4,24,256]{4,3,2,1,0:T(8,128)}, f32[5,1,4,24,256]{4,3,2,1,0:T(8,128)}, u32[]{:S(2)}, u32[]{:S(2)}) collective-permute-start(f32[5,1,4,24,256]{4,3,2,1,0:T(8,128)} %maximum_bitcast_fusion), channel_id=1, source_target_pairs={{0,1},{1,0},{2,3},{3,2},{4,5},{5,4},{6,7},{7,6},{8,9},{9,8},{10,11... | collective-permute-start | bytes 1474568 | tf_op jit(solution)/shard_map/ppermute | solution.py:23
  126.0 1.1 bitcast_select_fusion.2
  130.0 10.8 %collective-permute-start.14 = (f32[5,1,4,24,256]{4,3,2,1,0:T(8,128)S(1)}, f32[5,1,4,24,256]{4,3,2,1,0:T(8,128)S(1)}, u32[]{:S(2)}, u32[]{:S(2)}) collective-permute-start(f32[5,1,4,24,256]{4,3,2,1,0:T(8,128)S(1)} %maximum_bitcast_fusion.1), channel_id=1, source_target_pairs={{0,1},{1,0},{2,3},{3,2},{4,5},{5,4},{6,7},{7,6},{8,9},{9,8},{10,11... | collective-permute-start | bytes 1474568 | tf_op jit(solution)/shard_map/ppermute | solution.py:23
  148.0 13.6 %all-to-all-start.1 = ((f32[32,1,1280]{2,1,0:T(1,128)}), f32[32,1,1280]{2,1,0:T(1,128)S(1)}, u32[]{:S(2)}, u32[]{:S(2)}) async-start(f32[32,1,1280]{2,1,0:T(1,128)} %all_to_all.25), calls=%async_computation.1 | async-start | bytes 327680 | tf_op jit(solution)/shard_map/all_to_all | solution.py:265
  162.9 7.2 %all-to-all-done.1 = f32[32,1,1280]{2,1,0:T(1,128)S(1)} async-done(((f32[32,1,1280]{2,1,0:T(1,128)}), f32[32,1,1280]{2,1,0:T(1,128)S(1)}, u32[]{:S(2)}, u32[]{:S(2)}) %all-to-all-start.1) | async-done | bytes 163872 | tf_op jit(solution)/shard_map/all_to_all | solution.py:265
  (370 shorter events, 57.9 us)
Async XLA Ops:
  7.7 19.6 %all-to-all-start = ((f32[32,1,2688]{2,1,0:T(1,128)}), f32[32,1,2688]{2,1,0:T(1,128)S(1)}, u32[]{:S(2)}, u32[]{:S(2)}) async-start(f32[32,1,2688]{2,1,0:T(1,128)} %reshape.1054), calls=%async_computation | async-start | bytes 688128 | tf_op jit(solution)/shard_map/all_to_all | solution.py:103
  35.7 3.0 %collective-permute-start.1 = (f32[2,1,4,24,256]{4,3,2,1,0:T(8,128)S(1)}, f32[2,1,4,24,256]{4,3,2,1,0:T(8,128)S(1)}, u32[]{:S(2)}, u32[]{:S(2)}) collective-permute-start(f32[2,1,4,24,256]{4,3,2,1,0:T(8,128)S(1)} %maximum_bitcast_fusion.6), channel_id=1, source_target_pairs={{1,2},{3,4},{5,6},{7,8},{9,10},{11,12},{13,14},{15,16},{17,18},{19... | collective-permute-start | bytes 589832 | tf_op jit(solution)/shard_map/ppermute | solution.py:24
  36.5 2.8 %collective-permute-start = (f32[2,1,4,24,256]{4,3,2,1,0:T(8,128)S(1)}, f32[2,1,4,24,256]{4,3,2,1,0:T(8,128)S(1)}, u32[]{:S(2)}, u32[]{:S(2)}) collective-permute-start(f32[2,1,4,24,256]{4,3,2,1,0:T(8,128)S(1)} %maximum_bitcast_fusion.6), channel_id=1, source_target_pairs={{0,1},{1,0},{2,3},{3,2},{4,5},{5,4},{6,7},{7,6},{8,9},{9,8},{10,11... | collective-permute-start | bytes 589832 | tf_op jit(solution)/shard_map/ppermute | solution.py:23
  40.6 8.5 %collective-permute-start.3 = (f32[2,1,4,24,256]{4,3,2,1,0:T(8,128)S(1)}, f32[2,1,4,24,256]{4,3,2,1,0:T(8,128)S(1)}, u32[]{:S(2)}, u32[]{:S(2)}) collective-permute-start(f32[2,1,4,24,256]{4,3,2,1,0:T(8,128)S(1)} %maximum_bitcast_fusion.7), channel_id=1, source_target_pairs={{1,2},{3,4},{5,6},{7,8},{9,10},{11,12},{13,14},{15,16},{17,18},{19... | collective-permute-start | bytes 589832 | tf_op jit(solution)/shard_map/ppermute | solution.py:24
  41.3 8.4 %collective-permute-start.2 = (f32[2,1,4,24,256]{4,3,2,1,0:T(8,128)S(1)}, f32[2,1,4,24,256]{4,3,2,1,0:T(8,128)S(1)}, u32[]{:S(2)}, u32[]{:S(2)}) collective-permute-start(f32[2,1,4,24,256]{4,3,2,1,0:T(8,128)S(1)} %maximum_bitcast_fusion.7), channel_id=1, source_target_pairs={{0,1},{1,0},{2,3},{3,2},{4,5},{5,4},{6,7},{7,6},{8,9},{9,8},{10,11... | collective-permute-start | bytes 589832 | tf_op jit(solution)/shard_map/ppermute | solution.py:23
  54.7 8.8 %collective-permute-start.5 = (f32[3,1,4,24,256]{4,3,2,1,0:T(8,128)S(1)}, f32[3,1,4,24,256]{4,3,2,1,0:T(8,128)S(1)}, u32[]{:S(2)}, u32[]{:S(2)}) collective-permute-start(f32[3,1,4,24,256]{4,3,2,1,0:T(8,128)S(1)} %maximum_bitcast_fusion.4), channel_id=1, source_target_pairs={{1,2},{3,4},{5,6},{7,8},{9,10},{11,12},{13,14},{15,16},{17,18},{19... | collective-permute-start | bytes 884744 | tf_op jit(solution)/shard_map/ppermute | solution.py:24
  55.4 8.6 %collective-permute-start.4 = (f32[3,1,4,24,256]{4,3,2,1,0:T(8,128)S(1)}, f32[3,1,4,24,256]{4,3,2,1,0:T(8,128)S(1)}, u32[]{:S(2)}, u32[]{:S(2)}) collective-permute-start(f32[3,1,4,24,256]{4,3,2,1,0:T(8,128)S(1)} %maximum_bitcast_fusion.4), channel_id=1, source_target_pairs={{0,1},{1,0},{2,3},{3,2},{4,5},{5,4},{6,7},{7,6},{8,9},{9,8},{10,11... | collective-permute-start | bytes 884744 | tf_op jit(solution)/shard_map/ppermute | solution.py:23
  65.2 12.0 %collective-permute-start.7 = (f32[3,1,4,24,256]{4,3,2,1,0:T(8,128)S(1)}, f32[3,1,4,24,256]{4,3,2,1,0:T(8,128)S(1)}, u32[]{:S(2)}, u32[]{:S(2)}) collective-permute-start(f32[3,1,4,24,256]{4,3,2,1,0:T(8,128)S(1)} %maximum_bitcast_fusion.5), channel_id=1, source_target_pairs={{1,2},{3,4},{5,6},{7,8},{9,10},{11,12},{13,14},{15,16},{17,18},{19... | collective-permute-start | bytes 884744 | tf_op jit(solution)/shard_map/ppermute | solution.py:24
  65.9 11.3 %collective-permute-start.6 = (f32[3,1,4,24,256]{4,3,2,1,0:T(8,128)S(1)}, f32[3,1,4,24,256]{4,3,2,1,0:T(8,128)S(1)}, u32[]{:S(2)}, u32[]{:S(2)}) collective-permute-start(f32[3,1,4,24,256]{4,3,2,1,0:T(8,128)S(1)} %maximum_bitcast_fusion.5), channel_id=1, source_target_pairs={{0,1},{1,0},{2,3},{3,2},{4,5},{5,4},{6,7},{7,6},{8,9},{9,8},{10,11... | collective-permute-start | bytes 884744 | tf_op jit(solution)/shard_map/ppermute | solution.py:23
  81.7 13.6 %copy-start.5 = (f32[2,1,4,4,256]{4,3,2,0,1:T(4,128)S(1)}, f32[2,1,4,4,256]{4,3,2,0,1:T(4,128)}, u32[]{:S(2)}) copy-start(f32[2,1,4,4,256]{4,3,2,0,1:T(4,128)} %copy-done.4) | copy-start | bytes 98308
  81.7 13.6 %copy-start.24 = (f32[2,1,4,4,256]{4,3,2,0,1:T(4,128)S(1)}, f32[2,1,4,4,256]{4,3,2,0,1:T(4,128)}, u32[]{:S(2)}) copy-start(f32[2,1,4,4,256]{4,3,2,0,1:T(4,128)} %get-tuple-element.320) | copy-start | bytes 98308
  81.7 15.1 %copy-start.13 = (f32[2,1,4,4,256]{4,3,2,0,1:T(4,128)S(1)}, f32[2,1,4,4,256]{4,3,2,0,1:T(4,128)}, u32[]{:S(2)}) copy-start(f32[2,1,4,4,256]{4,3,2,0,1:T(4,128)} %copy-done.12) | copy-start | bytes 98308
  82.4 15.1 %copy-start.17 = (f32[1,1,4,12,256]{4,3,2,0,1:T(8,128)S(1)}, f32[1,1,4,12,256]{4,3,2,0,1:T(8,128)}, u32[]{:S(2)}) copy-start(f32[1,1,4,12,256]{4,3,2,0,1:T(8,128)} %get-tuple-element.392) | copy-start | bytes 147460
  82.4 15.1 %copy-start.18 = (f32[1,1,4,12,256]{4,3,2,0,1:T(8,128)S(1)}, f32[1,1,4,12,256]{4,3,2,0,1:T(8,128)}, u32[]{:S(2)}) copy-start(f32[1,1,4,12,256]{4,3,2,0,1:T(8,128)} %get-tuple-element.393) | copy-start | bytes 147460
  83.2 15.0 %collective-permute-start.9 = (f32[4,1,4,24,256]{4,3,2,1,0:T(8,128)S(1)}, f32[4,1,4,24,256]{4,3,2,1,0:T(8,128)S(1)}, u32[]{:S(2)}, u32[]{:S(2)}) collective-permute-start(f32[4,1,4,24,256]{4,3,2,1,0:T(8,128)S(1)} %maximum_bitcast_fusion.2), channel_id=1, source_target_pairs={{1,2},{3,4},{5,6},{7,8},{9,10},{11,12},{13,14},{15,16},{17,18},{19... | collective-permute-start | bytes 1179656 | tf_op jit(solution)/shard_map/ppermute | solution.py:24
  83.9 14.3 %collective-permute-start.8 = (f32[4,1,4,24,256]{4,3,2,1,0:T(8,128)S(1)}, f32[4,1,4,24,256]{4,3,2,1,0:T(8,128)S(1)}, u32[]{:S(2)}, u32[]{:S(2)}) collective-permute-start(f32[4,1,4,24,256]{4,3,2,1,0:T(8,128)S(1)} %maximum_bitcast_fusion.2), channel_id=1, source_target_pairs={{0,1},{1,0},{2,3},{3,2},{4,5},{5,4},{6,7},{7,6},{8,9},{9,8},{10,11... | collective-permute-start | bytes 1179656 | tf_op jit(solution)/shard_map/ppermute | solution.py:23
  101.2 9.8 %collective-permute-start.11 = (f32[4,1,4,24,256]{4,3,2,1,0:T(8,128)S(1)}, f32[4,1,4,24,256]{4,3,2,1,0:T(8,128)S(1)}, u32[]{:S(2)}, u32[]{:S(2)}) collective-permute-start(f32[4,1,4,24,256]{4,3,2,1,0:T(8,128)S(1)} %maximum_bitcast_fusion.3), channel_id=1, source_target_pairs={{1,2},{3,4},{5,6},{7,8},{9,10},{11,12},{13,14},{15,16},{17,18},{19... | collective-permute-start | bytes 1179656 | tf_op jit(solution)/shard_map/ppermute | solution.py:24
  101.9 9.1 %collective-permute-start.10 = (f32[4,1,4,24,256]{4,3,2,1,0:T(8,128)S(1)}, f32[4,1,4,24,256]{4,3,2,1,0:T(8,128)S(1)}, u32[]{:S(2)}, u32[]{:S(2)}) collective-permute-start(f32[4,1,4,24,256]{4,3,2,1,0:T(8,128)S(1)} %maximum_bitcast_fusion.3), channel_id=1, source_target_pairs={{0,1},{1,0},{2,3},{3,2},{4,5},{5,4},{6,7},{7,6},{8,9},{9,8},{10,11... | collective-permute-start | bytes 1179656 | tf_op jit(solution)/shard_map/ppermute | solution.py:23
  116.6 9.0 %collective-permute-start.13 = (f32[5,1,4,24,256]{4,3,2,1,0:T(8,128)}, f32[5,1,4,24,256]{4,3,2,1,0:T(8,128)S(1)}, u32[]{:S(2)}, u32[]{:S(2)}) collective-permute-start(f32[5,1,4,24,256]{4,3,2,1,0:T(8,128)} %maximum_bitcast_fusion), channel_id=1, source_target_pairs={{1,2},{3,4},{5,6},{7,8},{9,10},{11,12},{13,14},{15,16},{17,18},{19... | collective-permute-start | bytes 1474568 | tf_op jit(solution)/shard_map/ppermute | solution.py:24
  117.4 8.6 %collective-permute-start.12 = (f32[5,1,4,24,256]{4,3,2,1,0:T(8,128)}, f32[5,1,4,24,256]{4,3,2,1,0:T(8,128)}, u32[]{:S(2)}, u32[]{:S(2)}) collective-permute-start(f32[5,1,4,24,256]{4,3,2,1,0:T(8,128)} %maximum_bitcast_fusion), channel_id=1, source_target_pairs={{0,1},{1,0},{2,3},{3,2},{4,5},{5,4},{6,7},{7,6},{8,9},{9,8},{10,11... | collective-permute-start | bytes 1474568 | tf_op jit(solution)/shard_map/ppermute | solution.py:23
  129.3 13.2 %collective-permute-start.15 = (f32[5,1,4,24,256]{4,3,2,1,0:T(8,128)S(1)}, f32[5,1,4,24,256]{4,3,2,1,0:T(8,128)S(1)}, u32[]{:S(2)}, u32[]{:S(2)}) collective-permute-start(f32[5,1,4,24,256]{4,3,2,1,0:T(8,128)S(1)} %maximum_bitcast_fusion.1), channel_id=1, source_target_pairs={{1,2},{3,4},{5,6},{7,8},{9,10},{11,12},{13,14},{15,16},{17,18},{19... | collective-permute-start | bytes 1474568 | tf_op jit(solution)/shard_map/ppermute | solution.py:24
  130.0 12.5 %collective-permute-start.14 = (f32[5,1,4,24,256]{4,3,2,1,0:T(8,128)S(1)}, f32[5,1,4,24,256]{4,3,2,1,0:T(8,128)S(1)}, u32[]{:S(2)}, u32[]{:S(2)}) collective-permute-start(f32[5,1,4,24,256]{4,3,2,1,0:T(8,128)S(1)} %maximum_bitcast_fusion.1), channel_id=1, source_target_pairs={{0,1},{1,0},{2,3},{3,2},{4,5},{5,4},{6,7},{7,6},{8,9},{9,8},{10,11... | collective-permute-start | bytes 1474568 | tf_op jit(solution)/shard_map/ppermute | solution.py:23
  146.5 15.1 %copy-start.19 = (f32[1,1,4,12,256]{4,3,2,0,1:T(8,128)S(1)}, f32[1,1,4,12,256]{4,3,2,0,1:T(8,128)}, u32[]{:S(2)}) copy-start(f32[1,1,4,12,256]{4,3,2,0,1:T(8,128)} %get-tuple-element.427) | copy-start | bytes 147460
  148.0 22.2 %all-to-all-start.1 = ((f32[32,1,1280]{2,1,0:T(1,128)}), f32[32,1,1280]{2,1,0:T(1,128)S(1)}, u32[]{:S(2)}, u32[]{:S(2)}) async-start(f32[32,1,1280]{2,1,0:T(1,128)} %all_to_all.25), calls=%async_computation.1 | async-start | bytes 327680 | tf_op jit(solution)/shard_map/all_to_all | solution.py:265
  (43 other events, 308.3 us)

commit v15 on v12

--- a/solution.py
+++ b/solution.py
@@ -208,13 +208,12 @@
         sig_xz = sig_xz + TIME_STEP * mu * shear_xz
         sig_yz = sig_yz + TIME_STEP * mu * shear_yz
         sig_zz = sig_zz.at[:, :, :, 0, :].set(-floor_pressure[:rock_waves])
-        lam_acc = lam_acc + dilation[:1] * dilation[1:]
-        normal_part = (
-            strain_x[:1] * strain_x[1:] + strain_y[:1] * strain_y[1:] + strain_z[:1] * strain_z[1:]
-        )
-        shear_part = (
-            shear_xy[:1] * shear_xy[1:] + shear_xz[:1] * shear_xz[1:] + shear_yz[:1] * shear_yz[1:]
-        )
+        (g_dil, g_sx, g_sy, g_sz, g_xy, g_xz, g_yz) = lax.optimization_barrier(
+            (dilation, strain_x, strain_y, strain_z, shear_xy, shear_xz, shear_yz)
+        )
+        lam_acc = lam_acc + g_dil[:1] * g_dil[1:]
+        normal_part = g_sx[:1] * g_sx[1:] + g_sy[:1] * g_sy[1:] + g_sz[:1] * g_sz[1:]
+        shear_part = g_xy[:1] * g_xy[1:] + g_xz[:1] * g_xz[1:] + g_yz[:1] * g_yz[1:]
         mu_acc = mu_acc + (2.0 * normal_part + shear_part)
         pressure = (
             pressure

time: 170 us -> 170 us (level)
    add x32, other arithmetic: 7.37 us -> 9.24 us  [stencil(): summed = addend if summed is None else summed + addend]
    unnamed x76 -> x108, local copies, waits for them, and re-layouts: 8.88 us -> 9.1 us
  transfers between devices with their start and end apart: 19 -> 19, of which waited for: 8 -> 9; matrix products, arithmetic and copies ran while one was open for 8% -> 9% of each run, Pallas kernels for 0% -> 0%
where the time goes in v15:
time: 170 us; the launch traced here: 169 us
  starting transfers between devices  82.5 us (49%)
  other arithmetic  35.7 us (21%)
  waiting for transfers between devices  23.3 us (14%)
  local copies, waits for them, and re-layouts  20.3 us (12%)
  between operations  3.81 us (2%)
  matrix products  3.44 us (2%)
    ppermute x8, starting transfers between devices, halo_rows(): got_within = lax.ppermute(jnp.where(odd, first, last), 'gx', within)  52.5 us
    all_to_all x1, waiting for transfers between devices, on_device(): lax.all_to_all(rock_in, 'gx', split_axis=3, concat_axis=1, tiled=True)  9.95 us
    add x32, other arithmetic, stencil(): summed = addend if summed is None else summed + addend  9.24 us
    unnamed x108, local copies, waits for them, and re-layouts  9.1 us
    all_to_all x1, starting transfers between devices, on_device(): got = lax.all_to_all(packed, 'gx', 0, 0, tiled=True)  8.78 us
    all_to_all x1, starting transfers between devices, gather_sum(): return jnp.sum(lax.all_to_all(copies, 'gx', 0, 0, tiled=True), axis=0)  8.06 us
    all_to_all x1, starting transfers between devices, on_device(): lax.all_to_all(rock_in, 'gx', split_axis=3, concat_axis=1, tiled=True)  7.3 us
    all_to_all x1, waiting for transfers between devices, on_device(): got = lax.all_to_all(packed, 'gx', 0, 0, tiled=True)  6.25 us
  transfers between devices with their start and end apart: 19, of which 9 were waited for; matrix products, arithmetic and copies ran while one was open for 9% of the time, Pallas kernels for 0%

profile of v15, /device:TPU:0, one launch (start us, length us, event | category | flops | bytes accessed | tf_op | source)
XLA Modules:
  0.0 169.0 jit_solution(18261804788124094447)
XLA Ops:
  3.1 1.9 %copy.3162 = f32[21,8,4,128]{0,1,2,3:T(8,128)S(1)} copy(f32[21,8,4,128]{3,1,2,0:T(8,128)S(1)} %pad_maximum_fusion.8) | data formatting | bytes 688128 | tf_op jit(solution)/shard_map/concatenate | solution.py:95
  5.1 2.7 %reshape.1017 = f32[32,1,2688]{2,1,0:T(1,128)} reshape(f32[128,4,8,21]{3,2,1,0:T(8,128)S(1)} %bitcast.354) | data formatting | bytes 688128
  7.7 7.3 %all-to-all-start = ((f32[32,1,2688]{2,1,0:T(1,128)}), f32[32,1,2688]{2,1,0:T(1,128)S(1)}, u32[]{:S(2)}, u32[]{:S(2)}) async-start(f32[32,1,2688]{2,1,0:T(1,128)} %reshape.1017), calls=%async_computation | async-start | bytes 688128 | tf_op jit(solution)/shard_map/all_to_all | solution.py:103
  17.4 10.0 %all-to-all-done = f32[32,1,2688]{2,1,0:T(1,128)S(1)} async-done(((f32[32,1,2688]{2,1,0:T(1,128)}), f32[32,1,2688]{2,1,0:T(1,128)S(1)}, u32[]{:S(2)}, u32[]{:S(2)}) %all-to-all-start) | async-done | bytes 344096 | tf_op jit(solution)/shard_map/all_to_all | solution.py:103
  27.8 1.5 reduce.33
  29.3 2.3 %reshape.1018 = f32[128,4,8,21]{3,2,1,0:T(8,128)S(1)} reshape(f32[32,2688]{1,0:T(8,128)S(1)} %reduce.33) | data formatting | bytes 688128
  31.6 1.5 copy.3296
  33.1 2.3 %copy.3165 = f32[21,256,4,4]{1,2,3,0:T(4,128)S(1)} copy(f32[21,256,4,4]{0,1,3,2:T(8,128)} %bitcast.356) | data formatting | bytes 688128 | tf_op jit(solution)/shard_map/all_to_all | solution.py:103
  36.4 1.7 %collective-permute-start = (f32[2,1,4,24,256]{4,3,2,1,0:T(8,128)S(1)}, f32[2,1,4,24,256]{4,3,2,1,0:T(8,128)S(1)}, u32[]{:S(2)}, u32[]{:S(2)}) collective-permute-start(f32[2,1,4,24,256]{4,3,2,1,0:T(8,128)S(1)} %maximum_bitcast_fusion.4), channel_id=1, source_target_pairs={{0,1},{1,0},{2,3},{3,2},{4,5},{5,4},{6,7},{7,6},{8,9},{9,8},{10,11... | collective-permute-start | bytes 589832 | tf_op jit(solution)/shard_map/ppermute | solution.py:23
  41.1 7.3 %collective-permute-start.2 = (f32[2,1,4,24,256]{4,3,2,1,0:T(8,128)S(1)}, f32[2,1,4,24,256]{4,3,2,1,0:T(8,128)S(1)}, u32[]{:S(2)}, u32[]{:S(2)}) collective-permute-start(f32[2,1,4,24,256]{4,3,2,1,0:T(8,128)S(1)} %maximum_bitcast_fusion.5), channel_id=1, source_target_pairs={{0,1},{1,0},{2,3},{3,2},{4,5},{5,4},{6,7},{7,6},{8,9},{9,8},{10,11... | collective-permute-start | bytes 589832 | tf_op jit(solution)/shard_map/ppermute | solution.py:23
  51.7 8.1 %all-to-all-start.1 = ((f32[32,1,128]{2,1,0:T(1,128)}), f32[32,1,128]{2,1,0:T(1,128)S(1)}, u32[]{:S(2)}, u32[]{:S(2)}) async-start(f32[32,1,128]{2,1,0:T(1,128)} %broadcast_in_dim.6), calls=%async_computation.1 | async-start | bytes 32768 | tf_op jit(solution)/shard_map/all_to_all | solution.py:45
  62.8 4.0 %all-to-all-done.1 = f32[32,1,128]{2,1,0:T(1,128)S(1)} async-done(((f32[32,1,128]{2,1,0:T(1,128)}), f32[32,1,128]{2,1,0:T(1,128)S(1)}, u32[]{:S(2)}, u32[]{:S(2)}) %all-to-all-start.1) | async-done | bytes 16416 | tf_op jit(solution)/shard_map/all_to_all | solution.py:45
  69.6 1.9 %collective-permute-start.4 = (f32[2,1,4,24,256]{4,3,2,1,0:T(8,128)S(1)}, f32[2,1,4,24,256]{4,3,2,1,0:T(8,128)S(1)}, u32[]{:S(2)}, u32[]{:S(2)}) collective-permute-start(f32[2,1,4,24,256]{4,3,2,1,0:T(8,128)S(1)} %maximum_bitcast_fusion.6), channel_id=1, source_target_pairs={{0,1},{1,0},{2,3},{3,2},{4,5},{5,4},{6,7},{7,6},{8,9},{9,8},{10,11... | collective-permute-start | bytes 589832 | tf_op jit(solution)/shard_map/ppermute | solution.py:23
  75.5 7.2 %collective-permute-start.6 = (f32[2,1,4,24,256]{4,3,2,1,0:T(8,128)S(1)}, f32[2,1,4,24,256]{4,3,2,1,0:T(8,128)S(1)}, u32[]{:S(2)}, u32[]{:S(2)}) collective-permute-start(f32[2,1,4,24,256]{4,3,2,1,0:T(8,128)S(1)} %maximum_bitcast_fusion.7), channel_id=1, source_target_pairs={{0,1},{1,0},{2,3},{3,2},{4,5},{5,4},{6,7},{7,6},{8,9},{9,8},{10,11... | collective-permute-start | bytes 589832 | tf_op jit(solution)/shard_map/ppermute | solution.py:23
  89.4 7.3 %collective-permute-start.8 = (f32[3,1,4,24,256]{4,3,2,1,0:T(8,128)S(1)}, f32[3,1,4,24,256]{4,3,2,1,0:T(8,128)S(1)}, u32[]{:S(2)}, u32[]{:S(2)}) collective-permute-start(f32[3,1,4,24,256]{4,3,2,1,0:T(8,128)S(1)} %maximum_bitcast_fusion.2), channel_id=1, source_target_pairs={{0,1},{1,0},{2,3},{3,2},{4,5},{5,4},{6,7},{7,6},{8,9},{9,8},{10,11... | collective-permute-start | bytes 884744 | tf_op jit(solution)/shard_map/ppermute | solution.py:23
  99.9 9.3 %collective-permute-start.10 = (f32[3,1,4,24,256]{4,3,2,1,0:T(8,128)S(1)}, f32[3,1,4,24,256]{4,3,2,1,0:T(8,128)S(1)}, u32[]{:S(2)}, u32[]{:S(2)}) collective-permute-start(f32[3,1,4,24,256]{4,3,2,1,0:T(8,128)S(1)} %maximum_bitcast_fusion.3), channel_id=1, source_target_pairs={{0,1},{1,0},{2,3},{3,2},{4,5},{5,4},{6,7},{7,6},{8,9},{9,8},{10,11... | collective-permute-start | bytes 884744 | tf_op jit(solution)/shard_map/ppermute | solution.py:23
  115.7 7.8 %collective-permute-start.12 = (f32[4,1,4,24,256]{4,3,2,1,0:T(8,128)S(1)}, f32[4,1,4,24,256]{4,3,2,1,0:T(8,128)}, u32[]{:S(2)}, u32[]{:S(2)}) collective-permute-start(f32[4,1,4,24,256]{4,3,2,1,0:T(8,128)S(1)} %maximum_bitcast_fusion), channel_id=1, source_target_pairs={{0,1},{1,0},{2,3},{3,2},{4,5},{5,4},{6,7},{7,6},{8,9},{9,8},{10,11... | collective-permute-start | bytes 1179656 | tf_op jit(solution)/shard_map/ppermute | solution.py:23
  124.9 1.1 bitcast_select_fusion.2
  128.7 9.9 %collective-permute-start.14 = (f32[4,1,4,24,256]{4,3,2,1,0:T(8,128)S(1)}, f32[4,1,4,24,256]{4,3,2,1,0:T(8,128)S(1)}, u32[]{:S(2)}, u32[]{:S(2)}) collective-permute-start(f32[4,1,4,24,256]{4,3,2,1,0:T(8,128)S(1)} %maximum_bitcast_fusion.1), channel_id=1, source_target_pairs={{0,1},{1,0},{2,3},{3,2},{4,5},{5,4},{6,7},{7,6},{8,9},{9,8},{10,11... | collective-permute-start | bytes 1179656 | tf_op jit(solution)/shard_map/ppermute | solution.py:23
  139.2 1.3 fusion.44
  141.5 1.1 maximum_maximum_fusion.1
  144.1 1.8 %fusion.68 = f32[4,1,4,12,256]{4,3,2,0,1:T(8,128)S(1)} fusion(f32[4,1,4,12,256]{4,3,2,0,1:T(8,128)} %fusion.55, f32[4,1,4,12,256]{4,3,2,0,1:T(8,128)} %fusion.44, f32[4,1,4,24,256]{4,3,2,0,1:T(8,128)S(1)} %get-tuple-element.382, f32[4,1,8,24,256]{4,3,2,0,1:T(8,128)} %get-tuple-element.390, f32[4,1,8,24,256]{4,3,2,0,1:T(8,128)S(1)} %get-tuple-element.389, ...), kind=kLoop, calls=%fused_computation.354 | loop fusion | flops 835584 | bytes 2457600 | tf_op jit(solution)/shard_map/mul | solution.py:218
  148.4 8.8 %all-to-all-start.2 = ((f32[32,1,896]{2,1,0:T(1,128)}), f32[32,1,896]{2,1,0:T(1,128)S(1)}, u32[]{:S(2)}, u32[]{:S(2)}) async-start(f32[32,1,896]{2,1,0:T(1,128)} %all_to_all.29), calls=%async_computation.2 | async-start | bytes 229376 | tf_op jit(solution)/shard_map/all_to_all | solution.py:264
  159.0 6.3 %all-to-all-done.2 = f32[32,1,896]{2,1,0:T(1,128)S(1)} async-done(((f32[32,1,896]{2,1,0:T(1,128)}), f32[32,1,896]{2,1,0:T(1,128)S(1)}, u32[]{:S(2)}, u32[]{:S(2)}) %all-to-all-start.2) | async-done | bytes 114720 | tf_op jit(solution)/shard_map/all_to_all | solution.py:264
  (346 shorter events, 51.0 us)
Async XLA Ops:
  7.7 19.6 %all-to-all-start = ((f32[32,1,2688]{2,1,0:T(1,128)}), f32[32,1,2688]{2,1,0:T(1,128)S(1)}, u32[]{:S(2)}, u32[]{:S(2)}) async-start(f32[32,1,2688]{2,1,0:T(1,128)} %reshape.1017), calls=%async_computation | async-start | bytes 688128 | tf_op jit(solution)/shard_map/all_to_all | solution.py:103
  17.3 33.3 %copy-start.29 = (pred[128]{0:T(512)(128)(4,1)}, pred[128]{0:T(512)(128)(4,1)S(1)}, u32[]{:S(2)}) copy-start(pred[128]{0:T(512)(128)(4,1)S(1)} %get-tuple-element.373) | copy-start | bytes 388
  17.3 33.3 %copy-start.38 = (s32[128]{0:T(128)}, s32[128]{0:T(128)S(1)}, u32[]{:S(2)}) copy-start(s32[128]{0:T(128)S(1)} %fusion.1122) | copy-start | bytes 1540
  35.7 2.9 %collective-permute-start.1 = (f32[2,1,4,24,256]{4,3,2,1,0:T(8,128)S(1)}, f32[2,1,4,24,256]{4,3,2,1,0:T(8,128)S(1)}, u32[]{:S(2)}, u32[]{:S(2)}) collective-permute-start(f32[2,1,4,24,256]{4,3,2,1,0:T(8,128)S(1)} %maximum_bitcast_fusion.4), channel_id=1, source_target_pairs={{1,2},{3,4},{5,6},{7,8},{9,10},{11,12},{13,14},{15,16},{17,18},{19... | collective-permute-start | bytes 589832 | tf_op jit(solution)/shard_map/ppermute | solution.py:24
  36.4 2.8 %collective-permute-start = (f32[2,1,4,24,256]{4,3,2,1,0:T(8,128)S(1)}, f32[2,1,4,24,256]{4,3,2,1,0:T(8,128)S(1)}, u32[]{:S(2)}, u32[]{:S(2)}) collective-permute-start(f32[2,1,4,24,256]{4,3,2,1,0:T(8,128)S(1)} %maximum_bitcast_fusion.4), channel_id=1, source_target_pairs={{0,1},{1,0},{2,3},{3,2},{4,5},{5,4},{6,7},{7,6},{8,9},{9,8},{10,11... | collective-permute-start | bytes 589832 | tf_op jit(solution)/shard_map/ppermute | solution.py:23
  40.4 8.5 %collective-permute-start.3 = (f32[2,1,4,24,256]{4,3,2,1,0:T(8,128)S(1)}, f32[2,1,4,24,256]{4,3,2,1,0:T(8,128)S(1)}, u32[]{:S(2)}, u32[]{:S(2)}) collective-permute-start(f32[2,1,4,24,256]{4,3,2,1,0:T(8,128)S(1)} %maximum_bitcast_fusion.5), channel_id=1, source_target_pairs={{1,2},{3,4},{5,6},{7,8},{9,10},{11,12},{13,14},{15,16},{17,18},{19... | collective-permute-start | bytes 589832 | tf_op jit(solution)/shard_map/ppermute | solution.py:24
  41.1 8.4 %collective-permute-start.2 = (f32[2,1,4,24,256]{4,3,2,1,0:T(8,128)S(1)}, f32[2,1,4,24,256]{4,3,2,1,0:T(8,128)S(1)}, u32[]{:S(2)}, u32[]{:S(2)}) collective-permute-start(f32[2,1,4,24,256]{4,3,2,1,0:T(8,128)S(1)} %maximum_bitcast_fusion.5), channel_id=1, source_target_pairs={{0,1},{1,0},{2,3},{3,2},{4,5},{5,4},{6,7},{7,6},{8,9},{9,8},{10,11... | collective-permute-start | bytes 589832 | tf_op jit(solution)/shard_map/ppermute | solution.py:23
  49.7 17.2 %copy-start.27 = (f32[4,1,128]{2,1,0:T(1,128)S(1)}, f32[4,1,128]{2,1,0:T(1,128)}, u32[]{:S(2)}) copy-start(f32[4,1,128]{2,1,0:T(1,128)} %param.41) | copy-start | bytes 6148
  49.7 18.5 %copy-start.24 = (s32[4,256]{1,0:T(4,128)S(1)}, s32[4,256]{1,0:T(4,128)}, u32[]{:S(2)}) copy-start(s32[4,256]{1,0:T(4,128)} %multiply_add_fusion.25) | copy-start | bytes 12292
  51.0 17.1 %copy-start.39 = (s32[128]{0:T(128)S(1)}, s32[128]{0:T(128)}, u32[]{:S(2)}) copy-start(s32[128]{0:T(128)} %copy-done.38) | copy-start | bytes 1540
  51.7 15.1 %all-to-all-start.1 = ((f32[32,1,128]{2,1,0:T(1,128)}), f32[32,1,128]{2,1,0:T(1,128)S(1)}, u32[]{:S(2)}, u32[]{:S(2)}) async-start(f32[32,1,128]{2,1,0:T(1,128)} %broadcast_in_dim.6), calls=%async_computation.1 | async-start | bytes 32768 | tf_op jit(solution)/shard_map/all_to_all | solution.py:45
  68.7 3.6 %collective-permute-start.5 = (f32[2,1,4,24,256]{4,3,2,1,0:T(8,128)S(1)}, f32[2,1,4,24,256]{4,3,2,1,0:T(8,128)S(1)}, u32[]{:S(2)}, u32[]{:S(2)}) collective-permute-start(f32[2,1,4,24,256]{4,3,2,1,0:T(8,128)S(1)} %maximum_bitcast_fusion.6), channel_id=1, source_target_pairs={{1,2},{3,4},{5,6},{7,8},{9,10},{11,12},{13,14},{15,16},{17,18},{19... | collective-permute-start | bytes 589832 | tf_op jit(solution)/shard_map/ppermute | solution.py:24
  69.6 3.0 %collective-permute-start.4 = (f32[2,1,4,24,256]{4,3,2,1,0:T(8,128)S(1)}, f32[2,1,4,24,256]{4,3,2,1,0:T(8,128)S(1)}, u32[]{:S(2)}, u32[]{:S(2)}) collective-permute-start(f32[2,1,4,24,256]{4,3,2,1,0:T(8,128)S(1)} %maximum_bitcast_fusion.6), channel_id=1, source_target_pairs={{0,1},{1,0},{2,3},{3,2},{4,5},{5,4},{6,7},{7,6},{8,9},{9,8},{10,11... | collective-permute-start | bytes 589832 | tf_op jit(solution)/shard_map/ppermute | solution.py:23
  74.8 8.3 %collective-permute-start.7 = (f32[2,1,4,24,256]{4,3,2,1,0:T(8,128)S(1)}, f32[2,1,4,24,256]{4,3,2,1,0:T(8,128)S(1)}, u32[]{:S(2)}, u32[]{:S(2)}) collective-permute-start(f32[2,1,4,24,256]{4,3,2,1,0:T(8,128)S(1)} %maximum_bitcast_fusion.7), channel_id=1, source_target_pairs={{1,2},{3,4},{5,6},{7,8},{9,10},{11,12},{13,14},{15,16},{17,18},{19... | collective-permute-start | bytes 589832 | tf_op jit(solution)/shard_map/ppermute | solution.py:24
  75.5 8.2 %collective-permute-start.6 = (f32[2,1,4,24,256]{4,3,2,1,0:T(8,128)S(1)}, f32[2,1,4,24,256]{4,3,2,1,0:T(8,128)S(1)}, u32[]{:S(2)}, u32[]{:S(2)}) collective-permute-start(f32[2,1,4,24,256]{4,3,2,1,0:T(8,128)S(1)} %maximum_bitcast_fusion.7), channel_id=1, source_target_pairs={{0,1},{1,0},{2,3},{3,2},{4,5},{5,4},{6,7},{7,6},{8,9},{9,8},{10,11... | collective-permute-start | bytes 589832 | tf_op jit(solution)/shard_map/ppermute | solution.py:23
  88.8 8.6 %collective-permute-start.9 = (f32[3,1,4,24,256]{4,3,2,1,0:T(8,128)S(1)}, f32[3,1,4,24,256]{4,3,2,1,0:T(8,128)S(1)}, u32[]{:S(2)}, u32[]{:S(2)}) collective-permute-start(f32[3,1,4,24,256]{4,3,2,1,0:T(8,128)S(1)} %maximum_bitcast_fusion.2), channel_id=1, source_target_pairs={{1,2},{3,4},{5,6},{7,8},{9,10},{11,12},{13,14},{15,16},{17,18},{19... | collective-permute-start | bytes 884744 | tf_op jit(solution)/shard_map/ppermute | solution.py:24
  89.4 8.6 %collective-permute-start.8 = (f32[3,1,4,24,256]{4,3,2,1,0:T(8,128)S(1)}, f32[3,1,4,24,256]{4,3,2,1,0:T(8,128)S(1)}, u32[]{:S(2)}, u32[]{:S(2)}) collective-permute-start(f32[3,1,4,24,256]{4,3,2,1,0:T(8,128)S(1)} %maximum_bitcast_fusion.2), channel_id=1, source_target_pairs={{0,1},{1,0},{2,3},{3,2},{4,5},{5,4},{6,7},{7,6},{8,9},{9,8},{10,11... | collective-permute-start | bytes 884744 | tf_op jit(solution)/shard_map/ppermute | solution.py:23
  99.2 12.0 %collective-permute-start.11 = (f32[3,1,4,24,256]{4,3,2,1,0:T(8,128)S(1)}, f32[3,1,4,24,256]{4,3,2,1,0:T(8,128)S(1)}, u32[]{:S(2)}, u32[]{:S(2)}) collective-permute-start(f32[3,1,4,24,256]{4,3,2,1,0:T(8,128)S(1)} %maximum_bitcast_fusion.3), channel_id=1, source_target_pairs={{1,2},{3,4},{5,6},{7,8},{9,10},{11,12},{13,14},{15,16},{17,18},{19... | collective-permute-start | bytes 884744 | tf_op jit(solution)/shard_map/ppermute | solution.py:24
  99.9 11.3 %collective-permute-start.10 = (f32[3,1,4,24,256]{4,3,2,1,0:T(8,128)S(1)}, f32[3,1,4,24,256]{4,3,2,1,0:T(8,128)S(1)}, u32[]{:S(2)}, u32[]{:S(2)}) collective-permute-start(f32[3,1,4,24,256]{4,3,2,1,0:T(8,128)S(1)} %maximum_bitcast_fusion.3), channel_id=1, source_target_pairs={{0,1},{1,0},{2,3},{3,2},{4,5},{5,4},{6,7},{7,6},{8,9},{9,8},{10,11... | collective-permute-start | bytes 884744 | tf_op jit(solution)/shard_map/ppermute | solution.py:23
  115.0 9.5 %collective-permute-start.13 = (f32[4,1,4,24,256]{4,3,2,1,0:T(8,128)S(1)}, f32[4,1,4,24,256]{4,3,2,1,0:T(8,128)S(1)}, u32[]{:S(2)}, u32[]{:S(2)}) collective-permute-start(f32[4,1,4,24,256]{4,3,2,1,0:T(8,128)S(1)} %maximum_bitcast_fusion), channel_id=1, source_target_pairs={{1,2},{3,4},{5,6},{7,8},{9,10},{11,12},{13,14},{15,16},{17,18},{19... | collective-permute-start | bytes 1179656 | tf_op jit(solution)/shard_map/ppermute | solution.py:24
  115.7 9.3 %collective-permute-start.12 = (f32[4,1,4,24,256]{4,3,2,1,0:T(8,128)S(1)}, f32[4,1,4,24,256]{4,3,2,1,0:T(8,128)}, u32[]{:S(2)}, u32[]{:S(2)}) collective-permute-start(f32[4,1,4,24,256]{4,3,2,1,0:T(8,128)S(1)} %maximum_bitcast_fusion), channel_id=1, source_target_pairs={{0,1},{1,0},{2,3},{3,2},{4,5},{5,4},{6,7},{7,6},{8,9},{9,8},{10,11... | collective-permute-start | bytes 1179656 | tf_op jit(solution)/shard_map/ppermute | solution.py:23
  127.8 13.7 %collective-permute-start.15 = (f32[4,1,4,24,256]{4,3,2,1,0:T(8,128)S(1)}, f32[4,1,4,24,256]{4,3,2,1,0:T(8,128)S(1)}, u32[]{:S(2)}, u32[]{:S(2)}) collective-permute-start(f32[4,1,4,24,256]{4,3,2,1,0:T(8,128)S(1)} %maximum_bitcast_fusion.1), channel_id=1, source_target_pairs={{1,2},{3,4},{5,6},{7,8},{9,10},{11,12},{13,14},{15,16},{17,18},{19... | collective-permute-start | bytes 1179656 | tf_op jit(solution)/shard_map/ppermute | solution.py:24
  128.7 12.7 %collective-permute-start.14 = (f32[4,1,4,24,256]{4,3,2,1,0:T(8,128)S(1)}, f32[4,1,4,24,256]{4,3,2,1,0:T(8,128)S(1)}, u32[]{:S(2)}, u32[]{:S(2)}) collective-permute-start(f32[4,1,4,24,256]{4,3,2,1,0:T(8,128)S(1)} %maximum_bitcast_fusion.1), channel_id=1, source_target_pairs={{0,1},{1,0},{2,3},{3,2},{4,5},{5,4},{6,7},{7,6},{8,9},{9,8},{10,11... | collective-permute-start | bytes 1179656 | tf_op jit(solution)/shard_map/ppermute | solution.py:23
  148.4 16.8 %all-to-all-start.2 = ((f32[32,1,896]{2,1,0:T(1,128)}), f32[32,1,896]{2,1,0:T(1,128)S(1)}, u32[]{:S(2)}, u32[]{:S(2)}) async-start(f32[32,1,896]{2,1,0:T(1,128)} %all_to_all.29), calls=%async_computation.2 | async-start | bytes 229376 | tf_op jit(solution)/shard_map/all_to_all | solution.py:264
  (40 other events, 314.6 us)

commit v16 on v12

--- a/solution.py
+++ b/solution.py
@@ -38,6 +38,23 @@
     if extra == 0:
         return field
     return jnp.concatenate([field, jnp.zeros((extra,) + field.shape[1:], field.dtype)])
+
+
+def halo_pair(rock_fields, water_field):
+    rock_waves, water_waves = rock_fields[0].shape[0], water_field.shape[0]
+    rock_pack = jnp.concatenate(rock_fields, axis=DEPTH_AXIS)
+    if rock_pack.shape[1:] == water_field.shape[1:]:
+        (padded,) = halo_rows([jnp.concatenate([rock_pack, water_field])])
+        rock_pad, water_pad = padded[:rock_waves], padded[rock_waves:]
+    else:
+        rock_pad, water_pad = halo_rows([fill_waves(rock_pack, water_waves), water_field])
+        rock_pad = rock_pad[:rock_waves]
+    out, start = [], 0
+    for f in rock_fields:
+        depth = f.shape[DEPTH_AXIS]
+        out.append(lax.slice_in_dim(rock_pad, start, start + depth, axis=DEPTH_AXIS))
+        start += depth
+    return out + [water_pad]
 
 
 def gather_sum(partial, parts):
@@ -170,10 +187,7 @@
                 derive(sig_zz, 3, True),
             )
         )
-        sxy_pad, syy_pad, syz_pad, p_pad = halo_rows(
-            [fill_waves(f, water_waves) for f in (sig_xy, sig_yy, sig_yz)] + [pressure]
-        )
-        sxy_pad, syy_pad, syz_pad = [f[:rock_waves] for f in (sxy_pad, syy_pad, syz_pad)]
+        sxy_pad, syy_pad, syz_pad, p_pad = halo_pair([sig_xy, sig_yy, sig_yz], pressure)
         vel_x = vel_x + TIME_STEP * buoy * (dx_sxx + stencil(sxy_pad, 2, False) + dz_sxz)
         vel_y = vel_y + TIME_STEP * buoy * (dx_sxy + stencil(syy_pad, 2, True) + dz_syz)
         vel_z = vel_z + TIME_STEP * buoy * (dx_sxz + stencil(syz_pad, 2, False) + dz_szz)
@@ -192,10 +206,7 @@
                 derive(vel_x, 3, True) + derive(vel_z, 4, True),
             )
         )
-        vx_pad, vy_pad, vz_pad, uy_pad = halo_rows(
-            [fill_waves(f, water_waves) for f in (vel_x, vel_y, vel_z)] + [flow_y]
-        )
-        vx_pad, vy_pad, vz_pad = [f[:rock_waves] for f in (vx_pad, vy_pad, vz_pad)]
+        vx_pad, vy_pad, vz_pad, uy_pad = halo_pair([vel_x, vel_y, vel_z], flow_y)
         strain_y = stencil(vy_pad, 2, False)
         dilation = strain_x + strain_y + strain_z
         shear_xy = stencil(vx_pad, 2, True) + dx_vy

time: 170 us -> 177 us (1.041)
  other arithmetic: 35.5 us -> 40.4 us
  local copies, waits for them, and re-layouts: 20.8 us -> 23.7 us
  starting transfers between devices: 81.9 us -> 79.7 us
    add x32, other arithmetic: 7.37 us -> 9.76 us  [stencil(): summed = addend if summed is None else summed + addend]
    unnamed x76 -> x94, local copies, waits for them, and re-layouts: 8.88 us -> 8.94 us
  transfers between devices with their start and end apart: 19 -> 19, of which waited for: 8 -> 8; matrix products, arithmetic and copies ran while one was open for 8% -> 7% of each run, Pallas kernels for 0% -> 0%
where the time goes in v16:
time: 177 us; the launch traced here: 176 us
  starting transfers between devices  79.7 us (45%)
  other arithmetic  40.4 us (23%)
  waiting for transfers between devices  24.6 us (14%)
  local copies, waits for them, and re-layouts  23.7 us (13%)
  matrix products  4.12 us (2%)
  between operations  3.52 us (2%)
    ppermute x8, starting transfers between devices, halo_rows(): got_within = lax.ppermute(jnp.where(odd, first, last), 'gx', within)  51 us
    add x32, other arithmetic, stencil(): summed = addend if summed is None else summed + addend  9.76 us
    unnamed x94, local copies, waits for them, and re-layouts  8.94 us
    all_to_all x1, waiting for transfers between devices, on_device(): lax.all_to_all(rock_in, 'gx', split_axis=3, concat_axis=1, tiled=True)  8.36 us
    all_to_all x1, starting transfers between devices, gather_sum(): return jnp.sum(lax.all_to_all(copies, 'gx', 0, 0, tiled=True), axis=0)  8.06 us
    all_to_all x1, starting transfers between devices, on_device(): got = lax.all_to_all(packed, 'gx', 0, 0, tiled=True)  7.53 us
    all_to_all x1, waiting for transfers between devices, on_device(): got = lax.all_to_all(packed, 'gx', 0, 0, tiled=True)  7.33 us
    all_to_all x1, starting transfers between devices, on_device(): lax.all_to_all(rock_in, 'gx', split_axis=3, concat_axis=1, tiled=True)  7.3 us
  transfers between devices with their start and end apart: 19, of which 8 were waited for; matrix products, arithmetic and copies ran while one was open for 7% of the time, Pallas kernels for 0%

profile of v16, /device:TPU:0, one launch (start us, length us, event | category | flops | bytes accessed | tf_op | source)
XLA Modules:
  0.0 176.0 jit_solution(12692034365854612007)
XLA Ops:
  3.1 1.9 %copy.3574 = f32[21,8,4,128]{0,1,2,3:T(8,128)S(1)} copy(f32[21,8,4,128]{3,1,2,0:T(8,128)S(1)} %pad_maximum_fusion.10) | data formatting | bytes 688128 | tf_op jit(solution)/shard_map/concatenate | solution.py:112
  5.1 2.7 %reshape.1017 = f32[32,1,2688]{2,1,0:T(1,128)} reshape(f32[128,4,8,21]{3,2,1,0:T(8,128)S(1)} %bitcast.267) | data formatting | bytes 688128
  7.7 7.3 %all-to-all-start = ((f32[32,1,2688]{2,1,0:T(1,128)}), f32[32,1,2688]{2,1,0:T(1,128)S(1)}, u32[]{:S(2)}, u32[]{:S(2)}) async-start(f32[32,1,2688]{2,1,0:T(1,128)} %reshape.1017), calls=%async_computation | async-start | bytes 688128 | tf_op jit(solution)/shard_map/all_to_all | solution.py:120
  19.0 8.4 %all-to-all-done = f32[32,1,2688]{2,1,0:T(1,128)S(1)} async-done(((f32[32,1,2688]{2,1,0:T(1,128)}), f32[32,1,2688]{2,1,0:T(1,128)S(1)}, u32[]{:S(2)}, u32[]{:S(2)}) %all-to-all-start) | async-done | bytes 344096 | tf_op jit(solution)/shard_map/all_to_all | solution.py:120
  27.9 1.5 reduce.33
  29.3 2.3 %reshape.1018 = f32[128,4,8,21]{3,2,1,0:T(8,128)S(1)} reshape(f32[32,2688]{1,0:T(8,128)S(1)} %reduce.33) | data formatting | bytes 688128
  31.6 1.5 copy.3743
  33.1 2.3 %copy.3577 = f32[21,256,4,4]{1,2,3,0:T(4,128)S(1)} copy(f32[21,256,4,4]{0,1,3,2:T(8,128)} %bitcast.269) | data formatting | bytes 688128 | tf_op jit(solution)/shard_map/all_to_all | solution.py:120
  36.6 1.7 collective-permute-start
  41.6 7.3 %collective-permute-start.2 = (f32[4,1,4,12,256]{4,2,3,1,0:T(4,128)S(1)}, f32[4,1,4,12,256]{4,2,3,1,0:T(4,128)S(1)}, u32[]{:S(2)}, u32[]{:S(2)}) collective-permute-start(f32[4,1,4,12,256]{4,2,3,1,0:T(4,128)S(1)} %copy.3585), channel_id=1, source_target_pairs={{0,1},{1,0},{2,3},{3,2},{4,5},{5,4},{6,7},{7,6},{8,9},{9,8},{10,11... | collective-permute-start | bytes 589832 | tf_op jit(solution)/shard_map/ppermute | solution.py:23
  55.7 8.1 %all-to-all-start.1 = ((f32[32,1,128]{2,1,0:T(1,128)}), f32[32,1,128]{2,1,0:T(1,128)S(1)}, u32[]{:S(2)}, u32[]{:S(2)}) async-start(f32[32,1,128]{2,1,0:T(1,128)} %broadcast_in_dim.6), calls=%async_computation.1 | async-start | bytes 32768 | tf_op jit(solution)/shard_map/all_to_all | solution.py:62
  64.6 6.3 %all-to-all-done.1 = f32[32,1,128]{2,1,0:T(1,128)S(1)} async-done(((f32[32,1,128]{2,1,0:T(1,128)}), f32[32,1,128]{2,1,0:T(1,128)S(1)}, u32[]{:S(2)}, u32[]{:S(2)}) %all-to-all-start.1) | async-done | bytes 16416 | tf_op jit(solution)/shard_map/all_to_all | solution.py:62
  73.7 1.9 %collective-permute-start.4 = (f32[4,1,4,12,256]{4,2,3,1,0:T(4,128)S(1)}, f32[4,1,4,12,256]{4,2,3,1,0:T(4,128)S(1)}, u32[]{:S(2)}, u32[]{:S(2)}) collective-permute-start(f32[4,1,4,12,256]{4,2,3,1,0:T(4,128)S(1)} %copy.3593), channel_id=1, source_target_pairs={{0,1},{1,0},{2,3},{3,2},{4,5},{5,4},{6,7},{7,6},{8,9},{9,8},{10,11... | collective-permute-start | bytes 589832 | tf_op jit(solution)/shard_map/ppermute | solution.py:23
  81.2 7.2 %collective-permute-start.6 = (f32[4,1,4,12,256]{4,2,3,1,0:T(4,128)S(1)}, f32[4,1,4,12,256]{4,2,3,1,0:T(4,128)S(1)}, u32[]{:S(2)}, u32[]{:S(2)}) collective-permute-start(f32[4,1,4,12,256]{4,2,3,1,0:T(4,128)S(1)} %copy.3599), channel_id=1, source_target_pairs={{0,1},{1,0},{2,3},{3,2},{4,5},{5,4},{6,7},{7,6},{8,9},{9,8},{10,11... | collective-permute-start | bytes 589832 | tf_op jit(solution)/shard_map/ppermute | solution.py:23
  92.6 1.1 fusion.10
  95.9 7.3 %collective-permute-start.8 = (f32[5,1,4,12,256]{4,2,3,1,0:T(4,128)S(1)}, f32[5,1,4,12,256]{4,2,3,1,0:T(4,128)S(1)}, u32[]{:S(2)}, u32[]{:S(2)}) collective-permute-start(f32[5,1,4,12,256]{4,2,3,1,0:T(4,128)S(1)} %copy.3608), channel_id=1, source_target_pairs={{0,1},{1,0},{2,3},{3,2},{4,5},{5,4},{6,7},{7,6},{8,9},{9,8},{10,11... | collective-permute-start | bytes 737288 | tf_op jit(solution)/shard_map/ppermute | solution.py:23
  106.5 8.3 %collective-permute-start.10 = (f32[5,1,4,12,256]{4,2,3,1,0:T(4,128)S(1)}, f32[5,1,4,12,256]{4,2,3,1,0:T(4,128)S(1)}, u32[]{:S(2)}, u32[]{:S(2)}) collective-permute-start(f32[5,1,4,12,256]{4,2,3,1,0:T(4,128)S(1)} %copy.3614), channel_id=1, source_target_pairs={{0,1},{1,0},{2,3},{3,2},{4,5},{5,4},{6,7},{7,6},{8,9},{9,8},{10,11... | collective-permute-start | bytes 737288 | tf_op jit(solution)/shard_map/ppermute | solution.py:23
  123.0 7.9 %collective-permute-start.12 = (f32[7,1,4,12,256]{4,2,3,1,0:T(4,128)S(1)}, f32[7,1,4,12,256]{4,2,3,1,0:T(4,128)S(1)}, u32[]{:S(2)}, u32[]{:S(2)}) collective-permute-start(f32[7,1,4,12,256]{4,2,3,1,0:T(4,128)S(1)} %copy.3626), channel_id=1, source_target_pairs={{0,1},{1,0},{2,3},{3,2},{4,5},{5,4},{6,7},{7,6},{8,9},{9,8},{10,11... | collective-permute-start | bytes 1032200 | tf_op jit(solution)/shard_map/ppermute | solution.py:23
  135.3 9.3 %collective-permute-start.14 = (f32[7,1,4,12,256]{4,2,3,1,0:T(4,128)S(1)}, f32[7,1,4,12,256]{4,2,3,1,0:T(4,128)S(1)}, u32[]{:S(2)}, u32[]{:S(2)}) collective-permute-start(f32[7,1,4,12,256]{4,2,3,1,0:T(4,128)S(1)} %copy.3632), channel_id=1, source_target_pairs={{0,1},{1,0},{2,3},{3,2},{4,5},{5,4},{6,7},{7,6},{8,9},{9,8},{10,11... | collective-permute-start | bytes 1032200 | tf_op jit(solution)/shard_map/ppermute | solution.py:23
  145.1 1.2 fusion.44
  147.6 1.2 maximum_maximum_fusion.1
  151.9 1.6 fusion.68
  156.7 7.5 %all-to-all-start.2 = ((f32[32,1,896]{2,1,0:T(1,128)}), f32[32,1,896]{2,1,0:T(1,128)S(1)}, u32[]{:S(2)}, u32[]{:S(2)}) async-start(f32[32,1,896]{2,1,0:T(1,128)} %all_to_all.29), calls=%async_computation.2 | async-start | bytes 229376 | tf_op jit(solution)/shard_map/all_to_all | solution.py:276
  164.9 7.3 %all-to-all-done.2 = f32[32,1,896]{2,1,0:T(1,128)S(1)} async-done(((f32[32,1,896]{2,1,0:T(1,128)}), f32[32,1,896]{2,1,0:T(1,128)S(1)}, u32[]{:S(2)}, u32[]{:S(2)}) %all-to-all-start.2) | async-done | bytes 114720 | tf_op jit(solution)/shard_map/all_to_all | solution.py:276
  (331 shorter events, 59.4 us)
Async XLA Ops:
  7.7 19.6 %all-to-all-start = ((f32[32,1,2688]{2,1,0:T(1,128)}), f32[32,1,2688]{2,1,0:T(1,128)S(1)}, u32[]{:S(2)}, u32[]{:S(2)}) async-start(f32[32,1,2688]{2,1,0:T(1,128)} %reshape.1017), calls=%async_computation | async-start | bytes 688128 | tf_op jit(solution)/shard_map/all_to_all | solution.py:120
  35.9 2.9 %collective-permute-start.1 = (f32[4,1,4,12,256]{4,2,3,1,0:T(4,128)S(1)}, f32[4,1,4,12,256]{4,2,3,1,0:T(4,128)S(1)}, u32[]{:S(2)}, u32[]{:S(2)}) collective-permute-start(f32[4,1,4,12,256]{4,2,3,1,0:T(4,128)S(1)} %copy.3578), channel_id=1, source_target_pairs={{1,2},{3,4},{5,6},{7,8},{9,10},{11,12},{13,14},{15,16},{17,18},{19... | collective-permute-start | bytes 589832 | tf_op jit(solution)/shard_map/ppermute | solution.py:24
  36.6 2.8 %collective-permute-start = (f32[4,1,4,12,256]{4,2,3,1,0:T(4,128)S(1)}, f32[4,1,4,12,256]{4,2,3,1,0:T(4,128)S(1)}, u32[]{:S(2)}, u32[]{:S(2)}) collective-permute-start(f32[4,1,4,12,256]{4,2,3,1,0:T(4,128)S(1)} %copy.3578), channel_id=1, source_target_pairs={{0,1},{1,0},{2,3},{3,2},{4,5},{5,4},{6,7},{7,6},{8,9},{9,8},{10,11... | collective-permute-start | bytes 589832 | tf_op jit(solution)/shard_map/ppermute | solution.py:23
  40.9 8.5 %collective-permute-start.3 = (f32[4,1,4,12,256]{4,2,3,1,0:T(4,128)S(1)}, f32[4,1,4,12,256]{4,2,3,1,0:T(4,128)S(1)}, u32[]{:S(2)}, u32[]{:S(2)}) collective-permute-start(f32[4,1,4,12,256]{4,2,3,1,0:T(4,128)S(1)} %copy.3585), channel_id=1, source_target_pairs={{1,2},{3,4},{5,6},{7,8},{9,10},{11,12},{13,14},{15,16},{17,18},{19... | collective-permute-start | bytes 589832 | tf_op jit(solution)/shard_map/ppermute | solution.py:24
  41.6 8.4 %collective-permute-start.2 = (f32[4,1,4,12,256]{4,2,3,1,0:T(4,128)S(1)}, f32[4,1,4,12,256]{4,2,3,1,0:T(4,128)S(1)}, u32[]{:S(2)}, u32[]{:S(2)}) collective-permute-start(f32[4,1,4,12,256]{4,2,3,1,0:T(4,128)S(1)} %copy.3585), channel_id=1, source_target_pairs={{0,1},{1,0},{2,3},{3,2},{4,5},{5,4},{6,7},{7,6},{8,9},{9,8},{10,11... | collective-permute-start | bytes 589832 | tf_op jit(solution)/shard_map/ppermute | solution.py:23
  52.2 18.7 %copy-start.22 = (f32[4,1,128]{2,1,0:T(1,128)S(1)}, f32[4,1,128]{2,1,0:T(1,128)}, u32[]{:S(2)}) copy-start(f32[4,1,128]{2,1,0:T(1,128)} %param.41) | copy-start | bytes 6148
  52.2 20.0 %copy-start.18 = (s32[4,256]{1,0:T(4,128)S(1)}, s32[4,256]{1,0:T(4,128)}, u32[]{:S(2)}) copy-start(s32[4,256]{1,0:T(4,128)} %multiply_add_fusion.22) | copy-start | bytes 12292
  55.7 15.1 %all-to-all-start.1 = ((f32[32,1,128]{2,1,0:T(1,128)}), f32[32,1,128]{2,1,0:T(1,128)S(1)}, u32[]{:S(2)}, u32[]{:S(2)}) async-start(f32[32,1,128]{2,1,0:T(1,128)} %broadcast_in_dim.6), calls=%async_computation.1 | async-start | bytes 32768 | tf_op jit(solution)/shard_map/all_to_all | solution.py:62
  72.9 3.6 %collective-permute-start.5 = (f32[4,1,4,12,256]{4,2,3,1,0:T(4,128)S(1)}, f32[4,1,4,12,256]{4,2,3,1,0:T(4,128)S(1)}, u32[]{:S(2)}, u32[]{:S(2)}) collective-permute-start(f32[4,1,4,12,256]{4,2,3,1,0:T(4,128)S(1)} %copy.3593), channel_id=1, source_target_pairs={{1,2},{3,4},{5,6},{7,8},{9,10},{11,12},{13,14},{15,16},{17,18},{19... | collective-permute-start | bytes 589832 | tf_op jit(solution)/shard_map/ppermute | solution.py:24
  73.7 3.0 %collective-permute-start.4 = (f32[4,1,4,12,256]{4,2,3,1,0:T(4,128)S(1)}, f32[4,1,4,12,256]{4,2,3,1,0:T(4,128)S(1)}, u32[]{:S(2)}, u32[]{:S(2)}) collective-permute-start(f32[4,1,4,12,256]{4,2,3,1,0:T(4,128)S(1)} %copy.3593), channel_id=1, source_target_pairs={{0,1},{1,0},{2,3},{3,2},{4,5},{5,4},{6,7},{7,6},{8,9},{9,8},{10,11... | collective-permute-start | bytes 589832 | tf_op jit(solution)/shard_map/ppermute | solution.py:23
  80.5 8.5 %collective-permute-start.7 = (f32[4,1,4,12,256]{4,2,3,1,0:T(4,128)S(1)}, f32[4,1,4,12,256]{4,2,3,1,0:T(4,128)S(1)}, u32[]{:S(2)}, u32[]{:S(2)}) collective-permute-start(f32[4,1,4,12,256]{4,2,3,1,0:T(4,128)S(1)} %copy.3599), channel_id=1, source_target_pairs={{1,2},{3,4},{5,6},{7,8},{9,10},{11,12},{13,14},{15,16},{17,18},{19... | collective-permute-start | bytes 589832 | tf_op jit(solution)/shard_map/ppermute | solution.py:24
  81.2 8.2 %collective-permute-start.6 = (f32[4,1,4,12,256]{4,2,3,1,0:T(4,128)S(1)}, f32[4,1,4,12,256]{4,2,3,1,0:T(4,128)S(1)}, u32[]{:S(2)}, u32[]{:S(2)}) collective-permute-start(f32[4,1,4,12,256]{4,2,3,1,0:T(4,128)S(1)} %copy.3599), channel_id=1, source_target_pairs={{0,1},{1,0},{2,3},{3,2},{4,5},{5,4},{6,7},{7,6},{8,9},{9,8},{10,11... | collective-permute-start | bytes 589832 | tf_op jit(solution)/shard_map/ppermute | solution.py:23
  95.2 8.4 %collective-permute-start.9 = (f32[5,1,4,12,256]{4,2,3,1,0:T(4,128)S(1)}, f32[5,1,4,12,256]{4,2,3,1,0:T(4,128)S(1)}, u32[]{:S(2)}, u32[]{:S(2)}) collective-permute-start(f32[5,1,4,12,256]{4,2,3,1,0:T(4,128)S(1)} %copy.3608), channel_id=1, source_target_pairs={{1,2},{3,4},{5,6},{7,8},{9,10},{11,12},{13,14},{15,16},{17,18},{19... | collective-permute-start | bytes 737288 | tf_op jit(solution)/shard_map/ppermute | solution.py:24
  95.9 8.5 %collective-permute-start.8 = (f32[5,1,4,12,256]{4,2,3,1,0:T(4,128)S(1)}, f32[5,1,4,12,256]{4,2,3,1,0:T(4,128)S(1)}, u32[]{:S(2)}, u32[]{:S(2)}) collective-permute-start(f32[5,1,4,12,256]{4,2,3,1,0:T(4,128)S(1)} %copy.3608), channel_id=1, source_target_pairs={{0,1},{1,0},{2,3},{3,2},{4,5},{5,4},{6,7},{7,6},{8,9},{9,8},{10,11... | collective-permute-start | bytes 737288 | tf_op jit(solution)/shard_map/ppermute | solution.py:23
  105.8 10.4 %collective-permute-start.11 = (f32[5,1,4,12,256]{4,2,3,1,0:T(4,128)S(1)}, f32[5,1,4,12,256]{4,2,3,1,0:T(4,128)S(1)}, u32[]{:S(2)}, u32[]{:S(2)}) collective-permute-start(f32[5,1,4,12,256]{4,2,3,1,0:T(4,128)S(1)} %copy.3614), channel_id=1, source_target_pairs={{1,2},{3,4},{5,6},{7,8},{9,10},{11,12},{13,14},{15,16},{17,18},{19... | collective-permute-start | bytes 737288 | tf_op jit(solution)/shard_map/ppermute | solution.py:24
  106.5 9.7 %collective-permute-start.10 = (f32[5,1,4,12,256]{4,2,3,1,0:T(4,128)S(1)}, f32[5,1,4,12,256]{4,2,3,1,0:T(4,128)S(1)}, u32[]{:S(2)}, u32[]{:S(2)}) collective-permute-start(f32[5,1,4,12,256]{4,2,3,1,0:T(4,128)S(1)} %copy.3614), channel_id=1, source_target_pairs={{0,1},{1,0},{2,3},{3,2},{4,5},{5,4},{6,7},{7,6},{8,9},{9,8},{10,11... | collective-permute-start | bytes 737288 | tf_op jit(solution)/shard_map/ppermute | solution.py:23
  118.4 13.0 %copy-start.7 = (f32[2,1,4,4,256]{4,3,2,0,1:T(4,128)S(1)}, f32[2,1,4,4,256]{4,3,2,0,1:T(4,128)}, u32[]{:S(2)}) copy-start(f32[2,1,4,4,256]{4,3,2,0,1:T(4,128)} %get-tuple-element.326) | copy-start | bytes 98308
  119.2 13.3 %copy-start.5 = (f32[1,1,4,12,256]{4,3,2,0,1:T(8,128)S(1)}, f32[1,1,4,12,256]{4,3,2,0,1:T(8,128)}, u32[]{:S(2)}) copy-start(f32[1,1,4,12,256]{4,3,2,0,1:T(8,128)} %get-tuple-element.397) | copy-start | bytes 147460
  122.3 10.1 %collective-permute-start.13 = (f32[7,1,4,12,256]{4,2,3,1,0:T(4,128)S(1)}, f32[7,1,4,12,256]{4,2,3,1,0:T(4,128)S(1)}, u32[]{:S(2)}, u32[]{:S(2)}) collective-permute-start(f32[7,1,4,12,256]{4,2,3,1,0:T(4,128)S(1)} %copy.3626), channel_id=1, source_target_pairs={{1,2},{3,4},{5,6},{7,8},{9,10},{11,12},{13,14},{15,16},{17,18},{19... | collective-permute-start | bytes 1032200 | tf_op jit(solution)/shard_map/ppermute | solution.py:24
  123.0 9.5 %collective-permute-start.12 = (f32[7,1,4,12,256]{4,2,3,1,0:T(4,128)S(1)}, f32[7,1,4,12,256]{4,2,3,1,0:T(4,128)S(1)}, u32[]{:S(2)}, u32[]{:S(2)}) collective-permute-start(f32[7,1,4,12,256]{4,2,3,1,0:T(4,128)S(1)} %copy.3626), channel_id=1, source_target_pairs={{0,1},{1,0},{2,3},{3,2},{4,5},{5,4},{6,7},{7,6},{8,9},{9,8},{10,11... | collective-permute-start | bytes 1032200 | tf_op jit(solution)/shard_map/ppermute | solution.py:23
  134.4 13.0 %collective-permute-start.15 = (f32[7,1,4,12,256]{4,2,3,1,0:T(4,128)S(1)}, f32[7,1,4,12,256]{4,2,3,1,0:T(4,128)S(1)}, u32[]{:S(2)}, u32[]{:S(2)}) collective-permute-start(f32[7,1,4,12,256]{4,2,3,1,0:T(4,128)S(1)} %copy.3632), channel_id=1, source_target_pairs={{1,2},{3,4},{5,6},{7,8},{9,10},{11,12},{13,14},{15,16},{17,18},{19... | collective-permute-start | bytes 1032200 | tf_op jit(solution)/shard_map/ppermute | solution.py:24
  135.3 12.1 %collective-permute-start.14 = (f32[7,1,4,12,256]{4,2,3,1,0:T(4,128)S(1)}, f32[7,1,4,12,256]{4,2,3,1,0:T(4,128)S(1)}, u32[]{:S(2)}, u32[]{:S(2)}) collective-permute-start(f32[7,1,4,12,256]{4,2,3,1,0:T(4,128)S(1)} %copy.3632), channel_id=1, source_target_pairs={{0,1},{1,0},{2,3},{3,2},{4,5},{5,4},{6,7},{7,6},{8,9},{9,8},{10,11... | collective-permute-start | bytes 1032200 | tf_op jit(solution)/shard_map/ppermute | solution.py:23
  153.4 19.4 %copy-start.37 = (f32[1,1,128]{2,1,0:T(1,128)S(1)}, f32[1,1,128]{2,1,0:T(1,128)}, u32[]{:S(2)}) copy-start(f32[1,1,128]{2,1,0:T(1,128)} %copy-done.36) | copy-start | bytes 1540
  156.7 15.6 %all-to-all-start.2 = ((f32[32,1,896]{2,1,0:T(1,128)}), f32[32,1,896]{2,1,0:T(1,128)S(1)}, u32[]{:S(2)}, u32[]{:S(2)}) async-start(f32[32,1,896]{2,1,0:T(1,128)} %all_to_all.29), calls=%async_computation.2 | async-start | bytes 229376 | tf_op jit(solution)/shard_map/all_to_all | solution.py:276
  (33 other events, 186.1 us)
